TPU v7x, 32 devices: a whole 2x2x4 slice. The times are simulated.
32 devices in a mesh: ox: 8 (over z, x), oy: 4 (over y, core).
Axes of the slice: x: 2, y: 2, z: 4, core: 2. Of those that a mesh axis runs over, the one named last changes fastest.
Arguments:
- atm_flux: bfloat16 [4, 40, 1024], P(None, 'oy', 'ox'), may hold values from -6 to 6
- remap_weights: bfloat16 [128, 12, 128, 128], P('ox', 'oy'), may hold values from -0.3125 to 0.3125
- tile_slots: int32 [128, 12], P('ox', 'oy'), may hold values from 0 to 23, as said below
- need_blocks: int32 [64, 12], P('ox', 'oy'), may hold values from -1 to 9, as said below
- send_blocks: int32 [64, 12], P('ox', 'oy'), may hold values from -1 to 9, as said below
- ocean_state: float32 [4, 16, 128, 512], P(None, None, 'ox', 'oy'), may hold values from -6 to 6
- land_mask: int32 [128, 512], P('ox', 'oy'), may hold values 0 or 1
- diffusivity: float32 [16], replicated, may hold values from 0.02 to 0.2
Outputs:
- ocean_final: float32 [4, 16, 128, 512], P(None, None, 'ox', 'oy')
- atmos_surface: float32 [40, 1024], P('oy', 'ox')
Inputs may be any that keep to these rules, and one draw needn't show every extreme that they name: `tile_slots`: entry [x, j * 3 + k] is q * 3 + s: the s-th block that owner q sends the ocean device of row x and latitude group j, with s below the number of blocks that owner sends it. `need_blocks`: entry [i * 8 + q, j * 3 + s] is the local block of owner (q, j) that ocean device (i, j) takes in place s, or -1; the first 1 to 3 places hold distinct blocks and the rest -1; every ocean device takes 3 blocks from some owner, and some device takes 3 from every owner. `send_blocks`: entry [q * 8 + i, j * 3 + s] equals need_blocks[i * 8 + q, j * 3 + s].
All inputs are finite; a program needn't handle non-finite values. No bound on the sum of `land_mask` on one device may be relied on, other than what follows from the above.
Results may differ from a plain program's by a relative error of at most 0.0022.
Values may be sent and summed in bfloat16 or wider, within the bound.
No kernel may reach another device: no remote copies, remote signals or barrier semaphores. Data moves between devices by JAX's collectives and lax.ppermute only.
A program may use at most 64 MiB of HBM per device.

v0:
```python
import jax
import jax.numpy as jnp
from jax import lax
from jax.sharding import PartitionSpec as P

STEPS = 3


advect_coef = 0.25
pressure_coef = 0.1
thermal_coef = 0.2
haline_coef = 0.8
coriolis_coef = 0.5
vertical_coef = 0.1
forcing_coef = 0.5


def with_halo(block, sides, width):
    for axis, dim in sides:
        count = lax.axis_size(axis)
        forward = [(i, i + 1) for i in range(count - 1)]
        backward = [(target, source) for source, target in forward]
        low = lax.ppermute(
            lax.slice_in_dim(block, block.shape[dim] - width, None, axis=dim), axis, forward
        )
        high = lax.ppermute(lax.slice_in_dim(block, 0, width, axis=dim), axis, backward)
        block = jnp.concatenate([low, block, high], axis=dim)
    return block


def advance(padded, center, diffusivity, coriolis, forcing, wetness):
    east = padded[:, :, 2:, 1:-1]
    west = padded[:, :, :-2, 1:-1]
    north = padded[:, :, 1:-1, 2:]
    south = padded[:, :, 1:-1, :-2]
    zonal = center[0]
    meridional = center[1]
    advection = (
        -advect_coef * 0.5 * (zonal[None] * (east - west) + meridional[None] * (north - south))
    )
    laplace = diffusivity[None, :, None, None] * (east + west + north + south - 4.0 * center)
    upper = jnp.concatenate([center[:, :1], center[:, :-1]], axis=1)
    lower = jnp.concatenate([center[:, 1:], center[:, -1:]], axis=1)
    mixing = vertical_coef * (upper + lower - 2.0 * center)
    density = haline_coef * padded[3] - thermal_coef * padded[2]
    pressure = jnp.cumsum(density, axis=0) - 0.5 * density
    grad_east = pressure[:, 2:, 1:-1] - pressure[:, :-2, 1:-1]
    grad_north = pressure[:, 1:-1, 2:] - pressure[:, 1:-1, :-2]
    zonal_push = coriolis * meridional - pressure_coef * 0.5 * grad_east
    merid_push = -coriolis * zonal - pressure_coef * 0.5 * grad_north
    tracer_zero = jnp.zeros((2,) + zonal.shape, jnp.float32)
    momentum = jnp.concatenate([zonal_push[None], merid_push[None], tracer_zero], axis=0)
    total = advection + laplace + mixing + momentum
    total = total.at[:, 0].add(forcing_coef * forcing)
    return center + wetness * total


def row_targets(tile_slots, need_blocks, capacity, owners):
    owner_of = tile_slots // capacity
    place_of = tile_slots % capacity
    return need_blocks[owner_of, place_of] * owners + owner_of


def lat_factor(first_cell, count, lat_total):
    latitude = (first_cell + jnp.arange(count, dtype=jnp.int32)).astype(jnp.float32)
    return coriolis_coef * (2.0 * (latitude + 0.5) / lat_total - 1.0)


def per_device(
    atm_flux,
    remap_weights,
    tile_slots,
    need_blocks,
    send_blocks,
    ocean_state,
    land_mask,
    diffusivity,
):
    flux_fields = atm_flux.shape[0]
    blocks_here = atm_flux.shape[1]
    block_width = atm_flux.shape[2]
    owners = lax.axis_size("ox")
    tile_count = tile_slots.shape[0]
    refs_tile = tile_slots.shape[1]
    capacity = send_blocks.shape[1]
    whole = lax.all_gather(atm_flux, "ox", axis=2, tiled=True)
    table = whole.reshape(flux_fields, blocks_here * owners, block_width)
    picks = table[:, row_targets(tile_slots, need_blocks, capacity, owners)]
    forcing = jnp.einsum("ftka,tkra->ftr", picks, remap_weights, preferred_element_type=jnp.float32)
    lat_cells = ocean_state.shape[3]
    lat_total = lat_cells * lax.axis_size("oy")
    lat_start = lax.axis_index("oy") * lat_cells
    wetness = land_mask.astype(jnp.float32)
    state = ocean_state
    coriolis = lat_factor(lat_start, lat_cells, lat_total)
    for repeat in range(STEPS):
        padded = with_halo(state, (("ox", 2), ("oy", 3)), 1)
        state = advance(padded, state, diffusivity, coriolis, forcing, wetness)
    surface = state[2, 0].astype(jnp.bfloat16)
    pieces = jnp.einsum("tkra,tr->tka", remap_weights, surface, preferred_element_type=jnp.float32)
    pieces = pieces.reshape(tile_count * refs_tile, block_width)
    targets = row_targets(tile_slots, need_blocks, capacity, owners).reshape(-1)
    segment_line = jnp.arange(blocks_here * owners, dtype=jnp.int32)
    select = (targets[:, None] == segment_line[None, :]).astype(jnp.float32)
    dense = lax.dot_general(
        select, pieces, (((0,), (0,)), ((), ())), precision=lax.Precision.HIGHEST
    )
    dense = dense.reshape(blocks_here, owners * block_width)
    atmos_surface = lax.psum_scatter(dense, "ox", scatter_dimension=1, tiled=True)
    return (state, atmos_surface)


def solution(mesh):
    return jax.shard_map(
        per_device,
        mesh=mesh,
        in_specs=(
            P(None, "oy", "ox"),
            P("ox", "oy", None, None),
            P("ox", "oy"),
            P("ox", "oy"),
            P("ox", "oy"),
            P(None, None, "ox", "oy"),
            P("ox", "oy"),
            P(),
        ),
        out_specs=(P(None, None, "ox", "oy"), P("oy", "ox")),
        check_vma=False,
    )
```

profile of v0, /device:TPU:0, one launch (start us, length us, event | category | flops | bytes accessed | tf_op | source)
XLA Modules:
  0.0 182.9 jit_solution(17034254981242002225)
XLA Ops:
  7.2 1.2 fusion.83
  8.4 4.8 %collective-permute-start.1 = (f32[4,16,1,128]{3,2,1,0:T(1,128)S(1)}, f32[4,16,1,128]{3,2,1,0:T(1,128)S(1)}, u32[]{:S(2)}, u32[]{:S(2)}) collective-permute-start(f32[4,16,1,128]{3,2,1,0:T(1,128)S(1)} %get-tuple-element.76), channel_id=1, source_target_pairs={{0,4},{4,8},{8,12},{12,16},{16,20},{20,24},{24,28},{1,5},{5,9},{9,... | collective-permute-start | bytes 98312 | tf_op jit(solution)/shard_map/ppermute | solution.py:23
  13.3 1.3 collective-permute-start
  14.6 0.8 fusion.85
  15.4 1.7 slice_bitcast_fusion.5
  17.1 2.1 %fusion.84 = (f32[4,15,16,128]{3,2,1,0:T(8,128)S(1)}, f32[4,15,16,128]{3,2,1,0:T(8,128)}) fusion(f32[4,16,16,128]{3,2,1,0:T(8,128)} %param.18), kind=kLoop, calls=%fused_computation.163 | loop fusion | bytes 1966080 | tf_op jit(solution)/shard_map/slice | solution.py:43
  19.4 1.1 gather_fusion
  20.7 22.4 %all_gather.3 = bf16[4,10,1024]{2,0,1:T(4,128)(2,1)S(1)} all-gather(bf16[4,10,128]{2,0,1:T(4,128)(2,1)S(1)} %copy-done.16), channel_id=1, replica_groups=mesh['ox'=8,'oy'=4] {'ox'}, dimensions={2}, use_global_device_ids=true | all-gather | bytes 92160 | tf_op jit(solution)/shard_map/all_gather | solution.py:86
  44.5 1.2 fusion.76
  45.7 2.2 %copy.144 = f32[4,16,18,1]{2,1,3,0:T(8,128)} copy(f32[4,16,18,1]{3,2,1,0:T(8,128)} %get-tuple-element.56) | data formatting | bytes 9216 | tf_op jit(solution)/shard_map/slice | solution.py:24
  47.9 1.1 copy.142
  49.0 1.3 collective-permute-start.2
  50.2 3.6 %collective-permute-start.3 = (f32[4,16,18,1]{2,1,3,0:T(8,128)}, f32[4,16,18,1]{2,1,3,0:T(8,128)}, u32[]{:S(2)}, u32[]{:S(2)}) collective-permute-start(f32[4,16,18,1]{2,1,3,0:T(8,128)} %copy.144), channel_id=1, source_target_pairs={{0,1},{1,2},{2,3},{4,5},{5,6},{6,7},{8,9},{9,10},{10,11},{12,13},{... | collective-permute-start | bytes 13832 | tf_op jit(solution)/shard_map/ppermute | solution.py:23
  56.5 1.3 copy.145
  57.7 2.1 %copy.143 = f32[4,16,18,1]{3,2,1,0:T(8,128)} copy(f32[4,16,18,1]{2,1,3,0:T(8,128)} %collective-permute-done.2) | data formatting | bytes 9216 | tf_op jit(solution)/shard_map/ppermute | solution.py:26
  59.9 2.2 %reduce-window_subtract_fusion.2 = f32[16,18,130]{2,1,0:T(8,128)S(1)} fusion(f32[4,16,18,1]{3,2,1,0:T(8,128)} %copy.143, f32[4,16,1,128]{3,2,1,0:T(1,128)S(1)} %collective-permute-done, f32[4,16,16,128]{3,2,1,0:T(8,128)S(1)} %copy-done.2, f32[4,16,1,128]{3,2,1,0:T(1,128)S(1)} %collective-permute-done.1, f32[4,16,18,1]{3,2,1,0:T(8,128)S(1)} %copy.145), kind=kOutput, calls=%fused_computation.4 | output fusion | flops 1460160 | bytes 748800 | tf_op jit(solution)/shard_map/jit(cumsum)/reduce_window_sum | solution.py:46
  62.4 0.9 copy-done.4
  63.3 0.9 fusion.3
  64.3 0.9 fusion.81
  65.2 1.3 collective-permute-start.5
  66.5 1.3 collective-permute-start.4
  67.8 0.7 slice_bitcast_fusion.3
  68.5 3.8 %collective-permute-done.4 = f32[4,16,1,128]{3,2,1,0:T(1,128)S(1)} collective-permute-done((f32[4,16,1,128]{3,2,1,0:T(1,128)S(1)}, f32[4,16,1,128]{3,2,1,0:T(1,128)S(1)}, u32[]{:S(2)}, u32[]{:S(2)}) %collective-permute-start.4) | collective-permute-done | bytes 32800 | tf_op jit(solution)/shard_map/ppermute | solution.py:26
  72.4 1.2 fusion.75
  73.6 2.2 %copy.156 = f32[4,16,18,1]{2,1,3,0:T(8,128)} copy(f32[4,16,18,1]{3,2,1,0:T(8,128)} %get-tuple-element.54) | data formatting | bytes 9216 | tf_op jit(solution)/shard_map/slice | solution.py:24
  75.8 1.1 copy.154
  76.9 1.3 collective-permute-start.6
  78.2 3.6 %collective-permute-start.7 = (f32[4,16,18,1]{2,1,3,0:T(8,128)}, f32[4,16,18,1]{2,1,3,0:T(8,128)}, u32[]{:S(2)}, u32[]{:S(2)}) collective-permute-start(f32[4,16,18,1]{2,1,3,0:T(8,128)} %copy.156), channel_id=1, source_target_pairs={{0,1},{1,2},{2,3},{4,5},{5,6},{6,7},{8,9},{9,10},{10,11},{12,13},{... | collective-permute-start | bytes 13832 | tf_op jit(solution)/shard_map/ppermute | solution.py:23
  82.4 1.3 copy.157
  83.6 2.1 %copy.155 = f32[4,16,18,1]{3,2,1,0:T(8,128)} copy(f32[4,16,18,1]{2,1,3,0:T(8,128)} %collective-permute-done.6) | data formatting | bytes 9216 | tf_op jit(solution)/shard_map/ppermute | solution.py:26
  85.8 2.2 %reduce-window_subtract_fusion.1 = f32[16,18,130]{2,1,0:T(8,128)S(1)} fusion(f32[4,16,18,1]{3,2,1,0:T(8,128)} %copy.155, f32[4,16,1,128]{3,2,1,0:T(1,128)S(1)} %collective-permute-done.4, f32[4,16,16,128]{3,2,1,0:T(8,128)S(1)} %multiply_add_fusion.2, f32[4,16,1,128]{3,2,1,0:T(1,128)S(1)} %collective-permute-done.5, f32[4,16,18,1]{3,2,1,0:T(8,128)S(1)} %copy.157), kind=kOutput, calls=%fused_computation.3 | output fusion | flops 1460160 | bytes 748800 | tf_op jit(solution)/shard_map/jit(cumsum)/reduce_window_sum | solution.py:46
  88.3 0.9 copy-done.5
  89.2 0.9 fusion.7
  90.2 0.9 fusion.78
  91.1 3.6 %collective-permute-start.9 = (f32[4,16,1,128]{3,2,1,0:T(1,128)S(1)}, f32[4,16,1,128]{3,2,1,0:T(1,128)S(1)}, u32[]{:S(2)}, u32[]{:S(2)}) collective-permute-start(f32[4,16,1,128]{3,2,1,0:T(1,128)S(1)} %get-tuple-element.60), channel_id=1, source_target_pairs={{0,4},{4,8},{8,12},{12,16},{16,20},{20,24},{24,28},{1,5},{5,9},{9,... | collective-permute-start | bytes 98312 | tf_op jit(solution)/shard_map/ppermute | solution.py:23
  94.7 1.3 collective-permute-start.8
  96.7 4.1 %collective-permute-done.8 = f32[4,16,1,128]{3,2,1,0:T(1,128)S(1)} collective-permute-done((f32[4,16,1,128]{3,2,1,0:T(1,128)S(1)}, f32[4,16,1,128]{3,2,1,0:T(1,128)S(1)}, u32[]{:S(2)}, u32[]{:S(2)}) %collective-permute-start.8) | collective-permute-done | bytes 32800 | tf_op jit(solution)/shard_map/ppermute | solution.py:26
  101.0 1.2 fusion.74
  102.2 2.2 %copy.162 = f32[4,16,18,1]{2,1,3,0:T(8,128)} copy(f32[4,16,18,1]{3,2,1,0:T(8,128)} %get-tuple-element.52) | data formatting | bytes 9216 | tf_op jit(solution)/shard_map/slice | solution.py:24
  104.4 1.1 copy.160
  105.5 1.3 collective-permute-start.10
  106.7 3.6 %collective-permute-start.11 = (f32[4,16,18,1]{2,1,3,0:T(8,128)}, f32[4,16,18,1]{2,1,3,0:T(8,128)}, u32[]{:S(2)}, u32[]{:S(2)}) collective-permute-start(f32[4,16,18,1]{2,1,3,0:T(8,128)} %copy.162), channel_id=1, source_target_pairs={{0,1},{1,2},{2,3},{4,5},{5,6},{6,7},{8,9},{9,10},{10,11},{12,13},{... | collective-permute-start | bytes 13832 | tf_op jit(solution)/shard_map/ppermute | solution.py:23
  111.0 1.3 copy.163
  112.2 2.1 %copy.161 = f32[4,16,18,1]{3,2,1,0:T(8,128)} copy(f32[4,16,18,1]{2,1,3,0:T(8,128)} %collective-permute-done.10) | data formatting | bytes 9216 | tf_op jit(solution)/shard_map/ppermute | solution.py:26
  114.4 2.2 %reduce-window_subtract_fusion = f32[16,18,130]{2,1,0:T(8,128)S(1)} fusion(f32[4,16,18,1]{3,2,1,0:T(8,128)} %copy.161, f32[4,16,1,128]{3,2,1,0:T(1,128)S(1)} %collective-permute-done.8, f32[4,16,16,128]{3,2,1,0:T(8,128)S(1)} %multiply_add_fusion.1, f32[4,16,1,128]{3,2,1,0:T(1,128)S(1)} %collective-permute-done.9, f32[4,16,18,1]{3,2,1,0:T(8,128)S(1)} %copy.163), kind=kOutput, calls=%fused_computation.2 | output fusion | flops 1460160 | bytes 748800 | tf_op jit(solution)/shard_map/jit(cumsum)/reduce_window_sum | solution.py:46
  116.9 0.9 copy-done.3
  117.8 0.9 fusion.11
  120.3 55.7 %reduce-scatter.2.cloned.1.call-done = f32[10,128]{1,0:T(8,128)} async-done(((f32[10,1024]{1,0:T(8,128)}), f32[10,128]{1,0:T(8,128)}) %reduce-scatter.2.cloned.1.call-update) | async-done | bytes 5136 | tf_op jit(solution)/shard_map/reduce_scatter | solution.py:109
  (101 shorter events, 9.0 us)
Async XLA Ops:
  7.2 36.5 %copy-start = (bf16[16,3,128,128]{3,2,1,0:T(8,128)(2,1)S(1)}, bf16[16,3,128,128]{3,2,1,0:T(8,128)(2,1)}, u32[]{:S(2)}) copy-start(bf16[16,3,128,128]{3,2,1,0:T(8,128)(2,1)} %param.15) | copy-start | bytes 4718596
  7.2 12.0 %copy-start.26 = (s32[16,3]{0,1:T(4,128)S(1)}, s32[16,3]{0,1:T(4,128)}, u32[]{:S(2)}) copy-start(s32[16,3]{0,1:T(4,128)} %param.16) | copy-start | bytes 580
  7.2 12.2 %copy-start.1 = (s32[8,3]{0,1:T(4,128)S(1)}, s32[8,3]{0,1:T(4,128)}, u32[]{:S(2)}) copy-start(s32[8,3]{0,1:T(4,128)} %param.17) | copy-start | bytes 292
  7.2 168.8 %reduce-scatter.2.cloned.1.call-start = ((), (), s32[]{:S(2)}) async-start(), calls=%async_computation.1 | async-start | bytes 73728 | tf_op jit(solution)/shard_map/reduce_scatter | solution.py:109
  8.4 35.9 %collective-permute-start.1 = (f32[4,16,1,128]{3,2,1,0:T(1,128)S(1)}, f32[4,16,1,128]{3,2,1,0:T(1,128)S(1)}, u32[]{:S(2)}, u32[]{:S(2)}) collective-permute-start(f32[4,16,1,128]{3,2,1,0:T(1,128)S(1)} %get-tuple-element.76), channel_id=1, source_target_pairs={{0,4},{4,8},{8,12},{12,16},{16,20},{20,24},{24,28},{1,5},{5,9},{9,... | collective-permute-start | bytes 98312 | tf_op jit(solution)/shard_map/ppermute | solution.py:23
  13.3 31.0 %collective-permute-start = (f32[4,16,1,128]{3,2,1,0:T(1,128)S(1)}, f32[4,16,1,128]{3,2,1,0:T(1,128)S(1)}, u32[]{:S(2)}, u32[]{:S(2)}) collective-permute-start(f32[4,16,1,128]{3,2,1,0:T(1,128)S(1)} %get-tuple-element.77), channel_id=1, source_target_pairs={{4,0},{8,4},{12,8},{16,12},{20,16},{24,20},{28,24},{5,1},{9,5},{13... | collective-permute-start | bytes 98312 | tf_op jit(solution)/shard_map/ppermute | solution.py:26
  19.4 1.3 copy-start.16
  20.4 23.9 %copy-start.2 = (f32[4,16,16,128]{3,2,1,0:T(8,128)S(1)}, f32[4,16,16,128]{3,2,1,0:T(8,128)}, u32[]{:S(2)}) copy-start(f32[4,16,16,128]{3,2,1,0:T(8,128)} %param.18) | copy-start | bytes 1572868
  49.0 8.8 %collective-permute-start.2 = (f32[4,16,18,1]{2,1,3,0:T(8,128)}, f32[4,16,18,1]{2,1,3,0:T(8,128)}, u32[]{:S(2)}, u32[]{:S(2)}) collective-permute-start(f32[4,16,18,1]{2,1,3,0:T(8,128)} %copy.142), channel_id=1, source_target_pairs={{1,0},{2,1},{3,2},{5,4},{6,5},{7,6},{9,8},{10,9},{11,10},{13,12},{... | collective-permute-start | bytes 13832 | tf_op jit(solution)/shard_map/ppermute | solution.py:26
  50.2 6.2 %collective-permute-start.3 = (f32[4,16,18,1]{2,1,3,0:T(8,128)}, f32[4,16,18,1]{2,1,3,0:T(8,128)}, u32[]{:S(2)}, u32[]{:S(2)}) collective-permute-start(f32[4,16,18,1]{2,1,3,0:T(8,128)} %copy.144), channel_id=1, source_target_pairs={{0,1},{1,2},{2,3},{4,5},{5,6},{6,7},{8,9},{9,10},{10,11},{12,13},{... | collective-permute-start | bytes 13832 | tf_op jit(solution)/shard_map/ppermute | solution.py:23
  59.9 2.3 %copy-start.17 = (f32[128]{0:T(128)S(1)}, f32[128]{0:T(128)}, u32[]{:S(2)}) copy-start(f32[128]{0:T(128)} %get-tuple-element.82) | copy-start | bytes 1540
  59.9 2.3 %copy-start.18 = (f32[128]{0:T(128)S(1)}, f32[128]{0:T(128)}, u32[]{:S(2)}) copy-start(f32[128]{0:T(128)} %get-tuple-element.83) | copy-start | bytes 1540
  59.9 2.5 %copy-start.6 = (f32[4,15,16,128]{3,2,1,0:T(8,128)S(1)}, f32[4,15,16,128]{3,2,1,0:T(8,128)}, u32[]{:S(2)}) copy-start(f32[4,15,16,128]{3,2,1,0:T(8,128)} %get-tuple-element.79) | copy-start | bytes 1474564
  59.9 2.5 %copy-start.10 = (f32[16,16,128]{2,1,0:T(8,128)S(1)}, f32[16,16,128]{2,1,0:T(8,128)}, u32[]{:S(2)}) copy-start(f32[16,16,128]{2,1,0:T(8,128)} %get-tuple-element.74) | copy-start | bytes 393220
  59.9 2.5 %copy-start.11 = (f32[16,16,128]{2,1,0:T(8,128)S(1)}, f32[16,16,128]{2,1,0:T(8,128)}, u32[]{:S(2)}) copy-start(f32[16,16,128]{2,1,0:T(8,128)} %get-tuple-element.75) | copy-start | bytes 393220
  59.9 2.5 %copy-start.19 = (f32[16]{0:T(128)S(1)}, f32[16]{0:T(128)}, u32[]{:S(2)}) copy-start(f32[16]{0:T(128)} %param.20) | copy-start | bytes 196
  59.9 2.5 %copy-start.22 = (f32[4]{0:T(128)S(1)}, f32[4]{0:T(128)}, u32[]{:S(2)}) copy-start(f32[4]{0:T(128)} %pad.62.clone) | copy-start | bytes 52
  62.1 1.1 copy-start.4
  65.2 3.3 %collective-permute-start.5 = (f32[4,16,1,128]{3,2,1,0:T(1,128)S(1)}, f32[4,16,1,128]{3,2,1,0:T(1,128)S(1)}, u32[]{:S(2)}, u32[]{:S(2)}) collective-permute-start(f32[4,16,1,128]{3,2,1,0:T(1,128)S(1)} %get-tuple-element.68), channel_id=1, source_target_pairs={{0,4},{4,8},{8,12},{12,16},{16,20},{20,24},{24,28},{1,5},{5,9},{9,... | collective-permute-start | bytes 98312 | tf_op jit(solution)/shard_map/ppermute | solution.py:23
  66.5 5.8 %collective-permute-start.4 = (f32[4,16,1,128]{3,2,1,0:T(1,128)S(1)}, f32[4,16,1,128]{3,2,1,0:T(1,128)S(1)}, u32[]{:S(2)}, u32[]{:S(2)}) collective-permute-start(f32[4,16,1,128]{3,2,1,0:T(1,128)S(1)} %get-tuple-element.69), channel_id=1, source_target_pairs={{4,0},{8,4},{12,8},{16,12},{20,16},{24,20},{28,24},{5,1},{9,5},{13... | collective-permute-start | bytes 98312 | tf_op jit(solution)/shard_map/ppermute | solution.py:26
  76.9 6.8 %collective-permute-start.6 = (f32[4,16,18,1]{2,1,3,0:T(8,128)}, f32[4,16,18,1]{2,1,3,0:T(8,128)}, u32[]{:S(2)}, u32[]{:S(2)}) collective-permute-start(f32[4,16,18,1]{2,1,3,0:T(8,128)} %copy.154), channel_id=1, source_target_pairs={{1,0},{2,1},{3,2},{5,4},{6,5},{7,6},{9,8},{10,9},{11,10},{13,12},{... | collective-permute-start | bytes 13832 | tf_op jit(solution)/shard_map/ppermute | solution.py:26
  78.2 4.2 %collective-permute-start.7 = (f32[4,16,18,1]{2,1,3,0:T(8,128)}, f32[4,16,18,1]{2,1,3,0:T(8,128)}, u32[]{:S(2)}, u32[]{:S(2)}) collective-permute-start(f32[4,16,18,1]{2,1,3,0:T(8,128)} %copy.156), channel_id=1, source_target_pairs={{0,1},{1,2},{2,3},{4,5},{5,6},{6,7},{8,9},{9,10},{10,11},{12,13},{... | collective-permute-start | bytes 13832 | tf_op jit(solution)/shard_map/ppermute | solution.py:23
  85.8 2.4 %copy-start.8 = (f32[4,15,16,128]{3,2,1,0:T(8,128)S(1)}, f32[4,15,16,128]{3,2,1,0:T(8,128)}, u32[]{:S(2)}) copy-start(f32[4,15,16,128]{3,2,1,0:T(8,128)} %get-tuple-element.71) | copy-start | bytes 1474564
  85.8 2.4 %copy-start.14 = (f32[16,16,128]{2,1,0:T(8,128)S(1)}, f32[16,16,128]{2,1,0:T(8,128)}, u32[]{:S(2)}) copy-start(f32[16,16,128]{2,1,0:T(8,128)} %get-tuple-element.66) | copy-start | bytes 393220
  85.8 2.5 %copy-start.15 = (f32[16,16,128]{2,1,0:T(8,128)S(1)}, f32[16,16,128]{2,1,0:T(8,128)}, u32[]{:S(2)}) copy-start(f32[16,16,128]{2,1,0:T(8,128)} %get-tuple-element.67) | copy-start | bytes 393220
  85.8 2.5 %copy-start.20 = (f32[16]{0:T(128)S(1)}, f32[16]{0:T(128)}, u32[]{:S(2)}) copy-start(f32[16]{0:T(128)} %param.20) | copy-start | bytes 196
  85.8 2.5 %copy-start.23 = (f32[4]{0:T(128)S(1)}, f32[4]{0:T(128)}, u32[]{:S(2)}) copy-start(f32[4]{0:T(128)} %pad.62.clone) | copy-start | bytes 52
  88.0 1.1 copy-start.5
  91.1 5.7 %collective-permute-start.9 = (f32[4,16,1,128]{3,2,1,0:T(1,128)S(1)}, f32[4,16,1,128]{3,2,1,0:T(1,128)S(1)}, u32[]{:S(2)}, u32[]{:S(2)}) collective-permute-start(f32[4,16,1,128]{3,2,1,0:T(1,128)S(1)} %get-tuple-element.60), channel_id=1, source_target_pairs={{0,4},{4,8},{8,12},{12,16},{16,20},{20,24},{24,28},{1,5},{5,9},{9,... | collective-permute-start | bytes 98312 | tf_op jit(solution)/shard_map/ppermute | solution.py:23
  94.7 6.1 %collective-permute-start.8 = (f32[4,16,1,128]{3,2,1,0:T(1,128)S(1)}, f32[4,16,1,128]{3,2,1,0:T(1,128)S(1)}, u32[]{:S(2)}, u32[]{:S(2)}) collective-permute-start(f32[4,16,1,128]{3,2,1,0:T(1,128)S(1)} %get-tuple-element.61), channel_id=1, source_target_pairs={{4,0},{8,4},{12,8},{16,12},{20,16},{24,20},{28,24},{5,1},{9,5},{13... | collective-permute-start | bytes 98312 | tf_op jit(solution)/shard_map/ppermute | solution.py:26
  105.5 6.8 %collective-permute-start.10 = (f32[4,16,18,1]{2,1,3,0:T(8,128)}, f32[4,16,18,1]{2,1,3,0:T(8,128)}, u32[]{:S(2)}, u32[]{:S(2)}) collective-permute-start(f32[4,16,18,1]{2,1,3,0:T(8,128)} %copy.160), channel_id=1, source_target_pairs={{1,0},{2,1},{3,2},{5,4},{6,5},{7,6},{9,8},{10,9},{11,10},{13,12},{... | collective-permute-start | bytes 13832 | tf_op jit(solution)/shard_map/ppermute | solution.py:26
  106.7 4.2 %collective-permute-start.11 = (f32[4,16,18,1]{2,1,3,0:T(8,128)}, f32[4,16,18,1]{2,1,3,0:T(8,128)}, u32[]{:S(2)}, u32[]{:S(2)}) collective-permute-start(f32[4,16,18,1]{2,1,3,0:T(8,128)} %copy.162), channel_id=1, source_target_pairs={{0,1},{1,2},{2,3},{4,5},{5,6},{6,7},{8,9},{9,10},{10,11},{12,13},{... | collective-permute-start | bytes 13832 | tf_op jit(solution)/shard_map/ppermute | solution.py:23
  114.4 2.4 %copy-start.7 = (f32[4,15,16,128]{3,2,1,0:T(8,128)S(1)}, f32[4,15,16,128]{3,2,1,0:T(8,128)}, u32[]{:S(2)}) copy-start(f32[4,15,16,128]{3,2,1,0:T(8,128)} %get-tuple-element.63) | copy-start | bytes 1474564
  114.4 2.4 %copy-start.12 = (f32[16,16,128]{2,1,0:T(8,128)S(1)}, f32[16,16,128]{2,1,0:T(8,128)}, u32[]{:S(2)}) copy-start(f32[16,16,128]{2,1,0:T(8,128)} %get-tuple-element.58) | copy-start | bytes 393220
  114.4 2.5 %copy-start.13 = (f32[16,16,128]{2,1,0:T(8,128)S(1)}, f32[16,16,128]{2,1,0:T(8,128)}, u32[]{:S(2)}) copy-start(f32[16,16,128]{2,1,0:T(8,128)} %get-tuple-element.59) | copy-start | bytes 393220
  114.4 2.5 %copy-start.21 = (f32[16]{0:T(128)S(1)}, f32[16]{0:T(128)}, u32[]{:S(2)}) copy-start(f32[16]{0:T(128)} %param.20) | copy-start | bytes 196
  114.4 2.5 %copy-start.24 = (f32[4]{0:T(128)S(1)}, f32[4]{0:T(128)}, u32[]{:S(2)}) copy-start(f32[4]{0:T(128)} %pad.62.clone) | copy-start | bytes 52
  116.6 1.1 copy-start.3
  118.7 0.7 copy-start.25
  118.8 57.2 %copy-start.9 = (f32[4,16,16,128]{3,2,1,0:T(8,128)}, f32[4,16,16,128]{3,2,1,0:T(8,128)S(1)}, u32[]{:S(2)}) copy-start(f32[4,16,16,128]{3,2,1,0:T(8,128)S(1)} %multiply_add_fusion) | copy-start | bytes 1572868
Sparse Core Ops, SparseCore 0:
  120.4 55.5 reduce-scatter.1
where the time goes:
time: 184 us; the launch traced here: 183 us
  waiting for transfers between devices  64.8 us (35%)
  local copies, waits for them, and re-layouts  39.6 us (22%)
  starting transfers between devices  28.5 us (15%)
  blocking collectives  22.4 us (12%)
  between operations  14.6 us (8%)
  other arithmetic  11.8 us (6%)
    reduce_scatter x1, waiting for transfers between devices, per_device(): lax.psum_scatter(dense, 'ox', scatter_dimension=1, tiled=True)  55.7 us
    all_gather x1, blocking collectives, per_device(): whole = lax.all_gather(atm_flux, 'ox', axis=2, tiled=True)  22.4 us
    ppermute x6, starting transfers between devices, with_halo(): lax.ppermute(lax.slice_in_dim(block, block.shape[dim] - width, None, axis...  20.7 us
    slice x9, local copies, waits for them, and re-layouts, with_halo(): lax.slice_in_dim(block, block.shape[dim] - width, None, axis=dim)  11.5 us
    ppermute x6, waiting for transfers between devices, with_halo(): lax.ppermute(lax.slice_in_dim(block, 0, width, axis=dim), axis, backward)  7.92 us
    ppermute x6, starting transfers between devices, with_halo(): lax.ppermute(lax.slice_in_dim(block, 0, width, axis=dim), axis, backward)  7.72 us
    another operation x3, other arithmetic, advance(): pressure = jnp.cumsum(density, axis=0) - 0.5 * density  6.68 us
    ppermute x3, local copies, waits for them, and re-layouts, with_halo(): lax.ppermute(lax.slice_in_dim(block, 0, width, axis=dim), axis, backward)  6.43 us
  transfers between devices with their start and end apart: 13, of which 5 were waited for; matrix products, arithmetic and copies ran while one was open for 8% of the time, Pallas kernels for 0%

commit v1 on v0

--- a/solution.py
+++ b/solution.py
@@ -76,17 +76,17 @@
     land_mask,
     diffusivity,
 ):
-    flux_fields = atm_flux.shape[0]
     blocks_here = atm_flux.shape[1]
     block_width = atm_flux.shape[2]
     owners = lax.axis_size("ox")
-    tile_count = tile_slots.shape[0]
-    refs_tile = tile_slots.shape[1]
     capacity = send_blocks.shape[1]
-    whole = lax.all_gather(atm_flux, "ox", axis=2, tiled=True)
-    table = whole.reshape(flux_fields, blocks_here * owners, block_width)
-    picks = table[:, row_targets(tile_slots, need_blocks, capacity, owners)]
-    forcing = jnp.einsum("ftka,tkra->ftr", picks, remap_weights, preferred_element_type=jnp.float32)
+    slots = owners * capacity
+    given = jnp.clip(send_blocks, 0, blocks_here - 1)
+    outgoing = jnp.transpose(atm_flux[:, given, :], (1, 2, 0, 3))
+    incoming = lax.all_to_all(outgoing, "ox", 0, 0, tiled=True)
+    incoming = incoming.reshape((slots,) + incoming.shape[2:])
+    picks = incoming[tile_slots]
+    forcing = jnp.einsum("tkfa,tkra->ftr", picks, remap_weights, preferred_element_type=jnp.float32)
     lat_cells = ocean_state.shape[3]
     lat_total = lat_cells * lax.axis_size("oy")
     lat_start = lax.axis_index("oy") * lat_cells
@@ -98,15 +98,16 @@
         state = advance(padded, state, diffusivity, coriolis, forcing, wetness)
     surface = state[2, 0].astype(jnp.bfloat16)
     pieces = jnp.einsum("tkra,tr->tka", remap_weights, surface, preferred_element_type=jnp.float32)
-    pieces = pieces.reshape(tile_count * refs_tile, block_width)
-    targets = row_targets(tile_slots, need_blocks, capacity, owners).reshape(-1)
-    segment_line = jnp.arange(blocks_here * owners, dtype=jnp.int32)
-    select = (targets[:, None] == segment_line[None, :]).astype(jnp.float32)
-    dense = lax.dot_general(
-        select, pieces, (((0,), (0,)), ((), ())), precision=lax.Precision.HIGHEST
+    slot_line = jnp.arange(slots, dtype=jnp.int32)
+    to_slot = (tile_slots[:, :, None] == slot_line[None, None, :]).astype(jnp.float32)
+    per_slot = jnp.einsum("tks,tka->sa", to_slot, pieces, precision=lax.Precision.HIGHEST)
+    per_slot = per_slot.reshape(owners, capacity, block_width)
+    returned = lax.all_to_all(per_slot, "ox", 0, 0, tiled=True)
+    block_line = jnp.arange(blocks_here, dtype=jnp.int32)
+    to_block = (send_blocks[:, :, None] == block_line[None, None, :]).astype(jnp.float32)
+    atmos_surface = jnp.einsum(
+        "isb,isa->ba", to_block, returned, precision=lax.Precision.HIGHEST
     )
-    dense = dense.reshape(blocks_here, owners * block_width)
-    atmos_surface = lax.psum_scatter(dense, "ox", scatter_dimension=1, tiled=True)
     return (state, atmos_surface)
 
 

time: 184 us -> 114 us (0.62)
  the two profiles are of different devices: /device:TPU:0 before, /device:TPU:4 now
where the time goes in v1:
time: 114 us; the launch traced here: 113 us
  local copies, waits for them, and re-layouts  37.1 us (33%)
  starting transfers between devices  37.1 us (33%)
  waiting for transfers between devices  14 us (12%)
  other arithmetic  11.4 us (10%)
  blocking collectives  10.4 us (9%)
  matrix products  2.14 us (2%)
  between operations  1.19 us (1%)
    ppermute x6, starting transfers between devices, with_halo(): lax.ppermute(lax.slice_in_dim(block, block.shape[dim] - width, None, axis...  21.7 us
    slice x9, local copies, waits for them, and re-layouts, with_halo(): lax.slice_in_dim(block, block.shape[dim] - width, None, axis=dim)  10.7 us
    all_to_all x1, blocking collectives, per_device(): returned = lax.all_to_all(per_slot, 'ox', 0, 0, tiled=True)  10.4 us
    ppermute x6, starting transfers between devices, with_halo(): lax.ppermute(lax.slice_in_dim(block, 0, width, axis=dim), axis, backward)  9.61 us
    ppermute x6, waiting for transfers between devices, with_halo(): lax.ppermute(lax.slice_in_dim(block, 0, width, axis=dim), axis, backward)  8.1 us
    another operation x3, other arithmetic, advance(): pressure = jnp.cumsum(density, axis=0) - 0.5 * density  6.71 us
    ppermute x6, waiting for transfers between devices, with_halo(): lax.ppermute(lax.slice_in_dim(block, block.shape[dim] - width, None, axis...  5.87 us
    all_to_all x1, starting transfers between devices, per_device(): incoming = lax.all_to_all(outgoing, 'ox', 0, 0, tiled=True)  5.81 us
  transfers between devices with their start and end apart: 13, of which 6 were waited for; matrix products, arithmetic and copies ran while one was open for 17% of the time, Pallas kernels for 0%

profile of v1, /device:TPU:4, one launch (start us, length us, event | category | flops | bytes accessed | tf_op | source)
XLA Modules:
  0.0 113.2 jit_solution(14842315247944613707)
XLA Ops:
  1.7 1.9 %gather_fusion = bf16[24,4,128]{2,1,0:T(4,128)(2,1)} fusion(bf16[4,10,128]{2,0,1:T(4,128)(2,1)} %param.14, s32[1024]{0:T(1024)S(1)} %pad_clamp_fusion.1), kind=kCustom, calls=%fused_computation | custom fusion | bytes 49248 | tf_op jit(solution)/shard_map/gather | solution.py:85
  3.6 5.8 %all-to-all-start = ((bf16[8,3,4,128]{3,2,1,0:T(4,128)(2,1)}), bf16[8,3,4,128]{3,2,1,0:T(4,128)(2,1)S(1)}, u32[]{:S(2)}, u32[]{:S(2)}) async-start(bf16[8,3,4,128]{3,2,1,0:T(4,128)(2,1)} %bitcast.5), calls=%async_computation | async-start | bytes 49152 | tf_op jit(solution)/shard_map/all_to_all | solution.py:86
  9.4 1.1 fusion.78
  10.5 3.9 %collective-permute-start.1 = (f32[4,16,1,128]{3,2,1,0:T(1,128)S(1)}, f32[4,16,1,128]{3,2,1,0:T(1,128)S(1)}, u32[]{:S(2)}, u32[]{:S(2)}) collective-permute-start(f32[4,16,1,128]{3,2,1,0:T(1,128)S(1)} %get-tuple-element.74), channel_id=1, source_target_pairs={{0,4},{4,8},{8,12},{12,16},{16,20},{20,24},{24,28},{1,5},{5,9},{9,... | collective-permute-start | bytes 98312 | tf_op jit(solution)/shard_map/ppermute | solution.py:23
  14.4 1.3 %collective-permute-start = (f32[4,16,1,128]{3,2,1,0:T(1,128)S(1)}, f32[4,16,1,128]{3,2,1,0:T(1,128)S(1)}, u32[]{:S(2)}, u32[]{:S(2)}) collective-permute-start(f32[4,16,1,128]{3,2,1,0:T(1,128)S(1)} %get-tuple-element.75), channel_id=1, source_target_pairs={{4,0},{8,4},{12,8},{16,12},{20,16},{24,20},{28,24},{5,1},{9,5},{13... | collective-permute-start | bytes 98312 | tf_op jit(solution)/shard_map/ppermute | solution.py:26
  15.7 1.4 %fusion.80 = (f32[4,1,16,128]{3,2,1,0:T(8,128)S(1)}, f32[4,1,16,128]{3,2,1,0:T(8,128)}) fusion(f32[4,16,16,128]{3,2,1,0:T(8,128)} %param.18), kind=kLoop, calls=%fused_computation.157 | loop fusion | bytes 131072 | tf_op jit(solution)/shard_map/slice | solution.py:43
  17.1 1.7 %slice_bitcast_fusion.5 = (f32[16,16,128]{2,1,0:T(8,128)}, f32[16,16,128]{2,1,0:T(8,128)}) fusion(f32[4,16,16,128]{3,2,1,0:T(8,128)} %param.18), kind=kLoop, calls=%fused_computation.112 | loop fusion | bytes 524288 | tf_op jit(solution)/shard_map/mul | solution.py:39
  18.8 1.0 fusion.79
  20.3 1.2 %fusion.71 = (f32[4,16,18,1]{3,2,1,0:T(8,128)}, f32[4,16,18,1]{3,2,1,0:T(8,128)S(1)}) fusion(f32[4,16,18,128]{3,2,1,0:T(8,128)S(1)} %pad_maximum_fusion), kind=kLoop, calls=%fused_computation.148 | loop fusion | bytes 18432 | tf_op jit(solution)/shard_map/slice | solution.py:24
  21.5 1.6 %copy.140 = f32[4,16,18,1]{2,1,3,0:T(8,128)S(1)} copy(f32[4,16,18,1]{3,2,1,0:T(8,128)} %get-tuple-element.54) | data formatting | bytes 9216 | tf_op jit(solution)/shard_map/slice | solution.py:24
  23.6 1.9 %collective-permute-start.2 = (f32[4,16,18,1]{2,1,3,0:T(8,128)S(1)}, f32[4,16,18,1]{2,1,3,0:T(8,128)S(1)}, u32[]{:S(2)}, u32[]{:S(2)}) collective-permute-start(f32[4,16,18,1]{2,1,3,0:T(8,128)S(1)} %copy.138), channel_id=1, source_target_pairs={{1,0},{2,1},{3,2},{5,4},{6,5},{7,6},{9,8},{10,9},{11,10},{13,12},{... | collective-permute-start | bytes 13832 | tf_op jit(solution)/shard_map/ppermute | solution.py:26
  25.5 2.4 %collective-permute-start.3 = (f32[4,16,18,1]{2,1,3,0:T(8,128)S(1)}, f32[4,16,18,1]{2,1,3,0:T(8,128)S(1)}, u32[]{:S(2)}, u32[]{:S(2)}) collective-permute-start(f32[4,16,18,1]{2,1,3,0:T(8,128)S(1)} %copy.140), channel_id=1, source_target_pairs={{0,1},{1,2},{2,3},{4,5},{5,6},{6,7},{8,9},{9,10},{10,11},{12,13},{... | collective-permute-start | bytes 13832 | tf_op jit(solution)/shard_map/ppermute | solution.py:23
  28.6 2.2 %collective-permute-done.3 = f32[4,16,18,1]{2,1,3,0:T(8,128)S(1)} collective-permute-done((f32[4,16,18,1]{2,1,3,0:T(8,128)S(1)}, f32[4,16,18,1]{2,1,3,0:T(8,128)S(1)}, u32[]{:S(2)}, u32[]{:S(2)}) %collective-permute-start.3) | collective-permute-done | bytes 4640 | tf_op jit(solution)/shard_map/ppermute | solution.py:23
  31.3 1.4 %copy.139 = f32[4,16,18,1]{3,2,1,0:T(8,128)} copy(f32[4,16,18,1]{2,1,3,0:T(8,128)S(1)} %collective-permute-done.2) | data formatting | bytes 9216 | tf_op jit(solution)/shard_map/ppermute | solution.py:26
  32.7 2.3 %reduce-window_subtract_fusion.2 = f32[16,18,130]{2,1,0:T(8,128)S(1)} fusion(f32[4,16,18,1]{3,2,1,0:T(8,128)} %copy.139, f32[4,16,1,128]{3,2,1,0:T(1,128)S(1)} %collective-permute-done, f32[4,16,16,128]{3,2,1,0:T(8,128)S(1)} %copy-done.1, f32[4,16,1,128]{3,2,1,0:T(1,128)S(1)} %collective-permute-done.1, f32[4,16,18,1]{3,2,1,0:T(8,128)S(1)} %copy.141), kind=kOutput, calls=%fused_computation.4 | output fusion | flops 1460160 | bytes 748800 | tf_op jit(solution)/shard_map/jit(cumsum)/reduce_window_sum | solution.py:46
  35.2 0.9 copy-done.3
  36.1 0.9 fusion.3
  39.3 4.4 %collective-permute-start.5 = (f32[4,16,1,128]{3,2,1,0:T(1,128)S(1)}, f32[4,16,1,128]{3,2,1,0:T(1,128)S(1)}, u32[]{:S(2)}, u32[]{:S(2)}) collective-permute-start(f32[4,16,1,128]{3,2,1,0:T(1,128)S(1)} %get-tuple-element.66), channel_id=1, source_target_pairs={{0,4},{4,8},{8,12},{12,16},{16,20},{20,24},{24,28},{1,5},{5,9},{9,... | collective-permute-start | bytes 98312 | tf_op jit(solution)/shard_map/ppermute | solution.py:23
  43.7 1.3 %collective-permute-start.4 = (f32[4,16,1,128]{3,2,1,0:T(1,128)S(1)}, f32[4,16,1,128]{3,2,1,0:T(1,128)S(1)}, u32[]{:S(2)}, u32[]{:S(2)}) collective-permute-start(f32[4,16,1,128]{3,2,1,0:T(1,128)S(1)} %get-tuple-element.67), channel_id=1, source_target_pairs={{4,0},{8,4},{12,8},{16,12},{20,16},{24,20},{28,24},{5,1},{9,5},{13... | collective-permute-start | bytes 98312 | tf_op jit(solution)/shard_map/ppermute | solution.py:26
  45.7 4.1 %collective-permute-done.4 = f32[4,16,1,128]{3,2,1,0:T(1,128)S(1)} collective-permute-done((f32[4,16,1,128]{3,2,1,0:T(1,128)S(1)}, f32[4,16,1,128]{3,2,1,0:T(1,128)S(1)}, u32[]{:S(2)}, u32[]{:S(2)}) %collective-permute-start.4) | collective-permute-done | bytes 32800 | tf_op jit(solution)/shard_map/ppermute | solution.py:26
  50.0 1.2 %fusion.70 = (f32[4,16,18,1]{3,2,1,0:T(8,128)}, f32[4,16,18,1]{3,2,1,0:T(8,128)S(1)}) fusion(f32[4,16,18,128]{3,2,1,0:T(8,128)S(1)} %pad_maximum_fusion.1), kind=kLoop, calls=%fused_computation.147 | loop fusion | bytes 18432 | tf_op jit(solution)/shard_map/slice | solution.py:24
  51.2 2.2 %copy.149 = f32[4,16,18,1]{2,1,3,0:T(8,128)} copy(f32[4,16,18,1]{3,2,1,0:T(8,128)} %get-tuple-element.52) | data formatting | bytes 9216 | tf_op jit(solution)/shard_map/slice | solution.py:24
  53.4 1.1 copy.147
  54.5 1.9 %collective-permute-start.6 = (f32[4,16,18,1]{2,1,3,0:T(8,128)}, f32[4,16,18,1]{2,1,3,0:T(8,128)}, u32[]{:S(2)}, u32[]{:S(2)}) collective-permute-start(f32[4,16,18,1]{2,1,3,0:T(8,128)} %copy.147), channel_id=1, source_target_pairs={{1,0},{2,1},{3,2},{5,4},{6,5},{7,6},{9,8},{10,9},{11,10},{13,12},{... | collective-permute-start | bytes 13832 | tf_op jit(solution)/shard_map/ppermute | solution.py:26
  56.4 3.0 %collective-permute-start.7 = (f32[4,16,18,1]{2,1,3,0:T(8,128)}, f32[4,16,18,1]{2,1,3,0:T(8,128)}, u32[]{:S(2)}, u32[]{:S(2)}) collective-permute-start(f32[4,16,18,1]{2,1,3,0:T(8,128)} %copy.149), channel_id=1, source_target_pairs={{0,1},{1,2},{2,3},{4,5},{5,6},{6,7},{8,9},{9,10},{10,11},{12,13},{... | collective-permute-start | bytes 13832 | tf_op jit(solution)/shard_map/ppermute | solution.py:23
  60.0 1.9 %collective-permute-done.7 = f32[4,16,18,1]{2,1,3,0:T(8,128)} collective-permute-done((f32[4,16,18,1]{2,1,3,0:T(8,128)}, f32[4,16,18,1]{2,1,3,0:T(8,128)}, u32[]{:S(2)}, u32[]{:S(2)}) %collective-permute-start.7) | collective-permute-done | bytes 4640 | tf_op jit(solution)/shard_map/ppermute | solution.py:23
  61.9 1.3 %copy.150 = f32[4,16,18,1]{3,2,1,0:T(8,128)S(1)} copy(f32[4,16,18,1]{2,1,3,0:T(8,128)} %collective-permute-done.7) | data formatting | bytes 9216 | tf_op jit(solution)/shard_map/ppermute | solution.py:23
  63.2 2.1 %copy.148 = f32[4,16,18,1]{3,2,1,0:T(8,128)} copy(f32[4,16,18,1]{2,1,3,0:T(8,128)} %collective-permute-done.6) | data formatting | bytes 9216 | tf_op jit(solution)/shard_map/ppermute | solution.py:26
  65.4 2.2 %reduce-window_subtract_fusion.1 = f32[16,18,130]{2,1,0:T(8,128)S(1)} fusion(f32[4,16,18,1]{3,2,1,0:T(8,128)} %copy.148, f32[4,16,1,128]{3,2,1,0:T(1,128)S(1)} %collective-permute-done.4, f32[4,16,16,128]{3,2,1,0:T(8,128)S(1)} %multiply_add_fusion.2, f32[4,16,1,128]{3,2,1,0:T(1,128)S(1)} %collective-permute-done.5, f32[4,16,18,1]{3,2,1,0:T(8,128)S(1)} %copy.150), kind=kOutput, calls=%fused_computation.3 | output fusion | flops 1460160 | bytes 748800 | tf_op jit(solution)/shard_map/jit(cumsum)/reduce_window_sum | solution.py:46
  67.8 0.9 copy-done.4
  68.7 0.9 fusion.7
  69.8 0.9 fusion.73
  70.6 4.8 %collective-permute-start.9 = (f32[4,16,1,128]{3,2,1,0:T(1,128)S(1)}, f32[4,16,1,128]{3,2,1,0:T(1,128)S(1)}, u32[]{:S(2)}, u32[]{:S(2)}) collective-permute-start(f32[4,16,1,128]{3,2,1,0:T(1,128)S(1)} %get-tuple-element.58), channel_id=1, source_target_pairs={{0,4},{4,8},{8,12},{12,16},{16,20},{20,24},{24,28},{1,5},{5,9},{9,... | collective-permute-start | bytes 98312 | tf_op jit(solution)/shard_map/ppermute | solution.py:23
  75.4 1.3 %collective-permute-start.8 = (f32[4,16,1,128]{3,2,1,0:T(1,128)S(1)}, f32[4,16,1,128]{3,2,1,0:T(1,128)S(1)}, u32[]{:S(2)}, u32[]{:S(2)}) collective-permute-start(f32[4,16,1,128]{3,2,1,0:T(1,128)S(1)} %get-tuple-element.59), channel_id=1, source_target_pairs={{4,0},{8,4},{12,8},{16,12},{20,16},{24,20},{28,24},{5,1},{9,5},{13... | collective-permute-start | bytes 98312 | tf_op jit(solution)/shard_map/ppermute | solution.py:26
  77.5 3.8 %collective-permute-done.8 = f32[4,16,1,128]{3,2,1,0:T(1,128)S(1)} collective-permute-done((f32[4,16,1,128]{3,2,1,0:T(1,128)S(1)}, f32[4,16,1,128]{3,2,1,0:T(1,128)S(1)}, u32[]{:S(2)}, u32[]{:S(2)}) %collective-permute-start.8) | collective-permute-done | bytes 32800 | tf_op jit(solution)/shard_map/ppermute | solution.py:26
  81.4 1.2 %fusion.69 = (f32[4,16,18,1]{3,2,1,0:T(8,128)}, f32[4,16,18,1]{3,2,1,0:T(8,128)S(1)}) fusion(f32[4,16,18,128]{3,2,1,0:T(8,128)S(1)} %pad_maximum_fusion.2), kind=kLoop, calls=%fused_computation.146 | loop fusion | bytes 18432 | tf_op jit(solution)/shard_map/slice | solution.py:24
  82.5 2.2 %copy.155 = f32[4,16,18,1]{2,1,3,0:T(8,128)} copy(f32[4,16,18,1]{3,2,1,0:T(8,128)} %get-tuple-element.50) | data formatting | bytes 9216 | tf_op jit(solution)/shard_map/slice | solution.py:24
  84.7 1.1 copy.153
  85.8 1.9 %collective-permute-start.10 = (f32[4,16,18,1]{2,1,3,0:T(8,128)}, f32[4,16,18,1]{2,1,3,0:T(8,128)}, u32[]{:S(2)}, u32[]{:S(2)}) collective-permute-start(f32[4,16,18,1]{2,1,3,0:T(8,128)} %copy.153), channel_id=1, source_target_pairs={{1,0},{2,1},{3,2},{5,4},{6,5},{7,6},{9,8},{10,9},{11,10},{13,12},{... | collective-permute-start | bytes 13832 | tf_op jit(solution)/shard_map/ppermute | solution.py:26
  87.7 3.2 %collective-permute-start.11 = (f32[4,16,18,1]{2,1,3,0:T(8,128)}, f32[4,16,18,1]{2,1,3,0:T(8,128)}, u32[]{:S(2)}, u32[]{:S(2)}) collective-permute-start(f32[4,16,18,1]{2,1,3,0:T(8,128)} %copy.155), channel_id=1, source_target_pairs={{0,1},{1,2},{2,3},{4,5},{5,6},{6,7},{8,9},{9,10},{10,11},{12,13},{... | collective-permute-start | bytes 13832 | tf_op jit(solution)/shard_map/ppermute | solution.py:23
  91.6 1.7 %collective-permute-done.11 = f32[4,16,18,1]{2,1,3,0:T(8,128)} collective-permute-done((f32[4,16,18,1]{2,1,3,0:T(8,128)}, f32[4,16,18,1]{2,1,3,0:T(8,128)}, u32[]{:S(2)}, u32[]{:S(2)}) %collective-permute-start.11) | collective-permute-done | bytes 4640 | tf_op jit(solution)/shard_map/ppermute | solution.py:23
  93.3 1.3 %copy.156 = f32[4,16,18,1]{3,2,1,0:T(8,128)S(1)} copy(f32[4,16,18,1]{2,1,3,0:T(8,128)} %collective-permute-done.11) | data formatting | bytes 9216 | tf_op jit(solution)/shard_map/ppermute | solution.py:23
  94.6 2.1 %copy.154 = f32[4,16,18,1]{3,2,1,0:T(8,128)} copy(f32[4,16,18,1]{2,1,3,0:T(8,128)} %collective-permute-done.10) | data formatting | bytes 9216 | tf_op jit(solution)/shard_map/ppermute | solution.py:26
  96.7 2.2 %reduce-window_subtract_fusion = f32[16,18,130]{2,1,0:T(8,128)S(1)} fusion(f32[4,16,18,1]{3,2,1,0:T(8,128)} %copy.154, f32[4,16,1,128]{3,2,1,0:T(1,128)S(1)} %collective-permute-done.8, f32[4,16,16,128]{3,2,1,0:T(8,128)S(1)} %multiply_add_fusion.1, f32[4,16,1,128]{3,2,1,0:T(1,128)S(1)} %collective-permute-done.9, f32[4,16,18,1]{3,2,1,0:T(8,128)S(1)} %copy.156), kind=kOutput, calls=%fused_computation.2 | output fusion | flops 1460160 | bytes 748800 | tf_op jit(solution)/shard_map/jit(cumsum)/reduce_window_sum | solution.py:46
  99.2 0.9 copy-done.2
  100.1 0.9 fusion.11
  102.0 10.4 %all_to_all.10 = f32[8,3,128]{2,1,0:T(4,128)S(1)} all-to-all(f32[8,3,128]{2,1,0:T(4,128)S(1)} %reshape.140), channel_id=1, replica_groups=mesh['ox'=8,'oy'=4] {'ox'}, dimensions={0} | all-to-all | bytes 24576 | tf_op jit(solution)/shard_map/all_to_all | solution.py:105
  112.3 0.9 convolution_bitcast_fusion.2
  (96 shorter events, 9.9 us)
Async XLA Ops:
  0.6 37.0 %copy-start = (bf16[16,3,128,128]{3,2,1,0:T(8,128)(2,1)S(1)}, bf16[16,3,128,128]{3,2,1,0:T(8,128)(2,1)}, u32[]{:S(2)}) copy-start(bf16[16,3,128,128]{3,2,1,0:T(8,128)(2,1)} %param.15) | copy-start | bytes 4718596
  0.6 18.2 %copy-start.1 = (f32[4,16,16,128]{3,2,1,0:T(8,128)S(1)}, f32[4,16,16,128]{3,2,1,0:T(8,128)}, u32[]{:S(2)}) copy-start(f32[4,16,16,128]{3,2,1,0:T(8,128)} %param.18) | copy-start | bytes 1572868
  0.7 19.2 %copy-start.23 = (s32[16,3]{0,1:T(4,128)S(1)}, s32[16,3]{0,1:T(4,128)}, u32[]{:S(2)}) copy-start(s32[16,3]{0,1:T(4,128)} %param.16) | copy-start | bytes 580
  3.6 33.4 %all-to-all-start = ((bf16[8,3,4,128]{3,2,1,0:T(4,128)(2,1)}), bf16[8,3,4,128]{3,2,1,0:T(4,128)(2,1)S(1)}, u32[]{:S(2)}, u32[]{:S(2)}) async-start(bf16[8,3,4,128]{3,2,1,0:T(4,128)(2,1)} %bitcast.5), calls=%async_computation | async-start | bytes 49152 | tf_op jit(solution)/shard_map/all_to_all | solution.py:86
  10.5 9.6 %collective-permute-start.1 = (f32[4,16,1,128]{3,2,1,0:T(1,128)S(1)}, f32[4,16,1,128]{3,2,1,0:T(1,128)S(1)}, u32[]{:S(2)}, u32[]{:S(2)}) collective-permute-start(f32[4,16,1,128]{3,2,1,0:T(1,128)S(1)} %get-tuple-element.74), channel_id=1, source_target_pairs={{0,4},{4,8},{8,12},{12,16},{16,20},{20,24},{24,28},{1,5},{5,9},{9,... | collective-permute-start | bytes 98312 | tf_op jit(solution)/shard_map/ppermute | solution.py:23
  14.4 5.8 %collective-permute-start = (f32[4,16,1,128]{3,2,1,0:T(1,128)S(1)}, f32[4,16,1,128]{3,2,1,0:T(1,128)S(1)}, u32[]{:S(2)}, u32[]{:S(2)}) collective-permute-start(f32[4,16,1,128]{3,2,1,0:T(1,128)S(1)} %get-tuple-element.75), channel_id=1, source_target_pairs={{4,0},{8,4},{12,8},{16,12},{20,16},{24,20},{28,24},{5,1},{9,5},{13... | collective-permute-start | bytes 98312 | tf_op jit(solution)/shard_map/ppermute | solution.py:26
  21.5 6.4 %copy-start.19 = (s32[16,128]{1,0:T(8,128)S(1)}, s32[16,128]{1,0:T(8,128)}, u32[]{:S(2)}) copy-start(s32[16,128]{1,0:T(8,128)} %param.19) | copy-start | bytes 24580
  23.6 7.7 %collective-permute-start.2 = (f32[4,16,18,1]{2,1,3,0:T(8,128)S(1)}, f32[4,16,18,1]{2,1,3,0:T(8,128)S(1)}, u32[]{:S(2)}, u32[]{:S(2)}) collective-permute-start(f32[4,16,18,1]{2,1,3,0:T(8,128)S(1)} %copy.138), channel_id=1, source_target_pairs={{1,0},{2,1},{3,2},{5,4},{6,5},{7,6},{9,8},{10,9},{11,10},{13,12},{... | collective-permute-start | bytes 13832 | tf_op jit(solution)/shard_map/ppermute | solution.py:26
  25.5 5.2 %collective-permute-start.3 = (f32[4,16,18,1]{2,1,3,0:T(8,128)S(1)}, f32[4,16,18,1]{2,1,3,0:T(8,128)S(1)}, u32[]{:S(2)}, u32[]{:S(2)}) collective-permute-start(f32[4,16,18,1]{2,1,3,0:T(8,128)S(1)} %copy.140), channel_id=1, source_target_pairs={{0,1},{1,2},{2,3},{4,5},{5,6},{6,7},{8,9},{9,10},{10,11},{12,13},{... | collective-permute-start | bytes 13832 | tf_op jit(solution)/shard_map/ppermute | solution.py:23
  32.7 2.5 %copy-start.5 = (f32[4,15,16,128]{3,2,1,0:T(8,128)S(1)}, f32[4,15,16,128]{3,2,1,0:T(8,128)}, u32[]{:S(2)}) copy-start(f32[4,15,16,128]{3,2,1,0:T(8,128)} %get-tuple-element.76) | copy-start | bytes 1474564
  32.7 2.5 %copy-start.6 = (f32[4,15,16,128]{3,2,1,0:T(8,128)S(1)}, f32[4,15,16,128]{3,2,1,0:T(8,128)}, u32[]{:S(2)}) copy-start(f32[4,15,16,128]{3,2,1,0:T(8,128)} %get-tuple-element.77) | copy-start | bytes 1474564
  32.7 2.5 %copy-start.10 = (f32[16,16,128]{2,1,0:T(8,128)S(1)}, f32[16,16,128]{2,1,0:T(8,128)}, u32[]{:S(2)}) copy-start(f32[16,16,128]{2,1,0:T(8,128)} %get-tuple-element.72) | copy-start | bytes 393220
  32.7 2.5 %copy-start.11 = (f32[16,16,128]{2,1,0:T(8,128)S(1)}, f32[16,16,128]{2,1,0:T(8,128)}, u32[]{:S(2)}) copy-start(f32[16,16,128]{2,1,0:T(8,128)} %get-tuple-element.73) | copy-start | bytes 393220
  32.7 2.5 %copy-start.16 = (f32[4,1,16,128]{3,2,1,0:T(8,128)S(1)}, f32[4,1,16,128]{3,2,1,0:T(8,128)}, u32[]{:S(2)}) copy-start(f32[4,1,16,128]{3,2,1,0:T(8,128)} %get-tuple-element.79) | copy-start | bytes 98308
  32.7 2.5 %copy-start.20 = (f32[16]{0:T(128)S(1)}, f32[16]{0:T(128)}, u32[]{:S(2)}) copy-start(f32[16]{0:T(128)} %param.20) | copy-start | bytes 196
  32.7 2.5 %copy-start.21 = (f32[4]{0:T(128)S(1)}, f32[4]{0:T(128)}, u32[]{:S(2)}) copy-start(f32[4]{0:T(128)} %pad.62.clone) | copy-start | bytes 52
  35.0 1.1 %copy-start.3 = (f32[4,16,18,1]{3,2,1,0:T(8,128)S(1)}, f32[4,16,18,1]{3,2,1,0:T(8,128)}, u32[]{:S(2)}) copy-start(f32[4,16,18,1]{3,2,1,0:T(8,128)} %copy.139) | copy-start | bytes 13828
  39.3 6.4 %collective-permute-start.5 = (f32[4,16,1,128]{3,2,1,0:T(1,128)S(1)}, f32[4,16,1,128]{3,2,1,0:T(1,128)S(1)}, u32[]{:S(2)}, u32[]{:S(2)}) collective-permute-start(f32[4,16,1,128]{3,2,1,0:T(1,128)S(1)} %get-tuple-element.66), channel_id=1, source_target_pairs={{0,4},{4,8},{8,12},{12,16},{16,20},{20,24},{24,28},{1,5},{5,9},{9,... | collective-permute-start | bytes 98312 | tf_op jit(solution)/shard_map/ppermute | solution.py:23
  43.7 6.2 %collective-permute-start.4 = (f32[4,16,1,128]{3,2,1,0:T(1,128)S(1)}, f32[4,16,1,128]{3,2,1,0:T(1,128)S(1)}, u32[]{:S(2)}, u32[]{:S(2)}) collective-permute-start(f32[4,16,1,128]{3,2,1,0:T(1,128)S(1)} %get-tuple-element.67), channel_id=1, source_target_pairs={{4,0},{8,4},{12,8},{16,12},{20,16},{24,20},{28,24},{5,1},{9,5},{13... | collective-permute-start | bytes 98312 | tf_op jit(solution)/shard_map/ppermute | solution.py:26
  54.5 8.7 %collective-permute-start.6 = (f32[4,16,18,1]{2,1,3,0:T(8,128)}, f32[4,16,18,1]{2,1,3,0:T(8,128)}, u32[]{:S(2)}, u32[]{:S(2)}) collective-permute-start(f32[4,16,18,1]{2,1,3,0:T(8,128)} %copy.147), channel_id=1, source_target_pairs={{1,0},{2,1},{3,2},{5,4},{6,5},{7,6},{9,8},{10,9},{11,10},{13,12},{... | collective-permute-start | bytes 13832 | tf_op jit(solution)/shard_map/ppermute | solution.py:26
  56.4 5.6 %collective-permute-start.7 = (f32[4,16,18,1]{2,1,3,0:T(8,128)}, f32[4,16,18,1]{2,1,3,0:T(8,128)}, u32[]{:S(2)}, u32[]{:S(2)}) collective-permute-start(f32[4,16,18,1]{2,1,3,0:T(8,128)} %copy.149), channel_id=1, source_target_pairs={{0,1},{1,2},{2,3},{4,5},{5,6},{6,7},{8,9},{9,10},{10,11},{12,13},{... | collective-permute-start | bytes 13832 | tf_op jit(solution)/shard_map/ppermute | solution.py:23
  65.3 2.4 %copy-start.8 = (f32[4,15,16,128]{3,2,1,0:T(8,128)S(1)}, f32[4,15,16,128]{3,2,1,0:T(8,128)}, u32[]{:S(2)}) copy-start(f32[4,15,16,128]{3,2,1,0:T(8,128)} %get-tuple-element.69) | copy-start | bytes 1474564
  65.3 2.5 %copy-start.14 = (f32[16,16,128]{2,1,0:T(8,128)S(1)}, f32[16,16,128]{2,1,0:T(8,128)}, u32[]{:S(2)}) copy-start(f32[16,16,128]{2,1,0:T(8,128)} %get-tuple-element.64) | copy-start | bytes 393220
  65.3 2.5 %copy-start.15 = (f32[16,16,128]{2,1,0:T(8,128)S(1)}, f32[16,16,128]{2,1,0:T(8,128)}, u32[]{:S(2)}) copy-start(f32[16,16,128]{2,1,0:T(8,128)} %get-tuple-element.65) | copy-start | bytes 393220
  65.3 2.5 %copy-start.18 = (f32[4,1,16,128]{3,2,1,0:T(8,128)S(1)}, f32[4,1,16,128]{3,2,1,0:T(8,128)}, u32[]{:S(2)}) copy-start(f32[4,1,16,128]{3,2,1,0:T(8,128)} %get-tuple-element.71) | copy-start | bytes 98308
  65.3 2.5 %copy-start.22 = (f32[4]{0:T(128)S(1)}, f32[4]{0:T(128)}, u32[]{:S(2)}) copy-start(f32[4]{0:T(128)} %pad.62.clone) | copy-start | bytes 52
  67.6 1.1 %copy-start.4 = (f32[4,16,18,1]{3,2,1,0:T(8,128)S(1)}, f32[4,16,18,1]{3,2,1,0:T(8,128)}, u32[]{:S(2)}) copy-start(f32[4,16,18,1]{3,2,1,0:T(8,128)} %copy.148) | copy-start | bytes 13828
  70.6 6.8 %collective-permute-start.9 = (f32[4,16,1,128]{3,2,1,0:T(1,128)S(1)}, f32[4,16,1,128]{3,2,1,0:T(1,128)S(1)}, u32[]{:S(2)}, u32[]{:S(2)}) collective-permute-start(f32[4,16,1,128]{3,2,1,0:T(1,128)S(1)} %get-tuple-element.58), channel_id=1, source_target_pairs={{0,4},{4,8},{8,12},{12,16},{16,20},{20,24},{24,28},{1,5},{5,9},{9,... | collective-permute-start | bytes 98312 | tf_op jit(solution)/shard_map/ppermute | solution.py:23
  75.4 5.8 %collective-permute-start.8 = (f32[4,16,1,128]{3,2,1,0:T(1,128)S(1)}, f32[4,16,1,128]{3,2,1,0:T(1,128)S(1)}, u32[]{:S(2)}, u32[]{:S(2)}) collective-permute-start(f32[4,16,1,128]{3,2,1,0:T(1,128)S(1)} %get-tuple-element.59), channel_id=1, source_target_pairs={{4,0},{8,4},{12,8},{16,12},{20,16},{24,20},{28,24},{5,1},{9,5},{13... | collective-permute-start | bytes 98312 | tf_op jit(solution)/shard_map/ppermute | solution.py:26
  85.8 8.7 %collective-permute-start.10 = (f32[4,16,18,1]{2,1,3,0:T(8,128)}, f32[4,16,18,1]{2,1,3,0:T(8,128)}, u32[]{:S(2)}, u32[]{:S(2)}) collective-permute-start(f32[4,16,18,1]{2,1,3,0:T(8,128)} %copy.153), channel_id=1, source_target_pairs={{1,0},{2,1},{3,2},{5,4},{6,5},{7,6},{9,8},{10,9},{11,10},{13,12},{... | collective-permute-start | bytes 13832 | tf_op jit(solution)/shard_map/ppermute | solution.py:26
  87.7 5.6 %collective-permute-start.11 = (f32[4,16,18,1]{2,1,3,0:T(8,128)}, f32[4,16,18,1]{2,1,3,0:T(8,128)}, u32[]{:S(2)}, u32[]{:S(2)}) collective-permute-start(f32[4,16,18,1]{2,1,3,0:T(8,128)} %copy.155), channel_id=1, source_target_pairs={{0,1},{1,2},{2,3},{4,5},{5,6},{6,7},{8,9},{9,10},{10,11},{12,13},{... | collective-permute-start | bytes 13832 | tf_op jit(solution)/shard_map/ppermute | solution.py:23
  96.7 2.4 %copy-start.7 = (f32[4,15,16,128]{3,2,1,0:T(8,128)S(1)}, f32[4,15,16,128]{3,2,1,0:T(8,128)}, u32[]{:S(2)}) copy-start(f32[4,15,16,128]{3,2,1,0:T(8,128)} %get-tuple-element.61) | copy-start | bytes 1474564
  96.7 2.4 %copy-start.12 = (f32[16,16,128]{2,1,0:T(8,128)S(1)}, f32[16,16,128]{2,1,0:T(8,128)}, u32[]{:S(2)}) copy-start(f32[16,16,128]{2,1,0:T(8,128)} %get-tuple-element.56) | copy-start | bytes 393220
  96.7 2.4 %copy-start.13 = (f32[16,16,128]{2,1,0:T(8,128)S(1)}, f32[16,16,128]{2,1,0:T(8,128)}, u32[]{:S(2)}) copy-start(f32[16,16,128]{2,1,0:T(8,128)} %get-tuple-element.57) | copy-start | bytes 393220
  96.7 2.5 %copy-start.17 = (f32[4,1,16,128]{3,2,1,0:T(8,128)S(1)}, f32[4,1,16,128]{3,2,1,0:T(8,128)}, u32[]{:S(2)}) copy-start(f32[4,1,16,128]{3,2,1,0:T(8,128)} %get-tuple-element.63) | copy-start | bytes 98308
  99.0 1.1 %copy-start.2 = (f32[4,16,18,1]{3,2,1,0:T(8,128)S(1)}, f32[4,16,18,1]{3,2,1,0:T(8,128)}, u32[]{:S(2)}) copy-start(f32[4,16,18,1]{3,2,1,0:T(8,128)} %copy.154) | copy-start | bytes 13828
  101.0 0.7 copy-start.24
  101.0 11.3 %copy-start.25 = (s32[8,3]{0,1:T(4,128)S(1)}, s32[8,3]{0,1:T(4,128)}, u32[]{:S(2)}) copy-start(s32[8,3]{0,1:T(4,128)} %param.17) | copy-start | bytes 292
  101.1 12.1 %copy-start.9 = (f32[4,16,16,128]{3,2,1,0:T(8,128)}, f32[4,16,16,128]{3,2,1,0:T(8,128)S(1)}, u32[]{:S(2)}) copy-start(f32[4,16,16,128]{3,2,1,0:T(8,128)S(1)} %multiply_add_fusion) | copy-start | bytes 1572868

commit v2 on v1

--- a/solution.py
+++ b/solution.py
@@ -87,15 +87,30 @@
     incoming = incoming.reshape((slots,) + incoming.shape[2:])
     picks = incoming[tile_slots]
     forcing = jnp.einsum("tkfa,tkra->ftr", picks, remap_weights, preferred_element_type=jnp.float32)
-    lat_cells = ocean_state.shape[3]
+    fields, levels, rows, lat_cells = ocean_state.shape
     lat_total = lat_cells * lax.axis_size("oy")
     lat_start = lax.axis_index("oy") * lat_cells
     wetness = land_mask.astype(jnp.float32)
-    state = ocean_state
-    coriolis = lat_factor(lat_start, lat_cells, lat_total)
+    packed = jnp.concatenate(
+        [ocean_state.reshape(fields * levels, rows, lat_cells), forcing, wetness[None]], axis=0
+    )
+    packed = with_halo(packed, (("ox", 1), ("oy", 2)), STEPS)
+    state = packed[: fields * levels].reshape(fields, levels, rows + 2 * STEPS, lat_cells + 2 * STEPS)
+    forcing_wide = packed[fields * levels : fields * levels + fields]
+    wetness_wide = packed[fields * levels + fields]
+    coriolis_wide = lat_factor(lat_start - STEPS, lat_cells + 2 * STEPS, lat_total)
     for repeat in range(STEPS):
-        padded = with_halo(state, (("ox", 2), ("oy", 3)), 1)
-        state = advance(padded, state, diffusivity, coriolis, forcing, wetness)
+        lo = repeat + 1
+        hi_x = rows + 2 * STEPS - lo
+        hi_y = lat_cells + 2 * STEPS - lo
+        state = advance(
+            state,
+            state[:, :, 1:-1, 1:-1],
+            diffusivity,
+            coriolis_wide[lo:hi_y],
+            forcing_wide[:, lo:hi_x, lo:hi_y],
+            wetness_wide[lo:hi_x, lo:hi_y],
+        )
     surface = state[2, 0].astype(jnp.bfloat16)
     pieces = jnp.einsum("tkra,tr->tka", remap_weights, surface, preferred_element_type=jnp.float32)
     slot_line = jnp.arange(slots, dtype=jnp.int32)

time: 114 us -> 85 us (0.75)
  starting transfers between devices: 37.1 us -> 18.1 us
  local copies, waits for them, and re-layouts: 37.1 us -> 25.6 us
  other arithmetic: 11.4 us -> 22.1 us
  blocking collectives: 10.4 us -> 0 us
    ppermute x6 -> x2, starting transfers between devices: 21.7 us -> 5.41 us  [with_halo(): lax.ppermute(lax.slice_in_dim(block, block.shape[dim] - width, None, axis...]
    all_to_all x1 -> x0, blocking collectives: 10.4 us -> none  [per_device(): returned = lax.all_to_all(per_slot, 'ox', 0, 0, tiled=True)]
    slice x9 -> x2, local copies, waits for them, and re-layouts: 10.7 us -> 1.27 us  [with_halo(): lax.slice_in_dim(block, block.shape[dim] - width, None, axis=dim)]
    ppermute x6 -> x2, starting transfers between devices: 9.61 us -> 3.22 us  [with_halo(): lax.ppermute(lax.slice_in_dim(block, 0, width, axis=dim), axis, backward)]
    all_to_all x0 -> x1, waiting for transfers between devices: none -> 5.62 us  [per_device(): returned = lax.all_to_all(per_slot, 'ox', 0, 0, tiled=True)]
    another operation x3, other arithmetic: 6.71 us -> 1.19 us  [advance(): pressure = jnp.cumsum(density, axis=0) - 0.5 * density]
    add x3, other arithmetic: 0.22 us -> 5.43 us  [advance(): return center + wetness * total]
    scatter-add x0 -> x3, local copies, waits for them, and re-layouts: none -> 5.21 us  [advance(): total = total.at[:, 0].add(forcing_coef * forcing)]
  transfers between devices with their start and end apart: 13 -> 6, of which waited for: 6 -> 5; matrix products, arithmetic and copies ran while one was open for 17% -> 8% of each run, Pallas kernels for 0% -> 0%
where the time goes in v2:
time: 85 us; the launch traced here: 84.1 us
  local copies, waits for them, and re-layouts  25.6 us (30%)
  other arithmetic  22.1 us (26%)
  starting transfers between devices  18.1 us (21%)
  waiting for transfers between devices  14.9 us (18%)
  matrix products  2.15 us (3%)
  between operations  1.27 us (1%)
    all_to_all x1, starting transfers between devices, per_device(): incoming = lax.all_to_all(outgoing, 'ox', 0, 0, tiled=True)  5.81 us
    all_to_all x1, waiting for transfers between devices, per_device(): returned = lax.all_to_all(per_slot, 'ox', 0, 0, tiled=True)  5.62 us
    add x3, other arithmetic, advance(): total = advection + laplace + mixing + momentum  5.53 us
    add x3, other arithmetic, advance(): return center + wetness * total  5.43 us
    ppermute x2, starting transfers between devices, with_halo(): lax.ppermute(lax.slice_in_dim(block, block.shape[dim] - width, None, axis...  5.41 us
    scatter-add x3, local copies, waits for them, and re-layouts, advance(): total = total.at[:, 0].add(forcing_coef * forcing)  5.21 us
    unnamed x73, local copies, waits for them, and re-layouts  5.2 us
    ppermute x2, waiting for transfers between devices, with_halo(): lax.ppermute(lax.slice_in_dim(block, 0, width, axis=dim), axis, backward)  4.34 us
  transfers between devices with their start and end apart: 6, of which 5 were waited for; matrix products, arithmetic and copies ran while one was open for 8% of the time, Pallas kernels for 0%

profile of v2, /device:TPU:4, one launch (start us, length us, event | category | flops | bytes accessed | tf_op | source)
XLA Modules:
  0.0 84.1 jit_solution(116284407046223444)
XLA Ops:
  0.7 0.8 compare_select_fusion.1
  1.7 1.9 %gather_fusion = bf16[24,4,128]{2,1,0:T(4,128)(2,1)} fusion(bf16[4,10,128]{2,0,1:T(4,128)(2,1)} %param.14, s32[1024]{0:T(1024)S(1)} %pad_clamp_fusion.1), kind=kCustom, calls=%fused_computation | custom fusion | bytes 49248 | tf_op jit(solution)/shard_map/gather | solution.py:85
  3.6 5.8 %all-to-all-start = ((bf16[8,3,4,128]{3,2,1,0:T(4,128)(2,1)}), bf16[8,3,4,128]{3,2,1,0:T(4,128)(2,1)S(1)}, u32[]{:S(2)}, u32[]{:S(2)}) async-start(bf16[8,3,4,128]{3,2,1,0:T(4,128)(2,1)} %bitcast.1), calls=%async_computation | async-start | bytes 49152 | tf_op jit(solution)/shard_map/all_to_all | solution.py:86
  9.4 0.7 fusion.61
  10.0 0.7 fusion.62
  10.7 0.7 compare_select_fusion
  11.6 0.7 convert_bitcast_fusion
  12.3 3.7 %all-to-all-done = bf16[8,3,4,128]{3,2,1,0:T(4,128)(2,1)S(1)} async-done(((bf16[8,3,4,128]{3,2,1,0:T(4,128)(2,1)}), bf16[8,3,4,128]{3,2,1,0:T(4,128)(2,1)S(1)}, u32[]{:S(2)}, u32[]{:S(2)}) %all-to-all-start) | async-done | bytes 24608 | tf_op jit(solution)/shard_map/all_to_all | solution.py:86
  16.0 0.6 gather_fusion.1
  16.6 0.6 convolution_bitcast_fusion
  17.4 2.4 %collective-permute-start = (f32[69,3,128]{2,1,0:T(4,128)S(1)}, f32[69,3,128]{2,1,0:T(4,128)S(1)}, u32[]{:S(2)}, u32[]{:S(2)}) collective-permute-start(f32[69,3,128]{2,1,0:T(4,128)S(1)} %get-tuple-element.85), channel_id=1, source_target_pairs={{0,4},{4,8},{8,12},{12,16},{16,20},{20,24},{24,28},{1,5},{5,9},{9,... | collective-permute-start | bytes 317960 | tf_op jit(solution)/shard_map/ppermute | solution.py:23
  19.8 1.3 %collective-permute-start.1 = (f32[69,3,128]{2,1,0:T(4,128)S(1)}, f32[69,3,128]{2,1,0:T(4,128)S(1)}, u32[]{:S(2)}, u32[]{:S(2)}) collective-permute-start(f32[69,3,128]{2,1,0:T(4,128)S(1)} %get-tuple-element.86), channel_id=1, source_target_pairs={{4,0},{8,4},{12,8},{16,12},{20,16},{24,20},{28,24},{5,1},{9,5},{13... | collective-permute-start | bytes 317960 | tf_op jit(solution)/shard_map/ppermute | solution.py:26
  21.1 0.6 fusion.60
  21.7 0.6 pad.22.clone
  22.4 4.3 %collective-permute-done.1 = f32[69,3,128]{2,1,0:T(4,128)S(1)} collective-permute-done((f32[69,3,128]{2,1,0:T(4,128)S(1)}, f32[69,3,128]{2,1,0:T(4,128)S(1)}, u32[]{:S(2)}, u32[]{:S(2)}) %collective-permute-start.1) | collective-permute-done | bytes 106016 | tf_op jit(solution)/shard_map/ppermute | solution.py:26
  27.2 1.0 %copy.314 = f32[69,22,3]{0,1,2:T(8,128)} copy(f32[69,22,3]{2,1,0:T(8,128)S(1)} %get-tuple-element.83) | data formatting | bytes 36432 | tf_op jit(solution)/shard_map/slice | solution.py:24
  28.5 1.9 %collective-permute-start.3 = (f32[69,22,3]{0,1,2:T(8,128)S(1)}, f32[69,22,3]{0,1,2:T(8,128)}, u32[]{:S(2)}, u32[]{:S(2)}) collective-permute-start(f32[69,22,3]{0,1,2:T(8,128)S(1)} %copy.315), channel_id=1, source_target_pairs={{1,0},{2,1},{3,2},{5,4},{6,5},{7,6},{9,8},{10,9},{11,10},{13,12},{... | collective-permute-start | bytes 54656 | tf_op jit(solution)/shard_map/ppermute | solution.py:26
  30.5 3.0 %collective-permute-start.2 = (f32[69,22,3]{0,1,2:T(8,128)}, f32[69,22,3]{0,1,2:T(8,128)S(1)}, u32[]{:S(2)}, u32[]{:S(2)}) collective-permute-start(f32[69,22,3]{0,1,2:T(8,128)} %copy.314), channel_id=1, source_target_pairs={{0,1},{1,2},{2,3},{4,5},{5,6},{6,7},{8,9},{9,10},{10,11},{12,13},{... | collective-permute-start | bytes 54656 | tf_op jit(solution)/shard_map/ppermute | solution.py:23
  33.5 1.4 %broadcast_multiply_fusion = f32[4,16,128]{2,1,0:T(8,128)} fusion(f32[16,4,128]{2,1,0:T(4,128)} %copy-done.18), kind=kLoop, calls=%fused_computation.91 | loop fusion | flops 8192 | bytes 65536 | tf_op jit(solution)/shard_map/mul | solution.py:54
  34.8 1.1 %collective-permute-done.2 = f32[69,22,3]{0,1,2:T(8,128)S(1)} collective-permute-done((f32[69,22,3]{0,1,2:T(8,128)}, f32[69,22,3]{0,1,2:T(8,128)S(1)}, u32[]{:S(2)}, u32[]{:S(2)}) %collective-permute-start.2) | collective-permute-done | bytes 18248 | tf_op jit(solution)/shard_map/ppermute | solution.py:23
  36.4 1.2 %copy.317 = f32[69,22,3]{2,1,0:T(8,128)S(1)} copy(f32[69,22,3]{0,1,2:T(8,128)} %collective-permute-done.3) | data formatting | bytes 36432 | tf_op jit(solution)/shard_map/ppermute | solution.py:26
  37.7 0.9 %maximum_bitcast_fusion = f32[22,134]{1,0:T(8,128)S(1)} fusion(f32[69,22,3]{2,1,0:T(8,128)S(1)} %copy.317, f32[69,22,3]{2,1,0:T(8,128)S(1)} %copy.316, f32[69,3,128]{2,1,0:T(4,128)S(1)} %collective-permute-done.1, f32[69,3,128]{2,1,0:T(4,128)S(1)} %collective-permute-done, f32[1,16,128]{2,1,0:T(8,128)} %copy-done.15, f32[4,16,128]{2,1,0:T(8,128)} %bitcast.101, ...), kind=kLoop, calls=%fused_computation.87 | loop fusion | flops 17688 | bytes 825440 | tf_op jit(solution)/shard_map/squeeze | solution.py:100
  38.6 0.7 slice.424
  39.3 0.7 slice.405
  39.9 0.7 slice.386
  40.6 1.1 %pad_maximum_fusion = f32[69,22,134]{2,1,0:T(8,128)S(1)} fusion(f32[69,22,3]{2,1,0:T(8,128)S(1)} %copy.317, f32[69,3,128]{2,1,0:T(4,128)S(1)} %collective-permute-done.1, f32[1,16,128]{2,1,0:T(8,128)S(1)} %copy-done.16, f32[4,16,128]{2,1,0:T(8,128)S(1)} %bitcast.102, f32[64,16,128]{2,1,0:T(8,128)S(1)} %bitcast.95, f32[69,3,128]{2,1,0:T(4,128)S(1)} %collective-permute-done, ...), kind=kLoop, calls=%fused_computation.2 | loop fusion | flops 1220472 | bytes 1627296 | tf_op jit(solution)/shard_map/concatenate | solution.py:27
  42.5 0.5 copy.318
  43.0 0.8 fusion.53
  43.8 1.8 %fusion.52 = (f32[4,16,20,132]{3,2,1,0:T(8,128)S(1)}, f32[4,16,20,132]{3,2,1,0:T(8,128)S(1)}, f32[4,16,20,132]{3,2,1,0:T(8,128)S(1)}, f32[4,16,20,132]{3,2,1,0:T(8,128)S(1)}, f32[4,16,20,132]{3,2,1,0:T(8,128)S(1)}) fusion(f32[4,16,22,134]{3,2,1,0:T(8,128)S(1)} %bitcast.90), kind=kLoop, calls=%fused_computation.110 | loop fusion | bytes 6758400 | tf_op jit(solution)/shard_map/slice | solution.py:108
  47.2 0.5 fusion.15
  48.3 3.6 %fusion.3 = f32[4,16,20,132]{3,1,2,0:T(8,128)S(1)} fusion(f32[4,15,20,132]{3,1,2,0:T(8,128)S(1)} %copy.366, f32[4,1,20,132]{3,1,2,0:T(1,128)S(1)} %copy.365, f32[4,1,20,132]{3,1,2,0:T(1,128)S(1)} %copy.368, f32[4,15,20,132]{3,1,2,0:T(8,128)S(1)} %copy.367, f32[1,16,20,132]{3,1,2,0:T(8,128)S(1)} %get-tuple-element.95, ...), kind=kLoop, calls=%fused_computation.7 | loop fusion | flops 3886080 | bytes 6082640 | tf_op jit(solution)/shard_map/add | solution.py:53
  52.1 0.9 %copy-done.10 = f32[4,16,20,132]{3,1,2,0:T(8,128)} copy-done((f32[4,16,20,132]{3,1,2,0:T(8,128)}, f32[4,16,20,132]{3,1,2,0:T(8,128)S(1)}, u32[]{:S(2)}) %copy-start.10) | copy-done | bytes 675864
  53.1 2.6 %scatter-add.10 = f32[4,16,20,132]{3,1,2,0:T(8,128)} dynamic-update-slice(f32[4,16,20,132]{3,1,2,0:T(8,128)} %copy-done.10, f32[4,1,20,132]{3,1,2,0:T(1,128)S(1)} %slice_add_fusion, s32[]{:T(128)} %constant.124.clone.1, s32[]{:T(128)} %constant.124.clone.1, s32[]{:T(128)} %constant.124.clone.1, s32[]{:T(128)} %constant.124.clone.1) | dynamic-update-slice | bytes 84484 | tf_op jit(solution)/shard_map/scatter-add | solution.py:54
  55.7 2.3 %multiply_add_fusion = f32[4,16,20,132]{3,1,2,0:T(8,128)S(1)} fusion(f32[4,16,20,132]{3,1,2,0:T(8,128)} %scatter-add.10, f32[4,16,20,132]{3,2,1,0:T(8,128)} %copy-done.9, f32[20,132]{1,0:T(8,128)} %slice.386), kind=kLoop, calls=%fused_computation.8 | loop fusion | flops 337920 | bytes 2038080 | tf_op jit(solution)/shard_map/add | solution.py:55
  58.7 0.7 fusion.55
  59.4 0.5 fusion.19
  60.2 0.4 fusion.31
  60.8 1.3 %fusion.7 = f32[4,16,18,130]{3,1,2,0:T(8,128)S(1)} fusion(f32[4,15,18,130]{3,1,2,0:T(8,128)S(1)} %get-tuple-element.74, f32[4,1,18,130]{3,1,2,0:T(1,128)S(1)} %get-tuple-element.76, f32[4,1,18,130]{3,1,2,0:T(1,128)S(1)} %get-tuple-element.75, f32[4,15,18,130]{3,1,2,0:T(8,128)S(1)} %get-tuple-element.73, f32[1,16,18,130]{3,1,2,0:T(8,128)S(1)} %get-tuple-element.59, ...), kind=kLoop, calls=%fused_computation.14 | loop fusion | flops 3444480 | bytes 5391440 | tf_op jit(solution)/shard_map/add | solution.py:53
  62.5 0.9 %copy-done.11 = f32[4,16,18,130]{3,1,2,0:T(8,128)} copy-done((f32[4,16,18,130]{3,1,2,0:T(8,128)}, f32[4,16,18,130]{3,1,2,0:T(8,128)S(1)}, u32[]{:S(2)}) %copy-start.11) | copy-done | bytes 599064
  63.5 2.5 %scatter-add.11 = f32[4,16,18,130]{3,1,2,0:T(8,128)} dynamic-update-slice(f32[4,16,18,130]{3,1,2,0:T(8,128)} %copy-done.11, f32[4,1,18,130]{3,1,2,0:T(1,128)S(1)} %slice_add_fusion.1, s32[]{:T(128)} %constant.124.clone.1, s32[]{:T(128)} %constant.124.clone.1, s32[]{:T(128)} %constant.124.clone.1, s32[]{:T(128)} %constant.124.clone.1) | dynamic-update-slice | bytes 74884 | tf_op jit(solution)/shard_map/scatter-add | solution.py:54
  66.0 1.7 %multiply_add_fusion.1 = f32[4,16,18,130]{3,1,2,0:T(8,128)S(1)} fusion(f32[4,16,18,130]{3,1,2,0:T(8,128)} %scatter-add.11, f32[4,16,20,132]{3,1,2,0:T(8,128)S(1)} %multiply_add_fusion, f32[18,130]{1,0:T(8,128)S(1)} %copy-done.20), kind=kLoop, calls=%fused_computation.15 | loop fusion | flops 299520 | bytes 1806480 | tf_op jit(solution)/shard_map/add | solution.py:55
  69.3 0.6 fusion.11
  70.3 1.4 %multiply_add_fusion.2 = f32[4,16,16,128]{3,1,2,0:T(8,128)S(1)} fusion(f32[4,16,16,128]{3,1,2,0:T(8,128)S(1)} %scatter-add.14, f32[4,16,18,130]{3,1,2,0:T(8,128)} %copy-done.1, f32[16,128]{1,0:T(8,128)S(1)} %copy-done.21), kind=kLoop, calls=%fused_computation.25 | loop fusion | flops 262144 | bytes 1581056 | tf_op jit(solution)/shard_map/add | solution.py:55
  72.4 0.6 reshape.155
  73.0 3.7 %all-to-all-start.1 = ((f32[8,3,128]{2,1,0:T(4,128)}), f32[8,3,128]{2,1,0:T(4,128)S(1)}, u32[]{:S(2)}, u32[]{:S(2)}) async-start(f32[8,3,128]{2,1,0:T(4,128)} %reshape.155), calls=%async_computation.1 | async-start | bytes 32768 | tf_op jit(solution)/shard_map/all_to_all | solution.py:120
  76.7 1.0 %copy.342 = f32[4,16,16,128]{3,2,1,0:T(8,128)} copy(f32[4,16,16,128]{3,1,2,0:T(8,128)S(1)} %multiply_add_fusion.2) | data formatting | bytes 1048576
  77.7 5.6 %all-to-all-done.1 = f32[8,3,128]{2,1,0:T(4,128)S(1)} async-done(((f32[8,3,128]{2,1,0:T(4,128)}), f32[8,3,128]{2,1,0:T(4,128)S(1)}, u32[]{:S(2)}, u32[]{:S(2)}) %all-to-all-start.1) | async-done | bytes 12320 | tf_op jit(solution)/shard_map/all_to_all | solution.py:120
  83.3 0.9 %convolution_bitcast_fusion.2 = f32[10,128]{1,0:T(8,128)} fusion(f32[8,3,128]{2,1,0:T(4,128)S(1)} %all-to-all-done.1, s32[8,3]{0,1:T(4,128)S(1)} %copy-done.31), kind=kOutput, calls=%fused_computation.18 | convolution fusion | flops 368880 | bytes 17504 | tf_op jit(solution)/shard_map/isb,isa->ba/dot_general | solution.py:123
  (112 shorter events, 8.9 us)
Async XLA Ops:
  0.6 16.0 %copy-start = (bf16[16,3,128,128]{3,2,1,0:T(8,128)(2,1)S(1)}, bf16[16,3,128,128]{3,2,1,0:T(8,128)(2,1)}, u32[]{:S(2)}) copy-start(bf16[16,3,128,128]{3,2,1,0:T(8,128)(2,1)} %param.15) | copy-start | bytes 4718596
  0.6 16.7 %copy-start.6 = (f32[4,16,16,128]{3,2,1,0:T(8,128)S(1)}, f32[4,16,16,128]{3,2,1,0:T(8,128)}, u32[]{:S(2)}) copy-start(f32[4,16,16,128]{3,2,1,0:T(8,128)} %param.18) | copy-start | bytes 1572868
  3.6 12.4 %all-to-all-start = ((bf16[8,3,4,128]{3,2,1,0:T(4,128)(2,1)}), bf16[8,3,4,128]{3,2,1,0:T(4,128)(2,1)S(1)}, u32[]{:S(2)}, u32[]{:S(2)}) async-start(bf16[8,3,4,128]{3,2,1,0:T(4,128)(2,1)} %bitcast.1), calls=%async_computation | async-start | bytes 49152 | tf_op jit(solution)/shard_map/all_to_all | solution.py:86
  12.3 14.5 %copy-start.15 = (f32[1,16,128]{2,1,0:T(8,128)}, f32[1,16,128]{2,1,0:T(8,128)S(1)}, u32[]{:S(2)}) copy-start(f32[1,16,128]{2,1,0:T(8,128)S(1)} %convert_bitcast_fusion) | copy-start | bytes 24580
  17.3 9.5 %copy-start.18 = (f32[16,4,128]{2,1,0:T(4,128)}, f32[16,4,128]{2,1,0:T(4,128)S(1)}, u32[]{:S(2)}) copy-start(f32[16,4,128]{2,1,0:T(4,128)S(1)} %convolution_bitcast_fusion) | copy-start | bytes 98308
  17.3 9.5 %copy-start.12 = (f32[16,4,128]{2,0,1:T(8,128)}, f32[16,4,128]{2,0,1:T(8,128)S(1)}, u32[]{:S(2)}) copy-start(f32[16,4,128]{2,0,1:T(8,128)S(1)} %copy.397) | copy-start | bytes 98308
  17.4 5.1 %collective-permute-start = (f32[69,3,128]{2,1,0:T(4,128)S(1)}, f32[69,3,128]{2,1,0:T(4,128)S(1)}, u32[]{:S(2)}, u32[]{:S(2)}) collective-permute-start(f32[69,3,128]{2,1,0:T(4,128)S(1)} %get-tuple-element.85), channel_id=1, source_target_pairs={{0,4},{4,8},{8,12},{12,16},{16,20},{20,24},{24,28},{1,5},{5,9},{9,... | collective-permute-start | bytes 317960 | tf_op jit(solution)/shard_map/ppermute | solution.py:23
  19.8 7.0 %collective-permute-start.1 = (f32[69,3,128]{2,1,0:T(4,128)S(1)}, f32[69,3,128]{2,1,0:T(4,128)S(1)}, u32[]{:S(2)}, u32[]{:S(2)}) collective-permute-start(f32[69,3,128]{2,1,0:T(4,128)S(1)} %get-tuple-element.86), channel_id=1, source_target_pairs={{4,0},{8,4},{12,8},{16,12},{20,16},{24,20},{28,24},{5,1},{9,5},{13... | collective-permute-start | bytes 317960 | tf_op jit(solution)/shard_map/ppermute | solution.py:26
  28.5 7.8 %collective-permute-start.3 = (f32[69,22,3]{0,1,2:T(8,128)S(1)}, f32[69,22,3]{0,1,2:T(8,128)}, u32[]{:S(2)}, u32[]{:S(2)}) collective-permute-start(f32[69,22,3]{0,1,2:T(8,128)S(1)} %copy.315), channel_id=1, source_target_pairs={{1,0},{2,1},{3,2},{5,4},{6,5},{7,6},{9,8},{10,9},{11,10},{13,12},{... | collective-permute-start | bytes 54656 | tf_op jit(solution)/shard_map/ppermute | solution.py:26
  30.5 5.5 %collective-permute-start.2 = (f32[69,22,3]{0,1,2:T(8,128)}, f32[69,22,3]{0,1,2:T(8,128)S(1)}, u32[]{:S(2)}, u32[]{:S(2)}) collective-permute-start(f32[69,22,3]{0,1,2:T(8,128)} %copy.314), channel_id=1, source_target_pairs={{0,1},{1,2},{2,3},{4,5},{5,6},{6,7},{8,9},{9,10},{10,11},{12,13},{... | collective-permute-start | bytes 54656 | tf_op jit(solution)/shard_map/ppermute | solution.py:23
  36.4 15.5 %copy-start.2 = (f32[69,22,3]{2,1,0:T(8,128)}, f32[69,22,3]{2,1,0:T(8,128)S(1)}, u32[]{:S(2)}) copy-start(f32[69,22,3]{2,1,0:T(8,128)S(1)} %copy.316) | copy-start | bytes 54652
  37.6 14.3 %copy-start.4 = (f32[69,22,3]{2,1,0:T(8,128)}, f32[69,22,3]{2,1,0:T(8,128)S(1)}, u32[]{:S(2)}) copy-start(f32[69,22,3]{2,1,0:T(8,128)S(1)} %copy.317) | copy-start | bytes 54652
  37.6 3.0 %copy-start.7 = (f32[4,16,16,128]{3,2,1,0:T(8,128)S(1)}, f32[4,16,16,128]{3,2,1,0:T(8,128)}, u32[]{:S(2)}) copy-start(f32[4,16,16,128]{3,2,1,0:T(8,128)} %param.18) | copy-start | bytes 1572868
  37.6 3.0 %copy-start.13 = (f32[16,4,128]{2,0,1:T(8,128)S(1)}, f32[16,4,128]{2,0,1:T(8,128)}, u32[]{:S(2)}) copy-start(f32[16,4,128]{2,0,1:T(8,128)} %copy-done.12) | copy-start | bytes 98308
  37.6 3.0 %copy-start.16 = (f32[1,16,128]{2,1,0:T(8,128)S(1)}, f32[1,16,128]{2,1,0:T(8,128)}, u32[]{:S(2)}) copy-start(f32[1,16,128]{2,1,0:T(8,128)} %copy-done.15) | copy-start | bytes 24580
  45.6 2.3 %copy-start.9 = (f32[4,16,20,132]{3,2,1,0:T(8,128)}, f32[4,16,20,132]{3,2,1,0:T(8,128)S(1)}, u32[]{:S(2)}) copy-start(f32[4,16,20,132]{3,2,1,0:T(8,128)S(1)} %get-tuple-element.60) | copy-start | bytes 2027524
  46.5 0.7 copy-start.28
  46.5 0.7 copy-start.29
  47.7 0.7 copy-start.22
  47.7 0.6 copy-start.24
  51.9 1.1 %copy-start.10 = (f32[4,16,20,132]{3,1,2,0:T(8,128)}, f32[4,16,20,132]{3,1,2,0:T(8,128)S(1)}, u32[]{:S(2)}) copy-start(f32[4,16,20,132]{3,1,2,0:T(8,128)S(1)} %fusion.3) | copy-start | bytes 2027524
  59.4 0.7 copy-start.26
  59.4 0.7 copy-start.27
  60.1 0.7 copy-start.23
  60.1 0.6 copy-start.25
  60.8 1.4 %copy-start.3 = (f32[69,22,3]{2,1,0:T(8,128)S(1)}, f32[69,22,3]{2,1,0:T(8,128)}, u32[]{:S(2)}) copy-start(f32[69,22,3]{2,1,0:T(8,128)} %copy-done.2) | copy-start | bytes 54652
  60.8 1.4 %copy-start.5 = (f32[69,22,3]{2,1,0:T(8,128)S(1)}, f32[69,22,3]{2,1,0:T(8,128)}, u32[]{:S(2)}) copy-start(f32[69,22,3]{2,1,0:T(8,128)} %copy-done.4) | copy-start | bytes 54652
  60.8 1.5 %copy-start.8 = (f32[4,16,16,128]{3,2,1,0:T(8,128)S(1)}, f32[4,16,16,128]{3,2,1,0:T(8,128)}, u32[]{:S(2)}) copy-start(f32[4,16,16,128]{3,2,1,0:T(8,128)} %param.18) | copy-start | bytes 1572868
  60.8 1.5 %copy-start.14 = (f32[16,4,128]{2,0,1:T(8,128)S(1)}, f32[16,4,128]{2,0,1:T(8,128)}, u32[]{:S(2)}) copy-start(f32[16,4,128]{2,0,1:T(8,128)} %copy-done.12) | copy-start | bytes 98308
  60.8 1.5 %copy-start.17 = (f32[1,16,128]{2,1,0:T(8,128)S(1)}, f32[1,16,128]{2,1,0:T(8,128)}, u32[]{:S(2)}) copy-start(f32[1,16,128]{2,1,0:T(8,128)} %copy-done.15) | copy-start | bytes 24580
  62.3 1.1 %copy-start.11 = (f32[4,16,18,130]{3,1,2,0:T(8,128)}, f32[4,16,18,130]{3,1,2,0:T(8,128)S(1)}, u32[]{:S(2)}) copy-start(f32[4,16,18,130]{3,1,2,0:T(8,128)S(1)} %fusion.7) | copy-start | bytes 1797124
  62.3 3.6 %copy-start.20 = (f32[18,130]{1,0:T(8,128)S(1)}, f32[18,130]{1,0:T(8,128)}, u32[]{:S(2)}) copy-start(f32[18,130]{1,0:T(8,128)} %slice.405) | copy-start | bytes 28084
  67.6 1.7 %copy-start.1 = (f32[4,16,18,130]{3,1,2,0:T(8,128)}, f32[4,16,18,130]{3,1,2,0:T(8,128)S(1)}, u32[]{:S(2)}) copy-start(f32[4,16,18,130]{3,1,2,0:T(8,128)S(1)} %multiply_add_fusion.1) | copy-start | bytes 1797124
  68.4 0.6 copy-start.32
  68.4 0.7 copy-start.33
  69.3 0.8 copy-start.19
  69.3 0.9 %copy-start.21 = (f32[16,128]{1,0:T(8,128)S(1)}, f32[16,128]{1,0:T(8,128)}, u32[]{:S(2)}) copy-start(f32[16,128]{1,0:T(8,128)} %slice.424) | copy-start | bytes 24580
  70.3 1.8 %copy-start.30 = (s32[16,3]{0,1:T(4,128)S(1)}, s32[16,3]{0,1:T(4,128)}, u32[]{:S(2)}) copy-start(s32[16,3]{0,1:T(4,128)} %param.16) | copy-start | bytes 580
  71.7 11.6 %copy-start.31 = (s32[8,3]{0,1:T(4,128)S(1)}, s32[8,3]{0,1:T(4,128)}, u32[]{:S(2)}) copy-start(s32[8,3]{0,1:T(4,128)} %param.17) | copy-start | bytes 292
  73.0 10.3 %all-to-all-start.1 = ((f32[8,3,128]{2,1,0:T(4,128)}), f32[8,3,128]{2,1,0:T(4,128)S(1)}, u32[]{:S(2)}, u32[]{:S(2)}) async-start(f32[8,3,128]{2,1,0:T(4,128)} %reshape.155), calls=%async_computation.1 | async-start | bytes 32768 | tf_op jit(solution)/shard_map/all_to_all | solution.py:120

commit v3 on v1

--- a/solution.py
+++ b/solution.py
@@ -1,6 +1,8 @@
 import jax
 import jax.numpy as jnp
 from jax import lax
+from jax.experimental import pallas as pl
+from jax.experimental.pallas import tpu as pltpu
 from jax.sharding import PartitionSpec as P
 
 STEPS = 3
@@ -53,6 +55,106 @@
     total = advection + laplace + mixing + momentum
     total = total.at[:, 0].add(forcing_coef * forcing)
     return center + wetness * total
+
+
+def stencil_kernel(diff_ref, cor_ref, src_ref, out_ref, first, second):
+    fields, levels, rows, lanes = out_ref.shape
+    channels = fields * levels
+    tall, wide = src_ref.shape[1], src_ref.shape[2]
+
+    def one_step(read, write):
+        def level(l, cum):
+            up = jnp.maximum(l - 1, 0)
+            down = jnp.minimum(l + 1, levels - 1)
+            here = [read(f * levels + l) for f in range(fields)]
+            density = haline_coef * here[3] - thermal_coef * here[2]
+            cum = cum + density
+            pressure = cum - 0.5 * density
+            zonal = here[0]
+            meridional = here[1]
+            top = jnp.where(l == 0, forcing_coef, 0.0)
+            diff = diff_ref[l]
+            coriolis = cor_ref[...]
+            for f in range(fields):
+                center = here[f]
+                east = pltpu.roll(center, tall - 1, 0)
+                west = pltpu.roll(center, 1, 0)
+                north = pltpu.roll(center, wide - 1, 1)
+                south = pltpu.roll(center, 1, 1)
+                advection = -advect_coef * 0.5 * (zonal * (east - west) + meridional * (north - south))
+                laplace = diff * (east + west + north + south - 4.0 * center)
+                mixing = vertical_coef * (
+                    read(f * levels + up) + read(f * levels + down) - 2.0 * center
+                )
+                total = advection + laplace + mixing
+                if f == 0:
+                    grad = pltpu.roll(pressure, tall - 1, 0) - pltpu.roll(pressure, 1, 0)
+                    total = total + (coriolis * meridional - pressure_coef * 0.5 * grad)
+                if f == 1:
+                    grad = pltpu.roll(pressure, wide - 1, 1) - pltpu.roll(pressure, 1, 1)
+                    total = total + (-coriolis * zonal - pressure_coef * 0.5 * grad)
+                total = total + top * src_ref[channels + f]
+                write(f, l, center + src_ref[channels + fields] * total)
+            return cum
+
+        lax.fori_loop(0, levels, level, jnp.zeros((tall, wide), jnp.float32))
+
+    def read_src(ch):
+        return src_ref[ch]
+
+    def read_first(ch):
+        return first[ch]
+
+    def read_second(ch):
+        return second[ch]
+
+    def write_first(f, l, value):
+        first[f * levels + l] = value
+
+    def write_second(f, l, value):
+        second[f * levels + l] = value
+
+    def write_out(f, l, value):
+        out_ref[f, l] = value[:rows, :lanes]
+
+    writers = [write_first, write_second]
+    for repeat in range(STEPS):
+        write = write_out if repeat == STEPS - 1 else writers[repeat % 2]
+        read = read_src if repeat == 0 else (read_first if repeat % 2 == 1 else read_second)
+        one_step(read, write)
+
+
+def cyclic_halo(block, axis, dim, width, total):
+    count = lax.axis_size(axis)
+    forward = [(i, i + 1) for i in range(count - 1)]
+    backward = [(target, source) for source, target in forward]
+    size = block.shape[dim]
+    low = lax.ppermute(lax.slice_in_dim(block, size - width, None, axis=dim), axis, forward)
+    high = lax.ppermute(lax.slice_in_dim(block, 0, width, axis=dim), axis, backward)
+    gap_shape = list(block.shape)
+    gap_shape[dim] = total - size - 2 * width
+    gap = jnp.zeros(gap_shape, block.dtype)
+    return jnp.concatenate([block, high, gap, low], axis=dim)
+
+
+def run_steps(packed, coriolis, diffusivity, out_shape):
+    fields, levels = out_shape[0], out_shape[1]
+    channels = fields * levels
+    tall, wide = packed.shape[1], packed.shape[2]
+    return pl.pallas_call(
+        stencil_kernel,
+        out_shape=jax.ShapeDtypeStruct(out_shape, jnp.float32),
+        in_specs=[
+            pl.BlockSpec(memory_space=pltpu.SMEM),
+            pl.BlockSpec(memory_space=pltpu.VMEM),
+            pl.BlockSpec(memory_space=pltpu.VMEM),
+        ],
+        out_specs=pl.BlockSpec(memory_space=pltpu.VMEM),
+        scratch_shapes=[
+            pltpu.VMEM((channels, tall, wide), jnp.float32),
+            pltpu.VMEM((channels, tall, wide), jnp.float32),
+        ],
+    )(diffusivity, coriolis, packed)
 
 
 def row_targets(tile_slots, need_blocks, capacity, owners):
@@ -87,15 +189,22 @@
     incoming = incoming.reshape((slots,) + incoming.shape[2:])
     picks = incoming[tile_slots]
     forcing = jnp.einsum("tkfa,tkra->ftr", picks, remap_weights, preferred_element_type=jnp.float32)
-    lat_cells = ocean_state.shape[3]
+    fields, levels, rows, lat_cells = ocean_state.shape
     lat_total = lat_cells * lax.axis_size("oy")
     lat_start = lax.axis_index("oy") * lat_cells
     wetness = land_mask.astype(jnp.float32)
-    state = ocean_state
-    coriolis = lat_factor(lat_start, lat_cells, lat_total)
-    for repeat in range(STEPS):
-        padded = with_halo(state, (("ox", 2), ("oy", 3)), 1)
-        state = advance(padded, state, diffusivity, coriolis, forcing, wetness)
+    packed = jnp.concatenate(
+        [ocean_state.reshape(fields * levels, rows, lat_cells), forcing, wetness[None]], axis=0
+    )
+    tall = -(-(rows + 2 * STEPS) // 8) * 8
+    wide = -(-(lat_cells + 2 * STEPS) // 128) * 128
+    packed = cyclic_halo(packed, "ox", 1, STEPS, tall)
+    packed = cyclic_halo(packed, "oy", 2, STEPS, wide)
+    lane = jnp.arange(wide, dtype=jnp.int32)
+    offset = jnp.where(lane < lat_cells + STEPS, lane, lane - wide)
+    latitude = (lat_start + offset).astype(jnp.float32)
+    coriolis_wide = (coriolis_coef * (2.0 * (latitude + 0.5) / lat_total - 1.0))[None, :]
+    state = run_steps(packed, coriolis_wide, diffusivity, ocean_state.shape)
     surface = state[2, 0].astype(jnp.bfloat16)
     pieces = jnp.einsum("tkra,tr->tka", remap_weights, surface, preferred_element_type=jnp.float32)
     slot_line = jnp.arange(slots, dtype=jnp.int32)

time: 114 us -> 63 us (0.55)
  local copies, waits for them, and re-layouts: 37.1 us -> 8.44 us
  starting transfers between devices: 37.1 us -> 16 us
  Pallas kernels: 0 us -> 8.96 us
  other arithmetic: 11.4 us -> 5.75 us
  waiting for transfers between devices: 14 us -> 9.61 us
    ppermute x12 -> x4, starting transfers between devices: 31.3 us -> 10.2 us  [the longest x2 6.96 us: cyclic_halo(): lax.ppermute(lax.slice_in_dim(block, size - width, None, axis=dim), axis,...]
    slice x18 -> x3, local copies, waits for them, and re-layouts: 18.7 us -> 3.03 us  [the longest x2 2.67 us: cyclic_halo(): lax.slice_in_dim(block, 0, width, axis=dim)]
    ppermute x12 -> x4, waiting for transfers between devices: 14 us -> 4.54 us  [the longest x2 3.44 us: cyclic_halo(): lax.ppermute(lax.slice_in_dim(block, size - width, None, axis=dim), axis,...]
    pallas_call x0 -> x1, Pallas kernels: none -> 8.96 us  [run_steps(): pl.pallas_call(stencil_kernel, out_shape=jax.ShapeDtypeStruct(out_shape,...]
    ppermute x6 -> x2, local copies, waits for them, and re-layouts: 8.71 us -> 1.7 us  [the longest x1 1.29 us: cyclic_halo(): lax.ppermute(lax.slice_in_dim(block, size - width, None, axis=dim), axis,...]
    another operation x3 -> x0, other arithmetic: 6.71 us -> none  [advance(): pressure = jnp.cumsum(density, axis=0) - 0.5 * density]
    all_to_all x1, waiting for transfers between devices: 0.01 us -> 5.06 us  [per_device(): incoming = lax.all_to_all(outgoing, 'ox', 0, 0, tiled=True)]
    mul x3 -> x0, local copies, waits for them, and re-layouts: 3.16 us -> none  [advance(): zonal[None] * (east - west) + meridional[None] * (north - south)]
  transfers between devices with their start and end apart: 13 -> 5, of which waited for: 6 -> 4; matrix products, arithmetic and copies ran while one was open for 17% -> 5% of each run, Pallas kernels for 0% -> 0%
where the time goes in v3:
time: 63 us; the launch traced here: 62.5 us
  starting transfers between devices  16 us (25%)
  blocking collectives  10.9 us (17%)
  waiting for transfers between devices  9.61 us (15%)
  Pallas kernels  8.96 us (14%)
  local copies, waits for them, and re-layouts  8.44 us (13%)
  other arithmetic  5.75 us (9%)
  matrix products  2.15 us (3%)
  between operations  0.73 us (1%)
    all_to_all x1, blocking collectives, per_device(): returned = lax.all_to_all(per_slot, 'ox', 0, 0, tiled=True)  10.9 us
    pallas_call x1, Pallas kernels, run_steps(): pl.pallas_call(stencil_kernel, out_shape=jax.ShapeDtypeStruct(out_shape,...  8.96 us
    ppermute x2, starting transfers between devices, cyclic_halo(): lax.ppermute(lax.slice_in_dim(block, size - width, None, axis=dim), axis,...  6.96 us
    all_to_all x1, starting transfers between devices, per_device(): incoming = lax.all_to_all(outgoing, 'ox', 0, 0, tiled=True)  5.81 us
    all_to_all x1, waiting for transfers between devices, per_device(): incoming = lax.all_to_all(outgoing, 'ox', 0, 0, tiled=True)  5.06 us
    ppermute x2, waiting for transfers between devices, cyclic_halo(): lax.ppermute(lax.slice_in_dim(block, size - width, None, axis=dim), axis,...  3.44 us
    ppermute x2, starting transfers between devices, cyclic_halo(): lax.ppermute(lax.slice_in_dim(block, 0, width, axis=dim), axis, backward)  3.21 us
    concatenate x2, other arithmetic, cyclic_halo(): return jnp.concatenate([block, high, gap, low], axis=dim)  2.87 us
  transfers between devices with their start and end apart: 5, of which 4 were waited for; matrix products, arithmetic and copies ran while one was open for 5% of the time, Pallas kernels for 0%

profile of v3, /device:TPU:4, one launch (start us, length us, event | category | flops | bytes accessed | tf_op | source)
XLA Modules:
  0.0 62.5 jit_solution(4214384564039211469)
XLA Ops:
  0.6 0.0 copy-start
  0.6 0.0 copy-start.1
  0.7 0.8 %compare_select_fusion.2 = s32[8,3]{0,1:T(4,128)S(1)} fusion(s32[8,3]{0,1:T(4,128)} %param.11), kind=kLoop, calls=%fused_computation.24 | loop fusion | flops 96 | bytes 192 | tf_op jit(solution)/shard_map/select_n | solution.py:187
  1.5 0.1 copy.17
  1.6 0.1 reshape.58
  1.7 1.9 %gather_fusion = bf16[24,4,128]{2,1,0:T(4,128)(2,1)} fusion(bf16[4,10,128]{2,0,1:T(4,128)(2,1)} %param.8, s32[1024]{0:T(1024)S(1)} %pad_clamp_fusion.1), kind=kCustom, calls=%fused_computation | custom fusion | bytes 49248 | tf_op jit(solution)/shard_map/gather | solution.py:187
  3.6 5.8 %all-to-all-start = ((bf16[8,3,4,128]{3,2,1,0:T(4,128)(2,1)}), bf16[8,3,4,128]{3,2,1,0:T(4,128)(2,1)S(1)}, u32[]{:S(2)}, u32[]{:S(2)}) async-start(bf16[8,3,4,128]{3,2,1,0:T(4,128)(2,1)} %bitcast.1), calls=%async_computation | async-start | bytes 49152 | tf_op jit(solution)/shard_map/all_to_all | solution.py:188
  9.4 0.7 %compare_select_fusion.1 = s32[16,3]{0,1:T(4,128)S(1)} fusion(s32[16,3]{0,1:T(4,128)} %param.10), kind=kLoop, calls=%fused_computation.23 | loop fusion | flops 144 | bytes 384 | tf_op jit(solution)/shard_map/select_n | solution.py:190
  10.1 0.1 copy.18
  10.1 0.1 reshape.66
  10.2 0.7 %convert_bitcast_fusion = f32[1,16,128]{2,1,0:T(8,128)S(1)} fusion(s32[16,128]{1,0:T(8,128)} %param.13), kind=kLoop, calls=%fused_computation.20 | loop fusion | flops 2048 | bytes 16384 | tf_op jit(solution)/shard_map/broadcast_in_dim | solution.py:197
  10.9 5.1 %all-to-all-done = bf16[8,3,4,128]{3,2,1,0:T(4,128)(2,1)S(1)} async-done(((bf16[8,3,4,128]{3,2,1,0:T(4,128)(2,1)}), bf16[8,3,4,128]{3,2,1,0:T(4,128)(2,1)S(1)}, u32[]{:S(2)}, u32[]{:S(2)}) %all-to-all-start) | async-done | bytes 24608 | tf_op jit(solution)/shard_map/all_to_all | solution.py:188
  16.0 0.6 %gather_fusion.1 = bf16[48,4,128]{2,1,0:T(4,128)(2,1)S(1)} fusion(bf16[24,4,128]{2,1,0:T(4,128)(2,1)S(1)} %bitcast.32, s32[1024]{0:T(1024)S(1)} %pad_clamp_fusion), kind=kCustom, calls=%fused_computation.1 | custom fusion | bytes 98496 | tf_op jit(solution)/shard_map/gather | solution.py:190
  16.6 0.0 copy-done
  16.6 0.6 %convolution_bitcast_fusion = f32[16,4,128]{2,1,0:T(4,128)S(1)} fusion(bf16[16,3,4,128]{3,2,1,0:T(4,128)(2,1)S(1)} %bitcast.33, bf16[16,3,128,128]{3,2,1,0:T(8,128)(2,1)S(1)} %copy-done), kind=kOutput, calls=%fused_computation.3 | convolution fusion | flops 6291456 | bytes 1654784 | tf_op jit(solution)/shard_map/tkfa,tkra->ftr/dot_general | solution.py:191
  17.3 0.0 copy-done.1
  17.3 0.1 pad_maximum_fusion.4
  17.4 1.3 %collective-permute-start = (f32[69,3,128]{2,1,0:T(4,128)S(1)}, f32[69,3,128]{2,1,0:T(4,128)S(1)}, u32[]{:S(2)}, u32[]{:S(2)}) collective-permute-start(f32[69,3,128]{2,1,0:T(4,128)S(1)} %get-tuple-element.4), channel_id=1, source_target_pairs={{4,0},{8,4},{12,8},{16,12},{20,16},{24,20},{28,24},{5,1},{9,5},{13... | collective-permute-start | bytes 317960 | tf_op jit(solution)/shard_map/ppermute | solution.py:133
  18.7 4.6 %collective-permute-start.1 = (f32[69,3,128]{2,1,0:T(4,128)S(1)}, f32[69,3,128]{2,1,0:T(4,128)S(1)}, u32[]{:S(2)}, u32[]{:S(2)}) collective-permute-start(f32[69,3,128]{2,1,0:T(4,128)S(1)} %get-tuple-element.5), channel_id=1, source_target_pairs={{0,4},{4,8},{8,12},{12,16},{16,20},{20,24},{24,28},{1,5},{5,9},{9,... | collective-permute-start | bytes 317960 | tf_op jit(solution)/shard_map/ppermute | solution.py:132
  23.2 1.1 %collective-permute-done = f32[69,3,128]{2,1,0:T(4,128)S(1)} collective-permute-done((f32[69,3,128]{2,1,0:T(4,128)S(1)}, f32[69,3,128]{2,1,0:T(4,128)S(1)}, u32[]{:S(2)}, u32[]{:S(2)}) %collective-permute-start) | collective-permute-done | bytes 106016 | tf_op jit(solution)/shard_map/ppermute | solution.py:133
  24.3 1.6 %collective-permute-done.1 = f32[69,3,128]{2,1,0:T(4,128)S(1)} collective-permute-done((f32[69,3,128]{2,1,0:T(4,128)S(1)}, f32[69,3,128]{2,1,0:T(4,128)S(1)}, u32[]{:S(2)}, u32[]{:S(2)}) %collective-permute-start.1) | collective-permute-done | bytes 106016 | tf_op jit(solution)/shard_map/ppermute | solution.py:132
  26.0 0.1 pad_maximum_fusion.1
  26.1 1.2 %fusion.14 = (f32[69,24,3]{2,1,0:T(8,128)}, f32[69,24,3]{2,1,0:T(8,128)S(1)}) fusion(f32[69,24,128]{2,1,0:T(8,128)S(1)} %pad_maximum_fusion.1), kind=kLoop, calls=%fused_computation.34 | loop fusion | bytes 79488 | tf_op jit(solution)/shard_map/slice | solution.py:133
  27.3 1.5 %copy.20 = f32[69,24,3]{0,1,2:T(8,128)S(1)} copy(f32[69,24,3]{2,1,0:T(8,128)} %get-tuple-element.2) | data formatting | bytes 39744 | tf_op jit(solution)/shard_map/slice | solution.py:133
  28.8 1.9 %collective-permute-start.2 = (f32[69,24,3]{0,1,2:T(8,128)S(1)}, f32[69,24,3]{0,1,2:T(8,128)S(1)}, u32[]{:S(2)}, u32[]{:S(2)}) collective-permute-start(f32[69,24,3]{0,1,2:T(8,128)S(1)} %copy.20), channel_id=1, source_target_pairs={{1,0},{2,1},{3,2},{5,4},{6,5},{7,6},{9,8},{10,9},{11,10},{13,12},{... | collective-permute-start | bytes 59624 | tf_op jit(solution)/shard_map/ppermute | solution.py:133
  30.7 0.4 copy.21
  31.1 2.4 %collective-permute-start.3 = (f32[69,24,3]{0,1,2:T(8,128)S(1)}, f32[69,24,3]{0,1,2:T(8,128)S(1)}, u32[]{:S(2)}, u32[]{:S(2)}) collective-permute-start(f32[69,24,3]{0,1,2:T(8,128)S(1)} %copy.21), channel_id=1, source_target_pairs={{0,1},{1,2},{2,3},{4,5},{5,6},{6,7},{8,9},{9,10},{10,11},{12,13},{... | collective-permute-start | bytes 59624 | tf_op jit(solution)/shard_map/ppermute | solution.py:132
  33.5 0.6 fusion.13.cor_ref
  34.1 0.1 pad.7.clone
  34.2 0.0 collective-permute-done.2
  34.2 0.4 copy.22
  34.6 1.8 %collective-permute-done.3 = f32[69,24,3]{0,1,2:T(8,128)S(1)} collective-permute-done((f32[69,24,3]{0,1,2:T(8,128)S(1)}, f32[69,24,3]{0,1,2:T(8,128)S(1)}, u32[]{:S(2)}, u32[]{:S(2)}) %collective-permute-start.3) | collective-permute-done | bytes 19904 | tf_op jit(solution)/shard_map/ppermute | solution.py:132
  36.4 1.3 %copy.23 = f32[69,24,3]{2,1,0:T(8,128)} copy(f32[69,24,3]{0,1,2:T(8,128)S(1)} %collective-permute-done.3) | data formatting | bytes 39744 | tf_op jit(solution)/shard_map/ppermute | solution.py:132
  37.7 2.7 %pad_maximum_fusion.src_ref = f32[69,24,256]{2,1,0:T(8,128)} fusion(f32[69,24,3]{2,1,0:T(8,128)} %copy.23, f32[69,24,3]{2,1,0:T(8,128)S(1)} %copy.22, f32[69,3,128]{2,1,0:T(4,128)S(1)} %collective-permute-done.1, f32[69,2,128]{2,1,0:T(2,128)S(1)} %broadcast_in_dim.23, f32[69,3,128]{2,1,0:T(4,128)S(1)} %collective-permute-done, ...), kind=kLoop, calls=%fused_computation.2 | loop fusion | flops 3391488 | bytes 2584384 | tf_op jit(solution)/shard_map/concatenate | solution.py:137
  40.4 0.0 copy-start.2
  40.4 0.0 copy-start.3
  40.4 9.0 %shard_map.86 = f32[4,16,16,128]{3,2,1,0:T(8,128)} custom-call(f32[16]{0:T(128)} %diff_ref.1, f32[1,256]{1,0:T(1,128)} %fusion.13.cor_ref, f32[69,24,256]{2,1,0:T(8,128)} %pad_maximum_fusion.src_ref), custom_call_target="tpu_custom_call" | custom-call | tf_op jit(solution)/shard_map/pallas_call | solution.py:144
  49.4 0.7 %fusion.7 = bf16[16,128,1,1]{1,0,2,3:T(8,128)(2,1)S(1)} fusion(f32[4,16,16,128]{3,2,1,0:T(8,128)} %shard_map.86), kind=kLoop, calls=%fused_computation.25 | loop fusion | bytes 8192 | tf_op jit(solution)/shard_map/convert_element_type | solution.py:208
  50.1 0.4 fusion.4
  50.5 0.0 copy-done.2
  50.5 0.3 convolution_bitcast_fusion.1
  50.7 10.9 %all_to_all.10 = f32[8,3,128]{2,1,0:T(4,128)S(1)} all-to-all(f32[8,3,128]{2,1,0:T(4,128)S(1)} %reshape.55), channel_id=1, replica_groups=mesh['ox'=8,'oy'=4] {'ox'}, dimensions={0} | all-to-all | bytes 24576 | tf_op jit(solution)/shard_map/all_to_all | solution.py:214
  61.6 0.0 copy-done.3
  61.6 0.9 %convolution_bitcast_fusion.2 = f32[10,128]{1,0:T(8,128)} fusion(f32[8,3,128]{2,1,0:T(4,128)S(1)} %all_to_all.10, s32[8,3]{0,1:T(4,128)S(1)} %copy-done.3), kind=kOutput, calls=%fused_computation.5 | convolution fusion | flops 368880 | bytes 17504 | tf_op jit(solution)/shard_map/isb,isa->ba/dot_general | solution.py:217
  (6 shorter events, 0.1 us)
Async XLA Ops:
  0.6 16.0 %copy-start = (bf16[16,3,128,128]{3,2,1,0:T(8,128)(2,1)S(1)}, bf16[16,3,128,128]{3,2,1,0:T(8,128)(2,1)}, u32[]{:S(2)}) copy-start(bf16[16,3,128,128]{3,2,1,0:T(8,128)(2,1)} %param.9) | copy-start | bytes 4718596
  0.6 16.6 %copy-start.1 = (f32[4,16,16,128]{3,2,1,0:T(8,128)S(1)}, f32[4,16,16,128]{3,2,1,0:T(8,128)}, u32[]{:S(2)}) copy-start(f32[4,16,16,128]{3,2,1,0:T(8,128)} %param.12) | copy-start | bytes 1572868
  3.6 12.4 %all-to-all-start = ((bf16[8,3,4,128]{3,2,1,0:T(4,128)(2,1)}), bf16[8,3,4,128]{3,2,1,0:T(4,128)(2,1)S(1)}, u32[]{:S(2)}, u32[]{:S(2)}) async-start(bf16[8,3,4,128]{3,2,1,0:T(4,128)(2,1)} %bitcast.1), calls=%async_computation | async-start | bytes 49152 | tf_op jit(solution)/shard_map/all_to_all | solution.py:188
  17.4 7.0 %collective-permute-start = (f32[69,3,128]{2,1,0:T(4,128)S(1)}, f32[69,3,128]{2,1,0:T(4,128)S(1)}, u32[]{:S(2)}, u32[]{:S(2)}) collective-permute-start(f32[69,3,128]{2,1,0:T(4,128)S(1)} %get-tuple-element.4), channel_id=1, source_target_pairs={{4,0},{8,4},{12,8},{16,12},{20,16},{24,20},{28,24},{5,1},{9,5},{13... | collective-permute-start | bytes 317960 | tf_op jit(solution)/shard_map/ppermute | solution.py:133
  18.7 7.3 %collective-permute-start.1 = (f32[69,3,128]{2,1,0:T(4,128)S(1)}, f32[69,3,128]{2,1,0:T(4,128)S(1)}, u32[]{:S(2)}, u32[]{:S(2)}) collective-permute-start(f32[69,3,128]{2,1,0:T(4,128)S(1)} %get-tuple-element.5), channel_id=1, source_target_pairs={{0,4},{4,8},{8,12},{12,16},{16,20},{20,24},{24,28},{1,5},{5,9},{9,... | collective-permute-start | bytes 317960 | tf_op jit(solution)/shard_map/ppermute | solution.py:132
  28.8 5.4 %collective-permute-start.2 = (f32[69,24,3]{0,1,2:T(8,128)S(1)}, f32[69,24,3]{0,1,2:T(8,128)S(1)}, u32[]{:S(2)}, u32[]{:S(2)}) collective-permute-start(f32[69,24,3]{0,1,2:T(8,128)S(1)} %copy.20), channel_id=1, source_target_pairs={{1,0},{2,1},{3,2},{5,4},{6,5},{7,6},{9,8},{10,9},{11,10},{13,12},{... | collective-permute-start | bytes 59624 | tf_op jit(solution)/shard_map/ppermute | solution.py:133
  31.1 5.3 %collective-permute-start.3 = (f32[69,24,3]{0,1,2:T(8,128)S(1)}, f32[69,24,3]{0,1,2:T(8,128)S(1)}, u32[]{:S(2)}, u32[]{:S(2)}) collective-permute-start(f32[69,24,3]{0,1,2:T(8,128)S(1)} %copy.21), channel_id=1, source_target_pairs={{0,1},{1,2},{2,3},{4,5},{5,6},{6,7},{8,9},{9,10},{10,11},{12,13},{... | collective-permute-start | bytes 59624 | tf_op jit(solution)/shard_map/ppermute | solution.py:132
  40.4 10.0 %copy-start.2 = (s32[16,3]{0,1:T(4,128)S(1)}, s32[16,3]{0,1:T(4,128)}, u32[]{:S(2)}) copy-start(s32[16,3]{0,1:T(4,128)} %param.10) | copy-start | bytes 580
  40.4 21.2 %copy-start.3 = (s32[8,3]{0,1:T(4,128)S(1)}, s32[8,3]{0,1:T(4,128)}, u32[]{:S(2)}) copy-start(s32[8,3]{0,1:T(4,128)} %param.11) | copy-start | bytes 292

commit v4 on v3

--- a/solution.py
+++ b/solution.py
@@ -15,19 +15,6 @@
 coriolis_coef = 0.5
 vertical_coef = 0.1
 forcing_coef = 0.5
-
-
-def with_halo(block, sides, width):
-    for axis, dim in sides:
-        count = lax.axis_size(axis)
-        forward = [(i, i + 1) for i in range(count - 1)]
-        backward = [(target, source) for source, target in forward]
-        low = lax.ppermute(
-            lax.slice_in_dim(block, block.shape[dim] - width, None, axis=dim), axis, forward
-        )
-        high = lax.ppermute(lax.slice_in_dim(block, 0, width, axis=dim), axis, backward)
-        block = jnp.concatenate([low, block, high], axis=dim)
-    return block
 
 
 def advance(padded, center, diffusivity, coriolis, forcing, wetness):
@@ -57,10 +44,18 @@
     return center + wetness * total
 
 
-def stencil_kernel(diff_ref, cor_ref, src_ref, out_ref, first, second):
+def stencil_kernel(diff_ref, cor_ref, state_ref, aux_ref, xt_ref, yt_ref, out_ref, first, second):
     fields, levels, rows, lanes = out_ref.shape
     channels = fields * levels
-    tall, wide = src_ref.shape[1], src_ref.shape[2]
+    tall = rows + xt_ref.shape[1]
+    wide = lanes + yt_ref.shape[2]
+
+    def widen(inner, ch):
+        left = jnp.concatenate([inner, xt_ref[ch]], axis=0)
+        return jnp.concatenate([left, yt_ref[ch]], axis=1)
+
+    def aux(index):
+        return widen(aux_ref[index], channels + index)
 
     def one_step(read, write):
         def level(l, cum):
@@ -93,14 +88,14 @@
                 if f == 1:
                     grad = pltpu.roll(pressure, wide - 1, 1) - pltpu.roll(pressure, 1, 1)
                     total = total + (-coriolis * zonal - pressure_coef * 0.5 * grad)
-                total = total + top * src_ref[channels + f]
-                write(f, l, center + src_ref[channels + fields] * total)
+                total = total + top * aux(f)
+                write(f, l, center + aux(fields) * total)
             return cum
 
         lax.fori_loop(0, levels, level, jnp.zeros((tall, wide), jnp.float32))
 
     def read_src(ch):
-        return src_ref[ch]
+        return widen(state_ref[ch], ch)
 
     def read_first(ch):
         return first[ch]
@@ -124,43 +119,31 @@
         one_step(read, write)
 
 
-def cyclic_halo(block, axis, dim, width, total):
+def run_steps(state, aux, x_tile, y_tile, coriolis, diffusivity, out_shape):
+    channels = state.shape[0]
+    tall = state.shape[1] + x_tile.shape[1]
+    wide = state.shape[2] + y_tile.shape[2]
+    vmem = pl.BlockSpec(memory_space=pltpu.VMEM)
+    return pl.pallas_call(
+        stencil_kernel,
+        out_shape=jax.ShapeDtypeStruct(out_shape, jnp.float32),
+        in_specs=[pl.BlockSpec(memory_space=pltpu.SMEM)] + [vmem] * 5,
+        out_specs=vmem,
+        scratch_shapes=[
+            pltpu.VMEM((channels, tall, wide), jnp.float32),
+            pltpu.VMEM((channels, tall, wide), jnp.float32),
+        ],
+    )(diffusivity, coriolis, state, aux, x_tile, y_tile)
+
+
+def shifted(block, axis, dim, width):
     count = lax.axis_size(axis)
     forward = [(i, i + 1) for i in range(count - 1)]
     backward = [(target, source) for source, target in forward]
     size = block.shape[dim]
     low = lax.ppermute(lax.slice_in_dim(block, size - width, None, axis=dim), axis, forward)
     high = lax.ppermute(lax.slice_in_dim(block, 0, width, axis=dim), axis, backward)
-    gap_shape = list(block.shape)
-    gap_shape[dim] = total - size - 2 * width
-    gap = jnp.zeros(gap_shape, block.dtype)
-    return jnp.concatenate([block, high, gap, low], axis=dim)
-
-
-def run_steps(packed, coriolis, diffusivity, out_shape):
-    fields, levels = out_shape[0], out_shape[1]
-    channels = fields * levels
-    tall, wide = packed.shape[1], packed.shape[2]
-    return pl.pallas_call(
-        stencil_kernel,
-        out_shape=jax.ShapeDtypeStruct(out_shape, jnp.float32),
-        in_specs=[
-            pl.BlockSpec(memory_space=pltpu.SMEM),
-            pl.BlockSpec(memory_space=pltpu.VMEM),
-            pl.BlockSpec(memory_space=pltpu.VMEM),
-        ],
-        out_specs=pl.BlockSpec(memory_space=pltpu.VMEM),
-        scratch_shapes=[
-            pltpu.VMEM((channels, tall, wide), jnp.float32),
-            pltpu.VMEM((channels, tall, wide), jnp.float32),
-        ],
-    )(diffusivity, coriolis, packed)
-
-
-def row_targets(tile_slots, need_blocks, capacity, owners):
-    owner_of = tile_slots // capacity
-    place_of = tile_slots % capacity
-    return need_blocks[owner_of, place_of] * owners + owner_of
+    return low, high
 
 
 def lat_factor(first_cell, count, lat_total):
@@ -183,8 +166,11 @@
     owners = lax.axis_size("ox")
     capacity = send_blocks.shape[1]
     slots = owners * capacity
-    given = jnp.clip(send_blocks, 0, blocks_here - 1)
-    outgoing = jnp.transpose(atm_flux[:, given, :], (1, 2, 0, 3))
+    block_line = jnp.arange(blocks_here, dtype=jnp.int32)
+    to_block = send_blocks[:, :, None] == block_line[None, None, :]
+    outgoing = jnp.einsum(
+        "isb,fba->isfa", to_block.astype(atm_flux.dtype), atm_flux, preferred_element_type=jnp.float32
+    ).astype(atm_flux.dtype)
     incoming = lax.all_to_all(outgoing, "ox", 0, 0, tiled=True)
     incoming = incoming.reshape((slots,) + incoming.shape[2:])
     picks = incoming[tile_slots]
@@ -193,18 +179,23 @@
     lat_total = lat_cells * lax.axis_size("oy")
     lat_start = lax.axis_index("oy") * lat_cells
     wetness = land_mask.astype(jnp.float32)
-    packed = jnp.concatenate(
-        [ocean_state.reshape(fields * levels, rows, lat_cells), forcing, wetness[None]], axis=0
-    )
+    inner = ocean_state.reshape(fields * levels, rows, lat_cells)
+    aux = jnp.concatenate([forcing, wetness[None]], axis=0)
+    packed = jnp.concatenate([inner, aux], axis=0)
     tall = -(-(rows + 2 * STEPS) // 8) * 8
     wide = -(-(lat_cells + 2 * STEPS) // 128) * 128
-    packed = cyclic_halo(packed, "ox", 1, STEPS, tall)
-    packed = cyclic_halo(packed, "oy", 2, STEPS, wide)
+    low, high = shifted(packed, "ox", 1, STEPS)
+    gap = jnp.zeros((packed.shape[0], tall - rows - 2 * STEPS, lat_cells), jnp.float32)
+    x_tile = jnp.concatenate([high, gap, low], axis=1)
+    tall_block = jnp.concatenate([packed, x_tile], axis=1)
+    south, north = shifted(tall_block, "oy", 2, STEPS)
+    gap = jnp.zeros((packed.shape[0], tall, wide - lat_cells - 2 * STEPS), jnp.float32)
+    y_tile = jnp.concatenate([north, gap, south], axis=2)
     lane = jnp.arange(wide, dtype=jnp.int32)
     offset = jnp.where(lane < lat_cells + STEPS, lane, lane - wide)
     latitude = (lat_start + offset).astype(jnp.float32)
     coriolis_wide = (coriolis_coef * (2.0 * (latitude + 0.5) / lat_total - 1.0))[None, :]
-    state = run_steps(packed, coriolis_wide, diffusivity, ocean_state.shape)
+    state = run_steps(inner, aux, x_tile, y_tile, coriolis_wide, diffusivity, ocean_state.shape)
     surface = state[2, 0].astype(jnp.bfloat16)
     pieces = jnp.einsum("tkra,tr->tka", remap_weights, surface, preferred_element_type=jnp.float32)
     slot_line = jnp.arange(slots, dtype=jnp.int32)
@@ -212,10 +203,8 @@
     per_slot = jnp.einsum("tks,tka->sa", to_slot, pieces, precision=lax.Precision.HIGHEST)
     per_slot = per_slot.reshape(owners, capacity, block_width)
     returned = lax.all_to_all(per_slot, "ox", 0, 0, tiled=True)
-    block_line = jnp.arange(blocks_here, dtype=jnp.int32)
-    to_block = (send_blocks[:, :, None] == block_line[None, None, :]).astype(jnp.float32)
     atmos_surface = jnp.einsum(
-        "isb,isa->ba", to_block, returned, precision=lax.Precision.HIGHEST
+        "isb,isa->ba", to_block.astype(jnp.float32), returned, precision=lax.Precision.HIGHEST
     )
     return (state, atmos_surface)
 

time: 63 us -> 60.4 us (0.959)
  the two profiles are of different devices: /device:TPU:4 before, /device:TPU:1 now
where the time goes in v4:
time: 60.4 us; the launch traced here: 59.8 us
  starting transfers between devices  18.3 us (30%)
  Pallas kernels  8.94 us (15%)
  blocking collectives  8.64 us (14%)
  waiting for transfers between devices  8.58 us (14%)
  other arithmetic  6.63 us (11%)
  local copies, waits for them, and re-layouts  4.84 us (8%)
  matrix products  3.2 us (5%)
  between operations  0.74 us (1%)
    pallas_call x1, Pallas kernels, run_steps(): pl.pallas_call(stencil_kernel, out_shape=jax.ShapeDtypeStruct(out_shape,...  8.94 us
    ppermute x2, starting transfers between devices, shifted(): lax.ppermute(lax.slice_in_dim(block, size - width, None, axis=dim), axis,...  8.7 us
    all_to_all x1, blocking collectives, per_device(): returned = lax.all_to_all(per_slot, 'ox', 0, 0, tiled=True)  8.64 us
    all_to_all x1, starting transfers between devices, per_device(): incoming = lax.all_to_all(outgoing, 'ox', 0, 0, tiled=True)  6.35 us
    ppermute x2, waiting for transfers between devices, shifted(): lax.ppermute(lax.slice_in_dim(block, 0, width, axis=dim), axis, backward)  5.22 us
    all_to_all x1, waiting for transfers between devices, per_device(): incoming = lax.all_to_all(outgoing, 'ox', 0, 0, tiled=True)  3.25 us
    ppermute x2, starting transfers between devices, shifted(): lax.ppermute(lax.slice_in_dim(block, 0, width, axis=dim), axis, backward)  3.22 us
    concatenate x1, other arithmetic, per_device(): x_tile = jnp.concatenate([high, gap, low], axis=1)  1.72 us
  transfers between devices with their start and end apart: 5, of which 4 were waited for; matrix products, arithmetic and copies ran while one was open for 9% of the time, Pallas kernels for 0%

profile of v4, /device:TPU:1, one launch (start us, length us, event | category | flops | bytes accessed | tf_op | source)
XLA Modules:
  0.0 59.8 jit_solution(238528861381586911)
XLA Ops:
  0.6 0.0 copy-start
  0.6 0.0 copy-start.1
  0.7 1.1 %convolution_convert_fusion = bf16[8,3,4,128]{3,0,2,1:T(8,128)(2,1)S(1)} fusion(bf16[4,10,128]{2,0,1:T(4,128)(2,1)} %param.8, s32[8,3]{0,1:T(4,128)} %param.11), kind=kOutput, calls=%fused_computation.1 | convolution fusion | flops 258288 | bytes 34912 | tf_op jit(solution)/shard_map/isb,fba->isfa/dot_general | solution.py:171
  1.7 0.6 %copy.19 = bf16[8,3,4,128]{3,2,1,0:T(4,128)(2,1)} copy(bf16[8,3,4,128]{3,0,2,1:T(8,128)(2,1)S(1)} %convolution_convert_fusion) | data formatting | bytes 49152 | tf_op jit(solution)/shard_map/convert_element_type | solution.py:173
  2.3 6.4 %all-to-all-start = ((bf16[8,3,4,128]{3,2,1,0:T(4,128)(2,1)}), bf16[8,3,4,128]{3,2,1,0:T(4,128)(2,1)S(1)}, u32[]{:S(2)}, u32[]{:S(2)}) async-start(bf16[8,3,4,128]{3,2,1,0:T(4,128)(2,1)} %copy.19), calls=%async_computation | async-start | bytes 49152 | tf_op jit(solution)/shard_map/all_to_all | solution.py:174
  8.7 0.7 %convert_bitcast_fusion = f32[1,16,128]{2,1,0:T(8,128)S(1)} fusion(s32[16,128]{1,0:T(8,128)} %param.13), kind=kLoop, calls=%fused_computation.25 | loop fusion | flops 2048 | bytes 16384 | tf_op jit(solution)/shard_map/broadcast_in_dim | solution.py:183
  9.4 0.7 %compare_select_fusion.1 = s32[16,3]{0,1:T(4,128)S(1)} fusion(s32[16,3]{0,1:T(4,128)} %param.10), kind=kLoop, calls=%fused_computation.29 | loop fusion | flops 144 | bytes 384 | tf_op jit(solution)/shard_map/select_n | solution.py:176
  10.1 0.1 copy.20
  10.2 0.1 reshape.58
  10.3 0.6 fusion.18.cor_ref
  10.8 0.1 pad.1.clone
  10.9 3.3 %all-to-all-done = bf16[8,3,4,128]{3,2,1,0:T(4,128)(2,1)S(1)} async-done(((bf16[8,3,4,128]{3,2,1,0:T(4,128)(2,1)}), bf16[8,3,4,128]{3,2,1,0:T(4,128)(2,1)S(1)}, u32[]{:S(2)}, u32[]{:S(2)}) %all-to-all-start) | async-done | bytes 24608 | tf_op jit(solution)/shard_map/all_to_all | solution.py:174
  14.2 0.6 %gather_fusion = bf16[48,4,128]{2,1,0:T(4,128)(2,1)S(1)} fusion(bf16[24,4,128]{2,1,0:T(4,128)(2,1)S(1)} %bitcast.39, s32[1024]{0:T(1024)S(1)} %pad_clamp_fusion), kind=kCustom, calls=%fused_computation | custom fusion | bytes 98496 | tf_op jit(solution)/shard_map/gather | solution.py:176
  14.8 0.0 copy-done
  14.8 0.6 %convolution_bitcast_fusion = f32[16,4,128]{2,1,0:T(4,128)S(1)} fusion(bf16[16,3,4,128]{3,2,1,0:T(4,128)(2,1)S(1)} %bitcast.40, bf16[16,3,128,128]{3,2,1,0:T(8,128)(2,1)S(1)} %copy-done), kind=kOutput, calls=%fused_computation.2 | convolution fusion | flops 6291456 | bytes 1654784 | tf_op jit(solution)/shard_map/tkfa,tkra->ftr/dot_general | solution.py:177
  15.5 0.0 copy-done.1
  15.5 0.1 pad_maximum_fusion.5
  15.5 2.1 %collective-permute-start.1 = (f32[69,3,128]{2,1,0:T(4,128)S(1)}, f32[69,3,128]{2,1,0:T(4,128)S(1)}, u32[]{:S(2)}, u32[]{:S(2)}) collective-permute-start(f32[69,3,128]{2,1,0:T(4,128)S(1)} %get-tuple-element.5), channel_id=1, source_target_pairs={{0,4},{4,8},{8,12},{12,16},{16,20},{20,24},{24,28},{1,5},{5,9},{9,... | collective-permute-start | bytes 317960 | tf_op jit(solution)/shard_map/ppermute | solution.py:144
  17.7 1.3 %collective-permute-start = (f32[69,3,128]{2,1,0:T(4,128)S(1)}, f32[69,3,128]{2,1,0:T(4,128)}, u32[]{:S(2)}, u32[]{:S(2)}) collective-permute-start(f32[69,3,128]{2,1,0:T(4,128)S(1)} %get-tuple-element.4), channel_id=1, source_target_pairs={{4,0},{8,4},{12,8},{16,12},{20,16},{24,20},{28,24},{5,1},{9,5},{13... | collective-permute-start | bytes 317960 | tf_op jit(solution)/shard_map/ppermute | solution.py:145
  19.0 0.6 %pad_maximum_fusion.6.aux_ref = f32[5,16,128]{2,1,0:T(8,128)} fusion(f32[1,16,128]{2,1,0:T(8,128)S(1)} %convert_bitcast_fusion, f32[4,16,128]{2,1,0:T(8,128)S(1)} %bitcast.37), kind=kLoop, calls=%fused_computation.11 | loop fusion | flops 10240 | bytes 81920 | tf_op jit(solution)/shard_map/concatenate | solution.py:183
  19.6 0.1 collective-permute-done.1
  19.7 3.9 %collective-permute-done = f32[69,3,128]{2,1,0:T(4,128)} collective-permute-done((f32[69,3,128]{2,1,0:T(4,128)S(1)}, f32[69,3,128]{2,1,0:T(4,128)}, u32[]{:S(2)}, u32[]{:S(2)}) %collective-permute-start) | collective-permute-done | bytes 106016 | tf_op jit(solution)/shard_map/ppermute | solution.py:145
  23.6 1.0 %pad_maximum_fusion = f32[69,24,128]{2,1,0:T(8,128)S(1)} fusion(f32[69,3,128]{2,1,0:T(4,128)S(1)} %collective-permute-done.1, f32[69,2,128]{2,1,0:T(2,128)S(1)} %broadcast_in_dim.19, f32[69,3,128]{2,1,0:T(4,128)} %collective-permute-done, f32[1,16,128]{2,1,0:T(8,128)S(1)} %convert_bitcast_fusion, f32[4,16,128]{2,1,0:T(8,128)S(1)} %bitcast.38, ...), kind=kLoop, calls=%fused_computation.5 | loop fusion | flops 1059840 | bytes 1695744 | tf_op jit(solution)/shard_map/concatenate | solution.py:190
  24.7 0.3 fusion.19
  24.9 0.4 copy.23
  25.3 6.6 %collective-permute-start.3 = (f32[69,24,3]{0,1,2:T(8,128)S(1)}, f32[69,24,3]{0,1,2:T(8,128)S(1)}, u32[]{:S(2)}, u32[]{:S(2)}) collective-permute-start(f32[69,24,3]{0,1,2:T(8,128)S(1)} %copy.23), channel_id=1, source_target_pairs={{0,1},{1,2},{2,3},{4,5},{5,6},{6,7},{8,9},{9,10},{10,11},{12,13},{... | collective-permute-start | bytes 59624 | tf_op jit(solution)/shard_map/ppermute | solution.py:144
  31.9 0.4 copy.22
  32.2 1.9 %collective-permute-start.2 = (f32[69,24,3]{0,1,2:T(8,128)S(1)}, f32[69,24,3]{0,1,2:T(8,128)}, u32[]{:S(2)}, u32[]{:S(2)}) collective-permute-start(f32[69,24,3]{0,1,2:T(8,128)S(1)} %copy.22), channel_id=1, source_target_pairs={{1,0},{2,1},{3,2},{5,4},{6,5},{7,6},{9,8},{10,9},{11,10},{13,12},{... | collective-permute-start | bytes 59624 | tf_op jit(solution)/shard_map/ppermute | solution.py:145
  34.2 1.7 %pad_maximum_fusion.2.xt_ref = f32[69,8,128]{2,1,0:T(8,128)} fusion(f32[69,3,128]{2,1,0:T(4,128)S(1)} %collective-permute-done.1, f32[69,2,128]{2,1,0:T(2,128)S(1)} %broadcast_in_dim.19, f32[69,3,128]{2,1,0:T(4,128)} %collective-permute-done), kind=kLoop, calls=%fused_computation.7 | loop fusion | flops 141312 | bytes 565248 | tf_op jit(solution)/shard_map/concatenate | solution.py:189
  35.9 0.0 collective-permute-done.3
  35.9 0.4 copy.25
  36.3 1.3 %collective-permute-done.2 = f32[69,24,3]{0,1,2:T(8,128)} collective-permute-done((f32[69,24,3]{0,1,2:T(8,128)S(1)}, f32[69,24,3]{0,1,2:T(8,128)}, u32[]{:S(2)}, u32[]{:S(2)}) %collective-permute-start.2) | collective-permute-done | bytes 19904 | tf_op jit(solution)/shard_map/ppermute | solution.py:145
  37.6 1.2 %copy.24 = f32[69,24,3]{2,1,0:T(8,128)S(1)} copy(f32[69,24,3]{0,1,2:T(8,128)} %collective-permute-done.2) | data formatting | bytes 39744 | tf_op jit(solution)/shard_map/ppermute | solution.py:145
  38.8 1.2 %pad_maximum_fusion.1.yt_ref = f32[69,24,128]{2,1,0:T(8,128)} fusion(f32[69,24,3]{2,1,0:T(8,128)S(1)} %copy.25, f32[69,24,3]{2,1,0:T(8,128)S(1)} %copy.24, f32[128]{0:T(128)S(1)} %pad.1.clone), kind=kLoop, calls=%fused_computation.6 | loop fusion | flops 423936 | bytes 888128 | tf_op jit(solution)/shard_map/concatenate | solution.py:193
  40.0 0.0 copy-start.2
  40.0 0.0 copy-start.3
  40.0 8.9 %shard_map.86 = f32[4,16,16,128]{3,2,1,0:T(8,128)} custom-call(f32[16]{0:T(128)} %diff_ref.1, f32[1,256]{1,0:T(1,128)} %fusion.18.cor_ref, f32[64,16,128]{2,1,0:T(8,128)} %bitcast.33, f32[5,16,128]{2,1,0:T(8,128)} %pad_maximum_fusion.6.aux_ref, f32[69,8,128]{2,1,0:T(8,128)} %pad_maximum_fusion.2.xt_ref, f32[69,24,128]{2,1,0:T(8,128)} %pad_maximum_fusion.1.yt_ref), custom_call_target="tpu_custom_call" | custom-call | tf_op jit(solution)/shard_map/pallas_call | solution.py:127
  49.0 0.7 %fusion.12 = bf16[16,128,1,1]{1,0,2,3:T(8,128)(2,1)S(1)} fusion(f32[4,16,16,128]{3,2,1,0:T(8,128)} %shard_map.86), kind=kLoop, calls=%fused_computation.30 | loop fusion | bytes 8192 | tf_op jit(solution)/shard_map/convert_element_type | solution.py:199
  49.7 0.4 fusion.8
  50.0 0.0 copy-done.2
  50.0 0.3 convolution_bitcast_fusion.1
  50.3 8.6 %all_to_all.10 = f32[8,3,128]{2,1,0:T(4,128)S(1)} all-to-all(f32[8,3,128]{2,1,0:T(4,128)S(1)} %reshape.55), channel_id=1, replica_groups=mesh['ox'=8,'oy'=4] {'ox'}, dimensions={0} | all-to-all | bytes 24576 | tf_op jit(solution)/shard_map/all_to_all | solution.py:205
  59.0 0.0 copy-done.3
  59.0 0.9 %convolution_bitcast_fusion.2 = f32[10,128]{1,0:T(8,128)} fusion(f32[8,3,128]{2,1,0:T(4,128)S(1)} %all_to_all.10, s32[8,3]{0,1:T(4,128)S(1)} %copy-done.3), kind=kOutput, calls=%fused_computation.4 | convolution fusion | flops 368880 | bytes 17504 | tf_op jit(solution)/shard_map/isb,isa->ba/dot_general | solution.py:206
  (5 shorter events, 0.0 us)
Async XLA Ops:
  0.6 14.2 %copy-start = (bf16[16,3,128,128]{3,2,1,0:T(8,128)(2,1)S(1)}, bf16[16,3,128,128]{3,2,1,0:T(8,128)(2,1)}, u32[]{:S(2)}) copy-start(bf16[16,3,128,128]{3,2,1,0:T(8,128)(2,1)} %param.9) | copy-start | bytes 4718596
  0.6 14.8 %copy-start.1 = (f32[4,16,16,128]{3,2,1,0:T(8,128)S(1)}, f32[4,16,16,128]{3,2,1,0:T(8,128)}, u32[]{:S(2)}) copy-start(f32[4,16,16,128]{3,2,1,0:T(8,128)} %param.12) | copy-start | bytes 1572868
  2.3 11.8 %all-to-all-start = ((bf16[8,3,4,128]{3,2,1,0:T(4,128)(2,1)}), bf16[8,3,4,128]{3,2,1,0:T(4,128)(2,1)S(1)}, u32[]{:S(2)}, u32[]{:S(2)}) async-start(bf16[8,3,4,128]{3,2,1,0:T(4,128)(2,1)} %copy.19), calls=%async_computation | async-start | bytes 49152 | tf_op jit(solution)/shard_map/all_to_all | solution.py:174
  15.5 4.2 %collective-permute-start.1 = (f32[69,3,128]{2,1,0:T(4,128)S(1)}, f32[69,3,128]{2,1,0:T(4,128)S(1)}, u32[]{:S(2)}, u32[]{:S(2)}) collective-permute-start(f32[69,3,128]{2,1,0:T(4,128)S(1)} %get-tuple-element.5), channel_id=1, source_target_pairs={{0,4},{4,8},{8,12},{12,16},{16,20},{20,24},{24,28},{1,5},{5,9},{9,... | collective-permute-start | bytes 317960 | tf_op jit(solution)/shard_map/ppermute | solution.py:144
  17.7 5.9 %collective-permute-start = (f32[69,3,128]{2,1,0:T(4,128)S(1)}, f32[69,3,128]{2,1,0:T(4,128)}, u32[]{:S(2)}, u32[]{:S(2)}) collective-permute-start(f32[69,3,128]{2,1,0:T(4,128)S(1)} %get-tuple-element.4), channel_id=1, source_target_pairs={{4,0},{8,4},{12,8},{16,12},{20,16},{24,20},{28,24},{5,1},{9,5},{13... | collective-permute-start | bytes 317960 | tf_op jit(solution)/shard_map/ppermute | solution.py:145
  25.3 10.6 %collective-permute-start.3 = (f32[69,24,3]{0,1,2:T(8,128)S(1)}, f32[69,24,3]{0,1,2:T(8,128)S(1)}, u32[]{:S(2)}, u32[]{:S(2)}) collective-permute-start(f32[69,24,3]{0,1,2:T(8,128)S(1)} %copy.23), channel_id=1, source_target_pairs={{0,1},{1,2},{2,3},{4,5},{5,6},{6,7},{8,9},{9,10},{10,11},{12,13},{... | collective-permute-start | bytes 59624 | tf_op jit(solution)/shard_map/ppermute | solution.py:144
  32.2 5.4 %collective-permute-start.2 = (f32[69,24,3]{0,1,2:T(8,128)S(1)}, f32[69,24,3]{0,1,2:T(8,128)}, u32[]{:S(2)}, u32[]{:S(2)}) collective-permute-start(f32[69,24,3]{0,1,2:T(8,128)S(1)} %copy.22), channel_id=1, source_target_pairs={{1,0},{2,1},{3,2},{5,4},{6,5},{7,6},{9,8},{10,9},{11,10},{13,12},{... | collective-permute-start | bytes 59624 | tf_op jit(solution)/shard_map/ppermute | solution.py:145
  40.0 10.0 %copy-start.2 = (s32[16,3]{0,1:T(4,128)S(1)}, s32[16,3]{0,1:T(4,128)}, u32[]{:S(2)}) copy-start(s32[16,3]{0,1:T(4,128)} %param.10) | copy-start | bytes 580
  40.0 19.0 %copy-start.3 = (s32[8,3]{0,1:T(4,128)S(1)}, s32[8,3]{0,1:T(4,128)}, u32[]{:S(2)}) copy-start(s32[8,3]{0,1:T(4,128)} %param.11) | copy-start | bytes 292

commit v5 on v1

v5 whole, which is shorter than its diff:
```python
import jax
import jax.numpy as jnp
from jax import lax
from jax.experimental import pallas as pl
from jax.experimental.pallas import tpu as pltpu
from jax.sharding import PartitionSpec as P

STEPS = 3


advect_coef = 0.25
pressure_coef = 0.1
thermal_coef = 0.2
haline_coef = 0.8
coriolis_coef = 0.5
vertical_coef = 0.1
forcing_coef = 0.5


def widen(inner, x_tile, y_tile):
    left = jnp.concatenate([inner, x_tile], axis=0)
    return jnp.concatenate([left, y_tile], axis=1)


def one_step(levels, shape, diff_ref, cor_ref, read, wet, force, write, partial):
    fields = 4
    tall, wide = shape

    def level(l, cum):
        up = jnp.maximum(l - 1, 0)
        down = jnp.minimum(l + 1, levels - 1)
        here = [read(f, l) for f in range(fields)]
        density = haline_coef * here[3] - thermal_coef * here[2]
        cum = cum + density
        pressure = cum - 0.5 * density
        zonal = here[0]
        meridional = here[1]
        top = jnp.where(l == 0, forcing_coef, 0.0)
        diff = diff_ref[l]
        coriolis = cor_ref[...]
        for f in range(fields):
            center = here[f]
            east = pltpu.roll(center, tall - 1, 0)
            west = pltpu.roll(center, 1, 0)
            north = pltpu.roll(center, wide - 1, 1)
            south = pltpu.roll(center, 1, 1)
            advection = -advect_coef * 0.5 * (zonal * (east - west) + meridional * (north - south))
            laplace = diff * (east + west + north + south - 4.0 * center)
            mixing = vertical_coef * (read(f, up) + read(f, down) - 2.0 * center)
            total = advection + laplace + mixing
            if f == 0:
                grad = pltpu.roll(pressure, tall - 1, 0) - pltpu.roll(pressure, 1, 0)
                total = total + (coriolis * meridional - pressure_coef * 0.5 * grad)
            if f == 1:
                grad = pltpu.roll(pressure, wide - 1, 1) - pltpu.roll(pressure, 1, 1)
                total = total + (-coriolis * zonal - pressure_coef * 0.5 * grad)
            if partial:
                write(f, l, jnp.where(l == 0, total, center + wet() * total))
            else:
                total = total + top * force(f)
                write(f, l, center + wet() * total)
        return cum

    lax.fori_loop(0, levels, level, jnp.zeros((tall, wide), jnp.float32))


def first_kernel(diff_ref, cor_ref, state_ref, xt_ref, yt_ref, out_ref):
    channels = state_ref.shape[0] - 1
    levels = channels // 4

    def read(f, l):
        ch = f * levels + l
        return widen(state_ref[ch], xt_ref[ch], yt_ref[ch])

    def wet():
        return widen(state_ref[channels], xt_ref[channels], yt_ref[channels])

    def write(f, l, value):
        out_ref[f * levels + l] = value

    one_step(levels, out_ref.shape[1:], diff_ref, cor_ref, read, wet, None, write, True)


def rest_kernel(
    diff_ref, cor_ref, state_ref, xt_ref, yt_ref, part_ref, force_ref, fxt_ref, fyt_ref,
    out_ref, bottom, second,
):
    fields, levels, rows, lanes = out_ref.shape
    channels = fields * levels

    def wet():
        return widen(state_ref[channels], xt_ref[channels], yt_ref[channels])

    def force(f):
        return widen(force_ref[f], fxt_ref[f], fyt_ref[f])

    for f in range(fields):
        ch = f * levels
        center = widen(state_ref[ch], xt_ref[ch], yt_ref[ch])
        bottom[f] = center + wet() * (part_ref[ch] + forcing_coef * force(f))

    def read_part(f, l):
        return jnp.where(l == 0, bottom[f], part_ref[f * levels + l])

    def read_second(f, l):
        return second[f * levels + l]

    def write_second(f, l, value):
        second[f * levels + l] = value

    def write_out(f, l, value):
        out_ref[f, l] = value[:rows, :lanes]

    shape = second.shape[1:]
    one_step(levels, shape, diff_ref, cor_ref, read_part, wet, force, write_second, False)
    one_step(levels, shape, diff_ref, cor_ref, read_second, wet, force, write_out, False)


def first_step(state, x_tile, y_tile, coriolis, diffusivity):
    channels = state.shape[0] - 1
    tall = state.shape[1] + x_tile.shape[1]
    wide = state.shape[2] + y_tile.shape[2]
    vmem = pl.BlockSpec(memory_space=pltpu.VMEM)
    return pl.pallas_call(
        first_kernel,
        out_shape=jax.ShapeDtypeStruct((channels, tall, wide), jnp.float32),
        in_specs=[pl.BlockSpec(memory_space=pltpu.SMEM)] + [vmem] * 4,
        out_specs=vmem,
    )(diffusivity, coriolis, state, x_tile, y_tile)


def rest_steps(state, x_tile, y_tile, part, forcing, fx_tile, fy_tile, coriolis, diffusivity, out_shape):
    channels = part.shape[0]
    tall, wide = part.shape[1], part.shape[2]
    vmem = pl.BlockSpec(memory_space=pltpu.VMEM)
    return pl.pallas_call(
        rest_kernel,
        out_shape=jax.ShapeDtypeStruct(out_shape, jnp.float32),
        in_specs=[pl.BlockSpec(memory_space=pltpu.SMEM)] + [vmem] * 8,
        out_specs=vmem,
        scratch_shapes=[
            pltpu.VMEM((out_shape[0], tall, wide), jnp.float32),
            pltpu.VMEM((channels, tall, wide), jnp.float32),
        ],
    )(diffusivity, coriolis, state, x_tile, y_tile, part, forcing, fx_tile, fy_tile)


def shifted(block, axis, dim, width):
    count = lax.axis_size(axis)
    forward = [(i, i + 1) for i in range(count - 1)]
    backward = [(target, source) for source, target in forward]
    size = block.shape[dim]
    low = lax.ppermute(lax.slice_in_dim(block, size - width, None, axis=dim), axis, forward)
    high = lax.ppermute(lax.slice_in_dim(block, 0, width, axis=dim), axis, backward)
    return low, high


def x_halo(block, tall):
    rows = block.shape[1]
    low, high = shifted(block, "ox", 1, STEPS)
    gap = jnp.zeros((block.shape[0], tall - rows - 2 * STEPS, block.shape[2]), block.dtype)
    return jnp.concatenate([high, gap, low], axis=1)


def y_halo(tall_block, wide):
    lat_cells = tall_block.shape[2]
    south, north = shifted(tall_block, "oy", 2, STEPS)
    gap = jnp.zeros(
        (tall_block.shape[0], tall_block.shape[1], wide - lat_cells - 2 * STEPS), tall_block.dtype
    )
    return jnp.concatenate([north, gap, south], axis=2)


def lat_factor(first_cell, count, lat_total):
    latitude = (first_cell + jnp.arange(count, dtype=jnp.int32)).astype(jnp.float32)
    return coriolis_coef * (2.0 * (latitude + 0.5) / lat_total - 1.0)


def per_device(
    atm_flux,
    remap_weights,
    tile_slots,
    need_blocks,
    send_blocks,
    ocean_state,
    land_mask,
    diffusivity,
):
    blocks_here = atm_flux.shape[1]
    block_width = atm_flux.shape[2]
    owners = lax.axis_size("ox")
    capacity = send_blocks.shape[1]
    slots = owners * capacity
    block_line = jnp.arange(blocks_here, dtype=jnp.int32)
    to_block = send_blocks[:, :, None] == block_line[None, None, :]
    outgoing = jnp.einsum(
        "isb,fba->isfa", to_block.astype(atm_flux.dtype), atm_flux, preferred_element_type=jnp.float32
    ).astype(atm_flux.dtype)
    incoming = lax.all_to_all(outgoing, "ox", 0, 0, tiled=True)
    fields, levels, rows, lat_cells = ocean_state.shape
    lat_total = lat_cells * lax.axis_size("oy")
    lat_start = lax.axis_index("oy") * lat_cells
    wetness = land_mask.astype(jnp.float32)
    inner = ocean_state.reshape(fields * levels, rows, lat_cells)
    packed = jnp.concatenate([inner, wetness[None]], axis=0)
    tall = -(-(rows + 2 * STEPS) // 8) * 8
    wide = -(-(lat_cells + 2 * STEPS) // 128) * 128
    x_tile = x_halo(packed, tall)
    y_tile = y_halo(jnp.concatenate([packed, x_tile], axis=1), wide)
    lane = jnp.arange(wide, dtype=jnp.int32)
    offset = jnp.where(lane < lat_cells + STEPS, lane, lane - wide)
    latitude = (lat_start + offset).astype(jnp.float32)
    coriolis_wide = (coriolis_coef * (2.0 * (latitude + 0.5) / lat_total - 1.0))[None, :]
    part = first_step(packed, x_tile, y_tile, coriolis_wide, diffusivity)
    incoming, part = lax.optimization_barrier((incoming, part))
    incoming = incoming.reshape((slots,) + incoming.shape[2:])
    picks = incoming[tile_slots]
    forcing = jnp.einsum("tkfa,tkra->ftr", picks, remap_weights, preferred_element_type=jnp.float32)
    fx_tile = x_halo(forcing, tall)
    forcing_tall = jnp.concatenate([forcing, fx_tile], axis=1)
    fy_tile = y_halo(forcing_tall, wide)
    state = rest_steps(
        packed, x_tile, y_tile, part, forcing, fx_tile, fy_tile, coriolis_wide, diffusivity, ocean_state.shape
    )
    surface = state[2, 0].astype(jnp.bfloat16)
    pieces = jnp.einsum("tkra,tr->tka", remap_weights, surface, preferred_element_type=jnp.float32)
    slot_line = jnp.arange(slots, dtype=jnp.int32)
    to_slot = (tile_slots[:, :, None] == slot_line[None, None, :]).astype(jnp.float32)
    per_slot = jnp.einsum("tks,tka->sa", to_slot, pieces, precision=lax.Precision.HIGHEST)
    per_slot = per_slot.reshape(owners, capacity, block_width)
    returned = lax.all_to_all(per_slot, "ox", 0, 0, tiled=True)
    atmos_surface = jnp.einsum(
        "isb,isa->ba", to_block.astype(jnp.float32), returned, precision=lax.Precision.HIGHEST
    )
    return (state, atmos_surface)


def solution(mesh):
    return jax.shard_map(
        per_device,
        mesh=mesh,
        in_specs=(
            P(None, "oy", "ox"),
            P("ox", "oy", None, None),
            P("ox", "oy"),
            P("ox", "oy"),
            P("ox", "oy"),
            P(None, None, "ox", "oy"),
            P("ox", "oy"),
            P(),
        ),
        out_specs=(P(None, None, "ox", "oy"), P("oy", "ox")),
        check_vma=False,
    )
```

time: 114 us -> 78.2 us (0.69)
  local copies, waits for them, and re-layouts: 37.1 us -> 5.56 us
  Pallas kernels: 0 us -> 12 us
  starting transfers between devices: 37.1 us -> 28.1 us
  waiting for transfers between devices: 14 us -> 6.63 us
  other arithmetic: 11.4 us -> 7.66 us
  blocking collectives: 10.4 us -> 13.5 us
    slice x18 -> x5, local copies, waits for them, and re-layouts: 18.7 us -> 1.71 us  [the longest x4 1.36 us: shifted(): lax.slice_in_dim(block, 0, width, axis=dim)]
    pallas_call x0 -> x2, Pallas kernels: none -> 12 us  [the longest x1 7.07 us: rest_steps(): pl.pallas_call(rest_kernel, out_shape=jax.ShapeDtypeStruct(out_shape, jnp...]
    ppermute x12 -> x8, starting transfers between devices: 31.3 us -> 22.3 us  [the longest x4 13.4 us: shifted(): lax.ppermute(lax.slice_in_dim(block, size - width, None, axis=dim), axis,...]
    ppermute x12 -> x8, waiting for transfers between devices: 14 us -> 6.63 us  [the longest x4 5.48 us: shifted(): lax.ppermute(lax.slice_in_dim(block, size - width, None, axis=dim), axis,...]
    ppermute x6 -> x2, local copies, waits for them, and re-layouts: 8.71 us -> 1.58 us  [the longest x1 1.17 us: shifted(): lax.ppermute(lax.slice_in_dim(block, size - width, None, axis=dim), axis,...]
    another operation x3 -> x0, other arithmetic: 6.71 us -> none  [advance(): pressure = jnp.cumsum(density, axis=0) - 0.5 * density]
    concatenate x3 -> x8, other arithmetic: 0.35 us -> 6.38 us  [the longest x2 2.97 us: per_device(): packed = jnp.concatenate([inner, wetness[None]], axis=0)]
    mul x3 -> x0, local copies, waits for them, and re-layouts: 3.16 us -> none  [advance(): zonal[None] * (east - west) + meridional[None] * (north - south)]
  transfers between devices with their start and end apart: 13 -> 9, of which waited for: 6 -> 4; matrix products, arithmetic and copies ran while one was open for 17% -> 13% of each run, Pallas kernels for 0% -> 6%
where the time goes in v5:
time: 78.2 us; the launch traced here: 77.5 us
  starting transfers between devices  28.1 us (36%)
  blocking collectives  13.5 us (17%)
  Pallas kernels  12 us (15%)
  other arithmetic  7.66 us (10%)
  waiting for transfers between devices  6.63 us (8%)
  local copies, waits for them, and re-layouts  5.56 us (7%)
  matrix products  3.2 us (4%)
  between operations  0.82 us (1%)
    all_to_all x1, blocking collectives, per_device(): returned = lax.all_to_all(per_slot, 'ox', 0, 0, tiled=True)  13.5 us
    ppermute x4, starting transfers between devices, shifted(): lax.ppermute(lax.slice_in_dim(block, size - width, None, axis=dim), axis,...  13.4 us
    ppermute x4, starting transfers between devices, shifted(): lax.ppermute(lax.slice_in_dim(block, 0, width, axis=dim), axis, backward)  8.92 us
    pallas_call x1, Pallas kernels, rest_steps(): pl.pallas_call(rest_kernel, out_shape=jax.ShapeDtypeStruct(out_shape, jnp...  7.07 us
    all_to_all x1, starting transfers between devices, per_device(): incoming = lax.all_to_all(outgoing, 'ox', 0, 0, tiled=True)  5.81 us
    ppermute x4, waiting for transfers between devices, shifted(): lax.ppermute(lax.slice_in_dim(block, size - width, None, axis=dim), axis,...  5.48 us
    pallas_call x1, Pallas kernels, first_step(): pl.pallas_call(first_kernel, out_shape=jax.ShapeDtypeStruct((channels, ta...  4.95 us
    concatenate x2, other arithmetic, per_device(): packed = jnp.concatenate([inner, wetness[None]], axis=0)  2.97 us
  transfers between devices with their start and end apart: 9, of which 4 were waited for; matrix products, arithmetic and copies ran while one was open for 13% of the time, Pallas kernels for 6%

profile of v5, /device:TPU:4, one launch (start us, length us, event | category | flops | bytes accessed | tf_op | source)
XLA Modules:
  0.0 77.5 jit_solution(4009381104470857840)
XLA Ops:
  0.6 0.0 copy-start
  0.6 0.0 copy-start.1
  0.7 1.1 %convolution_convert_fusion = bf16[8,3,4,128]{3,0,2,1:T(8,128)(2,1)S(1)} fusion(bf16[4,10,128]{2,0,1:T(4,128)(2,1)} %param.8, s32[8,3]{0,1:T(4,128)} %param.11), kind=kOutput, calls=%fused_computation.1 | convolution fusion | flops 258288 | bytes 34912 | tf_op jit(solution)/shard_map/isb,fba->isfa/dot_general | solution.py:196
  1.7 0.6 copy.23
  2.3 5.8 %all-to-all-start = ((bf16[8,3,4,128]{3,2,1,0:T(4,128)(2,1)}), bf16[8,3,4,128]{3,2,1,0:T(4,128)(2,1)S(1)}, u32[]{:S(2)}, u32[]{:S(2)}) async-start(bf16[8,3,4,128]{3,2,1,0:T(4,128)(2,1)} %copy.23), calls=%async_computation | async-start | bytes 49152 | tf_op jit(solution)/shard_map/all_to_all | solution.py:199
  8.1 0.7 convert_bitcast_fusion
  8.8 1.1 %fusion = (f32[65,3,128]{2,1,0:T(4,128)S(1)}, f32[65,3,128]{2,1,0:T(4,128)S(1)}) fusion(f32[64,16,128]{2,1,0:T(8,128)} %bitcast.33, f32[1,16,128]{2,1,0:T(8,128)S(1)} %convert_bitcast_fusion), kind=kLoop, calls=%fused_computation.13 | loop fusion | flops 49920 | bytes 732160 | tf_op jit(solution)/shard_map/concatenate | solution.py:205
  9.9 1.3 %collective-permute-start = (f32[65,3,128]{2,1,0:T(4,128)S(1)}, f32[65,3,128]{2,1,0:T(4,128)S(1)}, u32[]{:S(2)}, u32[]{:S(2)}) collective-permute-start(f32[65,3,128]{2,1,0:T(4,128)S(1)} %get-tuple-element.8), channel_id=1, source_target_pairs={{4,0},{8,4},{12,8},{16,12},{20,16},{24,20},{28,24},{5,1},{9,5},{13... | collective-permute-start | bytes 299528 | tf_op jit(solution)/shard_map/ppermute | solution.py:154
  11.2 4.6 %collective-permute-start.1 = (f32[65,3,128]{2,1,0:T(4,128)S(1)}, f32[65,3,128]{2,1,0:T(4,128)S(1)}, u32[]{:S(2)}, u32[]{:S(2)}) collective-permute-start(f32[65,3,128]{2,1,0:T(4,128)S(1)} %get-tuple-element.9), channel_id=1, source_target_pairs={{0,4},{4,8},{8,12},{12,16},{16,20},{20,24},{24,28},{1,5},{5,9},{9,... | collective-permute-start | bytes 299528 | tf_op jit(solution)/shard_map/ppermute | solution.py:153
  15.8 1.9 %pad_maximum_fusion.state_ref = f32[65,16,128]{2,1,0:T(8,128)} fusion(f32[1,16,128]{2,1,0:T(8,128)S(1)} %convert_bitcast_fusion, f32[64,16,128]{2,1,0:T(8,128)} %bitcast.34), kind=kLoop, calls=%fused_computation.7 | loop fusion | flops 133120 | bytes 1064960 | tf_op jit(solution)/shard_map/concatenate | solution.py:205
  17.7 0.1 copy.24
  17.8 0.1 reshape.58
  17.9 0.1 pad.11.clone
  18.0 0.6 fusion.20.cor_ref
  18.5 0.0 collective-permute-done
  18.6 1.3 %collective-permute-done.1 = f32[65,3,128]{2,1,0:T(4,128)S(1)} collective-permute-done((f32[65,3,128]{2,1,0:T(4,128)S(1)}, f32[65,3,128]{2,1,0:T(4,128)S(1)}, u32[]{:S(2)}, u32[]{:S(2)}) %collective-permute-start.1) | collective-permute-done | bytes 99872 | tf_op jit(solution)/shard_map/ppermute | solution.py:153
  19.9 0.1 pad_maximum_fusion.1
  20.0 0.3 fusion.21
  20.3 1.0 %copy.18 = f32[65,24,3]{0,1,2:T(8,128)} copy(f32[65,24,3]{2,1,0:T(8,128)S(1)} %get-tuple-element.6) | data formatting | bytes 37440 | tf_op jit(solution)/shard_map/slice | solution.py:154
  21.3 0.4 copy.19
  21.6 1.9 %collective-permute-start.3 = (f32[65,24,3]{0,1,2:T(8,128)S(1)}, f32[65,24,3]{0,1,2:T(8,128)}, u32[]{:S(2)}, u32[]{:S(2)}) collective-permute-start(f32[65,24,3]{0,1,2:T(8,128)S(1)} %copy.19), channel_id=1, source_target_pairs={{0,1},{1,2},{2,3},{4,5},{5,6},{6,7},{8,9},{9,10},{10,11},{12,13},{... | collective-permute-start | bytes 56168 | tf_op jit(solution)/shard_map/ppermute | solution.py:153
  23.5 3.6 %collective-permute-start.2 = (f32[65,24,3]{0,1,2:T(8,128)}, f32[65,24,3]{0,1,2:T(8,128)S(1)}, u32[]{:S(2)}, u32[]{:S(2)}) collective-permute-start(f32[65,24,3]{0,1,2:T(8,128)} %copy.18), channel_id=1, source_target_pairs={{1,0},{2,1},{3,2},{5,4},{6,5},{7,6},{9,8},{10,9},{11,10},{13,12},{... | collective-permute-start | bytes 56168 | tf_op jit(solution)/shard_map/ppermute | solution.py:154
  27.2 0.8 %pad_maximum_fusion.3.xt_ref = f32[65,8,128]{2,1,0:T(8,128)} fusion(f32[65,3,128]{2,1,0:T(4,128)S(1)} %collective-permute-done.1, f32[65,2,128]{2,1,0:T(2,128)S(1)} %broadcast_in_dim.24, f32[65,3,128]{2,1,0:T(4,128)S(1)} %collective-permute-done), kind=kLoop, calls=%fused_computation.12 | loop fusion | flops 133120 | bytes 532480 | tf_op jit(solution)/shard_map/concatenate | solution.py:162
  28.0 1.1 %collective-permute-done.2 = f32[65,24,3]{0,1,2:T(8,128)S(1)} collective-permute-done((f32[65,24,3]{0,1,2:T(8,128)}, f32[65,24,3]{0,1,2:T(8,128)S(1)}, u32[]{:S(2)}, u32[]{:S(2)}) %collective-permute-start.2) | collective-permute-done | bytes 18752 | tf_op jit(solution)/shard_map/ppermute | solution.py:154
  29.1 0.4 copy.20
  29.5 0.0 collective-permute-done.3
  29.5 1.2 %copy.21 = f32[65,24,3]{2,1,0:T(8,128)S(1)} copy(f32[65,24,3]{0,1,2:T(8,128)} %collective-permute-done.3) | data formatting | bytes 37440 | tf_op jit(solution)/shard_map/ppermute | solution.py:153
  30.7 1.2 %pad_maximum_fusion.2.yt_ref = f32[65,24,128]{2,1,0:T(8,128)} fusion(f32[65,24,3]{2,1,0:T(8,128)S(1)} %copy.21, f32[65,24,3]{2,1,0:T(8,128)S(1)} %copy.20, f32[128]{0:T(128)S(1)} %pad.11.clone), kind=kLoop, calls=%fused_computation.9 | loop fusion | flops 399360 | bytes 836672 | tf_op jit(solution)/shard_map/concatenate | solution.py:171
  31.9 5.0 %shard_map.86.part_ref = f32[64,24,256]{2,1,0:T(8,128)} custom-call(f32[16]{0:T(128)} %diff_ref.3, f32[1,256]{1,0:T(1,128)} %fusion.20.cor_ref, f32[65,16,128]{2,1,0:T(8,128)} %pad_maximum_fusion.state_ref, f32[65,8,128]{2,1,0:T(8,128)} %pad_maximum_fusion.3.xt_ref, f32[65,24,128]{2,1,0:T(8,128)} %pad_maximum_fusion.2.yt_ref), custom_call_target="tpu_custom_call" | custom-call | tf_op jit(solution)/shard_map/pallas_call | solution.py:124
  36.8 0.0 all-to-all-done
  36.8 0.6 gather_fusion
  37.5 0.6 convolution_bitcast_fusion
  38.1 1.3 %collective-permute-start.4 = (f32[4,3,128]{2,1,0:T(4,128)S(1)}, f32[4,3,128]{2,1,0:T(4,128)S(1)}, u32[]{:S(2)}, u32[]{:S(2)}) collective-permute-start(f32[4,3,128]{2,1,0:T(4,128)S(1)} %get-tuple-element.12), channel_id=1, source_target_pairs={{4,0},{8,4},{12,8},{16,12},{20,16},{24,20},{28,24},{5,1},{9,5},{13... | collective-permute-start | bytes 18440 | tf_op jit(solution)/shard_map/ppermute | solution.py:154
  39.4 5.0 %collective-permute-start.5 = (f32[4,3,128]{2,1,0:T(4,128)S(1)}, f32[4,3,128]{2,1,0:T(4,128)S(1)}, u32[]{:S(2)}, u32[]{:S(2)}) collective-permute-start(f32[4,3,128]{2,1,0:T(4,128)S(1)} %get-tuple-element.13), channel_id=1, source_target_pairs={{0,4},{4,8},{8,12},{12,16},{16,20},{20,24},{24,28},{1,5},{5,9},{9,... | collective-permute-start | bytes 18440 | tf_op jit(solution)/shard_map/ppermute | solution.py:153
  44.5 1.3 %collective-permute-done.5 = f32[4,3,128]{2,1,0:T(4,128)S(1)} collective-permute-done((f32[4,3,128]{2,1,0:T(4,128)S(1)}, f32[4,3,128]{2,1,0:T(4,128)S(1)}, u32[]{:S(2)}, u32[]{:S(2)}) %collective-permute-start.5) | collective-permute-done | bytes 6176 | tf_op jit(solution)/shard_map/ppermute | solution.py:153
  45.8 0.1 fusion.22
  45.9 2.7 %collective-permute-start.6 = (f32[4,24,3]{2,1,0:T(8,128)S(1)}, f32[4,24,3]{2,1,0:T(8,128)S(1)}, u32[]{:S(2)}, u32[]{:S(2)}) collective-permute-start(f32[4,24,3]{2,1,0:T(8,128)S(1)} %get-tuple-element.10), channel_id=1, source_target_pairs={{1,0},{2,1},{3,2},{5,4},{6,5},{7,6},{9,8},{10,9},{11,10},{13,12},{... | collective-permute-start | bytes 3464 | tf_op jit(solution)/shard_map/ppermute | solution.py:154
  48.6 1.9 %collective-permute-start.7 = (f32[4,24,3]{2,1,0:T(8,128)S(1)}, f32[4,24,3]{2,1,0:T(8,128)S(1)}, u32[]{:S(2)}, u32[]{:S(2)}) collective-permute-start(f32[4,24,3]{2,1,0:T(8,128)S(1)} %get-tuple-element.11), channel_id=1, source_target_pairs={{0,1},{1,2},{2,3},{4,5},{5,6},{6,7},{8,9},{9,10},{10,11},{12,13},{... | collective-permute-start | bytes 3464 | tf_op jit(solution)/shard_map/ppermute | solution.py:153
  50.5 0.6 pad_maximum_fusion.6.fxt_ref
  51.1 0.0 collective-permute-done.6
  51.1 2.9 %collective-permute-done.7 = f32[4,24,3]{2,1,0:T(8,128)S(1)} collective-permute-done((f32[4,24,3]{2,1,0:T(8,128)S(1)}, f32[4,24,3]{2,1,0:T(8,128)S(1)}, u32[]{:S(2)}, u32[]{:S(2)}) %collective-permute-start.7) | collective-permute-done | bytes 1184 | tf_op jit(solution)/shard_map/ppermute | solution.py:153
  54.0 0.7 pad_maximum_fusion.5.fyt_ref
  54.7 7.1 %shard_map.87 = f32[4,16,16,128]{3,2,1,0:T(8,128)} custom-call(f32[16]{0:T(128)} %diff_ref.3, f32[1,256]{1,0:T(1,128)} %fusion.20.cor_ref, f32[65,16,128]{2,1,0:T(8,128)} %pad_maximum_fusion.state_ref, f32[65,8,128]{2,1,0:T(8,128)} %pad_maximum_fusion.3.xt_ref, f32[65,24,128]{2,1,0:T(8,128)} %pad_maximum_fusion.2.yt_ref, f32[64,24,256]{2,1,0:T(8,128)} %shard_map.86.part_ref, ...), custom_call_target="tpu_custom_call" | custom-call | tf_op jit(solution)/shard_map/pallas_call | solution.py:136
  61.8 0.7 fusion.14
  62.5 0.4 fusion.10
  62.9 0.3 convolution_bitcast_fusion.1
  63.2 13.5 %all_to_all.10 = f32[8,3,128]{2,1,0:T(4,128)S(1)} all-to-all(f32[8,3,128]{2,1,0:T(4,128)S(1)} %reshape.55), channel_id=1, replica_groups=mesh['ox'=8,'oy'=4] {'ox'}, dimensions={0} | all-to-all | bytes 24576 | tf_op jit(solution)/shard_map/all_to_all | solution.py:231
  76.7 0.9 %convolution_bitcast_fusion.2 = f32[10,128]{1,0:T(8,128)} fusion(f32[8,3,128]{2,1,0:T(4,128)S(1)} %all_to_all.10, s32[8,3]{0,1:T(4,128)S(1)} %copy-done.4), kind=kOutput, calls=%fused_computation.4 | convolution fusion | flops 368880 | bytes 17504 | tf_op jit(solution)/shard_map/isb,isa->ba/dot_general | solution.py:232
  (18 shorter events, 0.1 us)
Async XLA Ops:
  0.6 36.8 %copy-start = (bf16[16,3,128,128]{3,2,1,0:T(8,128)(2,1)S(1)}, bf16[16,3,128,128]{3,2,1,0:T(8,128)(2,1)}, u32[]{:S(2)}) copy-start(bf16[16,3,128,128]{3,2,1,0:T(8,128)(2,1)} %param.9) | copy-start | bytes 4718596
  0.6 19.2 %copy-start.1 = (f32[4,16,16,128]{3,2,1,0:T(8,128)S(1)}, f32[4,16,16,128]{3,2,1,0:T(8,128)}, u32[]{:S(2)}) copy-start(f32[4,16,16,128]{3,2,1,0:T(8,128)} %param.12) | copy-start | bytes 1572868
  0.7 17.0 %copy-start.3 = (s32[16,3]{0,1:T(4,128)S(1)}, s32[16,3]{0,1:T(4,128)}, u32[]{:S(2)}) copy-start(s32[16,3]{0,1:T(4,128)} %param.10) | copy-start | bytes 580
  2.3 34.5 %all-to-all-start = ((bf16[8,3,4,128]{3,2,1,0:T(4,128)(2,1)}), bf16[8,3,4,128]{3,2,1,0:T(4,128)(2,1)S(1)}, u32[]{:S(2)}, u32[]{:S(2)}) async-start(bf16[8,3,4,128]{3,2,1,0:T(4,128)(2,1)} %copy.23), calls=%async_computation | async-start | bytes 49152 | tf_op jit(solution)/shard_map/all_to_all | solution.py:199
  9.9 8.6 %collective-permute-start = (f32[65,3,128]{2,1,0:T(4,128)S(1)}, f32[65,3,128]{2,1,0:T(4,128)S(1)}, u32[]{:S(2)}, u32[]{:S(2)}) collective-permute-start(f32[65,3,128]{2,1,0:T(4,128)S(1)} %get-tuple-element.8), channel_id=1, source_target_pairs={{4,0},{8,4},{12,8},{16,12},{20,16},{24,20},{28,24},{5,1},{9,5},{13... | collective-permute-start | bytes 299528 | tf_op jit(solution)/shard_map/ppermute | solution.py:154
  11.2 8.6 %collective-permute-start.1 = (f32[65,3,128]{2,1,0:T(4,128)S(1)}, f32[65,3,128]{2,1,0:T(4,128)S(1)}, u32[]{:S(2)}, u32[]{:S(2)}) collective-permute-start(f32[65,3,128]{2,1,0:T(4,128)S(1)} %get-tuple-element.9), channel_id=1, source_target_pairs={{0,4},{4,8},{8,12},{12,16},{16,20},{20,24},{24,28},{1,5},{5,9},{9,... | collective-permute-start | bytes 299528 | tf_op jit(solution)/shard_map/ppermute | solution.py:153
  21.6 7.9 %collective-permute-start.3 = (f32[65,24,3]{0,1,2:T(8,128)S(1)}, f32[65,24,3]{0,1,2:T(8,128)}, u32[]{:S(2)}, u32[]{:S(2)}) collective-permute-start(f32[65,24,3]{0,1,2:T(8,128)S(1)} %copy.19), channel_id=1, source_target_pairs={{0,1},{1,2},{2,3},{4,5},{5,6},{6,7},{8,9},{9,10},{10,11},{12,13},{... | collective-permute-start | bytes 56168 | tf_op jit(solution)/shard_map/ppermute | solution.py:153
  23.5 5.6 %collective-permute-start.2 = (f32[65,24,3]{0,1,2:T(8,128)}, f32[65,24,3]{0,1,2:T(8,128)S(1)}, u32[]{:S(2)}, u32[]{:S(2)}) collective-permute-start(f32[65,24,3]{0,1,2:T(8,128)} %copy.18), channel_id=1, source_target_pairs={{1,0},{2,1},{3,2},{5,4},{6,5},{7,6},{9,8},{10,9},{11,10},{13,12},{... | collective-permute-start | bytes 56168 | tf_op jit(solution)/shard_map/ppermute | solution.py:154
  38.1 16.6 %copy-start.2 = (f32[16,4,128]{2,0,1:T(8,128)}, f32[16,4,128]{2,0,1:T(8,128)S(1)}, u32[]{:S(2)}) copy-start(f32[16,4,128]{2,0,1:T(8,128)S(1)} %copy.44) | copy-start | bytes 98308
  38.1 6.3 %collective-permute-start.4 = (f32[4,3,128]{2,1,0:T(4,128)S(1)}, f32[4,3,128]{2,1,0:T(4,128)S(1)}, u32[]{:S(2)}, u32[]{:S(2)}) collective-permute-start(f32[4,3,128]{2,1,0:T(4,128)S(1)} %get-tuple-element.12), channel_id=1, source_target_pairs={{4,0},{8,4},{12,8},{16,12},{20,16},{24,20},{28,24},{5,1},{9,5},{13... | collective-permute-start | bytes 18440 | tf_op jit(solution)/shard_map/ppermute | solution.py:154
  39.4 6.4 %collective-permute-start.5 = (f32[4,3,128]{2,1,0:T(4,128)S(1)}, f32[4,3,128]{2,1,0:T(4,128)S(1)}, u32[]{:S(2)}, u32[]{:S(2)}) collective-permute-start(f32[4,3,128]{2,1,0:T(4,128)S(1)} %get-tuple-element.13), channel_id=1, source_target_pairs={{0,4},{4,8},{8,12},{12,16},{16,20},{20,24},{24,28},{1,5},{5,9},{9,... | collective-permute-start | bytes 18440 | tf_op jit(solution)/shard_map/ppermute | solution.py:153
  45.9 5.2 %collective-permute-start.6 = (f32[4,24,3]{2,1,0:T(8,128)S(1)}, f32[4,24,3]{2,1,0:T(8,128)S(1)}, u32[]{:S(2)}, u32[]{:S(2)}) collective-permute-start(f32[4,24,3]{2,1,0:T(8,128)S(1)} %get-tuple-element.10), channel_id=1, source_target_pairs={{1,0},{2,1},{3,2},{5,4},{6,5},{7,6},{9,8},{10,9},{11,10},{13,12},{... | collective-permute-start | bytes 3464 | tf_op jit(solution)/shard_map/ppermute | solution.py:154
  48.6 5.4 %collective-permute-start.7 = (f32[4,24,3]{2,1,0:T(8,128)S(1)}, f32[4,24,3]{2,1,0:T(8,128)S(1)}, u32[]{:S(2)}, u32[]{:S(2)}) collective-permute-start(f32[4,24,3]{2,1,0:T(8,128)S(1)} %get-tuple-element.11), channel_id=1, source_target_pairs={{0,1},{1,2},{2,3},{4,5},{5,6},{6,7},{8,9},{9,10},{10,11},{12,13},{... | collective-permute-start | bytes 3464 | tf_op jit(solution)/shard_map/ppermute | solution.py:153
  61.8 14.9 %copy-start.4 = (s32[8,3]{0,1:T(4,128)S(1)}, s32[8,3]{0,1:T(4,128)}, u32[]{:S(2)}) copy-start(s32[8,3]{0,1:T(4,128)} %param.11) | copy-start | bytes 292

commit v6 on v4

--- a/solution.py
+++ b/solution.py
@@ -17,45 +17,47 @@
 forcing_coef = 0.5
 
 
-def advance(padded, center, diffusivity, coriolis, forcing, wetness):
-    east = padded[:, :, 2:, 1:-1]
-    west = padded[:, :, :-2, 1:-1]
-    north = padded[:, :, 1:-1, 2:]
-    south = padded[:, :, 1:-1, :-2]
-    zonal = center[0]
-    meridional = center[1]
-    advection = (
-        -advect_coef * 0.5 * (zonal[None] * (east - west) + meridional[None] * (north - south))
-    )
-    laplace = diffusivity[None, :, None, None] * (east + west + north + south - 4.0 * center)
-    upper = jnp.concatenate([center[:, :1], center[:, :-1]], axis=1)
-    lower = jnp.concatenate([center[:, 1:], center[:, -1:]], axis=1)
-    mixing = vertical_coef * (upper + lower - 2.0 * center)
-    density = haline_coef * padded[3] - thermal_coef * padded[2]
-    pressure = jnp.cumsum(density, axis=0) - 0.5 * density
-    grad_east = pressure[:, 2:, 1:-1] - pressure[:, :-2, 1:-1]
-    grad_north = pressure[:, 1:-1, 2:] - pressure[:, 1:-1, :-2]
-    zonal_push = coriolis * meridional - pressure_coef * 0.5 * grad_east
-    merid_push = -coriolis * zonal - pressure_coef * 0.5 * grad_north
-    tracer_zero = jnp.zeros((2,) + zonal.shape, jnp.float32)
-    momentum = jnp.concatenate([zonal_push[None], merid_push[None], tracer_zero], axis=0)
-    total = advection + laplace + mixing + momentum
-    total = total.at[:, 0].add(forcing_coef * forcing)
-    return center + wetness * total
-
-
-def stencil_kernel(diff_ref, cor_ref, state_ref, aux_ref, xt_ref, yt_ref, out_ref, first, second):
+def stencil_kernel(
+    diff_ref, cor_ref, state_ref, aux_ref, high_ref, low_ref, north_ref, south_ref,
+    out_ref, source, first, second, x_pad, y_pad,
+):
     fields, levels, rows, lanes = out_ref.shape
     channels = fields * levels
-    tall = rows + xt_ref.shape[1]
-    wide = lanes + yt_ref.shape[2]
-
-    def widen(inner, ch):
-        left = jnp.concatenate([inner, xt_ref[ch]], axis=0)
-        return jnp.concatenate([left, yt_ref[ch]], axis=1)
+    tall, wide = source.shape[1], source.shape[2]
+    width = high_ref.shape[1]
+    x_pad[...] = jnp.zeros(x_pad.shape, jnp.float32)
+    y_pad[...] = jnp.zeros(y_pad.shape, jnp.float32)
+    row_line = lax.broadcasted_iota(jnp.int32, (tall - rows, lanes), 0)
+    lane_line = lax.broadcasted_iota(jnp.int32, (tall, wide - lanes), 1)
+
+    def assemble(ch, inner):
+        source[ch, :rows, :lanes] = inner
+        x_pad[0, :width] = high_ref[ch]
+        x_pad[1, :width] = low_ref[ch]
+        east_west = jnp.where(
+            row_line < width, x_pad[0], pltpu.roll(x_pad[1], tall - rows - width, 0)
+        )
+        source[ch, rows:, :lanes] = east_west
+        y_pad[0, :, :width] = north_ref[ch]
+        y_pad[1, :, :width] = south_ref[ch]
+        north_south = jnp.where(
+            lane_line < width, y_pad[0], pltpu.roll(y_pad[1], wide - lanes - width, 1)
+        )
+        source[ch, :, lanes:] = north_south
+
+    def assemble_state(ch, carry):
+        assemble(ch, state_ref[ch])
+        return carry
+
+    def assemble_aux(index, carry):
+        assemble(channels + index, aux_ref[index])
+        return carry
+
+    lax.fori_loop(0, channels, assemble_state, 0)
+    lax.fori_loop(0, aux_ref.shape[0], assemble_aux, 0)
 
     def aux(index):
-        return widen(aux_ref[index], channels + index)
+        return source[channels + index]
 
     def one_step(read, write):
         def level(l, cum):
@@ -95,7 +97,7 @@
         lax.fori_loop(0, levels, level, jnp.zeros((tall, wide), jnp.float32))
 
     def read_src(ch):
-        return widen(state_ref[ch], ch)
+        return source[ch]
 
     def read_first(ch):
         return first[ch]
@@ -119,21 +121,26 @@
         one_step(read, write)
 
 
-def run_steps(state, aux, x_tile, y_tile, coriolis, diffusivity, out_shape):
-    channels = state.shape[0]
-    tall = state.shape[1] + x_tile.shape[1]
-    wide = state.shape[2] + y_tile.shape[2]
+def run_steps(state, aux, high, low, north, south, coriolis, diffusivity, out_shape):
+    channels = state.shape[0] + aux.shape[0]
+    rows, lanes = state.shape[1], state.shape[2]
+    width = high.shape[1]
+    tall = -(-(rows + 2 * width) // 8) * 8
+    wide = -(-(lanes + 2 * width) // 128) * 128
     vmem = pl.BlockSpec(memory_space=pltpu.VMEM)
     return pl.pallas_call(
         stencil_kernel,
         out_shape=jax.ShapeDtypeStruct(out_shape, jnp.float32),
-        in_specs=[pl.BlockSpec(memory_space=pltpu.SMEM)] + [vmem] * 5,
+        in_specs=[pl.BlockSpec(memory_space=pltpu.SMEM)] + [vmem] * 7,
         out_specs=vmem,
         scratch_shapes=[
             pltpu.VMEM((channels, tall, wide), jnp.float32),
-            pltpu.VMEM((channels, tall, wide), jnp.float32),
+            pltpu.VMEM((state.shape[0], tall, wide), jnp.float32),
+            pltpu.VMEM((state.shape[0], tall, wide), jnp.float32),
+            pltpu.VMEM((2, tall - rows, lanes), jnp.float32),
+            pltpu.VMEM((2, tall, wide - lanes), jnp.float32),
         ],
-    )(diffusivity, coriolis, state, aux, x_tile, y_tile)
+    )(diffusivity, coriolis, state, aux, high, low, north, south)
 
 
 def shifted(block, axis, dim, width):
@@ -185,17 +192,23 @@
     tall = -(-(rows + 2 * STEPS) // 8) * 8
     wide = -(-(lat_cells + 2 * STEPS) // 128) * 128
     low, high = shifted(packed, "ox", 1, STEPS)
-    gap = jnp.zeros((packed.shape[0], tall - rows - 2 * STEPS, lat_cells), jnp.float32)
-    x_tile = jnp.concatenate([high, gap, low], axis=1)
-    tall_block = jnp.concatenate([packed, x_tile], axis=1)
-    south, north = shifted(tall_block, "oy", 2, STEPS)
-    gap = jnp.zeros((packed.shape[0], tall, wide - lat_cells - 2 * STEPS), jnp.float32)
-    y_tile = jnp.concatenate([north, gap, south], axis=2)
+    gap = jnp.zeros((packed.shape[0], tall - rows - 2 * STEPS, STEPS), jnp.float32)
+    south_edge = jnp.concatenate(
+        [packed[:, :, -STEPS:], high[:, :, -STEPS:], gap, low[:, :, -STEPS:]], axis=1
+    )
+    north_edge = jnp.concatenate(
+        [packed[:, :, :STEPS], high[:, :, :STEPS], gap, low[:, :, :STEPS]], axis=1
+    )
+    count = lax.axis_size("oy")
+    forward = [(i, i + 1) for i in range(count - 1)]
+    backward = [(target, source) for source, target in forward]
+    south = lax.ppermute(south_edge, "oy", forward)
+    north = lax.ppermute(north_edge, "oy", backward)
     lane = jnp.arange(wide, dtype=jnp.int32)
     offset = jnp.where(lane < lat_cells + STEPS, lane, lane - wide)
     latitude = (lat_start + offset).astype(jnp.float32)
     coriolis_wide = (coriolis_coef * (2.0 * (latitude + 0.5) / lat_total - 1.0))[None, :]
-    state = run_steps(inner, aux, x_tile, y_tile, coriolis_wide, diffusivity, ocean_state.shape)
+    state = run_steps(inner, aux, high, low, north, south, coriolis_wide, diffusivity, ocean_state.shape)
     surface = state[2, 0].astype(jnp.bfloat16)
     pieces = jnp.einsum("tkra,tr->tka", remap_weights, surface, preferred_element_type=jnp.float32)
     slot_line = jnp.arange(slots, dtype=jnp.int32)

time: 60.4 us -> 64.8 us (1.073)
  Pallas kernels: 8.94 us -> 14.6 us
  other arithmetic: 6.63 us -> 2.73 us
  local copies, waits for them, and re-layouts: 4.84 us -> 6.49 us
  blocking collectives: 8.64 us -> 9.45 us
    ppermute x0 -> x2, starting transfers between devices: none -> 6.85 us  [the longest x1 4.93 us: per_device(): south = lax.ppermute(south_edge, 'oy', forward)]
    pallas_call x1, Pallas kernels: 8.94 us -> 14.6 us  [run_steps(): pl.pallas_call(stencil_kernel, out_shape=jax.ShapeDtypeStruct(out_shape,...]
    ppermute x2 -> x1, waiting for transfers between devices: 5.22 us -> 0.01 us  [shifted(): lax.ppermute(lax.slice_in_dim(block, 0, width, axis=dim), axis, backward)]
    ppermute x2 -> x1, starting transfers between devices: 8.7 us -> 3.99 us  [shifted(): lax.ppermute(lax.slice_in_dim(block, size - width, None, axis=dim), axis,...]
    concatenate x3 -> x2, other arithmetic: 3.98 us -> 0.14 us  [the longest x1 0.09 us: per_device(): jnp.concatenate([packed[:, :, -STEPS:], high[:, :, -STEPS:], gap, low[:,...]
    ppermute x0 -> x2, waiting for transfers between devices: none -> 2.72 us  [the longest x1 2.72 us: per_device(): north = lax.ppermute(north_edge, 'oy', backward)]
    ppermute x2 -> x1, waiting for transfers between devices: 0.1 us -> 2.53 us  [shifted(): lax.ppermute(lax.slice_in_dim(block, size - width, None, axis=dim), axis,...]
    ppermute x2 -> x1, starting transfers between devices: 3.22 us -> 1.29 us  [shifted(): lax.ppermute(lax.slice_in_dim(block, 0, width, axis=dim), axis, backward)]
  transfers between devices with their start and end apart: 5 -> 5, of which waited for: 4 -> 3; matrix products, arithmetic and copies ran while one was open for 9% -> 8% of each run, Pallas kernels for 0% -> 0%
where the time goes in v6:
time: 64.8 us; the launch traced here: 64.3 us
  starting transfers between devices  18.5 us (29%)
  Pallas kernels  14.6 us (23%)
  blocking collectives  9.45 us (15%)
  waiting for transfers between devices  8.51 us (13%)
  local copies, waits for them, and re-layouts  6.49 us (10%)
  matrix products  3.2 us (5%)
  other arithmetic  2.73 us (4%)
  between operations  0.75 us (1%)
    pallas_call x1, Pallas kernels, run_steps(): pl.pallas_call(stencil_kernel, out_shape=jax.ShapeDtypeStruct(out_shape,...  14.6 us
    all_to_all x1, blocking collectives, per_device(): returned = lax.all_to_all(per_slot, 'ox', 0, 0, tiled=True)  9.45 us
    all_to_all x1, starting transfers between devices, per_device(): incoming = lax.all_to_all(outgoing, 'ox', 0, 0, tiled=True)  6.35 us
    ppermute x1, starting transfers between devices, per_device(): south = lax.ppermute(south_edge, 'oy', forward)  4.93 us
    ppermute x1, starting transfers between devices, shifted(): lax.ppermute(lax.slice_in_dim(block, size - width, None, axis=dim), axis,...  3.99 us
    all_to_all x1, waiting for transfers between devices, per_device(): incoming = lax.all_to_all(outgoing, 'ox', 0, 0, tiled=True)  3.25 us
    ppermute x1, waiting for transfers between devices, per_device(): north = lax.ppermute(north_edge, 'oy', backward)  2.72 us
    ppermute x1, waiting for transfers between devices, shifted(): lax.ppermute(lax.slice_in_dim(block, size - width, None, axis=dim), axis,...  2.53 us
  transfers between devices with their start and end apart: 5, of which 3 were waited for; matrix products, arithmetic and copies ran while one was open for 8% of the time, Pallas kernels for 0%

profile of v6, /device:TPU:1, one launch (start us, length us, event | category | flops | bytes accessed | tf_op | source)
XLA Modules:
  0.0 64.3 jit_solution(3125651556058347634)
XLA Ops:
  0.6 0.0 copy-start
  0.6 0.0 copy-start.1
  0.7 1.1 %convolution_convert_fusion = bf16[8,3,4,128]{3,0,2,1:T(8,128)(2,1)S(1)} fusion(bf16[4,10,128]{2,0,1:T(4,128)(2,1)} %param.8, s32[8,3]{0,1:T(4,128)} %param.11), kind=kOutput, calls=%fused_computation.1 | convolution fusion | flops 258288 | bytes 34912 | tf_op jit(solution)/shard_map/isb,fba->isfa/dot_general | solution.py:178
  1.7 0.6 copy.19
  2.3 6.4 %all-to-all-start = ((bf16[8,3,4,128]{3,2,1,0:T(4,128)(2,1)}), bf16[8,3,4,128]{3,2,1,0:T(4,128)(2,1)S(1)}, u32[]{:S(2)}, u32[]{:S(2)}) async-start(bf16[8,3,4,128]{3,2,1,0:T(4,128)(2,1)} %copy.19), calls=%async_computation | async-start | bytes 49152 | tf_op jit(solution)/shard_map/all_to_all | solution.py:181
  8.7 0.7 %compare_select_fusion.1 = s32[16,3]{0,1:T(4,128)S(1)} fusion(s32[16,3]{0,1:T(4,128)} %param.10), kind=kLoop, calls=%fused_computation.26 | loop fusion | flops 144 | bytes 384 | tf_op jit(solution)/shard_map/select_n | solution.py:183
  9.4 0.1 copy.20
  9.5 0.1 reshape.58
  9.6 0.7 %convert_bitcast_fusion = f32[1,16,128]{2,1,0:T(8,128)S(1)} fusion(s32[16,128]{1,0:T(8,128)} %param.13), kind=kLoop, calls=%fused_computation.22 | loop fusion | flops 2048 | bytes 16384 | tf_op jit(solution)/shard_map/broadcast_in_dim | solution.py:190
  10.3 0.6 fusion.18.cor_ref
  10.8 0.1 pad.6.clone
  10.9 3.3 %all-to-all-done = bf16[8,3,4,128]{3,2,1,0:T(4,128)(2,1)S(1)} async-done(((bf16[8,3,4,128]{3,2,1,0:T(4,128)(2,1)}), bf16[8,3,4,128]{3,2,1,0:T(4,128)(2,1)S(1)}, u32[]{:S(2)}, u32[]{:S(2)}) %all-to-all-start) | async-done | bytes 24608 | tf_op jit(solution)/shard_map/all_to_all | solution.py:181
  14.2 0.6 gather_fusion
  14.8 0.0 copy-done
  14.8 0.6 convolution_bitcast_fusion
  15.5 0.0 copy-done.1
  15.5 0.1 pad_maximum_fusion
  15.5 0.1 fusion.20
  15.6 1.3 %collective-permute-start = (f32[69,3,128]{2,1,0:T(4,128)S(1)}, f32[69,3,128]{2,1,0:T(4,128)S(1)}, u32[]{:S(2)}, u32[]{:S(2)}) collective-permute-start(f32[69,3,128]{2,1,0:T(4,128)S(1)} %get-tuple-element.5), channel_id=1, source_target_pairs={{4,0},{8,4},{12,8},{16,12},{20,16},{24,20},{28,24},{5,1},{9,5},{13... | collective-permute-start | bytes 317960 | tf_op jit(solution)/shard_map/ppermute | solution.py:152
  16.9 0.2 fusion.19
  17.1 4.0 %collective-permute-start.1 = (f32[69,3,128]{2,1,0:T(4,128)S(1)}, f32[69,3,128]{2,1,0:T(4,128)S(1)}, u32[]{:S(2)}, u32[]{:S(2)}) collective-permute-start(f32[69,3,128]{2,1,0:T(4,128)S(1)} %get-tuple-element.4), channel_id=1, source_target_pairs={{0,4},{4,8},{8,12},{12,16},{16,20},{20,24},{24,28},{1,5},{5,9},{9,... | collective-permute-start | bytes 317960 | tf_op jit(solution)/shard_map/ppermute | solution.py:151
  21.1 0.3 copy.25
  21.4 0.3 copy.22
  21.7 0.0 collective-permute-done.high_ref
  21.7 0.1 fusion.21
  21.8 0.1 copy.26
  22.0 0.1 copy.23
  22.1 2.5 %collective-permute-done.1.low_ref = f32[69,3,128]{2,1,0:T(4,128)S(1)} collective-permute-done((f32[69,3,128]{2,1,0:T(4,128)S(1)}, f32[69,3,128]{2,1,0:T(4,128)S(1)}, u32[]{:S(2)}, u32[]{:S(2)}) %collective-permute-start.1) | collective-permute-done | bytes 106016 | tf_op jit(solution)/shard_map/ppermute | solution.py:151
  24.6 0.1 fusion.22
  24.7 0.1 copy.27
  24.9 0.1 copy.24
  25.0 0.1 pad_maximum_fusion.3
  25.1 4.9 %collective-permute-start.3 = (f32[69,24,3]{0,1,2:T(8,128)S(1)}, f32[69,24,3]{0,1,2:T(8,128)S(1)}, u32[]{:S(2)}, u32[]{:S(2)}) collective-permute-start(f32[69,24,3]{0,1,2:T(8,128)S(1)} %get-tuple-element.10), channel_id=1, source_target_pairs={{0,1},{1,2},{2,3},{4,5},{5,6},{6,7},{8,9},{9,10},{10,11},{12,13},{... | collective-permute-start | bytes 59624 | tf_op jit(solution)/shard_map/ppermute | solution.py:205
  30.0 1.9 %collective-permute-start.2 = (f32[69,24,3]{0,1,2:T(8,128)S(1)}, f32[69,24,3]{0,1,2:T(8,128)S(1)}, u32[]{:S(2)}, u32[]{:S(2)}) collective-permute-start(f32[69,24,3]{0,1,2:T(8,128)S(1)} %get-tuple-element.11), channel_id=1, source_target_pairs={{1,0},{2,1},{3,2},{5,4},{6,5},{7,6},{9,8},{10,9},{11,10},{13,12},{... | collective-permute-start | bytes 59624 | tf_op jit(solution)/shard_map/ppermute | solution.py:206
  31.9 0.6 pad_maximum_fusion.1.aux_ref
  32.6 2.7 %collective-permute-done.2 = f32[69,24,3]{0,1,2:T(8,128)S(1)} collective-permute-done((f32[69,24,3]{0,1,2:T(8,128)S(1)}, f32[69,24,3]{0,1,2:T(8,128)S(1)}, u32[]{:S(2)}, u32[]{:S(2)}) %collective-permute-start.2) | collective-permute-done | bytes 19904 | tf_op jit(solution)/shard_map/ppermute | solution.py:206
  35.3 1.3 %copy.28.north_ref = f32[69,24,3]{2,1,0:T(8,128)} copy(f32[69,24,3]{0,1,2:T(8,128)S(1)} %collective-permute-done.2) | data formatting | bytes 39744 | tf_op jit(solution)/shard_map/ppermute | solution.py:206
  36.6 0.0 collective-permute-done.3
  36.6 1.3 %copy.29.south_ref = f32[69,24,3]{2,1,0:T(8,128)} copy(f32[69,24,3]{0,1,2:T(8,128)S(1)} %collective-permute-done.3) | data formatting | bytes 39744 | tf_op jit(solution)/shard_map/ppermute | solution.py:205
  37.9 0.0 copy-done.2
  37.9 0.0 copy-done.3
  37.9 14.6 %shard_map.86 = f32[4,16,16,128]{3,2,1,0:T(8,128)} custom-call(f32[16]{0:T(128)} %diff_ref.1, f32[1,256]{1,0:T(1,128)} %fusion.18.cor_ref, f32[64,16,128]{2,1,0:T(8,128)} %bitcast.33, f32[5,16,128]{2,1,0:T(8,128)} %pad_maximum_fusion.1.aux_ref, f32[69,3,128]{2,1,0:T(4,128)} %copy-done.2, f32[69,3,128]{2,1,0:T(4,128)} %copy-done.3, ...), custom_call_target="tpu_custom_call" | custom-call | tf_op jit(solution)/shard_map/pallas_call | solution.py:131
  52.6 0.7 %fusion.12 = bf16[16,128,1,1]{1,0,2,3:T(8,128)(2,1)S(1)} fusion(f32[4,16,16,128]{3,2,1,0:T(8,128)} %shard_map.86), kind=kLoop, calls=%fused_computation.27 | loop fusion | bytes 8192 | tf_op jit(solution)/shard_map/convert_element_type | solution.py:212
  53.3 0.4 fusion.8
  53.7 0.0 copy-done.4
  53.7 0.3 convolution_bitcast_fusion.1
  54.0 9.5 %all_to_all.10 = f32[8,3,128]{2,1,0:T(4,128)S(1)} all-to-all(f32[8,3,128]{2,1,0:T(4,128)S(1)} %reshape.55), channel_id=1, replica_groups=mesh['ox'=8,'oy'=4] {'ox'}, dimensions={0} | all-to-all | bytes 24576 | tf_op jit(solution)/shard_map/all_to_all | solution.py:218
  63.4 0.9 %convolution_bitcast_fusion.2 = f32[10,128]{1,0:T(8,128)} fusion(f32[8,3,128]{2,1,0:T(4,128)S(1)} %all_to_all.10, s32[8,3]{0,1:T(4,128)S(1)} %copy-done.5), kind=kOutput, calls=%fused_computation.4 | convolution fusion | flops 368880 | bytes 17504 | tf_op jit(solution)/shard_map/isb,isa->ba/dot_general | solution.py:219
  (9 shorter events, 0.0 us)
Async XLA Ops:
  0.6 14.2 %copy-start = (bf16[16,3,128,128]{3,2,1,0:T(8,128)(2,1)S(1)}, bf16[16,3,128,128]{3,2,1,0:T(8,128)(2,1)}, u32[]{:S(2)}) copy-start(bf16[16,3,128,128]{3,2,1,0:T(8,128)(2,1)} %param.9) | copy-start | bytes 4718596
  0.6 14.8 %copy-start.1 = (f32[4,16,16,128]{3,2,1,0:T(8,128)S(1)}, f32[4,16,16,128]{3,2,1,0:T(8,128)}, u32[]{:S(2)}) copy-start(f32[4,16,16,128]{3,2,1,0:T(8,128)} %param.12) | copy-start | bytes 1572868
  2.3 11.8 %all-to-all-start = ((bf16[8,3,4,128]{3,2,1,0:T(4,128)(2,1)}), bf16[8,3,4,128]{3,2,1,0:T(4,128)(2,1)S(1)}, u32[]{:S(2)}, u32[]{:S(2)}) async-start(bf16[8,3,4,128]{3,2,1,0:T(4,128)(2,1)} %copy.19), calls=%async_computation | async-start | bytes 49152 | tf_op jit(solution)/shard_map/all_to_all | solution.py:181
  15.6 6.1 %collective-permute-start = (f32[69,3,128]{2,1,0:T(4,128)S(1)}, f32[69,3,128]{2,1,0:T(4,128)S(1)}, u32[]{:S(2)}, u32[]{:S(2)}) collective-permute-start(f32[69,3,128]{2,1,0:T(4,128)S(1)} %get-tuple-element.5), channel_id=1, source_target_pairs={{4,0},{8,4},{12,8},{16,12},{20,16},{24,20},{28,24},{5,1},{9,5},{13... | collective-permute-start | bytes 317960 | tf_op jit(solution)/shard_map/ppermute | solution.py:152
  17.1 7.5 %collective-permute-start.1 = (f32[69,3,128]{2,1,0:T(4,128)S(1)}, f32[69,3,128]{2,1,0:T(4,128)S(1)}, u32[]{:S(2)}, u32[]{:S(2)}) collective-permute-start(f32[69,3,128]{2,1,0:T(4,128)S(1)} %get-tuple-element.4), channel_id=1, source_target_pairs={{0,4},{4,8},{8,12},{12,16},{16,20},{20,24},{24,28},{1,5},{5,9},{9,... | collective-permute-start | bytes 317960 | tf_op jit(solution)/shard_map/ppermute | solution.py:151
  21.7 16.2 %copy-start.2 = (f32[69,3,128]{2,1,0:T(4,128)}, f32[69,3,128]{2,1,0:T(4,128)S(1)}, u32[]{:S(2)}) copy-start(f32[69,3,128]{2,1,0:T(4,128)S(1)} %collective-permute-done.high_ref) | copy-start | bytes 317956
  24.6 13.3 %copy-start.3 = (f32[69,3,128]{2,1,0:T(4,128)}, f32[69,3,128]{2,1,0:T(4,128)S(1)}, u32[]{:S(2)}) copy-start(f32[69,3,128]{2,1,0:T(4,128)S(1)} %collective-permute-done.1.low_ref) | copy-start | bytes 317956
  25.1 11.5 %collective-permute-start.3 = (f32[69,24,3]{0,1,2:T(8,128)S(1)}, f32[69,24,3]{0,1,2:T(8,128)S(1)}, u32[]{:S(2)}, u32[]{:S(2)}) collective-permute-start(f32[69,24,3]{0,1,2:T(8,128)S(1)} %get-tuple-element.10), channel_id=1, source_target_pairs={{0,1},{1,2},{2,3},{4,5},{5,6},{6,7},{8,9},{9,10},{10,11},{12,13},{... | collective-permute-start | bytes 59624 | tf_op jit(solution)/shard_map/ppermute | solution.py:205
  30.0 5.3 %collective-permute-start.2 = (f32[69,24,3]{0,1,2:T(8,128)S(1)}, f32[69,24,3]{0,1,2:T(8,128)S(1)}, u32[]{:S(2)}, u32[]{:S(2)}) collective-permute-start(f32[69,24,3]{0,1,2:T(8,128)S(1)} %get-tuple-element.11), channel_id=1, source_target_pairs={{1,0},{2,1},{3,2},{5,4},{6,5},{7,6},{9,8},{10,9},{11,10},{13,12},{... | collective-permute-start | bytes 59624 | tf_op jit(solution)/shard_map/ppermute | solution.py:206
  52.6 1.1 %copy-start.4 = (s32[16,3]{0,1:T(4,128)S(1)}, s32[16,3]{0,1:T(4,128)}, u32[]{:S(2)}) copy-start(s32[16,3]{0,1:T(4,128)} %param.10) | copy-start | bytes 580
  52.6 10.9 %copy-start.5 = (s32[8,3]{0,1:T(4,128)S(1)}, s32[8,3]{0,1:T(4,128)}, u32[]{:S(2)}) copy-start(s32[8,3]{0,1:T(4,128)} %param.11) | copy-start | bytes 292

commit v7 on v6

--- a/solution.py
+++ b/solution.py
@@ -19,31 +19,21 @@
 
 def stencil_kernel(
     diff_ref, cor_ref, state_ref, aux_ref, high_ref, low_ref, north_ref, south_ref,
-    out_ref, source, first, second, x_pad, y_pad,
+    out_ref, source, first, second,
 ):
     fields, levels, rows, lanes = out_ref.shape
     channels = fields * levels
     tall, wide = source.shape[1], source.shape[2]
     width = high_ref.shape[1]
-    x_pad[...] = jnp.zeros(x_pad.shape, jnp.float32)
-    y_pad[...] = jnp.zeros(y_pad.shape, jnp.float32)
-    row_line = lax.broadcasted_iota(jnp.int32, (tall - rows, lanes), 0)
-    lane_line = lax.broadcasted_iota(jnp.int32, (tall, wide - lanes), 1)
 
     def assemble(ch, inner):
         source[ch, :rows, :lanes] = inner
-        x_pad[0, :width] = high_ref[ch]
-        x_pad[1, :width] = low_ref[ch]
-        east_west = jnp.where(
-            row_line < width, x_pad[0], pltpu.roll(x_pad[1], tall - rows - width, 0)
-        )
-        source[ch, rows:, :lanes] = east_west
-        y_pad[0, :, :width] = north_ref[ch]
-        y_pad[1, :, :width] = south_ref[ch]
-        north_south = jnp.where(
-            lane_line < width, y_pad[0], pltpu.roll(y_pad[1], wide - lanes - width, 1)
-        )
-        source[ch, :, lanes:] = north_south
+        source[ch, rows:, :] = jnp.zeros((tall - rows, wide), jnp.float32)
+        source[ch, :rows, lanes:] = jnp.zeros((rows, wide - lanes), jnp.float32)
+        source[ch, rows : rows + width, :lanes] = high_ref[ch]
+        source[ch, tall - width :, :lanes] = low_ref[ch]
+        source[ch, :, lanes : lanes + width] = north_ref[ch]
+        source[ch, :, wide - width :] = south_ref[ch]
 
     def assemble_state(ch, carry):
         assemble(ch, state_ref[ch])
@@ -53,8 +43,8 @@
         assemble(channels + index, aux_ref[index])
         return carry
 
-    lax.fori_loop(0, channels, assemble_state, 0)
-    lax.fori_loop(0, aux_ref.shape[0], assemble_aux, 0)
+    lax.fori_loop(0, channels, assemble_state, 0, unroll=4)
+    lax.fori_loop(0, aux_ref.shape[0], assemble_aux, 0, unroll=True)
 
     def aux(index):
         return source[channels + index]
@@ -137,8 +127,6 @@
             pltpu.VMEM((channels, tall, wide), jnp.float32),
             pltpu.VMEM((state.shape[0], tall, wide), jnp.float32),
             pltpu.VMEM((state.shape[0], tall, wide), jnp.float32),
-            pltpu.VMEM((2, tall - rows, lanes), jnp.float32),
-            pltpu.VMEM((2, tall, wide - lanes), jnp.float32),
         ],
     )(diffusivity, coriolis, state, aux, high, low, north, south)
 

time: 64.8 us -> 60.7 us (0.937)
  Pallas kernels: 14.6 us -> 10.6 us
    pallas_call x1, Pallas kernels: 14.6 us -> 10.6 us  [run_steps(): pl.pallas_call(stencil_kernel, out_shape=jax.ShapeDtypeStruct(out_shape,...]
  transfers between devices with their start and end apart: 5 -> 5, of which waited for: 3 -> 3; matrix products, arithmetic and copies ran while one was open for 8% -> 9% of each run, Pallas kernels for 0% -> 0%
where the time goes in v7:
time: 60.7 us; the launch traced here: 60.2 us
  starting transfers between devices  18.5 us (30%)
  Pallas kernels  10.6 us (17%)
  blocking collectives  9.45 us (16%)
  waiting for transfers between devices  8.51 us (14%)
  local copies, waits for them, and re-layouts  6.49 us (11%)
  matrix products  3.2 us (5%)
  other arithmetic  2.73 us (4%)
  between operations  0.75 us (1%)
    pallas_call x1, Pallas kernels, run_steps(): pl.pallas_call(stencil_kernel, out_shape=jax.ShapeDtypeStruct(out_shape,...  10.6 us
    all_to_all x1, blocking collectives, per_device(): returned = lax.all_to_all(per_slot, 'ox', 0, 0, tiled=True)  9.45 us
    all_to_all x1, starting transfers between devices, per_device(): incoming = lax.all_to_all(outgoing, 'ox', 0, 0, tiled=True)  6.35 us
    ppermute x1, starting transfers between devices, per_device(): south = lax.ppermute(south_edge, 'oy', forward)  4.93 us
    ppermute x1, starting transfers between devices, shifted(): lax.ppermute(lax.slice_in_dim(block, size - width, None, axis=dim), axis,...  3.99 us
    all_to_all x1, waiting for transfers between devices, per_device(): incoming = lax.all_to_all(outgoing, 'ox', 0, 0, tiled=True)  3.25 us
    ppermute x1, waiting for transfers between devices, per_device(): north = lax.ppermute(north_edge, 'oy', backward)  2.72 us
    ppermute x1, waiting for transfers between devices, shifted(): lax.ppermute(lax.slice_in_dim(block, size - width, None, axis=dim), axis,...  2.53 us
  transfers between devices with their start and end apart: 5, of which 3 were waited for; matrix products, arithmetic and copies ran while one was open for 9% of the time, Pallas kernels for 0%

profile of v7, /device:TPU:1, one launch (start us, length us, event | category | flops | bytes accessed | tf_op | source)
XLA Modules:
  0.0 60.2 jit_solution(3274365148207377403)
XLA Ops:
  0.6 0.0 copy-start
  0.6 0.0 copy-start.1
  0.7 1.1 %convolution_convert_fusion = bf16[8,3,4,128]{3,0,2,1:T(8,128)(2,1)S(1)} fusion(bf16[4,10,128]{2,0,1:T(4,128)(2,1)} %param.8, s32[8,3]{0,1:T(4,128)} %param.11), kind=kOutput, calls=%fused_computation.1 | convolution fusion | flops 258288 | bytes 34912 | tf_op jit(solution)/shard_map/isb,fba->isfa/dot_general | solution.py:166
  1.7 0.6 %copy.19 = bf16[8,3,4,128]{3,2,1,0:T(4,128)(2,1)} copy(bf16[8,3,4,128]{3,0,2,1:T(8,128)(2,1)S(1)} %convolution_convert_fusion) | data formatting | bytes 49152 | tf_op jit(solution)/shard_map/convert_element_type | solution.py:168
  2.3 6.4 %all-to-all-start = ((bf16[8,3,4,128]{3,2,1,0:T(4,128)(2,1)}), bf16[8,3,4,128]{3,2,1,0:T(4,128)(2,1)S(1)}, u32[]{:S(2)}, u32[]{:S(2)}) async-start(bf16[8,3,4,128]{3,2,1,0:T(4,128)(2,1)} %copy.19), calls=%async_computation | async-start | bytes 49152 | tf_op jit(solution)/shard_map/all_to_all | solution.py:169
  8.7 0.7 %compare_select_fusion.1 = s32[16,3]{0,1:T(4,128)S(1)} fusion(s32[16,3]{0,1:T(4,128)} %param.10), kind=kLoop, calls=%fused_computation.26 | loop fusion | flops 144 | bytes 384 | tf_op jit(solution)/shard_map/select_n | solution.py:171
  9.4 0.1 copy.20
  9.5 0.1 reshape.58
  9.6 0.7 %convert_bitcast_fusion = f32[1,16,128]{2,1,0:T(8,128)S(1)} fusion(s32[16,128]{1,0:T(8,128)} %param.13), kind=kLoop, calls=%fused_computation.22 | loop fusion | flops 2048 | bytes 16384 | tf_op jit(solution)/shard_map/broadcast_in_dim | solution.py:178
  10.3 0.6 fusion.18.cor_ref
  10.8 0.1 pad.6.clone
  10.9 3.3 %all-to-all-done = bf16[8,3,4,128]{3,2,1,0:T(4,128)(2,1)S(1)} async-done(((bf16[8,3,4,128]{3,2,1,0:T(4,128)(2,1)}), bf16[8,3,4,128]{3,2,1,0:T(4,128)(2,1)S(1)}, u32[]{:S(2)}, u32[]{:S(2)}) %all-to-all-start) | async-done | bytes 24608 | tf_op jit(solution)/shard_map/all_to_all | solution.py:169
  14.2 0.6 %gather_fusion = bf16[48,4,128]{2,1,0:T(4,128)(2,1)S(1)} fusion(bf16[24,4,128]{2,1,0:T(4,128)(2,1)S(1)} %bitcast.37, s32[1024]{0:T(1024)S(1)} %pad_clamp_fusion), kind=kCustom, calls=%fused_computation | custom fusion | bytes 98496 | tf_op jit(solution)/shard_map/gather | solution.py:171
  14.8 0.0 copy-done
  14.8 0.6 %convolution_bitcast_fusion = f32[16,4,128]{2,1,0:T(4,128)S(1)} fusion(bf16[16,3,4,128]{3,2,1,0:T(4,128)(2,1)S(1)} %bitcast.38, bf16[16,3,128,128]{3,2,1,0:T(8,128)(2,1)S(1)} %copy-done), kind=kOutput, calls=%fused_computation.2 | convolution fusion | flops 6291456 | bytes 1654784 | tf_op jit(solution)/shard_map/tkfa,tkra->ftr/dot_general | solution.py:172
  15.5 0.0 copy-done.1
  15.5 0.1 pad_maximum_fusion
  15.5 0.1 fusion.20
  15.6 1.3 %collective-permute-start = (f32[69,3,128]{2,1,0:T(4,128)S(1)}, f32[69,3,128]{2,1,0:T(4,128)S(1)}, u32[]{:S(2)}, u32[]{:S(2)}) collective-permute-start(f32[69,3,128]{2,1,0:T(4,128)S(1)} %get-tuple-element.5), channel_id=1, source_target_pairs={{4,0},{8,4},{12,8},{16,12},{20,16},{24,20},{28,24},{5,1},{9,5},{13... | collective-permute-start | bytes 317960 | tf_op jit(solution)/shard_map/ppermute | solution.py:140
  16.9 0.2 fusion.19
  17.1 4.0 %collective-permute-start.1 = (f32[69,3,128]{2,1,0:T(4,128)S(1)}, f32[69,3,128]{2,1,0:T(4,128)S(1)}, u32[]{:S(2)}, u32[]{:S(2)}) collective-permute-start(f32[69,3,128]{2,1,0:T(4,128)S(1)} %get-tuple-element.4), channel_id=1, source_target_pairs={{0,4},{4,8},{8,12},{12,16},{16,20},{20,24},{24,28},{1,5},{5,9},{9,... | collective-permute-start | bytes 317960 | tf_op jit(solution)/shard_map/ppermute | solution.py:139
  21.1 0.3 copy.25
  21.4 0.3 copy.22
  21.7 0.0 collective-permute-done.high_ref
  21.7 0.1 fusion.21
  21.8 0.1 copy.26
  22.0 0.1 copy.23
  22.1 2.5 %collective-permute-done.1.low_ref = f32[69,3,128]{2,1,0:T(4,128)S(1)} collective-permute-done((f32[69,3,128]{2,1,0:T(4,128)S(1)}, f32[69,3,128]{2,1,0:T(4,128)S(1)}, u32[]{:S(2)}, u32[]{:S(2)}) %collective-permute-start.1) | collective-permute-done | bytes 106016 | tf_op jit(solution)/shard_map/ppermute | solution.py:139
  24.6 0.1 fusion.22
  24.7 0.1 copy.27
  24.9 0.1 copy.24
  25.0 0.1 pad_maximum_fusion.3
  25.1 4.9 %collective-permute-start.3 = (f32[69,24,3]{0,1,2:T(8,128)S(1)}, f32[69,24,3]{0,1,2:T(8,128)S(1)}, u32[]{:S(2)}, u32[]{:S(2)}) collective-permute-start(f32[69,24,3]{0,1,2:T(8,128)S(1)} %get-tuple-element.10), channel_id=1, source_target_pairs={{0,1},{1,2},{2,3},{4,5},{5,6},{6,7},{8,9},{9,10},{10,11},{12,13},{... | collective-permute-start | bytes 59624 | tf_op jit(solution)/shard_map/ppermute | solution.py:193
  30.0 1.9 %collective-permute-start.2 = (f32[69,24,3]{0,1,2:T(8,128)S(1)}, f32[69,24,3]{0,1,2:T(8,128)S(1)}, u32[]{:S(2)}, u32[]{:S(2)}) collective-permute-start(f32[69,24,3]{0,1,2:T(8,128)S(1)} %get-tuple-element.11), channel_id=1, source_target_pairs={{1,0},{2,1},{3,2},{5,4},{6,5},{7,6},{9,8},{10,9},{11,10},{13,12},{... | collective-permute-start | bytes 59624 | tf_op jit(solution)/shard_map/ppermute | solution.py:194
  31.9 0.6 %pad_maximum_fusion.1.aux_ref = f32[5,16,128]{2,1,0:T(8,128)} fusion(f32[1,16,128]{2,1,0:T(8,128)S(1)} %convert_bitcast_fusion, f32[4,16,128]{2,1,0:T(8,128)S(1)} %bitcast.36), kind=kLoop, calls=%fused_computation.6 | loop fusion | flops 10240 | bytes 81920 | tf_op jit(solution)/shard_map/concatenate | solution.py:178
  32.6 2.7 %collective-permute-done.2 = f32[69,24,3]{0,1,2:T(8,128)S(1)} collective-permute-done((f32[69,24,3]{0,1,2:T(8,128)S(1)}, f32[69,24,3]{0,1,2:T(8,128)S(1)}, u32[]{:S(2)}, u32[]{:S(2)}) %collective-permute-start.2) | collective-permute-done | bytes 19904 | tf_op jit(solution)/shard_map/ppermute | solution.py:194
  35.3 1.3 %copy.28.north_ref = f32[69,24,3]{2,1,0:T(8,128)} copy(f32[69,24,3]{0,1,2:T(8,128)S(1)} %collective-permute-done.2) | data formatting | bytes 39744 | tf_op jit(solution)/shard_map/ppermute | solution.py:194
  36.6 0.0 collective-permute-done.3
  36.6 1.3 %copy.29.south_ref = f32[69,24,3]{2,1,0:T(8,128)} copy(f32[69,24,3]{0,1,2:T(8,128)S(1)} %collective-permute-done.3) | data formatting | bytes 39744 | tf_op jit(solution)/shard_map/ppermute | solution.py:193
  37.9 0.0 copy-done.2
  37.9 10.6 %shard_map.86 = f32[4,16,16,128]{3,2,1,0:T(8,128)} custom-call(f32[16]{0:T(128)} %diff_ref.1, f32[1,256]{1,0:T(1,128)} %fusion.18.cor_ref, f32[64,16,128]{2,1,0:T(8,128)} %bitcast.33, f32[5,16,128]{2,1,0:T(8,128)} %pad_maximum_fusion.1.aux_ref, f32[69,3,128]{2,1,0:T(4,128)} %copy-done.2, f32[69,3,128]{2,1,0:T(4,128)} %copy-done.3, ...), custom_call_target="tpu_custom_call" | custom-call | tf_op jit(solution)/shard_map/pallas_call | solution.py:121
  48.5 0.7 %fusion.12 = bf16[16,128,1,1]{1,0,2,3:T(8,128)(2,1)S(1)} fusion(f32[4,16,16,128]{3,2,1,0:T(8,128)} %shard_map.86), kind=kLoop, calls=%fused_computation.27 | loop fusion | bytes 8192 | tf_op jit(solution)/shard_map/convert_element_type | solution.py:200
  49.2 0.4 fusion.8
  49.6 0.0 copy-done.4
  49.6 0.3 convolution_bitcast_fusion.1
  49.9 9.5 %all_to_all.10 = f32[8,3,128]{2,1,0:T(4,128)S(1)} all-to-all(f32[8,3,128]{2,1,0:T(4,128)S(1)} %reshape.55), channel_id=1, replica_groups=mesh['ox'=8,'oy'=4] {'ox'}, dimensions={0} | all-to-all | bytes 24576 | tf_op jit(solution)/shard_map/all_to_all | solution.py:206
  59.4 0.0 copy-done.5
  59.4 0.9 %convolution_bitcast_fusion.2 = f32[10,128]{1,0:T(8,128)} fusion(f32[8,3,128]{2,1,0:T(4,128)S(1)} %all_to_all.10, s32[8,3]{0,1:T(4,128)S(1)} %copy-done.5), kind=kOutput, calls=%fused_computation.4 | convolution fusion | flops 368880 | bytes 17504 | tf_op jit(solution)/shard_map/isb,isa->ba/dot_general | solution.py:207
  (9 shorter events, 0.0 us)
Async XLA Ops:
  0.6 14.2 %copy-start = (bf16[16,3,128,128]{3,2,1,0:T(8,128)(2,1)S(1)}, bf16[16,3,128,128]{3,2,1,0:T(8,128)(2,1)}, u32[]{:S(2)}) copy-start(bf16[16,3,128,128]{3,2,1,0:T(8,128)(2,1)} %param.9) | copy-start | bytes 4718596
  0.6 14.8 %copy-start.1 = (f32[4,16,16,128]{3,2,1,0:T(8,128)S(1)}, f32[4,16,16,128]{3,2,1,0:T(8,128)}, u32[]{:S(2)}) copy-start(f32[4,16,16,128]{3,2,1,0:T(8,128)} %param.12) | copy-start | bytes 1572868
  2.3 11.8 %all-to-all-start = ((bf16[8,3,4,128]{3,2,1,0:T(4,128)(2,1)}), bf16[8,3,4,128]{3,2,1,0:T(4,128)(2,1)S(1)}, u32[]{:S(2)}, u32[]{:S(2)}) async-start(bf16[8,3,4,128]{3,2,1,0:T(4,128)(2,1)} %copy.19), calls=%async_computation | async-start | bytes 49152 | tf_op jit(solution)/shard_map/all_to_all | solution.py:169
  15.6 6.1 %collective-permute-start = (f32[69,3,128]{2,1,0:T(4,128)S(1)}, f32[69,3,128]{2,1,0:T(4,128)S(1)}, u32[]{:S(2)}, u32[]{:S(2)}) collective-permute-start(f32[69,3,128]{2,1,0:T(4,128)S(1)} %get-tuple-element.5), channel_id=1, source_target_pairs={{4,0},{8,4},{12,8},{16,12},{20,16},{24,20},{28,24},{5,1},{9,5},{13... | collective-permute-start | bytes 317960 | tf_op jit(solution)/shard_map/ppermute | solution.py:140
  17.1 7.5 %collective-permute-start.1 = (f32[69,3,128]{2,1,0:T(4,128)S(1)}, f32[69,3,128]{2,1,0:T(4,128)S(1)}, u32[]{:S(2)}, u32[]{:S(2)}) collective-permute-start(f32[69,3,128]{2,1,0:T(4,128)S(1)} %get-tuple-element.4), channel_id=1, source_target_pairs={{0,4},{4,8},{8,12},{12,16},{16,20},{20,24},{24,28},{1,5},{5,9},{9,... | collective-permute-start | bytes 317960 | tf_op jit(solution)/shard_map/ppermute | solution.py:139
  21.7 16.2 %copy-start.2 = (f32[69,3,128]{2,1,0:T(4,128)}, f32[69,3,128]{2,1,0:T(4,128)S(1)}, u32[]{:S(2)}) copy-start(f32[69,3,128]{2,1,0:T(4,128)S(1)} %collective-permute-done.high_ref) | copy-start | bytes 317956
  24.6 13.3 %copy-start.3 = (f32[69,3,128]{2,1,0:T(4,128)}, f32[69,3,128]{2,1,0:T(4,128)S(1)}, u32[]{:S(2)}) copy-start(f32[69,3,128]{2,1,0:T(4,128)S(1)} %collective-permute-done.1.low_ref) | copy-start | bytes 317956
  25.1 11.5 %collective-permute-start.3 = (f32[69,24,3]{0,1,2:T(8,128)S(1)}, f32[69,24,3]{0,1,2:T(8,128)S(1)}, u32[]{:S(2)}, u32[]{:S(2)}) collective-permute-start(f32[69,24,3]{0,1,2:T(8,128)S(1)} %get-tuple-element.10), channel_id=1, source_target_pairs={{0,1},{1,2},{2,3},{4,5},{5,6},{6,7},{8,9},{9,10},{10,11},{12,13},{... | collective-permute-start | bytes 59624 | tf_op jit(solution)/shard_map/ppermute | solution.py:193
  30.0 5.3 %collective-permute-start.2 = (f32[69,24,3]{0,1,2:T(8,128)S(1)}, f32[69,24,3]{0,1,2:T(8,128)S(1)}, u32[]{:S(2)}, u32[]{:S(2)}) collective-permute-start(f32[69,24,3]{0,1,2:T(8,128)S(1)} %get-tuple-element.11), channel_id=1, source_target_pairs={{1,0},{2,1},{3,2},{5,4},{6,5},{7,6},{9,8},{10,9},{11,10},{13,12},{... | collective-permute-start | bytes 59624 | tf_op jit(solution)/shard_map/ppermute | solution.py:194
  48.5 1.1 %copy-start.4 = (s32[16,3]{0,1:T(4,128)S(1)}, s32[16,3]{0,1:T(4,128)}, u32[]{:S(2)}) copy-start(s32[16,3]{0,1:T(4,128)} %param.10) | copy-start | bytes 580
  48.5 10.9 %copy-start.5 = (s32[8,3]{0,1:T(4,128)S(1)}, s32[8,3]{0,1:T(4,128)}, u32[]{:S(2)}) copy-start(s32[8,3]{0,1:T(4,128)} %param.11) | copy-start | bytes 292

commit v8 on v7

--- a/solution.py
+++ b/solution.py
@@ -49,7 +49,10 @@
     def aux(index):
         return source[channels + index]
 
-    def one_step(read, write):
+    def one_step(read, write, last):
+        def crop(value):
+            return value[:rows, :lanes] if last else value
+
         def level(l, cum):
             up = jnp.maximum(l - 1, 0)
             down = jnp.minimum(l + 1, levels - 1)
@@ -57,31 +60,32 @@
             density = haline_coef * here[3] - thermal_coef * here[2]
             cum = cum + density
             pressure = cum - 0.5 * density
-            zonal = here[0]
-            meridional = here[1]
+            zonal = crop(here[0])
+            meridional = crop(here[1])
             top = jnp.where(l == 0, forcing_coef, 0.0)
             diff = diff_ref[l]
-            coriolis = cor_ref[...]
+            coriolis = crop(jnp.broadcast_to(cor_ref[...], (tall, wide)))
             for f in range(fields):
-                center = here[f]
-                east = pltpu.roll(center, tall - 1, 0)
-                west = pltpu.roll(center, 1, 0)
-                north = pltpu.roll(center, wide - 1, 1)
-                south = pltpu.roll(center, 1, 1)
+                whole = here[f]
+                center = crop(whole)
+                east = crop(pltpu.roll(whole, tall - 1, 0))
+                west = crop(pltpu.roll(whole, 1, 0))
+                north = crop(pltpu.roll(whole, wide - 1, 1))
+                south = crop(pltpu.roll(whole, 1, 1))
                 advection = -advect_coef * 0.5 * (zonal * (east - west) + meridional * (north - south))
                 laplace = diff * (east + west + north + south - 4.0 * center)
                 mixing = vertical_coef * (
-                    read(f * levels + up) + read(f * levels + down) - 2.0 * center
+                    crop(read(f * levels + up)) + crop(read(f * levels + down)) - 2.0 * center
                 )
                 total = advection + laplace + mixing
                 if f == 0:
-                    grad = pltpu.roll(pressure, tall - 1, 0) - pltpu.roll(pressure, 1, 0)
+                    grad = crop(pltpu.roll(pressure, tall - 1, 0)) - crop(pltpu.roll(pressure, 1, 0))
                     total = total + (coriolis * meridional - pressure_coef * 0.5 * grad)
                 if f == 1:
-                    grad = pltpu.roll(pressure, wide - 1, 1) - pltpu.roll(pressure, 1, 1)
+                    grad = crop(pltpu.roll(pressure, wide - 1, 1)) - crop(pltpu.roll(pressure, 1, 1))
                     total = total + (-coriolis * zonal - pressure_coef * 0.5 * grad)
-                total = total + top * aux(f)
-                write(f, l, center + aux(fields) * total)
+                total = total + top * crop(aux(f))
+                write(f, l, center + crop(aux(fields)) * total)
             return cum
 
         lax.fori_loop(0, levels, level, jnp.zeros((tall, wide), jnp.float32))
@@ -102,13 +106,13 @@
         second[f * levels + l] = value
 
     def write_out(f, l, value):
-        out_ref[f, l] = value[:rows, :lanes]
+        out_ref[f, l] = value
 
     writers = [write_first, write_second]
     for repeat in range(STEPS):
         write = write_out if repeat == STEPS - 1 else writers[repeat % 2]
         read = read_src if repeat == 0 else (read_first if repeat % 2 == 1 else read_second)
-        one_step(read, write)
+        one_step(read, write, repeat == STEPS - 1)
 
 
 def run_steps(state, aux, high, low, north, south, coriolis, diffusivity, out_shape):

time: 60.7 us -> 60.7 us (level)
  no operation moved by 1% of the time
where the time goes in v8:
time: 60.7 us; the launch traced here: 60.2 us
  starting transfers between devices  18.5 us (30%)
  Pallas kernels  10.6 us (17%)
  blocking collectives  9.45 us (16%)
  waiting for transfers between devices  8.51 us (14%)
  local copies, waits for them, and re-layouts  6.49 us (11%)
  matrix products  3.2 us (5%)
  other arithmetic  2.73 us (4%)
  between operations  0.75 us (1%)
    pallas_call x1, Pallas kernels, run_steps(): pl.pallas_call(stencil_kernel, out_shape=jax.ShapeDtypeStruct(out_shape,...  10.6 us
    all_to_all x1, blocking collectives, per_device(): returned = lax.all_to_all(per_slot, 'ox', 0, 0, tiled=True)  9.45 us
    all_to_all x1, starting transfers between devices, per_device(): incoming = lax.all_to_all(outgoing, 'ox', 0, 0, tiled=True)  6.35 us
    ppermute x1, starting transfers between devices, per_device(): south = lax.ppermute(south_edge, 'oy', forward)  4.94 us
    ppermute x1, starting transfers between devices, shifted(): lax.ppermute(lax.slice_in_dim(block, size - width, None, axis=dim), axis,...  3.99 us
    all_to_all x1, waiting for transfers between devices, per_device(): incoming = lax.all_to_all(outgoing, 'ox', 0, 0, tiled=True)  3.25 us
    ppermute x1, waiting for transfers between devices, per_device(): north = lax.ppermute(north_edge, 'oy', backward)  2.72 us
    ppermute x1, waiting for transfers between devices, shifted(): lax.ppermute(lax.slice_in_dim(block, size - width, None, axis=dim), axis,...  2.53 us
  transfers between devices with their start and end apart: 5, of which 3 were waited for; matrix products, arithmetic and copies ran while one was open for 9% of the time, Pallas kernels for 0%

profile of v8, /device:TPU:1, one launch (start us, length us, event | category | flops | bytes accessed | tf_op | source)
XLA Modules:
  0.0 60.2 jit_solution(17090060476773642023)
XLA Ops:
  0.6 0.0 copy-start
  0.6 0.0 copy-start.1
  0.7 1.1 %convolution_convert_fusion = bf16[8,3,4,128]{3,0,2,1:T(8,128)(2,1)S(1)} fusion(bf16[4,10,128]{2,0,1:T(4,128)(2,1)} %param.8, s32[8,3]{0,1:T(4,128)} %param.11), kind=kOutput, calls=%fused_computation.1 | convolution fusion | flops 258288 | bytes 34912 | tf_op jit(solution)/shard_map/isb,fba->isfa/dot_general | solution.py:170
  1.7 0.6 %copy.19 = bf16[8,3,4,128]{3,2,1,0:T(4,128)(2,1)} copy(bf16[8,3,4,128]{3,0,2,1:T(8,128)(2,1)S(1)} %convolution_convert_fusion) | data formatting | bytes 49152 | tf_op jit(solution)/shard_map/convert_element_type | solution.py:172
  2.3 6.4 %all-to-all-start = ((bf16[8,3,4,128]{3,2,1,0:T(4,128)(2,1)}), bf16[8,3,4,128]{3,2,1,0:T(4,128)(2,1)S(1)}, u32[]{:S(2)}, u32[]{:S(2)}) async-start(bf16[8,3,4,128]{3,2,1,0:T(4,128)(2,1)} %copy.19), calls=%async_computation | async-start | bytes 49152 | tf_op jit(solution)/shard_map/all_to_all | solution.py:173
  8.7 0.7 %compare_select_fusion.1 = s32[16,3]{0,1:T(4,128)S(1)} fusion(s32[16,3]{0,1:T(4,128)} %param.10), kind=kLoop, calls=%fused_computation.26 | loop fusion | flops 144 | bytes 384 | tf_op jit(solution)/shard_map/select_n | solution.py:175
  9.4 0.1 copy.20
  9.5 0.1 reshape.58
  9.6 0.7 %convert_bitcast_fusion = f32[1,16,128]{2,1,0:T(8,128)S(1)} fusion(s32[16,128]{1,0:T(8,128)} %param.13), kind=kLoop, calls=%fused_computation.22 | loop fusion | flops 2048 | bytes 16384 | tf_op jit(solution)/shard_map/broadcast_in_dim | solution.py:182
  10.3 0.6 fusion.18.cor_ref
  10.8 0.1 pad.6.clone
  10.9 3.3 %all-to-all-done = bf16[8,3,4,128]{3,2,1,0:T(4,128)(2,1)S(1)} async-done(((bf16[8,3,4,128]{3,2,1,0:T(4,128)(2,1)}), bf16[8,3,4,128]{3,2,1,0:T(4,128)(2,1)S(1)}, u32[]{:S(2)}, u32[]{:S(2)}) %all-to-all-start) | async-done | bytes 24608 | tf_op jit(solution)/shard_map/all_to_all | solution.py:173
  14.2 0.6 %gather_fusion = bf16[48,4,128]{2,1,0:T(4,128)(2,1)S(1)} fusion(bf16[24,4,128]{2,1,0:T(4,128)(2,1)S(1)} %bitcast.37, s32[1024]{0:T(1024)S(1)} %pad_clamp_fusion), kind=kCustom, calls=%fused_computation | custom fusion | bytes 98496 | tf_op jit(solution)/shard_map/gather | solution.py:175
  14.8 0.0 copy-done
  14.8 0.6 %convolution_bitcast_fusion = f32[16,4,128]{2,1,0:T(4,128)S(1)} fusion(bf16[16,3,4,128]{3,2,1,0:T(4,128)(2,1)S(1)} %bitcast.38, bf16[16,3,128,128]{3,2,1,0:T(8,128)(2,1)S(1)} %copy-done), kind=kOutput, calls=%fused_computation.2 | convolution fusion | flops 6291456 | bytes 1654784 | tf_op jit(solution)/shard_map/tkfa,tkra->ftr/dot_general | solution.py:176
  15.5 0.0 copy-done.1
  15.5 0.1 pad_maximum_fusion
  15.5 0.1 fusion.20
  15.6 1.3 %collective-permute-start = (f32[69,3,128]{2,1,0:T(4,128)S(1)}, f32[69,3,128]{2,1,0:T(4,128)S(1)}, u32[]{:S(2)}, u32[]{:S(2)}) collective-permute-start(f32[69,3,128]{2,1,0:T(4,128)S(1)} %get-tuple-element.5), channel_id=1, source_target_pairs={{4,0},{8,4},{12,8},{16,12},{20,16},{24,20},{28,24},{5,1},{9,5},{13... | collective-permute-start | bytes 317960 | tf_op jit(solution)/shard_map/ppermute | solution.py:144
  16.9 0.2 fusion.19
  17.1 4.0 %collective-permute-start.1 = (f32[69,3,128]{2,1,0:T(4,128)S(1)}, f32[69,3,128]{2,1,0:T(4,128)S(1)}, u32[]{:S(2)}, u32[]{:S(2)}) collective-permute-start(f32[69,3,128]{2,1,0:T(4,128)S(1)} %get-tuple-element.4), channel_id=1, source_target_pairs={{0,4},{4,8},{8,12},{12,16},{16,20},{20,24},{24,28},{1,5},{5,9},{9,... | collective-permute-start | bytes 317960 | tf_op jit(solution)/shard_map/ppermute | solution.py:143
  21.1 0.3 copy.25
  21.4 0.3 copy.22
  21.7 0.0 collective-permute-done.high_ref
  21.7 0.1 fusion.21
  21.8 0.1 copy.26
  22.0 0.1 copy.23
  22.1 2.5 %collective-permute-done.1.low_ref = f32[69,3,128]{2,1,0:T(4,128)S(1)} collective-permute-done((f32[69,3,128]{2,1,0:T(4,128)S(1)}, f32[69,3,128]{2,1,0:T(4,128)S(1)}, u32[]{:S(2)}, u32[]{:S(2)}) %collective-permute-start.1) | collective-permute-done | bytes 106016 | tf_op jit(solution)/shard_map/ppermute | solution.py:143
  24.6 0.1 fusion.22
  24.7 0.1 copy.27
  24.9 0.1 copy.24
  25.0 0.1 pad_maximum_fusion.3
  25.1 4.9 %collective-permute-start.3 = (f32[69,24,3]{0,1,2:T(8,128)S(1)}, f32[69,24,3]{0,1,2:T(8,128)S(1)}, u32[]{:S(2)}, u32[]{:S(2)}) collective-permute-start(f32[69,24,3]{0,1,2:T(8,128)S(1)} %get-tuple-element.10), channel_id=1, source_target_pairs={{0,1},{1,2},{2,3},{4,5},{5,6},{6,7},{8,9},{9,10},{10,11},{12,13},{... | collective-permute-start | bytes 59624 | tf_op jit(solution)/shard_map/ppermute | solution.py:197
  30.0 1.9 %collective-permute-start.2 = (f32[69,24,3]{0,1,2:T(8,128)S(1)}, f32[69,24,3]{0,1,2:T(8,128)S(1)}, u32[]{:S(2)}, u32[]{:S(2)}) collective-permute-start(f32[69,24,3]{0,1,2:T(8,128)S(1)} %get-tuple-element.11), channel_id=1, source_target_pairs={{1,0},{2,1},{3,2},{5,4},{6,5},{7,6},{9,8},{10,9},{11,10},{13,12},{... | collective-permute-start | bytes 59624 | tf_op jit(solution)/shard_map/ppermute | solution.py:198
  31.9 0.6 %pad_maximum_fusion.1.aux_ref = f32[5,16,128]{2,1,0:T(8,128)} fusion(f32[1,16,128]{2,1,0:T(8,128)S(1)} %convert_bitcast_fusion, f32[4,16,128]{2,1,0:T(8,128)S(1)} %bitcast.36), kind=kLoop, calls=%fused_computation.6 | loop fusion | flops 10240 | bytes 81920 | tf_op jit(solution)/shard_map/concatenate | solution.py:182
  32.6 2.7 %collective-permute-done.2 = f32[69,24,3]{0,1,2:T(8,128)S(1)} collective-permute-done((f32[69,24,3]{0,1,2:T(8,128)S(1)}, f32[69,24,3]{0,1,2:T(8,128)S(1)}, u32[]{:S(2)}, u32[]{:S(2)}) %collective-permute-start.2) | collective-permute-done | bytes 19904 | tf_op jit(solution)/shard_map/ppermute | solution.py:198
  35.3 1.3 %copy.28.north_ref = f32[69,24,3]{2,1,0:T(8,128)} copy(f32[69,24,3]{0,1,2:T(8,128)S(1)} %collective-permute-done.2) | data formatting | bytes 39744 | tf_op jit(solution)/shard_map/ppermute | solution.py:198
  36.6 0.0 collective-permute-done.3
  36.6 1.3 %copy.29.south_ref = f32[69,24,3]{2,1,0:T(8,128)} copy(f32[69,24,3]{0,1,2:T(8,128)S(1)} %collective-permute-done.3) | data formatting | bytes 39744 | tf_op jit(solution)/shard_map/ppermute | solution.py:197
  37.9 0.0 copy-done.2
  37.9 0.0 copy-done.3
  37.9 10.6 %shard_map.86 = f32[4,16,16,128]{3,2,1,0:T(8,128)} custom-call(f32[16]{0:T(128)} %diff_ref.1, f32[1,256]{1,0:T(1,128)} %fusion.18.cor_ref, f32[64,16,128]{2,1,0:T(8,128)} %bitcast.33, f32[5,16,128]{2,1,0:T(8,128)} %pad_maximum_fusion.1.aux_ref, f32[69,3,128]{2,1,0:T(4,128)} %copy-done.2, f32[69,3,128]{2,1,0:T(4,128)} %copy-done.3, ...), custom_call_target="tpu_custom_call" | custom-call | tf_op jit(solution)/shard_map/pallas_call | solution.py:125
  48.5 0.7 %fusion.12 = bf16[16,128,1,1]{1,0,2,3:T(8,128)(2,1)S(1)} fusion(f32[4,16,16,128]{3,2,1,0:T(8,128)} %shard_map.86), kind=kLoop, calls=%fused_computation.27 | loop fusion | bytes 8192 | tf_op jit(solution)/shard_map/convert_element_type | solution.py:204
  49.2 0.4 fusion.8
  49.6 0.3 convolution_bitcast_fusion.1
  49.9 9.4 %all_to_all.10 = f32[8,3,128]{2,1,0:T(4,128)S(1)} all-to-all(f32[8,3,128]{2,1,0:T(4,128)S(1)} %reshape.55), channel_id=1, replica_groups=mesh['ox'=8,'oy'=4] {'ox'}, dimensions={0} | all-to-all | bytes 24576 | tf_op jit(solution)/shard_map/all_to_all | solution.py:210
  59.4 0.0 copy-done.5
  59.4 0.9 %convolution_bitcast_fusion.2 = f32[10,128]{1,0:T(8,128)} fusion(f32[8,3,128]{2,1,0:T(4,128)S(1)} %all_to_all.10, s32[8,3]{0,1:T(4,128)S(1)} %copy-done.5), kind=kOutput, calls=%fused_computation.4 | convolution fusion | flops 368880 | bytes 17504 | tf_op jit(solution)/shard_map/isb,isa->ba/dot_general | solution.py:211
  (9 shorter events, 0.0 us)
Async XLA Ops:
  0.6 14.2 %copy-start = (bf16[16,3,128,128]{3,2,1,0:T(8,128)(2,1)S(1)}, bf16[16,3,128,128]{3,2,1,0:T(8,128)(2,1)}, u32[]{:S(2)}) copy-start(bf16[16,3,128,128]{3,2,1,0:T(8,128)(2,1)} %param.9) | copy-start | bytes 4718596
  0.6 14.8 %copy-start.1 = (f32[4,16,16,128]{3,2,1,0:T(8,128)S(1)}, f32[4,16,16,128]{3,2,1,0:T(8,128)}, u32[]{:S(2)}) copy-start(f32[4,16,16,128]{3,2,1,0:T(8,128)} %param.12) | copy-start | bytes 1572868
  2.3 11.8 %all-to-all-start = ((bf16[8,3,4,128]{3,2,1,0:T(4,128)(2,1)}), bf16[8,3,4,128]{3,2,1,0:T(4,128)(2,1)S(1)}, u32[]{:S(2)}, u32[]{:S(2)}) async-start(bf16[8,3,4,128]{3,2,1,0:T(4,128)(2,1)} %copy.19), calls=%async_computation | async-start | bytes 49152 | tf_op jit(solution)/shard_map/all_to_all | solution.py:173
  15.6 6.1 %collective-permute-start = (f32[69,3,128]{2,1,0:T(4,128)S(1)}, f32[69,3,128]{2,1,0:T(4,128)S(1)}, u32[]{:S(2)}, u32[]{:S(2)}) collective-permute-start(f32[69,3,128]{2,1,0:T(4,128)S(1)} %get-tuple-element.5), channel_id=1, source_target_pairs={{4,0},{8,4},{12,8},{16,12},{20,16},{24,20},{28,24},{5,1},{9,5},{13... | collective-permute-start | bytes 317960 | tf_op jit(solution)/shard_map/ppermute | solution.py:144
  17.1 7.5 %collective-permute-start.1 = (f32[69,3,128]{2,1,0:T(4,128)S(1)}, f32[69,3,128]{2,1,0:T(4,128)S(1)}, u32[]{:S(2)}, u32[]{:S(2)}) collective-permute-start(f32[69,3,128]{2,1,0:T(4,128)S(1)} %get-tuple-element.4), channel_id=1, source_target_pairs={{0,4},{4,8},{8,12},{12,16},{16,20},{20,24},{24,28},{1,5},{5,9},{9,... | collective-permute-start | bytes 317960 | tf_op jit(solution)/shard_map/ppermute | solution.py:143
  21.7 16.2 %copy-start.2 = (f32[69,3,128]{2,1,0:T(4,128)}, f32[69,3,128]{2,1,0:T(4,128)S(1)}, u32[]{:S(2)}) copy-start(f32[69,3,128]{2,1,0:T(4,128)S(1)} %collective-permute-done.high_ref) | copy-start | bytes 317956
  24.6 13.3 %copy-start.3 = (f32[69,3,128]{2,1,0:T(4,128)}, f32[69,3,128]{2,1,0:T(4,128)S(1)}, u32[]{:S(2)}) copy-start(f32[69,3,128]{2,1,0:T(4,128)S(1)} %collective-permute-done.1.low_ref) | copy-start | bytes 317956
  25.1 11.5 %collective-permute-start.3 = (f32[69,24,3]{0,1,2:T(8,128)S(1)}, f32[69,24,3]{0,1,2:T(8,128)S(1)}, u32[]{:S(2)}, u32[]{:S(2)}) collective-permute-start(f32[69,24,3]{0,1,2:T(8,128)S(1)} %get-tuple-element.10), channel_id=1, source_target_pairs={{0,1},{1,2},{2,3},{4,5},{5,6},{6,7},{8,9},{9,10},{10,11},{12,13},{... | collective-permute-start | bytes 59624 | tf_op jit(solution)/shard_map/ppermute | solution.py:197
  30.0 5.3 %collective-permute-start.2 = (f32[69,24,3]{0,1,2:T(8,128)S(1)}, f32[69,24,3]{0,1,2:T(8,128)S(1)}, u32[]{:S(2)}, u32[]{:S(2)}) collective-permute-start(f32[69,24,3]{0,1,2:T(8,128)S(1)} %get-tuple-element.11), channel_id=1, source_target_pairs={{1,0},{2,1},{3,2},{5,4},{6,5},{7,6},{9,8},{10,9},{11,10},{13,12},{... | collective-permute-start | bytes 59624 | tf_op jit(solution)/shard_map/ppermute | solution.py:198
  48.5 1.1 %copy-start.4 = (s32[16,3]{0,1:T(4,128)S(1)}, s32[16,3]{0,1:T(4,128)}, u32[]{:S(2)}) copy-start(s32[16,3]{0,1:T(4,128)} %param.10) | copy-start | bytes 580
  48.5 10.9 %copy-start.5 = (s32[8,3]{0,1:T(4,128)S(1)}, s32[8,3]{0,1:T(4,128)}, u32[]{:S(2)}) copy-start(s32[8,3]{0,1:T(4,128)} %param.11) | copy-start | bytes 292

commit v9 on v8

--- a/solution.py
+++ b/solution.py
@@ -88,7 +88,7 @@
                 write(f, l, center + crop(aux(fields)) * total)
             return cum
 
-        lax.fori_loop(0, levels, level, jnp.zeros((tall, wide), jnp.float32))
+        lax.fori_loop(0, levels, level, jnp.zeros((tall, wide), jnp.float32), unroll=2)
 
     def read_src(ch):
         return source[ch]

time: 60.7 us -> 59.3 us (0.977)
  Pallas kernels: 10.6 us -> 9.19 us
    pallas_call x1, Pallas kernels: 10.6 us -> 9.19 us  [run_steps(): pl.pallas_call(stencil_kernel, out_shape=jax.ShapeDtypeStruct(out_shape,...]
where the time goes in v9:
time: 59.3 us; the launch traced here: 58.8 us
  starting transfers between devices  18.5 us (31%)
  blocking collectives  9.45 us (16%)
  Pallas kernels  9.19 us (15%)
  waiting for transfers between devices  8.51 us (14%)
  local copies, waits for them, and re-layouts  6.49 us (11%)
  matrix products  3.2 us (5%)
  other arithmetic  2.73 us (5%)
  between operations  0.75 us (1%)
    all_to_all x1, blocking collectives, per_device(): returned = lax.all_to_all(per_slot, 'ox', 0, 0, tiled=True)  9.45 us
    pallas_call x1, Pallas kernels, run_steps(): pl.pallas_call(stencil_kernel, out_shape=jax.ShapeDtypeStruct(out_shape,...  9.19 us
    all_to_all x1, starting transfers between devices, per_device(): incoming = lax.all_to_all(outgoing, 'ox', 0, 0, tiled=True)  6.35 us
    ppermute x1, starting transfers between devices, per_device(): south = lax.ppermute(south_edge, 'oy', forward)  4.94 us
    ppermute x1, starting transfers between devices, shifted(): lax.ppermute(lax.slice_in_dim(block, size - width, None, axis=dim), axis,...  3.99 us
    all_to_all x1, waiting for transfers between devices, per_device(): incoming = lax.all_to_all(outgoing, 'ox', 0, 0, tiled=True)  3.25 us
    ppermute x1, waiting for transfers between devices, per_device(): north = lax.ppermute(north_edge, 'oy', backward)  2.72 us
    ppermute x1, waiting for transfers between devices, shifted(): lax.ppermute(lax.slice_in_dim(block, size - width, None, axis=dim), axis,...  2.53 us
  transfers between devices with their start and end apart: 5, of which 3 were waited for; matrix products, arithmetic and copies ran while one was open for 9% of the time, Pallas kernels for 0%

profile of v9, /device:TPU:1, one launch (start us, length us, event | category | flops | bytes accessed | tf_op | source)
XLA Modules:
  0.0 58.8 jit_solution(16837934182338981286)
XLA Ops:
  0.6 0.0 copy-start
  0.6 0.0 copy-start.1
  0.7 1.1 %convolution_convert_fusion = bf16[8,3,4,128]{3,0,2,1:T(8,128)(2,1)S(1)} fusion(bf16[4,10,128]{2,0,1:T(4,128)(2,1)} %param.8, s32[8,3]{0,1:T(4,128)} %param.11), kind=kOutput, calls=%fused_computation.1 | convolution fusion | flops 258288 | bytes 34912 | tf_op jit(solution)/shard_map/isb,fba->isfa/dot_general | solution.py:170
  1.7 0.6 %copy.19 = bf16[8,3,4,128]{3,2,1,0:T(4,128)(2,1)} copy(bf16[8,3,4,128]{3,0,2,1:T(8,128)(2,1)S(1)} %convolution_convert_fusion) | data formatting | bytes 49152 | tf_op jit(solution)/shard_map/convert_element_type | solution.py:172
  2.3 6.4 %all-to-all-start = ((bf16[8,3,4,128]{3,2,1,0:T(4,128)(2,1)}), bf16[8,3,4,128]{3,2,1,0:T(4,128)(2,1)S(1)}, u32[]{:S(2)}, u32[]{:S(2)}) async-start(bf16[8,3,4,128]{3,2,1,0:T(4,128)(2,1)} %copy.19), calls=%async_computation | async-start | bytes 49152 | tf_op jit(solution)/shard_map/all_to_all | solution.py:173
  8.7 0.7 %compare_select_fusion.1 = s32[16,3]{0,1:T(4,128)S(1)} fusion(s32[16,3]{0,1:T(4,128)} %param.10), kind=kLoop, calls=%fused_computation.26 | loop fusion | flops 144 | bytes 384 | tf_op jit(solution)/shard_map/select_n | solution.py:175
  9.4 0.1 copy.20
  9.5 0.1 reshape.58
  9.6 0.7 %convert_bitcast_fusion = f32[1,16,128]{2,1,0:T(8,128)S(1)} fusion(s32[16,128]{1,0:T(8,128)} %param.13), kind=kLoop, calls=%fused_computation.22 | loop fusion | flops 2048 | bytes 16384 | tf_op jit(solution)/shard_map/broadcast_in_dim | solution.py:182
  10.3 0.6 fusion.18.cor_ref
  10.8 0.1 pad.6.clone
  10.9 3.3 %all-to-all-done = bf16[8,3,4,128]{3,2,1,0:T(4,128)(2,1)S(1)} async-done(((bf16[8,3,4,128]{3,2,1,0:T(4,128)(2,1)}), bf16[8,3,4,128]{3,2,1,0:T(4,128)(2,1)S(1)}, u32[]{:S(2)}, u32[]{:S(2)}) %all-to-all-start) | async-done | bytes 24608 | tf_op jit(solution)/shard_map/all_to_all | solution.py:173
  14.2 0.6 %gather_fusion = bf16[48,4,128]{2,1,0:T(4,128)(2,1)S(1)} fusion(bf16[24,4,128]{2,1,0:T(4,128)(2,1)S(1)} %bitcast.37, s32[1024]{0:T(1024)S(1)} %pad_clamp_fusion), kind=kCustom, calls=%fused_computation | custom fusion | bytes 98496 | tf_op jit(solution)/shard_map/gather | solution.py:175
  14.8 0.0 copy-done
  14.8 0.6 %convolution_bitcast_fusion = f32[16,4,128]{2,1,0:T(4,128)S(1)} fusion(bf16[16,3,4,128]{3,2,1,0:T(4,128)(2,1)S(1)} %bitcast.38, bf16[16,3,128,128]{3,2,1,0:T(8,128)(2,1)S(1)} %copy-done), kind=kOutput, calls=%fused_computation.2 | convolution fusion | flops 6291456 | bytes 1654784 | tf_op jit(solution)/shard_map/tkfa,tkra->ftr/dot_general | solution.py:176
  15.5 0.0 copy-done.1
  15.5 0.1 pad_maximum_fusion
  15.5 0.1 fusion.20
  15.6 1.3 %collective-permute-start = (f32[69,3,128]{2,1,0:T(4,128)S(1)}, f32[69,3,128]{2,1,0:T(4,128)S(1)}, u32[]{:S(2)}, u32[]{:S(2)}) collective-permute-start(f32[69,3,128]{2,1,0:T(4,128)S(1)} %get-tuple-element.5), channel_id=1, source_target_pairs={{4,0},{8,4},{12,8},{16,12},{20,16},{24,20},{28,24},{5,1},{9,5},{13... | collective-permute-start | bytes 317960 | tf_op jit(solution)/shard_map/ppermute | solution.py:144
  16.9 0.2 fusion.19
  17.1 4.0 %collective-permute-start.1 = (f32[69,3,128]{2,1,0:T(4,128)S(1)}, f32[69,3,128]{2,1,0:T(4,128)S(1)}, u32[]{:S(2)}, u32[]{:S(2)}) collective-permute-start(f32[69,3,128]{2,1,0:T(4,128)S(1)} %get-tuple-element.4), channel_id=1, source_target_pairs={{0,4},{4,8},{8,12},{12,16},{16,20},{20,24},{24,28},{1,5},{5,9},{9,... | collective-permute-start | bytes 317960 | tf_op jit(solution)/shard_map/ppermute | solution.py:143
  21.1 0.3 copy.25
  21.4 0.3 copy.22
  21.7 0.0 collective-permute-done.high_ref
  21.7 0.1 fusion.21
  21.8 0.1 copy.26
  22.0 0.1 copy.23
  22.1 2.5 %collective-permute-done.1.low_ref = f32[69,3,128]{2,1,0:T(4,128)S(1)} collective-permute-done((f32[69,3,128]{2,1,0:T(4,128)S(1)}, f32[69,3,128]{2,1,0:T(4,128)S(1)}, u32[]{:S(2)}, u32[]{:S(2)}) %collective-permute-start.1) | collective-permute-done | bytes 106016 | tf_op jit(solution)/shard_map/ppermute | solution.py:143
  24.6 0.1 fusion.22
  24.7 0.1 copy.27
  24.9 0.1 copy.24
  25.0 0.1 pad_maximum_fusion.3
  25.1 4.9 %collective-permute-start.3 = (f32[69,24,3]{0,1,2:T(8,128)S(1)}, f32[69,24,3]{0,1,2:T(8,128)S(1)}, u32[]{:S(2)}, u32[]{:S(2)}) collective-permute-start(f32[69,24,3]{0,1,2:T(8,128)S(1)} %get-tuple-element.10), channel_id=1, source_target_pairs={{0,1},{1,2},{2,3},{4,5},{5,6},{6,7},{8,9},{9,10},{10,11},{12,13},{... | collective-permute-start | bytes 59624 | tf_op jit(solution)/shard_map/ppermute | solution.py:197
  30.0 1.9 %collective-permute-start.2 = (f32[69,24,3]{0,1,2:T(8,128)S(1)}, f32[69,24,3]{0,1,2:T(8,128)S(1)}, u32[]{:S(2)}, u32[]{:S(2)}) collective-permute-start(f32[69,24,3]{0,1,2:T(8,128)S(1)} %get-tuple-element.11), channel_id=1, source_target_pairs={{1,0},{2,1},{3,2},{5,4},{6,5},{7,6},{9,8},{10,9},{11,10},{13,12},{... | collective-permute-start | bytes 59624 | tf_op jit(solution)/shard_map/ppermute | solution.py:198
  31.9 0.6 %pad_maximum_fusion.1.aux_ref = f32[5,16,128]{2,1,0:T(8,128)} fusion(f32[1,16,128]{2,1,0:T(8,128)S(1)} %convert_bitcast_fusion, f32[4,16,128]{2,1,0:T(8,128)S(1)} %bitcast.36), kind=kLoop, calls=%fused_computation.6 | loop fusion | flops 10240 | bytes 81920 | tf_op jit(solution)/shard_map/concatenate | solution.py:182
  32.6 2.7 %collective-permute-done.2 = f32[69,24,3]{0,1,2:T(8,128)S(1)} collective-permute-done((f32[69,24,3]{0,1,2:T(8,128)S(1)}, f32[69,24,3]{0,1,2:T(8,128)S(1)}, u32[]{:S(2)}, u32[]{:S(2)}) %collective-permute-start.2) | collective-permute-done | bytes 19904 | tf_op jit(solution)/shard_map/ppermute | solution.py:198
  35.3 1.3 %copy.28.north_ref = f32[69,24,3]{2,1,0:T(8,128)} copy(f32[69,24,3]{0,1,2:T(8,128)S(1)} %collective-permute-done.2) | data formatting | bytes 39744 | tf_op jit(solution)/shard_map/ppermute | solution.py:198
  36.6 0.0 collective-permute-done.3
  36.6 1.3 %copy.29.south_ref = f32[69,24,3]{2,1,0:T(8,128)} copy(f32[69,24,3]{0,1,2:T(8,128)S(1)} %collective-permute-done.3) | data formatting | bytes 39744 | tf_op jit(solution)/shard_map/ppermute | solution.py:197
  37.9 0.0 copy-done.2
  37.9 0.0 copy-done.3
  37.9 9.2 %shard_map.86 = f32[4,16,16,128]{3,2,1,0:T(8,128)} custom-call(f32[16]{0:T(128)} %diff_ref.1, f32[1,256]{1,0:T(1,128)} %fusion.18.cor_ref, f32[64,16,128]{2,1,0:T(8,128)} %bitcast.33, f32[5,16,128]{2,1,0:T(8,128)} %pad_maximum_fusion.1.aux_ref, f32[69,3,128]{2,1,0:T(4,128)} %copy-done.2, f32[69,3,128]{2,1,0:T(4,128)} %copy-done.3, ...), custom_call_target="tpu_custom_call" | custom-call | tf_op jit(solution)/shard_map/pallas_call | solution.py:125
  47.1 0.7 %fusion.12 = bf16[16,128,1,1]{1,0,2,3:T(8,128)(2,1)S(1)} fusion(f32[4,16,16,128]{3,2,1,0:T(8,128)} %shard_map.86), kind=kLoop, calls=%fused_computation.27 | loop fusion | bytes 8192 | tf_op jit(solution)/shard_map/convert_element_type | solution.py:204
  47.8 0.4 fusion.8
  48.2 0.0 copy-done.4
  48.2 0.3 convolution_bitcast_fusion.1
  48.5 9.4 %all_to_all.10 = f32[8,3,128]{2,1,0:T(4,128)S(1)} all-to-all(f32[8,3,128]{2,1,0:T(4,128)S(1)} %reshape.55), channel_id=1, replica_groups=mesh['ox'=8,'oy'=4] {'ox'}, dimensions={0} | all-to-all | bytes 24576 | tf_op jit(solution)/shard_map/all_to_all | solution.py:210
  58.0 0.9 %convolution_bitcast_fusion.2 = f32[10,128]{1,0:T(8,128)} fusion(f32[8,3,128]{2,1,0:T(4,128)S(1)} %all_to_all.10, s32[8,3]{0,1:T(4,128)S(1)} %copy-done.5), kind=kOutput, calls=%fused_computation.4 | convolution fusion | flops 368880 | bytes 17504 | tf_op jit(solution)/shard_map/isb,isa->ba/dot_general | solution.py:211
  (9 shorter events, 0.0 us)
Async XLA Ops:
  0.6 14.2 %copy-start = (bf16[16,3,128,128]{3,2,1,0:T(8,128)(2,1)S(1)}, bf16[16,3,128,128]{3,2,1,0:T(8,128)(2,1)}, u32[]{:S(2)}) copy-start(bf16[16,3,128,128]{3,2,1,0:T(8,128)(2,1)} %param.9) | copy-start | bytes 4718596
  0.6 14.8 %copy-start.1 = (f32[4,16,16,128]{3,2,1,0:T(8,128)S(1)}, f32[4,16,16,128]{3,2,1,0:T(8,128)}, u32[]{:S(2)}) copy-start(f32[4,16,16,128]{3,2,1,0:T(8,128)} %param.12) | copy-start | bytes 1572868
  2.3 11.8 %all-to-all-start = ((bf16[8,3,4,128]{3,2,1,0:T(4,128)(2,1)}), bf16[8,3,4,128]{3,2,1,0:T(4,128)(2,1)S(1)}, u32[]{:S(2)}, u32[]{:S(2)}) async-start(bf16[8,3,4,128]{3,2,1,0:T(4,128)(2,1)} %copy.19), calls=%async_computation | async-start | bytes 49152 | tf_op jit(solution)/shard_map/all_to_all | solution.py:173
  15.6 6.1 %collective-permute-start = (f32[69,3,128]{2,1,0:T(4,128)S(1)}, f32[69,3,128]{2,1,0:T(4,128)S(1)}, u32[]{:S(2)}, u32[]{:S(2)}) collective-permute-start(f32[69,3,128]{2,1,0:T(4,128)S(1)} %get-tuple-element.5), channel_id=1, source_target_pairs={{4,0},{8,4},{12,8},{16,12},{20,16},{24,20},{28,24},{5,1},{9,5},{13... | collective-permute-start | bytes 317960 | tf_op jit(solution)/shard_map/ppermute | solution.py:144
  17.1 7.5 %collective-permute-start.1 = (f32[69,3,128]{2,1,0:T(4,128)S(1)}, f32[69,3,128]{2,1,0:T(4,128)S(1)}, u32[]{:S(2)}, u32[]{:S(2)}) collective-permute-start(f32[69,3,128]{2,1,0:T(4,128)S(1)} %get-tuple-element.4), channel_id=1, source_target_pairs={{0,4},{4,8},{8,12},{12,16},{16,20},{20,24},{24,28},{1,5},{5,9},{9,... | collective-permute-start | bytes 317960 | tf_op jit(solution)/shard_map/ppermute | solution.py:143
  21.7 16.2 %copy-start.2 = (f32[69,3,128]{2,1,0:T(4,128)}, f32[69,3,128]{2,1,0:T(4,128)S(1)}, u32[]{:S(2)}) copy-start(f32[69,3,128]{2,1,0:T(4,128)S(1)} %collective-permute-done.high_ref) | copy-start | bytes 317956
  24.6 13.3 %copy-start.3 = (f32[69,3,128]{2,1,0:T(4,128)}, f32[69,3,128]{2,1,0:T(4,128)S(1)}, u32[]{:S(2)}) copy-start(f32[69,3,128]{2,1,0:T(4,128)S(1)} %collective-permute-done.1.low_ref) | copy-start | bytes 317956
  25.1 11.5 %collective-permute-start.3 = (f32[69,24,3]{0,1,2:T(8,128)S(1)}, f32[69,24,3]{0,1,2:T(8,128)S(1)}, u32[]{:S(2)}, u32[]{:S(2)}) collective-permute-start(f32[69,24,3]{0,1,2:T(8,128)S(1)} %get-tuple-element.10), channel_id=1, source_target_pairs={{0,1},{1,2},{2,3},{4,5},{5,6},{6,7},{8,9},{9,10},{10,11},{12,13},{... | collective-permute-start | bytes 59624 | tf_op jit(solution)/shard_map/ppermute | solution.py:197
  30.0 5.3 %collective-permute-start.2 = (f32[69,24,3]{0,1,2:T(8,128)S(1)}, f32[69,24,3]{0,1,2:T(8,128)S(1)}, u32[]{:S(2)}, u32[]{:S(2)}) collective-permute-start(f32[69,24,3]{0,1,2:T(8,128)S(1)} %get-tuple-element.11), channel_id=1, source_target_pairs={{1,0},{2,1},{3,2},{5,4},{6,5},{7,6},{9,8},{10,9},{11,10},{13,12},{... | collective-permute-start | bytes 59624 | tf_op jit(solution)/shard_map/ppermute | solution.py:198
  47.1 1.1 %copy-start.4 = (s32[16,3]{0,1:T(4,128)S(1)}, s32[16,3]{0,1:T(4,128)}, u32[]{:S(2)}) copy-start(s32[16,3]{0,1:T(4,128)} %param.10) | copy-start | bytes 580
  47.1 10.9 %copy-start.5 = (s32[8,3]{0,1:T(4,128)S(1)}, s32[8,3]{0,1:T(4,128)}, u32[]{:S(2)}) copy-start(s32[8,3]{0,1:T(4,128)} %param.11) | copy-start | bytes 292

commit v10 on v9

--- a/solution.py
+++ b/solution.py
@@ -88,7 +88,7 @@
                 write(f, l, center + crop(aux(fields)) * total)
             return cum
 
-        lax.fori_loop(0, levels, level, jnp.zeros((tall, wide), jnp.float32), unroll=2)
+        lax.fori_loop(0, levels, level, jnp.zeros((tall, wide), jnp.float32), unroll=4)
 
     def read_src(ch):
         return source[ch]

time: 59.3 us -> 58.8 us (level)
  no operation moved by 1% of the time
where the time goes in v10:
time: 58.8 us; the launch traced here: 58.3 us
  starting transfers between devices  18.5 us (31%)
  blocking collectives  9.45 us (16%)
  Pallas kernels  8.69 us (15%)
  waiting for transfers between devices  8.51 us (14%)
  local copies, waits for them, and re-layouts  6.49 us (11%)
  matrix products  3.2 us (5%)
  other arithmetic  2.73 us (5%)
  between operations  0.75 us (1%)
    all_to_all x1, blocking collectives, per_device(): returned = lax.all_to_all(per_slot, 'ox', 0, 0, tiled=True)  9.45 us
    pallas_call x1, Pallas kernels, run_steps(): pl.pallas_call(stencil_kernel, out_shape=jax.ShapeDtypeStruct(out_shape,...  8.69 us
    all_to_all x1, starting transfers between devices, per_device(): incoming = lax.all_to_all(outgoing, 'ox', 0, 0, tiled=True)  6.35 us
    ppermute x1, starting transfers between devices, per_device(): south = lax.ppermute(south_edge, 'oy', forward)  4.94 us
    ppermute x1, starting transfers between devices, shifted(): lax.ppermute(lax.slice_in_dim(block, size - width, None, axis=dim), axis,...  3.99 us
    all_to_all x1, waiting for transfers between devices, per_device(): incoming = lax.all_to_all(outgoing, 'ox', 0, 0, tiled=True)  3.25 us
    ppermute x1, waiting for transfers between devices, per_device(): north = lax.ppermute(north_edge, 'oy', backward)  2.72 us
    ppermute x1, waiting for transfers between devices, shifted(): lax.ppermute(lax.slice_in_dim(block, size - width, None, axis=dim), axis,...  2.53 us
  transfers between devices with their start and end apart: 5, of which 3 were waited for; matrix products, arithmetic and copies ran while one was open for 9% of the time, Pallas kernels for 0%

profile of v10, /device:TPU:1, one launch (start us, length us, event | category | flops | bytes accessed | tf_op | source)
XLA Modules:
  0.0 58.3 jit_solution(11530123117703678248)
XLA Ops:
  0.6 0.0 copy-start
  0.6 0.0 copy-start.1
  0.7 1.1 %convolution_convert_fusion = bf16[8,3,4,128]{3,0,2,1:T(8,128)(2,1)S(1)} fusion(bf16[4,10,128]{2,0,1:T(4,128)(2,1)} %param.8, s32[8,3]{0,1:T(4,128)} %param.11), kind=kOutput, calls=%fused_computation.1 | convolution fusion | flops 258288 | bytes 34912 | tf_op jit(solution)/shard_map/isb,fba->isfa/dot_general | solution.py:170
  1.7 0.6 %copy.19 = bf16[8,3,4,128]{3,2,1,0:T(4,128)(2,1)} copy(bf16[8,3,4,128]{3,0,2,1:T(8,128)(2,1)S(1)} %convolution_convert_fusion) | data formatting | bytes 49152 | tf_op jit(solution)/shard_map/convert_element_type | solution.py:172
  2.3 6.4 %all-to-all-start = ((bf16[8,3,4,128]{3,2,1,0:T(4,128)(2,1)}), bf16[8,3,4,128]{3,2,1,0:T(4,128)(2,1)S(1)}, u32[]{:S(2)}, u32[]{:S(2)}) async-start(bf16[8,3,4,128]{3,2,1,0:T(4,128)(2,1)} %copy.19), calls=%async_computation | async-start | bytes 49152 | tf_op jit(solution)/shard_map/all_to_all | solution.py:173
  8.7 0.7 %compare_select_fusion.1 = s32[16,3]{0,1:T(4,128)S(1)} fusion(s32[16,3]{0,1:T(4,128)} %param.10), kind=kLoop, calls=%fused_computation.26 | loop fusion | flops 144 | bytes 384 | tf_op jit(solution)/shard_map/select_n | solution.py:175
  9.4 0.1 copy.20
  9.5 0.1 reshape.58
  9.6 0.7 %convert_bitcast_fusion = f32[1,16,128]{2,1,0:T(8,128)S(1)} fusion(s32[16,128]{1,0:T(8,128)} %param.13), kind=kLoop, calls=%fused_computation.22 | loop fusion | flops 2048 | bytes 16384 | tf_op jit(solution)/shard_map/broadcast_in_dim | solution.py:182
  10.3 0.6 fusion.18.cor_ref
  10.8 0.1 pad.6.clone
  10.9 3.3 %all-to-all-done = bf16[8,3,4,128]{3,2,1,0:T(4,128)(2,1)S(1)} async-done(((bf16[8,3,4,128]{3,2,1,0:T(4,128)(2,1)}), bf16[8,3,4,128]{3,2,1,0:T(4,128)(2,1)S(1)}, u32[]{:S(2)}, u32[]{:S(2)}) %all-to-all-start) | async-done | bytes 24608 | tf_op jit(solution)/shard_map/all_to_all | solution.py:173
  14.2 0.6 %gather_fusion = bf16[48,4,128]{2,1,0:T(4,128)(2,1)S(1)} fusion(bf16[24,4,128]{2,1,0:T(4,128)(2,1)S(1)} %bitcast.37, s32[1024]{0:T(1024)S(1)} %pad_clamp_fusion), kind=kCustom, calls=%fused_computation | custom fusion | bytes 98496 | tf_op jit(solution)/shard_map/gather | solution.py:175
  14.8 0.0 copy-done
  14.8 0.6 %convolution_bitcast_fusion = f32[16,4,128]{2,1,0:T(4,128)S(1)} fusion(bf16[16,3,4,128]{3,2,1,0:T(4,128)(2,1)S(1)} %bitcast.38, bf16[16,3,128,128]{3,2,1,0:T(8,128)(2,1)S(1)} %copy-done), kind=kOutput, calls=%fused_computation.2 | convolution fusion | flops 6291456 | bytes 1654784 | tf_op jit(solution)/shard_map/tkfa,tkra->ftr/dot_general | solution.py:176
  15.5 0.0 copy-done.1
  15.5 0.1 pad_maximum_fusion
  15.5 0.1 fusion.20
  15.6 1.3 %collective-permute-start = (f32[69,3,128]{2,1,0:T(4,128)S(1)}, f32[69,3,128]{2,1,0:T(4,128)S(1)}, u32[]{:S(2)}, u32[]{:S(2)}) collective-permute-start(f32[69,3,128]{2,1,0:T(4,128)S(1)} %get-tuple-element.5), channel_id=1, source_target_pairs={{4,0},{8,4},{12,8},{16,12},{20,16},{24,20},{28,24},{5,1},{9,5},{13... | collective-permute-start | bytes 317960 | tf_op jit(solution)/shard_map/ppermute | solution.py:144
  16.9 0.2 fusion.19
  17.1 4.0 %collective-permute-start.1 = (f32[69,3,128]{2,1,0:T(4,128)S(1)}, f32[69,3,128]{2,1,0:T(4,128)S(1)}, u32[]{:S(2)}, u32[]{:S(2)}) collective-permute-start(f32[69,3,128]{2,1,0:T(4,128)S(1)} %get-tuple-element.4), channel_id=1, source_target_pairs={{0,4},{4,8},{8,12},{12,16},{16,20},{20,24},{24,28},{1,5},{5,9},{9,... | collective-permute-start | bytes 317960 | tf_op jit(solution)/shard_map/ppermute | solution.py:143
  21.1 0.3 copy.25
  21.4 0.3 copy.22
  21.7 0.0 collective-permute-done.high_ref
  21.7 0.1 fusion.21
  21.8 0.1 copy.26
  22.0 0.1 copy.23
  22.1 2.5 %collective-permute-done.1.low_ref = f32[69,3,128]{2,1,0:T(4,128)S(1)} collective-permute-done((f32[69,3,128]{2,1,0:T(4,128)S(1)}, f32[69,3,128]{2,1,0:T(4,128)S(1)}, u32[]{:S(2)}, u32[]{:S(2)}) %collective-permute-start.1) | collective-permute-done | bytes 106016 | tf_op jit(solution)/shard_map/ppermute | solution.py:143
  24.6 0.1 fusion.22
  24.7 0.1 copy.27
  24.9 0.1 copy.24
  25.0 0.1 pad_maximum_fusion.3
  25.1 4.9 %collective-permute-start.3 = (f32[69,24,3]{0,1,2:T(8,128)S(1)}, f32[69,24,3]{0,1,2:T(8,128)S(1)}, u32[]{:S(2)}, u32[]{:S(2)}) collective-permute-start(f32[69,24,3]{0,1,2:T(8,128)S(1)} %get-tuple-element.10), channel_id=1, source_target_pairs={{0,1},{1,2},{2,3},{4,5},{5,6},{6,7},{8,9},{9,10},{10,11},{12,13},{... | collective-permute-start | bytes 59624 | tf_op jit(solution)/shard_map/ppermute | solution.py:197
  30.0 1.9 %collective-permute-start.2 = (f32[69,24,3]{0,1,2:T(8,128)S(1)}, f32[69,24,3]{0,1,2:T(8,128)S(1)}, u32[]{:S(2)}, u32[]{:S(2)}) collective-permute-start(f32[69,24,3]{0,1,2:T(8,128)S(1)} %get-tuple-element.11), channel_id=1, source_target_pairs={{1,0},{2,1},{3,2},{5,4},{6,5},{7,6},{9,8},{10,9},{11,10},{13,12},{... | collective-permute-start | bytes 59624 | tf_op jit(solution)/shard_map/ppermute | solution.py:198
  31.9 0.6 %pad_maximum_fusion.1.aux_ref = f32[5,16,128]{2,1,0:T(8,128)} fusion(f32[1,16,128]{2,1,0:T(8,128)S(1)} %convert_bitcast_fusion, f32[4,16,128]{2,1,0:T(8,128)S(1)} %bitcast.36), kind=kLoop, calls=%fused_computation.6 | loop fusion | flops 10240 | bytes 81920 | tf_op jit(solution)/shard_map/concatenate | solution.py:182
  32.6 2.7 %collective-permute-done.2 = f32[69,24,3]{0,1,2:T(8,128)S(1)} collective-permute-done((f32[69,24,3]{0,1,2:T(8,128)S(1)}, f32[69,24,3]{0,1,2:T(8,128)S(1)}, u32[]{:S(2)}, u32[]{:S(2)}) %collective-permute-start.2) | collective-permute-done | bytes 19904 | tf_op jit(solution)/shard_map/ppermute | solution.py:198
  35.3 1.3 %copy.28.north_ref = f32[69,24,3]{2,1,0:T(8,128)} copy(f32[69,24,3]{0,1,2:T(8,128)S(1)} %collective-permute-done.2) | data formatting | bytes 39744 | tf_op jit(solution)/shard_map/ppermute | solution.py:198
  36.6 0.0 collective-permute-done.3
  36.6 1.3 %copy.29.south_ref = f32[69,24,3]{2,1,0:T(8,128)} copy(f32[69,24,3]{0,1,2:T(8,128)S(1)} %collective-permute-done.3) | data formatting | bytes 39744 | tf_op jit(solution)/shard_map/ppermute | solution.py:197
  37.9 0.0 copy-done.2
  37.9 0.0 copy-done.3
  37.9 8.7 %shard_map.86 = f32[4,16,16,128]{3,2,1,0:T(8,128)} custom-call(f32[16]{0:T(128)} %diff_ref.1, f32[1,256]{1,0:T(1,128)} %fusion.18.cor_ref, f32[64,16,128]{2,1,0:T(8,128)} %bitcast.33, f32[5,16,128]{2,1,0:T(8,128)} %pad_maximum_fusion.1.aux_ref, f32[69,3,128]{2,1,0:T(4,128)} %copy-done.2, f32[69,3,128]{2,1,0:T(4,128)} %copy-done.3, ...), custom_call_target="tpu_custom_call" | custom-call | tf_op jit(solution)/shard_map/pallas_call | solution.py:125
  46.6 0.7 %fusion.12 = bf16[16,128,1,1]{1,0,2,3:T(8,128)(2,1)S(1)} fusion(f32[4,16,16,128]{3,2,1,0:T(8,128)} %shard_map.86), kind=kLoop, calls=%fused_computation.27 | loop fusion | bytes 8192 | tf_op jit(solution)/shard_map/convert_element_type | solution.py:204
  47.3 0.4 fusion.8
  47.7 0.0 copy-done.4
  47.7 0.3 convolution_bitcast_fusion.1
  48.0 9.4 %all_to_all.10 = f32[8,3,128]{2,1,0:T(4,128)S(1)} all-to-all(f32[8,3,128]{2,1,0:T(4,128)S(1)} %reshape.55), channel_id=1, replica_groups=mesh['ox'=8,'oy'=4] {'ox'}, dimensions={0} | all-to-all | bytes 24576 | tf_op jit(solution)/shard_map/all_to_all | solution.py:210
  57.5 0.9 %convolution_bitcast_fusion.2 = f32[10,128]{1,0:T(8,128)} fusion(f32[8,3,128]{2,1,0:T(4,128)S(1)} %all_to_all.10, s32[8,3]{0,1:T(4,128)S(1)} %copy-done.5), kind=kOutput, calls=%fused_computation.4 | convolution fusion | flops 368880 | bytes 17504 | tf_op jit(solution)/shard_map/isb,isa->ba/dot_general | solution.py:211
  (9 shorter events, 0.0 us)
Async XLA Ops:
  0.6 14.2 %copy-start = (bf16[16,3,128,128]{3,2,1,0:T(8,128)(2,1)S(1)}, bf16[16,3,128,128]{3,2,1,0:T(8,128)(2,1)}, u32[]{:S(2)}) copy-start(bf16[16,3,128,128]{3,2,1,0:T(8,128)(2,1)} %param.9) | copy-start | bytes 4718596
  0.6 14.8 %copy-start.1 = (f32[4,16,16,128]{3,2,1,0:T(8,128)S(1)}, f32[4,16,16,128]{3,2,1,0:T(8,128)}, u32[]{:S(2)}) copy-start(f32[4,16,16,128]{3,2,1,0:T(8,128)} %param.12) | copy-start | bytes 1572868
  2.3 11.8 %all-to-all-start = ((bf16[8,3,4,128]{3,2,1,0:T(4,128)(2,1)}), bf16[8,3,4,128]{3,2,1,0:T(4,128)(2,1)S(1)}, u32[]{:S(2)}, u32[]{:S(2)}) async-start(bf16[8,3,4,128]{3,2,1,0:T(4,128)(2,1)} %copy.19), calls=%async_computation | async-start | bytes 49152 | tf_op jit(solution)/shard_map/all_to_all | solution.py:173
  15.6 6.1 %collective-permute-start = (f32[69,3,128]{2,1,0:T(4,128)S(1)}, f32[69,3,128]{2,1,0:T(4,128)S(1)}, u32[]{:S(2)}, u32[]{:S(2)}) collective-permute-start(f32[69,3,128]{2,1,0:T(4,128)S(1)} %get-tuple-element.5), channel_id=1, source_target_pairs={{4,0},{8,4},{12,8},{16,12},{20,16},{24,20},{28,24},{5,1},{9,5},{13... | collective-permute-start | bytes 317960 | tf_op jit(solution)/shard_map/ppermute | solution.py:144
  17.1 7.5 %collective-permute-start.1 = (f32[69,3,128]{2,1,0:T(4,128)S(1)}, f32[69,3,128]{2,1,0:T(4,128)S(1)}, u32[]{:S(2)}, u32[]{:S(2)}) collective-permute-start(f32[69,3,128]{2,1,0:T(4,128)S(1)} %get-tuple-element.4), channel_id=1, source_target_pairs={{0,4},{4,8},{8,12},{12,16},{16,20},{20,24},{24,28},{1,5},{5,9},{9,... | collective-permute-start | bytes 317960 | tf_op jit(solution)/shard_map/ppermute | solution.py:143
  21.7 16.2 %copy-start.2 = (f32[69,3,128]{2,1,0:T(4,128)}, f32[69,3,128]{2,1,0:T(4,128)S(1)}, u32[]{:S(2)}) copy-start(f32[69,3,128]{2,1,0:T(4,128)S(1)} %collective-permute-done.high_ref) | copy-start | bytes 317956
  24.6 13.3 %copy-start.3 = (f32[69,3,128]{2,1,0:T(4,128)}, f32[69,3,128]{2,1,0:T(4,128)S(1)}, u32[]{:S(2)}) copy-start(f32[69,3,128]{2,1,0:T(4,128)S(1)} %collective-permute-done.1.low_ref) | copy-start | bytes 317956
  25.1 11.5 %collective-permute-start.3 = (f32[69,24,3]{0,1,2:T(8,128)S(1)}, f32[69,24,3]{0,1,2:T(8,128)S(1)}, u32[]{:S(2)}, u32[]{:S(2)}) collective-permute-start(f32[69,24,3]{0,1,2:T(8,128)S(1)} %get-tuple-element.10), channel_id=1, source_target_pairs={{0,1},{1,2},{2,3},{4,5},{5,6},{6,7},{8,9},{9,10},{10,11},{12,13},{... | collective-permute-start | bytes 59624 | tf_op jit(solution)/shard_map/ppermute | solution.py:197
  30.0 5.3 %collective-permute-start.2 = (f32[69,24,3]{0,1,2:T(8,128)S(1)}, f32[69,24,3]{0,1,2:T(8,128)S(1)}, u32[]{:S(2)}, u32[]{:S(2)}) collective-permute-start(f32[69,24,3]{0,1,2:T(8,128)S(1)} %get-tuple-element.11), channel_id=1, source_target_pairs={{1,0},{2,1},{3,2},{5,4},{6,5},{7,6},{9,8},{10,9},{11,10},{13,12},{... | collective-permute-start | bytes 59624 | tf_op jit(solution)/shard_map/ppermute | solution.py:198
  46.6 1.1 %copy-start.4 = (s32[16,3]{0,1:T(4,128)S(1)}, s32[16,3]{0,1:T(4,128)}, u32[]{:S(2)}) copy-start(s32[16,3]{0,1:T(4,128)} %param.10) | copy-start | bytes 580
  46.6 10.8 %copy-start.5 = (s32[8,3]{0,1:T(4,128)S(1)}, s32[8,3]{0,1:T(4,128)}, u32[]{:S(2)}) copy-start(s32[8,3]{0,1:T(4,128)} %param.11) | copy-start | bytes 292

commit v11 on v10

--- a/solution.py
+++ b/solution.py
@@ -88,7 +88,7 @@
                 write(f, l, center + crop(aux(fields)) * total)
             return cum
 
-        lax.fori_loop(0, levels, level, jnp.zeros((tall, wide), jnp.float32), unroll=4)
+        lax.fori_loop(0, levels, level, jnp.zeros((tall, wide), jnp.float32), unroll=True)
 
     def read_src(ch):
         return source[ch]
@@ -167,12 +167,11 @@
     slots = owners * capacity
     block_line = jnp.arange(blocks_here, dtype=jnp.int32)
     to_block = send_blocks[:, :, None] == block_line[None, None, :]
-    outgoing = jnp.einsum(
-        "isb,fba->isfa", to_block.astype(atm_flux.dtype), atm_flux, preferred_element_type=jnp.float32
-    ).astype(atm_flux.dtype)
+    outgoing = jnp.broadcast_to(atm_flux[None], (owners,) + atm_flux.shape)
     incoming = lax.all_to_all(outgoing, "ox", 0, 0, tiled=True)
-    incoming = incoming.reshape((slots,) + incoming.shape[2:])
-    picks = incoming[tile_slots]
+    owner_of = tile_slots // capacity
+    block_of = need_blocks.reshape(-1)[tile_slots]
+    picks = incoming[owner_of, :, block_of, :]
     forcing = jnp.einsum("tkfa,tkra->ftr", picks, remap_weights, preferred_element_type=jnp.float32)
     fields, levels, rows, lat_cells = ocean_state.shape
     lat_total = lat_cells * lax.axis_size("oy")

time: 58.8 us -> 58.4 us (level)
  local copies, waits for them, and re-layouts: 6.49 us -> 9.54 us
  matrix products: 3.2 us -> 2.15 us
  waiting for transfers between devices: 8.51 us -> 7.51 us
  Pallas kernels: 8.69 us -> 7.79 us
  other arithmetic: 2.73 us -> 2.04 us
    broadcast_in_dim x1 -> x2, local copies, waits for them, and re-layouts: 0.09 us -> 1.57 us  [the longest x1 1.48 us: per_device(): outgoing = jnp.broadcast_to(atm_flux[None], (owners,) + atm_flux.shape)]
    gather x1 -> x4, local copies, waits for them, and re-layouts: 0.63 us -> 1.83 us  [the longest x3 0.94 us: per_device(): block_of = need_blocks.reshape(-1)[tile_slots]]
    dot_general x1 -> x0, matrix products: 1.05 us -> none  [per_device(): jnp.einsum('isb,fba->isfa', to_block.astype(atm_flux.dtype), atm_flux, pr...]
    all_to_all x1, waiting for transfers between devices: 3.25 us -> 2.3 us  [per_device(): incoming = lax.all_to_all(outgoing, 'ox', 0, 0, tiled=True)]
    pallas_call x1, Pallas kernels: 8.69 us -> 7.79 us  [run_steps(): pl.pallas_call(stencil_kernel, out_shape=jax.ShapeDtypeStruct(out_shape,...]
    unnamed x12 -> x15, local copies, waits for them, and re-layouts: 0.03 us -> 0.8 us
    broadcast_in_dim x1, other arithmetic: 0.7 us -> 0.01 us  [per_device(): aux = jnp.concatenate([forcing, wetness[None]], axis=0)]
    convert_element_type x1 -> x0, local copies, waits for them, and re-layouts: 0.62 us -> none  [per_device(): outgoing = jnp.einsum('isb,fba->isfa', to_block.astype(atm_flux.dtype), a...]
  transfers between devices with their start and end apart: 5 -> 5, of which waited for: 3 -> 3; matrix products, arithmetic and copies ran while one was open for 9% -> 11% of each run, Pallas kernels for 0% -> 0%
where the time goes in v11:
time: 58.4 us; the launch traced here: 57.9 us
  starting transfers between devices  18.5 us (32%)
  blocking collectives  9.59 us (16%)
  local copies, waits for them, and re-layouts  9.54 us (16%)
  Pallas kernels  7.79 us (13%)
  waiting for transfers between devices  7.51 us (13%)
  matrix products  2.15 us (4%)
  other arithmetic  2.04 us (3%)
  between operations  0.79 us (1%)
    all_to_all x1, blocking collectives, per_device(): returned = lax.all_to_all(per_slot, 'ox', 0, 0, tiled=True)  9.59 us
    pallas_call x1, Pallas kernels, run_steps(): pl.pallas_call(stencil_kernel, out_shape=jax.ShapeDtypeStruct(out_shape,...  7.79 us
    all_to_all x1, starting transfers between devices, per_device(): incoming = lax.all_to_all(outgoing, 'ox', 0, 0, tiled=True)  6.35 us
    ppermute x1, starting transfers between devices, per_device(): south = lax.ppermute(south_edge, 'oy', forward)  4.93 us
    ppermute x1, starting transfers between devices, shifted(): lax.ppermute(lax.slice_in_dim(block, size - width, None, axis=dim), axis,...  3.99 us
    ppermute x1, waiting for transfers between devices, per_device(): north = lax.ppermute(north_edge, 'oy', backward)  2.73 us
    ppermute x1, waiting for transfers between devices, shifted(): lax.ppermute(lax.slice_in_dim(block, size - width, None, axis=dim), axis,...  2.46 us
    all_to_all x1, waiting for transfers between devices, per_device(): incoming = lax.all_to_all(outgoing, 'ox', 0, 0, tiled=True)  2.3 us
  transfers between devices with their start and end apart: 5, of which 3 were waited for; matrix products, arithmetic and copies ran while one was open for 11% of the time, Pallas kernels for 0%

profile of v11, /device:TPU:1, one launch (start us, length us, event | category | flops | bytes accessed | tf_op | source)
XLA Modules:
  0.0 57.9 jit_solution(3565002643383540344)
XLA Ops:
  0.6 0.0 copy-start
  0.6 1.5 %broadcast_in_dim.10 = bf16[8,4,10,128]{3,1,2,0:T(4,128)(2,1)} broadcast(bf16[4,10,128]{2,0,1:T(4,128)(2,1)} %param.8), dimensions={1,2,3} | broadcast | bytes 92160 | tf_op jit(solution)/shard_map/broadcast_in_dim | solution.py:170
  2.1 6.4 %all-to-all-start = ((bf16[8,4,10,128]{3,1,2,0:T(4,128)(2,1)}), bf16[8,4,10,128]{3,1,2,0:T(4,128)(2,1)S(1)}, u32[]{:S(2)}, u32[]{:S(2)}) async-start(bf16[8,4,10,128]{3,1,2,0:T(4,128)(2,1)} %broadcast_in_dim.10), calls=%async_computation | async-start | bytes 163840 | tf_op jit(solution)/shard_map/all_to_all | solution.py:171
  8.5 0.7 %compare_select_fusion.2 = s32[16,3]{0,1:T(4,128)S(1)} fusion(s32[16,3]{0,1:T(4,128)} %param.10), kind=kLoop, calls=%fused_computation.23 | loop fusion | flops 144 | bytes 384 | tf_op jit(solution)/shard_map/select_n | solution.py:173
  9.2 0.8 %copy.27 = s32[8,3]{1,0:T(8,128)S(1)} copy(s32[8,3]{0,1:T(4,128)} %param.11) | data formatting | bytes 192 | tf_op args[3]
  9.9 0.1 reshape.68
  10.0 0.1 copy.28
  10.1 0.1 reshape.72
  10.2 0.0 copy-start.5
  10.2 0.0 copy-start.4
  10.2 0.8 %gather_fusion = s32[48]{0:T(128)S(1)} fusion(s32[24]{0:T(128)S(1)} %reshape.68, s32[1024]{0:T(1024)S(1)} %pad_clamp_fusion), kind=kCustom, calls=%fused_computation | custom fusion | bytes 576 | tf_op jit(solution)/shard_map/gather | solution.py:173
  11.0 0.1 gather.9
  11.1 0.1 copy.29
  11.2 0.0 copy-done.4
  11.2 0.1 copy.32
  11.3 0.1 reshape.78
  11.4 0.1 pad.6.clone
  11.5 0.6 fusion.20.cor_ref
  12.0 2.3 %all-to-all-done = bf16[8,4,10,128]{3,1,2,0:T(4,128)(2,1)S(1)} async-done(((bf16[8,4,10,128]{3,1,2,0:T(4,128)(2,1)}), bf16[8,4,10,128]{3,1,2,0:T(4,128)(2,1)S(1)}, u32[]{:S(2)}, u32[]{:S(2)}) %all-to-all-start) | async-done | bytes 81952 | tf_op jit(solution)/shard_map/all_to_all | solution.py:171
  14.3 0.9 %gather_fusion.1 = bf16[48,4,128]{2,1,0:T(4,128)(2,1)S(1)} fusion(bf16[8,4,10,128]{3,1,2,0:T(4,128)(2,1)S(1)} %all-to-all-done, s32[48]{0:T(128)S(1)} %reshape.78), kind=kCustom, calls=%fused_computation.1 | custom fusion | bytes 98688 | tf_op jit(solution)/shard_map/gather | solution.py:174
  15.2 0.6 %convolution_bitcast_fusion = f32[16,4,128]{2,1,0:T(4,128)S(1)} fusion(bf16[16,3,4,128]{3,2,1,0:T(4,128)(2,1)S(1)} %bitcast.34, bf16[16,3,128,128]{3,2,1,0:T(8,128)(2,1)S(1)} %copy-done), kind=kOutput, calls=%fused_computation.2 | convolution fusion | flops 6291456 | bytes 1654784 | tf_op jit(solution)/shard_map/tkfa,tkra->ftr/dot_general | solution.py:175
  15.9 0.1 pad_maximum_fusion
  16.0 0.1 fusion.22
  16.0 1.3 %collective-permute-start = (f32[69,3,128]{2,1,0:T(4,128)S(1)}, f32[69,3,128]{2,1,0:T(4,128)S(1)}, u32[]{:S(2)}, u32[]{:S(2)}) collective-permute-start(f32[69,3,128]{2,1,0:T(4,128)S(1)} %get-tuple-element.5), channel_id=1, source_target_pairs={{4,0},{8,4},{12,8},{16,12},{20,16},{24,20},{28,24},{5,1},{9,5},{13... | collective-permute-start | bytes 317960 | tf_op jit(solution)/shard_map/ppermute | solution.py:144
  17.3 0.2 fusion.21
  17.5 4.0 %collective-permute-start.1 = (f32[69,3,128]{2,1,0:T(4,128)S(1)}, f32[69,3,128]{2,1,0:T(4,128)S(1)}, u32[]{:S(2)}, u32[]{:S(2)}) collective-permute-start(f32[69,3,128]{2,1,0:T(4,128)S(1)} %get-tuple-element.4), channel_id=1, source_target_pairs={{0,4},{4,8},{8,12},{12,16},{16,20},{20,24},{24,28},{1,5},{5,9},{9,... | collective-permute-start | bytes 317960 | tf_op jit(solution)/shard_map/ppermute | solution.py:143
  21.5 0.3 copy.37
  21.8 0.3 copy.34
  22.1 0.1 fusion.23
  22.3 0.1 copy.38
  22.4 0.1 copy.35
  22.5 2.5 %collective-permute-done.1.low_ref = f32[69,3,128]{2,1,0:T(4,128)S(1)} collective-permute-done((f32[69,3,128]{2,1,0:T(4,128)S(1)}, f32[69,3,128]{2,1,0:T(4,128)S(1)}, u32[]{:S(2)}, u32[]{:S(2)}) %collective-permute-start.1) | collective-permute-done | bytes 106016 | tf_op jit(solution)/shard_map/ppermute | solution.py:143
  25.0 0.1 fusion.24
  25.1 0.1 copy.39
  25.2 0.1 copy.36
  25.3 0.1 pad_maximum_fusion.3
  25.4 4.9 %collective-permute-start.3 = (f32[69,24,3]{0,1,2:T(8,128)S(1)}, f32[69,24,3]{0,1,2:T(8,128)S(1)}, u32[]{:S(2)}, u32[]{:S(2)}) collective-permute-start(f32[69,24,3]{0,1,2:T(8,128)S(1)} %get-tuple-element.10), channel_id=1, source_target_pairs={{0,1},{1,2},{2,3},{4,5},{5,6},{6,7},{8,9},{9,10},{10,11},{12,13},{... | collective-permute-start | bytes 59624 | tf_op jit(solution)/shard_map/ppermute | solution.py:196
  30.4 1.9 %collective-permute-start.2 = (f32[69,24,3]{0,1,2:T(8,128)S(1)}, f32[69,24,3]{0,1,2:T(8,128)S(1)}, u32[]{:S(2)}, u32[]{:S(2)}) collective-permute-start(f32[69,24,3]{0,1,2:T(8,128)S(1)} %get-tuple-element.11), channel_id=1, source_target_pairs={{1,0},{2,1},{3,2},{5,4},{6,5},{7,6},{9,8},{10,9},{11,10},{13,12},{... | collective-permute-start | bytes 59624 | tf_op jit(solution)/shard_map/ppermute | solution.py:197
  32.3 0.6 %pad_maximum_fusion.1.aux_ref = f32[5,16,128]{2,1,0:T(8,128)} fusion(f32[1,16,128]{2,1,0:T(8,128)S(1)} %convert_bitcast_fusion, f32[4,16,128]{2,1,0:T(8,128)S(1)} %bitcast.33), kind=kLoop, calls=%fused_computation.6 | loop fusion | flops 10240 | bytes 81920 | tf_op jit(solution)/shard_map/concatenate | solution.py:181
  32.9 2.7 %collective-permute-done.2 = f32[69,24,3]{0,1,2:T(8,128)S(1)} collective-permute-done((f32[69,24,3]{0,1,2:T(8,128)S(1)}, f32[69,24,3]{0,1,2:T(8,128)S(1)}, u32[]{:S(2)}, u32[]{:S(2)}) %collective-permute-start.2) | collective-permute-done | bytes 19904 | tf_op jit(solution)/shard_map/ppermute | solution.py:197
  35.7 1.3 %copy.40.north_ref = f32[69,24,3]{2,1,0:T(8,128)} copy(f32[69,24,3]{0,1,2:T(8,128)S(1)} %collective-permute-done.2) | data formatting | bytes 39744 | tf_op jit(solution)/shard_map/ppermute | solution.py:197
  36.9 1.3 %copy.41.south_ref = f32[69,24,3]{2,1,0:T(8,128)} copy(f32[69,24,3]{0,1,2:T(8,128)S(1)} %collective-permute-done.3) | data formatting | bytes 39744 | tf_op jit(solution)/shard_map/ppermute | solution.py:196
  38.3 7.8 %shard_map.95 = f32[4,16,16,128]{3,2,1,0:T(8,128)} custom-call(f32[16]{0:T(128)} %diff_ref.1, f32[1,256]{1,0:T(1,128)} %fusion.20.cor_ref, f32[64,16,128]{2,1,0:T(8,128)} %bitcast.30, f32[5,16,128]{2,1,0:T(8,128)} %pad_maximum_fusion.1.aux_ref, f32[69,3,128]{2,1,0:T(4,128)} %copy-done.2, f32[69,3,128]{2,1,0:T(4,128)} %copy-done.3, ...), custom_call_target="tpu_custom_call" | custom-call | tf_op jit(solution)/shard_map/pallas_call | solution.py:125
  46.1 0.7 %fusion.7 = bf16[16,128,1,1]{1,0,2,3:T(8,128)(2,1)S(1)} fusion(f32[4,16,16,128]{3,2,1,0:T(8,128)} %shard_map.95), kind=kLoop, calls=%fused_computation.25 | loop fusion | bytes 8192 | tf_op jit(solution)/shard_map/convert_element_type | solution.py:203
  46.8 0.4 fusion.4
  47.2 0.3 convolution_bitcast_fusion.1
  47.4 9.6 %all_to_all.10 = f32[8,3,128]{2,1,0:T(4,128)S(1)} all-to-all(f32[8,3,128]{2,1,0:T(4,128)S(1)} %reshape.69), channel_id=1, replica_groups=mesh['ox'=8,'oy'=4] {'ox'}, dimensions={0} | all-to-all | bytes 24576 | tf_op jit(solution)/shard_map/all_to_all | solution.py:209
  57.0 0.9 %convolution_bitcast_fusion.2 = f32[10,128]{1,0:T(8,128)} fusion(f32[8,3,128]{2,1,0:T(4,128)S(1)} %all_to_all.10, s32[8,3]{0,1:T(4,128)S(1)} %copy-done.6), kind=kOutput, calls=%fused_computation.4 | convolution fusion | flops 368880 | bytes 17504 | tf_op jit(solution)/shard_map/isb,isa->ba/dot_general | solution.py:210
  (18 shorter events, 0.1 us)
Async XLA Ops:
  0.6 14.6 %copy-start = (bf16[16,3,128,128]{3,2,1,0:T(8,128)(2,1)S(1)}, bf16[16,3,128,128]{3,2,1,0:T(8,128)(2,1)}, u32[]{:S(2)}) copy-start(bf16[16,3,128,128]{3,2,1,0:T(8,128)(2,1)} %param.9) | copy-start | bytes 4718596
  2.1 12.2 %all-to-all-start = ((bf16[8,4,10,128]{3,1,2,0:T(4,128)(2,1)}), bf16[8,4,10,128]{3,1,2,0:T(4,128)(2,1)S(1)}, u32[]{:S(2)}, u32[]{:S(2)}) async-start(bf16[8,4,10,128]{3,1,2,0:T(4,128)(2,1)} %broadcast_in_dim.10), calls=%async_computation | async-start | bytes 163840 | tf_op jit(solution)/shard_map/all_to_all | solution.py:171
  10.2 1.0 %copy-start.5 = (s32[16,128]{1,0:T(8,128)S(1)}, s32[16,128]{1,0:T(8,128)}, u32[]{:S(2)}) copy-start(s32[16,128]{1,0:T(8,128)} %param.14) | copy-start | bytes 24580
  10.2 1.0 %copy-start.4 = (s32[16,3]{0,1:T(4,128)S(1)}, s32[16,3]{0,1:T(4,128)}, u32[]{:S(2)}) copy-start(s32[16,3]{0,1:T(4,128)} %param.10) | copy-start | bytes 580
  11.0 4.9 %copy-start.1 = (f32[4,16,16,128]{3,2,1,0:T(8,128)S(1)}, f32[4,16,16,128]{3,2,1,0:T(8,128)}, u32[]{:S(2)}) copy-start(f32[4,16,16,128]{3,2,1,0:T(8,128)} %param.13) | copy-start | bytes 1572868
  16.0 6.1 %collective-permute-start = (f32[69,3,128]{2,1,0:T(4,128)S(1)}, f32[69,3,128]{2,1,0:T(4,128)S(1)}, u32[]{:S(2)}, u32[]{:S(2)}) collective-permute-start(f32[69,3,128]{2,1,0:T(4,128)S(1)} %get-tuple-element.5), channel_id=1, source_target_pairs={{4,0},{8,4},{12,8},{16,12},{20,16},{24,20},{28,24},{5,1},{9,5},{13... | collective-permute-start | bytes 317960 | tf_op jit(solution)/shard_map/ppermute | solution.py:144
  17.5 7.4 %collective-permute-start.1 = (f32[69,3,128]{2,1,0:T(4,128)S(1)}, f32[69,3,128]{2,1,0:T(4,128)S(1)}, u32[]{:S(2)}, u32[]{:S(2)}) collective-permute-start(f32[69,3,128]{2,1,0:T(4,128)S(1)} %get-tuple-element.4), channel_id=1, source_target_pairs={{0,4},{4,8},{8,12},{12,16},{16,20},{20,24},{24,28},{1,5},{5,9},{9,... | collective-permute-start | bytes 317960 | tf_op jit(solution)/shard_map/ppermute | solution.py:143
  22.1 16.1 %copy-start.2 = (f32[69,3,128]{2,1,0:T(4,128)}, f32[69,3,128]{2,1,0:T(4,128)S(1)}, u32[]{:S(2)}) copy-start(f32[69,3,128]{2,1,0:T(4,128)S(1)} %collective-permute-done.high_ref) | copy-start | bytes 317956
  25.0 13.3 %copy-start.3 = (f32[69,3,128]{2,1,0:T(4,128)}, f32[69,3,128]{2,1,0:T(4,128)S(1)}, u32[]{:S(2)}) copy-start(f32[69,3,128]{2,1,0:T(4,128)S(1)} %collective-permute-done.1.low_ref) | copy-start | bytes 317956
  25.4 11.5 %collective-permute-start.3 = (f32[69,24,3]{0,1,2:T(8,128)S(1)}, f32[69,24,3]{0,1,2:T(8,128)S(1)}, u32[]{:S(2)}, u32[]{:S(2)}) collective-permute-start(f32[69,24,3]{0,1,2:T(8,128)S(1)} %get-tuple-element.10), channel_id=1, source_target_pairs={{0,1},{1,2},{2,3},{4,5},{5,6},{6,7},{8,9},{9,10},{10,11},{12,13},{... | collective-permute-start | bytes 59624 | tf_op jit(solution)/shard_map/ppermute | solution.py:196
  30.4 5.3 %collective-permute-start.2 = (f32[69,24,3]{0,1,2:T(8,128)S(1)}, f32[69,24,3]{0,1,2:T(8,128)S(1)}, u32[]{:S(2)}, u32[]{:S(2)}) collective-permute-start(f32[69,24,3]{0,1,2:T(8,128)S(1)} %get-tuple-element.11), channel_id=1, source_target_pairs={{1,0},{2,1},{3,2},{5,4},{6,5},{7,6},{9,8},{10,9},{11,10},{13,12},{... | collective-permute-start | bytes 59624 | tf_op jit(solution)/shard_map/ppermute | solution.py:197
  46.1 11.0 %copy-start.6 = (s32[8,3]{0,1:T(4,128)S(1)}, s32[8,3]{0,1:T(4,128)}, u32[]{:S(2)}) copy-start(s32[8,3]{0,1:T(4,128)} %param.12) | copy-start | bytes 292

commit v12 on v11

--- a/solution.py
+++ b/solution.py
@@ -26,14 +26,22 @@
     tall, wide = source.shape[1], source.shape[2]
     width = high_ref.shape[1]
 
+    north_rows = [north_ref[s] for s in range(width)]
+    south_rows = [south_ref[s] for s in range(width)]
+    spread = north_ref.shape[2]
+    far = wide - lanes - width
+
     def assemble(ch, inner):
         source[ch, :rows, :lanes] = inner
         source[ch, rows:, :] = jnp.zeros((tall - rows, wide), jnp.float32)
         source[ch, :rows, lanes:] = jnp.zeros((rows, wide - lanes), jnp.float32)
         source[ch, rows : rows + width, :lanes] = high_ref[ch]
         source[ch, tall - width :, :lanes] = low_ref[ch]
-        source[ch, :, lanes : lanes + width] = north_ref[ch]
-        source[ch, :, wide - width :] = south_ref[ch]
+        for s in range(width):
+            moved = pltpu.roll(north_rows[s], (s - ch + spread) % spread, 1)
+            source[ch, :, lanes + s : lanes + s + 1] = moved[:, s : s + 1]
+            moved = pltpu.roll(south_rows[s], (far + s - ch + spread) % spread, 1)
+            source[ch, :, lanes + far + s : lanes + far + s + 1] = moved[:, far + s : far + s + 1]
 
     def assemble_state(ch, carry):
         assemble(ch, state_ref[ch])
@@ -193,6 +201,10 @@
     count = lax.axis_size("oy")
     forward = [(i, i + 1) for i in range(count - 1)]
     backward = [(target, source) for source, target in forward]
+    spread = -(-packed.shape[0] // 128) * 128
+    lane_pad = ((0, 0), (0, 0), (0, spread - packed.shape[0]))
+    south_edge = jnp.pad(jnp.transpose(south_edge, (2, 1, 0)), lane_pad)
+    north_edge = jnp.pad(jnp.transpose(north_edge, (2, 1, 0)), lane_pad)
     south = lax.ppermute(south_edge, "oy", forward)
     north = lax.ppermute(north_edge, "oy", backward)
     lane = jnp.arange(wide, dtype=jnp.int32)

time: 58.4 us -> 66.4 us (1.14)
  waiting for transfers between devices: 7.51 us -> 10 us
  other arithmetic: 2.04 us -> 4.25 us
  local copies, waits for them, and re-layouts: 9.54 us -> 11.7 us
  blocking collectives: 9.59 us -> 10.9 us
  starting transfers between devices: 18.5 us -> 17.3 us
    ppermute x1, waiting for transfers between devices: 2.46 us -> 7.45 us  [shifted(): lax.ppermute(lax.slice_in_dim(block, size - width, None, axis=dim), axis,...]
    ppermute x1, waiting for transfers between devices: 2.73 us -> 0.01 us  [per_device(): north = lax.ppermute(north_edge, 'oy', backward)]
    concatenate x1, other arithmetic: 0.05 us -> 2.24 us  [per_device(): packed = jnp.concatenate([inner, aux], axis=0)]
    ppermute x1, starting transfers between devices: 4.93 us -> 3.16 us  [per_device(): south = lax.ppermute(south_edge, 'oy', forward)]
    ppermute x1, waiting for transfers between devices: 0.01 us -> 1.71 us  [shifted(): lax.ppermute(lax.slice_in_dim(block, 0, width, axis=dim), axis, backward)]
    reshape x0 -> x1, local copies, waits for them, and re-layouts: none -> 1.47 us  [per_device(): inner = ocean_state.reshape(fields * levels, rows, lat_cells)]
    dot_general x1, local copies, waits for them, and re-layouts: 0.01 us -> 1.45 us  [per_device(): jnp.einsum('tkfa,tkra->ftr', picks, remap_weights, preferred_element_type...]
    all_to_all x1, waiting for transfers between devices: 2.3 us -> 0.86 us  [per_device(): incoming = lax.all_to_all(outgoing, 'ox', 0, 0, tiled=True)]
  transfers between devices with their start and end apart: 5 -> 5, of which waited for: 3 -> 3; matrix products, arithmetic and copies ran while one was open for 11% -> 12% of each run, Pallas kernels for 0% -> 0%
where the time goes in v12:
time: 66.4 us; the launch traced here: 65.6 us
  starting transfers between devices  17.3 us (26%)
  local copies, waits for them, and re-layouts  11.7 us (18%)
  blocking collectives  10.9 us (16%)
  waiting for transfers between devices  10 us (15%)
  Pallas kernels  8.42 us (13%)
  other arithmetic  4.25 us (6%)
  matrix products  2.15 us (3%)
  between operations  0.81 us (1%)
    all_to_all x1, blocking collectives, per_device(): returned = lax.all_to_all(per_slot, 'ox', 0, 0, tiled=True)  10.9 us
    pallas_call x1, Pallas kernels, run_steps(): pl.pallas_call(stencil_kernel, out_shape=jax.ShapeDtypeStruct(out_shape,...  8.42 us
    ppermute x1, waiting for transfers between devices, shifted(): lax.ppermute(lax.slice_in_dim(block, size - width, None, axis=dim), axis,...  7.45 us
    all_to_all x1, starting transfers between devices, per_device(): incoming = lax.all_to_all(outgoing, 'ox', 0, 0, tiled=True)  6.35 us
    ppermute x1, starting transfers between devices, shifted(): lax.ppermute(lax.slice_in_dim(block, size - width, None, axis=dim), axis,...  3.99 us
    ppermute x1, starting transfers between devices, per_device(): south = lax.ppermute(south_edge, 'oy', forward)  3.16 us
    ppermute x1, starting transfers between devices, per_device(): north = lax.ppermute(north_edge, 'oy', backward)  2.4 us
    concatenate x1, other arithmetic, per_device(): packed = jnp.concatenate([inner, aux], axis=0)  2.24 us
  transfers between devices with their start and end apart: 5, of which 3 were waited for; matrix products, arithmetic and copies ran while one was open for 12% of the time, Pallas kernels for 0%

profile of v12, /device:TPU:1, one launch (start us, length us, event | category | flops | bytes accessed | tf_op | source)
XLA Modules:
  0.0 65.6 jit_solution(6682641609781035603)
XLA Ops:
  0.6 0.0 copy-start
  0.6 1.5 %broadcast_in_dim.10 = bf16[8,4,10,128]{3,1,2,0:T(4,128)(2,1)} broadcast(bf16[4,10,128]{2,0,1:T(4,128)(2,1)} %param.8), dimensions={1,2,3} | broadcast | bytes 92160 | tf_op jit(solution)/shard_map/broadcast_in_dim | solution.py:178
  2.1 6.4 %all-to-all-start = ((bf16[8,4,10,128]{3,1,2,0:T(4,128)(2,1)}), bf16[8,4,10,128]{3,1,2,0:T(4,128)(2,1)S(1)}, u32[]{:S(2)}, u32[]{:S(2)}) async-start(bf16[8,4,10,128]{3,1,2,0:T(4,128)(2,1)} %broadcast_in_dim.10), calls=%async_computation | async-start | bytes 163840 | tf_op jit(solution)/shard_map/all_to_all | solution.py:179
  8.5 0.7 %compare_select_fusion.2 = s32[16,3]{0,1:T(4,128)S(1)} fusion(s32[16,3]{0,1:T(4,128)} %param.10), kind=kLoop, calls=%fused_computation.33 | loop fusion | flops 144 | bytes 384 | tf_op jit(solution)/shard_map/select_n | solution.py:181
  9.2 0.1 copy.40
  9.2 0.1 reshape.72
  9.4 0.8 %copy.39 = s32[8,3]{1,0:T(8,128)S(1)} copy(s32[8,3]{0,1:T(4,128)} %param.11) | data formatting | bytes 192 | tf_op args[3]
  10.1 0.1 reshape.68
  10.2 0.0 copy-start.3
  10.2 0.8 %gather_fusion = s32[48]{0:T(128)S(1)} fusion(s32[24]{0:T(128)S(1)} %reshape.68, s32[1024]{0:T(1024)S(1)} %pad_clamp_fusion), kind=kCustom, calls=%fused_computation | custom fusion | bytes 576 | tf_op jit(solution)/shard_map/gather | solution.py:181
  11.0 0.1 gather.9
  11.1 0.1 copy.41
  11.2 0.0 copy-done.6
  11.2 0.1 copy.44
  11.3 0.1 reshape.78
  11.4 0.0 copy-done.7
  11.4 0.5 copy.48
  11.9 0.0 copy-done.3
  11.9 1.5 %copy.47 = f32[64,16,128]{0,1,2:T(8,128)} copy(f32[64,16,128]{2,1,0:T(8,128)S(1)} %bitcast.38) | data formatting | bytes 1048576 | tf_op jit(solution)/shard_map/reshape | solution.py:188
  13.4 0.1 pad.15.clone
  13.5 0.9 %all-to-all-done = bf16[8,4,10,128]{3,1,2,0:T(4,128)(2,1)S(1)} async-done(((bf16[8,4,10,128]{3,1,2,0:T(4,128)(2,1)}), bf16[8,4,10,128]{3,1,2,0:T(4,128)(2,1)S(1)}, u32[]{:S(2)}, u32[]{:S(2)}) %all-to-all-start) | async-done | bytes 81952 | tf_op jit(solution)/shard_map/all_to_all | solution.py:179
  14.3 0.9 %gather_fusion.1 = bf16[48,4,128]{2,1,0:T(4,128)(2,1)S(1)} fusion(bf16[8,4,10,128]{3,1,2,0:T(4,128)(2,1)S(1)} %all-to-all-done, s32[48]{0:T(128)S(1)} %reshape.78), kind=kCustom, calls=%fused_computation.1 | custom fusion | bytes 98688 | tf_op jit(solution)/shard_map/gather | solution.py:182
  15.2 0.6 convolution_bitcast_fusion
  15.9 1.4 %copy.45 = f32[16,4,128]{1,0,2:T(8,128)} copy(f32[16,4,128]{2,1,0:T(4,128)S(1)} %convolution_bitcast_fusion) | data formatting | bytes 65536 | tf_op jit(solution)/shard_map/tkfa,tkra->ftr/dot_general | solution.py:183
  17.3 2.2 %pad_maximum_fusion = f32[69,16,128]{0,1,2:T(8,128)S(1)} fusion(f32[1,16,128]{0,1,2:T(8,128)S(1)} %copy.48, f32[4,16,128]{0,1,2:T(8,128)} %bitcast.35, f32[64,16,128]{0,1,2:T(8,128)} %copy.47), kind=kLoop, calls=%fused_computation.5 | loop fusion | flops 282624 | bytes 1130496 | tf_op jit(solution)/shard_map/concatenate | solution.py:190
  19.6 0.1 fusion.29
  19.7 1.4 %collective-permute-start = (f32[69,3,128]{0,1,2:T(4,128)S(1)}, f32[69,3,128]{0,1,2:T(4,128)S(1)}, u32[]{:S(2)}, u32[]{:S(2)}) collective-permute-start(f32[69,3,128]{0,1,2:T(4,128)S(1)} %get-tuple-element.5), channel_id=1, source_target_pairs={{4,0},{8,4},{12,8},{16,12},{20,16},{24,20},{28,24},{5,1},{9,5},{13... | collective-permute-start | bytes 317960 | tf_op jit(solution)/shard_map/ppermute | solution.py:152
  21.1 0.6 fusion.28.cor_ref
  21.7 4.0 %collective-permute-start.1 = (f32[69,3,128]{0,1,2:T(4,128)S(1)}, f32[69,3,128]{0,1,2:T(4,128)S(1)}, u32[]{:S(2)}, u32[]{:S(2)}) collective-permute-start(f32[69,3,128]{0,1,2:T(4,128)S(1)} %get-tuple-element.4), channel_id=1, source_target_pairs={{0,4},{4,8},{8,12},{12,16},{16,20},{20,24},{24,28},{1,5},{5,9},{9,... | collective-permute-start | bytes 317960 | tf_op jit(solution)/shard_map/ppermute | solution.py:151
  25.7 1.7 %collective-permute-done = f32[69,3,128]{0,1,2:T(4,128)S(1)} collective-permute-done((f32[69,3,128]{0,1,2:T(4,128)S(1)}, f32[69,3,128]{0,1,2:T(4,128)S(1)}, u32[]{:S(2)}, u32[]{:S(2)}) %collective-permute-start) | collective-permute-done | bytes 106016 | tf_op jit(solution)/shard_map/ppermute | solution.py:152
  27.4 7.4 %collective-permute-done.1 = f32[69,3,128]{0,1,2:T(4,128)S(1)} collective-permute-done((f32[69,3,128]{0,1,2:T(4,128)S(1)}, f32[69,3,128]{0,1,2:T(4,128)S(1)}, u32[]{:S(2)}, u32[]{:S(2)}) %collective-permute-start.1) | collective-permute-done | bytes 106016 | tf_op jit(solution)/shard_map/ppermute | solution.py:151
  34.9 0.0 copy-done.2
  34.9 0.1 fusion.3
  35.0 2.4 %collective-permute-start.2 = (f32[3,24,128]{2,1,0:T(8,128)S(1)}, f32[3,24,128]{2,1,0:T(8,128)S(1)}, u32[]{:S(2)}, u32[]{:S(2)}) collective-permute-start(f32[3,24,128]{2,1,0:T(8,128)S(1)} %pad.7), channel_id=1, source_target_pairs={{1,0},{2,1},{3,2},{5,4},{6,5},{7,6},{9,8},{10,9},{11,10},{13,12},{... | collective-permute-start | bytes 110600 | tf_op jit(solution)/shard_map/ppermute | solution.py:209
  37.4 3.2 %collective-permute-start.3 = (f32[3,24,128]{2,1,0:T(8,128)S(1)}, f32[3,24,128]{2,1,0:T(8,128)S(1)}, u32[]{:S(2)}, u32[]{:S(2)}) collective-permute-start(f32[3,24,128]{2,1,0:T(8,128)S(1)} %pad.8), channel_id=1, source_target_pairs={{0,1},{1,2},{2,3},{4,5},{5,6},{6,7},{8,9},{9,10},{10,11},{12,13},{... | collective-permute-start | bytes 110600 | tf_op jit(solution)/shard_map/ppermute | solution.py:208
  40.6 0.6 pad_maximum_fusion.1.aux_ref
  41.2 0.8 %copy.49.high_ref = f32[69,3,128]{2,1,0:T(4,128)} copy(f32[69,3,128]{0,1,2:T(4,128)S(1)} %collective-permute-done) | data formatting | bytes 211968 | tf_op jit(solution)/shard_map/ppermute | solution.py:152
  42.0 0.8 %copy.50.low_ref = f32[69,3,128]{2,1,0:T(4,128)} copy(f32[69,3,128]{0,1,2:T(4,128)S(1)} %collective-permute-done.1) | data formatting | bytes 211968 | tf_op jit(solution)/shard_map/ppermute | solution.py:151
  42.8 0.0 collective-permute-done.2.north_ref
  42.8 0.0 collective-permute-done.3.south_ref
  42.8 0.6 copy-done.4
  43.4 0.6 copy-done.5
  44.0 8.4 %shard_map.95 = f32[4,16,16,128]{3,2,1,0:T(8,128)} custom-call(f32[16]{0:T(128)} %diff_ref.1, f32[1,256]{1,0:T(1,128)} %fusion.28.cor_ref, f32[64,16,128]{2,1,0:T(8,128)} %bitcast.37, f32[5,16,128]{2,1,0:T(8,128)} %pad_maximum_fusion.1.aux_ref, f32[69,3,128]{2,1,0:T(4,128)} %copy.49.high_ref, f32[69,3,128]{2,1,0:T(4,128)} %copy.50.low_ref, ...), custom_call_target="tpu_custom_call" | custom-call | tf_op jit(solution)/shard_map/pallas_call | solution.py:133
  52.5 0.7 %fusion.15 = bf16[16,128,1,1]{1,0,2,3:T(8,128)(2,1)S(1)} fusion(f32[4,16,16,128]{3,2,1,0:T(8,128)} %shard_map.95), kind=kLoop, calls=%fused_computation.35 | loop fusion | bytes 8192 | tf_op jit(solution)/shard_map/convert_element_type | solution.py:215
  53.2 0.4 fusion.12
  53.5 0.3 convolution_bitcast_fusion.1
  53.8 10.9 %all_to_all.10 = f32[8,3,128]{2,1,0:T(4,128)S(1)} all-to-all(f32[8,3,128]{2,1,0:T(4,128)S(1)} %reshape.69), channel_id=1, replica_groups=mesh['ox'=8,'oy'=4] {'ox'}, dimensions={0} | all-to-all | bytes 24576 | tf_op jit(solution)/shard_map/all_to_all | solution.py:221
  64.7 0.9 %convolution_bitcast_fusion.2 = f32[10,128]{1,0:T(8,128)} fusion(f32[8,3,128]{2,1,0:T(4,128)S(1)} %all_to_all.10, s32[8,3]{0,1:T(4,128)S(1)} %copy-done.8), kind=kOutput, calls=%fused_computation.4 | convolution fusion | flops 368880 | bytes 17504 | tf_op jit(solution)/shard_map/isb,isa->ba/dot_general | solution.py:222
  (20 shorter events, 0.1 us)
Async XLA Ops:
  0.6 14.6 %copy-start = (bf16[16,3,128,128]{3,2,1,0:T(8,128)(2,1)S(1)}, bf16[16,3,128,128]{3,2,1,0:T(8,128)(2,1)}, u32[]{:S(2)}) copy-start(bf16[16,3,128,128]{3,2,1,0:T(8,128)(2,1)} %param.9) | copy-start | bytes 4718596
  2.1 12.2 %all-to-all-start = ((bf16[8,4,10,128]{3,1,2,0:T(4,128)(2,1)}), bf16[8,4,10,128]{3,1,2,0:T(4,128)(2,1)S(1)}, u32[]{:S(2)}, u32[]{:S(2)}) async-start(bf16[8,4,10,128]{3,1,2,0:T(4,128)(2,1)} %broadcast_in_dim.10), calls=%async_computation | async-start | bytes 163840 | tf_op jit(solution)/shard_map/all_to_all | solution.py:179
  10.2 1.0 %copy-start.6 = (s32[16,3]{0,1:T(4,128)S(1)}, s32[16,3]{0,1:T(4,128)}, u32[]{:S(2)}) copy-start(s32[16,3]{0,1:T(4,128)} %param.10) | copy-start | bytes 580
  10.2 1.2 %copy-start.7 = (s32[16,128]{1,0:T(8,128)S(1)}, s32[16,128]{1,0:T(8,128)}, u32[]{:S(2)}) copy-start(s32[16,128]{1,0:T(8,128)} %param.14) | copy-start | bytes 24580
  10.2 1.7 %copy-start.3 = (f32[4,16,16,128]{3,2,1,0:T(8,128)S(1)}, f32[4,16,16,128]{3,2,1,0:T(8,128)}, u32[]{:S(2)}) copy-start(f32[4,16,16,128]{3,2,1,0:T(8,128)} %param.13) | copy-start | bytes 1572868
  17.3 17.5 %copy-start.2 = (f32[16,4,128]{1,0,2:T(8,128)S(1)}, f32[16,4,128]{1,0,2:T(8,128)}, u32[]{:S(2)}) copy-start(f32[16,4,128]{1,0,2:T(8,128)} %copy.45) | copy-start | bytes 98308
  19.6 15.3 %copy-start.1 = (f32[64,16,128]{0,1,2:T(8,128)S(1)}, f32[64,16,128]{0,1,2:T(8,128)}, u32[]{:S(2)}) copy-start(f32[64,16,128]{0,1,2:T(8,128)} %copy.47) | copy-start | bytes 1572868
  19.7 7.7 %collective-permute-start = (f32[69,3,128]{0,1,2:T(4,128)S(1)}, f32[69,3,128]{0,1,2:T(4,128)S(1)}, u32[]{:S(2)}, u32[]{:S(2)}) collective-permute-start(f32[69,3,128]{0,1,2:T(4,128)S(1)} %get-tuple-element.5), channel_id=1, source_target_pairs={{4,0},{8,4},{12,8},{16,12},{20,16},{24,20},{28,24},{5,1},{9,5},{13... | collective-permute-start | bytes 317960 | tf_op jit(solution)/shard_map/ppermute | solution.py:152
  21.7 13.2 %collective-permute-start.1 = (f32[69,3,128]{0,1,2:T(4,128)S(1)}, f32[69,3,128]{0,1,2:T(4,128)S(1)}, u32[]{:S(2)}, u32[]{:S(2)}) collective-permute-start(f32[69,3,128]{0,1,2:T(4,128)S(1)} %get-tuple-element.4), channel_id=1, source_target_pairs={{0,4},{4,8},{8,12},{12,16},{16,20},{20,24},{24,28},{1,5},{5,9},{9,... | collective-permute-start | bytes 317960 | tf_op jit(solution)/shard_map/ppermute | solution.py:151
  35.0 7.8 %collective-permute-start.2 = (f32[3,24,128]{2,1,0:T(8,128)S(1)}, f32[3,24,128]{2,1,0:T(8,128)S(1)}, u32[]{:S(2)}, u32[]{:S(2)}) collective-permute-start(f32[3,24,128]{2,1,0:T(8,128)S(1)} %pad.7), channel_id=1, source_target_pairs={{1,0},{2,1},{3,2},{5,4},{6,5},{7,6},{9,8},{10,9},{11,10},{13,12},{... | collective-permute-start | bytes 110600 | tf_op jit(solution)/shard_map/ppermute | solution.py:209
  37.4 5.4 %collective-permute-start.3 = (f32[3,24,128]{2,1,0:T(8,128)S(1)}, f32[3,24,128]{2,1,0:T(8,128)S(1)}, u32[]{:S(2)}, u32[]{:S(2)}) collective-permute-start(f32[3,24,128]{2,1,0:T(8,128)S(1)} %pad.8), channel_id=1, source_target_pairs={{0,1},{1,2},{2,3},{4,5},{5,6},{6,7},{8,9},{9,10},{10,11},{12,13},{... | collective-permute-start | bytes 110600 | tf_op jit(solution)/shard_map/ppermute | solution.py:208
  42.8 21.9 %copy-start.8 = (s32[8,3]{0,1:T(4,128)S(1)}, s32[8,3]{0,1:T(4,128)}, u32[]{:S(2)}) copy-start(s32[8,3]{0,1:T(4,128)} %param.12) | copy-start | bytes 292
  42.8 0.6 copy-start.4
  43.4 0.6 copy-start.5

commit v13 on v11

--- a/solution.py
+++ b/solution.py
@@ -1,3 +1,5 @@
+import functools
+
 import jax
 import jax.numpy as jnp
 from jax import lax
@@ -19,10 +21,11 @@
 
 def stencil_kernel(
     diff_ref, cor_ref, state_ref, aux_ref, high_ref, low_ref, north_ref, south_ref,
-    out_ref, source, first, second,
+    out_ref, source, first, second, surface_only,
 ):
-    fields, levels, rows, lanes = out_ref.shape
-    channels = fields * levels
+    fields = 4
+    channels, rows, lanes = state_ref.shape
+    levels = channels // fields
     tall, wide = source.shape[1], source.shape[2]
     width = high_ref.shape[1]
 
@@ -43,13 +46,18 @@
         assemble(channels + index, aux_ref[index])
         return carry
 
-    lax.fori_loop(0, channels, assemble_state, 0, unroll=4)
+    if surface_only:
+        for f in range(fields):
+            for l in range(min(levels, STEPS + 1)):
+                assemble(f * levels + l, state_ref[f * levels + l])
+    else:
+        lax.fori_loop(0, channels, assemble_state, 0, unroll=4)
     lax.fori_loop(0, aux_ref.shape[0], assemble_aux, 0, unroll=True)
 
     def aux(index):
         return source[channels + index]
 
-    def one_step(read, write, last):
+    def one_step(read, write, last, count):
         def crop(value):
             return value[:rows, :lanes] if last else value
 
@@ -88,7 +96,7 @@
                 write(f, l, center + crop(aux(fields)) * total)
             return cum
 
-        lax.fori_loop(0, levels, level, jnp.zeros((tall, wide), jnp.float32), unroll=True)
+        lax.fori_loop(0, count, level, jnp.zeros((tall, wide), jnp.float32), unroll=True)
 
     def read_src(ch):
         return source[ch]
@@ -106,13 +114,17 @@
         second[f * levels + l] = value
 
     def write_out(f, l, value):
-        out_ref[f, l] = value
+        if not surface_only:
+            out_ref[f, l] = value
+        elif f == 2:
+            out_ref[...] = value
 
     writers = [write_first, write_second]
     for repeat in range(STEPS):
         write = write_out if repeat == STEPS - 1 else writers[repeat % 2]
         read = read_src if repeat == 0 else (read_first if repeat % 2 == 1 else read_second)
-        one_step(read, write, repeat == STEPS - 1)
+        count = min(levels, STEPS - repeat) if surface_only else levels
+        one_step(read, write, repeat == STEPS - 1, count)
 
 
 def run_steps(state, aux, high, low, north, south, coriolis, diffusivity, out_shape):
@@ -122,17 +134,22 @@
     tall = -(-(rows + 2 * width) // 8) * 8
     wide = -(-(lanes + 2 * width) // 128) * 128
     vmem = pl.BlockSpec(memory_space=pltpu.VMEM)
-    return pl.pallas_call(
-        stencil_kernel,
-        out_shape=jax.ShapeDtypeStruct(out_shape, jnp.float32),
-        in_specs=[pl.BlockSpec(memory_space=pltpu.SMEM)] + [vmem] * 7,
-        out_specs=vmem,
-        scratch_shapes=[
-            pltpu.VMEM((channels, tall, wide), jnp.float32),
-            pltpu.VMEM((state.shape[0], tall, wide), jnp.float32),
-            pltpu.VMEM((state.shape[0], tall, wide), jnp.float32),
-        ],
-    )(diffusivity, coriolis, state, aux, high, low, north, south)
+    operands = (diffusivity, coriolis, state, aux, high, low, north, south)
+
+    def call(surface_only, shape):
+        return pl.pallas_call(
+            functools.partial(stencil_kernel, surface_only=surface_only),
+            out_shape=jax.ShapeDtypeStruct(shape, jnp.float32),
+            in_specs=[pl.BlockSpec(memory_space=pltpu.SMEM)] + [vmem] * 7,
+            out_specs=vmem,
+            scratch_shapes=[
+                pltpu.VMEM((channels, tall, wide), jnp.float32),
+                pltpu.VMEM((state.shape[0], tall, wide), jnp.float32),
+                pltpu.VMEM((state.shape[0], tall, wide), jnp.float32),
+            ],
+        )(*operands)
+
+    return call(True, (rows, lanes)), call(False, out_shape)
 
 
 def shifted(block, axis, dim, width):
@@ -199,8 +216,8 @@
     offset = jnp.where(lane < lat_cells + STEPS, lane, lane - wide)
     latitude = (lat_start + offset).astype(jnp.float32)
     coriolis_wide = (coriolis_coef * (2.0 * (latitude + 0.5) / lat_total - 1.0))[None, :]
-    state = run_steps(inner, aux, high, low, north, south, coriolis_wide, diffusivity, ocean_state.shape)
-    surface = state[2, 0].astype(jnp.bfloat16)
+    top, state = run_steps(inner, aux, high, low, north, south, coriolis_wide, diffusivity, ocean_state.shape)
+    surface = top.astype(jnp.bfloat16)
     pieces = jnp.einsum("tkra,tr->tka", remap_weights, surface, preferred_element_type=jnp.float32)
     slot_line = jnp.arange(slots, dtype=jnp.int32)
     to_slot = (tile_slots[:, :, None] == slot_line[None, None, :]).astype(jnp.float32)

time: 58.4 us -> 56.5 us (0.967)
  blocking collectives: 9.59 us -> 0 us
  starting transfers between devices: 18.5 us -> 22.9 us
  Pallas kernels: 7.79 us -> 10.4 us
  other arithmetic: 2.04 us -> 2.77 us
    all_to_all x1 -> x0, blocking collectives: 9.59 us -> none  [per_device(): returned = lax.all_to_all(per_slot, 'ox', 0, 0, tiled=True)]
    all_to_all x0 -> x1, starting transfers between devices: none -> 4.37 us  [per_device(): returned = lax.all_to_all(per_slot, 'ox', 0, 0, tiled=True)]
    pallas_call x1 -> x2, Pallas kernels: 7.79 us -> 10.4 us  [call(): pl.pallas_call(functools.partial(stencil_kernel, surface_only=surface_onl...]
    convert_element_type x1 -> x0, local copies, waits for them, and re-layouts: 0.71 us -> none  [per_device(): surface = state[2, 0].astype(jnp.bfloat16)]
    convert_element_type x0 -> x1, other arithmetic: none -> 0.7 us  [per_device(): surface = top.astype(jnp.bfloat16)]
    reshape x1, local copies, waits for them, and re-layouts: 0.01 us -> 0.61 us  [per_device(): per_slot = per_slot.reshape(owners, capacity, block_width)]
  transfers between devices with their start and end apart: 5 -> 6, of which waited for: 3 -> 3; matrix products, arithmetic and copies ran while one was open for 11% -> 12% of each run, Pallas kernels for 0% -> 14%
where the time goes in v13:
time: 56.5 us; the launch traced here: 56 us
  starting transfers between devices  22.9 us (41%)
  Pallas kernels  10.4 us (18%)
  local copies, waits for them, and re-layouts  9.46 us (17%)
  waiting for transfers between devices  7.47 us (13%)
  other arithmetic  2.77 us (5%)
  matrix products  2.15 us (4%)
  between operations  0.79 us (1%)
    pallas_call x2, Pallas kernels, call(): pl.pallas_call(functools.partial(stencil_kernel, surface_only=surface_onl...  10.4 us
    all_to_all x1, starting transfers between devices, per_device(): incoming = lax.all_to_all(outgoing, 'ox', 0, 0, tiled=True)  6.35 us
    ppermute x1, starting transfers between devices, per_device(): south = lax.ppermute(south_edge, 'oy', forward)  4.94 us
    all_to_all x1, starting transfers between devices, per_device(): returned = lax.all_to_all(per_slot, 'ox', 0, 0, tiled=True)  4.37 us
    ppermute x1, starting transfers between devices, shifted(): lax.ppermute(lax.slice_in_dim(block, size - width, None, axis=dim), axis,...  3.99 us
    ppermute x1, waiting for transfers between devices, per_device(): north = lax.ppermute(north_edge, 'oy', backward)  2.73 us
    ppermute x1, waiting for transfers between devices, shifted(): lax.ppermute(lax.slice_in_dim(block, size - width, None, axis=dim), axis,...  2.46 us
    all_to_all x1, waiting for transfers between devices, per_device(): incoming = lax.all_to_all(outgoing, 'ox', 0, 0, tiled=True)  2.28 us
  transfers between devices with their start and end apart: 6, of which 3 were waited for; matrix products, arithmetic and copies ran while one was open for 12% of the time, Pallas kernels for 14%

profile of v13, /device:TPU:1, one launch (start us, length us, event | category | flops | bytes accessed | tf_op | source)
XLA Modules:
  0.0 56.0 jit_solution(181502489095911161)
XLA Ops:
  0.6 0.0 copy-start
  0.6 1.5 %broadcast_in_dim.10 = bf16[8,4,10,128]{3,1,2,0:T(4,128)(2,1)} broadcast(bf16[4,10,128]{2,0,1:T(4,128)(2,1)} %param.8), dimensions={1,2,3} | broadcast | bytes 92160 | tf_op jit(solution)/shard_map/broadcast_in_dim | solution.py:187
  2.1 6.4 %all-to-all-start = ((bf16[8,4,10,128]{3,1,2,0:T(4,128)(2,1)}), bf16[8,4,10,128]{3,1,2,0:T(4,128)(2,1)S(1)}, u32[]{:S(2)}, u32[]{:S(2)}) async-start(bf16[8,4,10,128]{3,1,2,0:T(4,128)(2,1)} %broadcast_in_dim.10), calls=%async_computation | async-start | bytes 163840 | tf_op jit(solution)/shard_map/all_to_all | solution.py:188
  8.5 0.7 %compare_select_fusion.2 = s32[16,3]{0,1:T(4,128)S(1)} fusion(s32[16,3]{0,1:T(4,128)} %param.10), kind=kLoop, calls=%fused_computation.22 | loop fusion | flops 144 | bytes 384 | tf_op jit(solution)/shard_map/select_n | solution.py:190
  9.2 0.8 %copy.27 = s32[8,3]{1,0:T(8,128)S(1)} copy(s32[8,3]{0,1:T(4,128)} %param.11) | data formatting | bytes 192 | tf_op args[3]
  9.9 0.1 reshape.67
  10.0 0.1 copy.28
  10.1 0.1 reshape.71
  10.2 0.8 %gather_fusion = s32[48]{0:T(128)S(1)} fusion(s32[24]{0:T(128)S(1)} %reshape.67, s32[1024]{0:T(1024)S(1)} %pad_clamp_fusion), kind=kCustom, calls=%fused_computation | custom fusion | bytes 576 | tf_op jit(solution)/shard_map/gather | solution.py:190
  11.0 0.1 gather.9
  11.1 0.1 copy.29
  11.2 0.0 copy-done.4
  11.2 0.1 copy.32
  11.3 0.1 reshape.77
  11.4 0.1 pad.6.clone
  11.5 0.6 %fusion.19.cor_ref = f32[1,256]{1,0:T(1,128)} fusion(s32[]{:T(128)S(6)} %mul.16), kind=kLoop, calls=%fused_computation.41 | loop fusion | flops 2304 | bytes 1028 | tf_op jit(solution)/shard_map/mul | solution.py:218
  12.1 2.3 %all-to-all-done = bf16[8,4,10,128]{3,1,2,0:T(4,128)(2,1)S(1)} async-done(((bf16[8,4,10,128]{3,1,2,0:T(4,128)(2,1)}), bf16[8,4,10,128]{3,1,2,0:T(4,128)(2,1)S(1)}, u32[]{:S(2)}, u32[]{:S(2)}) %all-to-all-start) | async-done | bytes 81952 | tf_op jit(solution)/shard_map/all_to_all | solution.py:188
  14.3 0.9 %gather_fusion.1 = bf16[48,4,128]{2,1,0:T(4,128)(2,1)S(1)} fusion(bf16[8,4,10,128]{3,1,2,0:T(4,128)(2,1)S(1)} %all-to-all-done, s32[48]{0:T(128)S(1)} %reshape.77), kind=kCustom, calls=%fused_computation.1 | custom fusion | bytes 98688 | tf_op jit(solution)/shard_map/gather | solution.py:191
  15.2 0.6 %convolution_bitcast_fusion = f32[16,4,128]{2,1,0:T(4,128)S(1)} fusion(bf16[16,3,4,128]{3,2,1,0:T(4,128)(2,1)S(1)} %bitcast.33, bf16[16,3,128,128]{3,2,1,0:T(8,128)(2,1)S(1)} %copy-done), kind=kOutput, calls=%fused_computation.2 | convolution fusion | flops 6291456 | bytes 1654784 | tf_op jit(solution)/shard_map/tkfa,tkra->ftr/dot_general | solution.py:192
  15.9 0.1 pad_maximum_fusion
  15.9 0.1 fusion.21
  16.0 1.3 %collective-permute-start = (f32[69,3,128]{2,1,0:T(4,128)S(1)}, f32[69,3,128]{2,1,0:T(4,128)S(1)}, u32[]{:S(2)}, u32[]{:S(2)}) collective-permute-start(f32[69,3,128]{2,1,0:T(4,128)S(1)} %get-tuple-element.5), channel_id=1, source_target_pairs={{4,0},{8,4},{12,8},{16,12},{20,16},{24,20},{28,24},{5,1},{9,5},{13... | collective-permute-start | bytes 317960 | tf_op jit(solution)/shard_map/ppermute | solution.py:161
  17.3 0.2 fusion.20
  17.5 4.0 %collective-permute-start.1 = (f32[69,3,128]{2,1,0:T(4,128)S(1)}, f32[69,3,128]{2,1,0:T(4,128)S(1)}, u32[]{:S(2)}, u32[]{:S(2)}) collective-permute-start(f32[69,3,128]{2,1,0:T(4,128)S(1)} %get-tuple-element.4), channel_id=1, source_target_pairs={{0,4},{4,8},{8,12},{12,16},{16,20},{20,24},{24,28},{1,5},{5,9},{9,... | collective-permute-start | bytes 317960 | tf_op jit(solution)/shard_map/ppermute | solution.py:160
  21.5 0.3 copy.37
  21.8 0.3 copy.34
  22.1 0.1 fusion.22
  22.3 0.1 copy.38
  22.4 0.1 copy.35
  22.5 2.5 %collective-permute-done.1.low_ref = f32[69,3,128]{2,1,0:T(4,128)S(1)} collective-permute-done((f32[69,3,128]{2,1,0:T(4,128)S(1)}, f32[69,3,128]{2,1,0:T(4,128)S(1)}, u32[]{:S(2)}, u32[]{:S(2)}) %collective-permute-start.1) | collective-permute-done | bytes 106016 | tf_op jit(solution)/shard_map/ppermute | solution.py:160
  25.0 0.1 fusion.23
  25.1 0.1 copy.39
  25.2 0.1 copy.36
  25.3 0.1 pad_maximum_fusion.3
  25.4 4.9 %collective-permute-start.3 = (f32[69,24,3]{0,1,2:T(8,128)S(1)}, f32[69,24,3]{0,1,2:T(8,128)S(1)}, u32[]{:S(2)}, u32[]{:S(2)}) collective-permute-start(f32[69,24,3]{0,1,2:T(8,128)S(1)} %get-tuple-element.10), channel_id=1, source_target_pairs={{0,1},{1,2},{2,3},{4,5},{5,6},{6,7},{8,9},{9,10},{10,11},{12,13},{... | collective-permute-start | bytes 59624 | tf_op jit(solution)/shard_map/ppermute | solution.py:213
  30.4 1.9 %collective-permute-start.2 = (f32[69,24,3]{0,1,2:T(8,128)S(1)}, f32[69,24,3]{0,1,2:T(8,128)S(1)}, u32[]{:S(2)}, u32[]{:S(2)}) collective-permute-start(f32[69,24,3]{0,1,2:T(8,128)S(1)} %get-tuple-element.11), channel_id=1, source_target_pairs={{1,0},{2,1},{3,2},{5,4},{6,5},{7,6},{9,8},{10,9},{11,10},{13,12},{... | collective-permute-start | bytes 59624 | tf_op jit(solution)/shard_map/ppermute | solution.py:214
  32.3 0.6 %pad_maximum_fusion.1.aux_ref = f32[5,16,128]{2,1,0:T(8,128)} fusion(f32[1,16,128]{2,1,0:T(8,128)S(1)} %convert_bitcast_fusion, f32[4,16,128]{2,1,0:T(8,128)S(1)} %bitcast.32), kind=kLoop, calls=%fused_computation.6 | loop fusion | flops 10240 | bytes 81920 | tf_op jit(solution)/shard_map/concatenate | solution.py:198
  32.9 2.7 %collective-permute-done.2 = f32[69,24,3]{0,1,2:T(8,128)S(1)} collective-permute-done((f32[69,24,3]{0,1,2:T(8,128)S(1)}, f32[69,24,3]{0,1,2:T(8,128)S(1)}, u32[]{:S(2)}, u32[]{:S(2)}) %collective-permute-start.2) | collective-permute-done | bytes 19904 | tf_op jit(solution)/shard_map/ppermute | solution.py:214
  35.7 1.3 %copy.40.north_ref = f32[69,24,3]{2,1,0:T(8,128)} copy(f32[69,24,3]{0,1,2:T(8,128)S(1)} %collective-permute-done.2) | data formatting | bytes 39744 | tf_op jit(solution)/shard_map/ppermute | solution.py:214
  36.9 1.3 %copy.41.south_ref = f32[69,24,3]{2,1,0:T(8,128)} copy(f32[69,24,3]{0,1,2:T(8,128)S(1)} %collective-permute-done.3) | data formatting | bytes 39744 | tf_op jit(solution)/shard_map/ppermute | solution.py:213
  38.3 2.7 %shard_map.96 = f32[16,128]{1,0:T(8,128)} custom-call(f32[16]{0:T(128)} %diff_ref.3, f32[1,256]{1,0:T(1,128)} %fusion.19.cor_ref, f32[64,16,128]{2,1,0:T(8,128)} %bitcast.28, f32[5,16,128]{2,1,0:T(8,128)} %pad_maximum_fusion.1.aux_ref, f32[69,3,128]{2,1,0:T(4,128)} %copy-done.2, f32[69,3,128]{2,1,0:T(4,128)} %copy-done.3, f32[69,24,3]{2,1,0:T(8,128)} %copy.40.north_ref, ...), custom_call_target="tpu_custom_call" | custom-call | tf_op jit(solution)/shard_map/pallas_call | solution.py:140
  41.0 0.7 %convert_bitcast_fusion.1 = bf16[16,128,1,1]{1,0,2,3:T(8,128)(2,1)S(1)} fusion(f32[16,128]{1,0:T(8,128)} %shard_map.96), kind=kLoop, calls=%fused_computation.25 | loop fusion | flops 2048 | bytes 12288 | tf_op jit(solution)/shard_map/convert_element_type | solution.py:220
  41.7 0.4 fusion.4
  42.0 0.3 convolution_bitcast_fusion.1
  42.3 0.6 %reshape.68 = f32[8,3,128]{2,1,0:T(4,128)} reshape(f32[24,128]{1,0:T(8,128)S(1)} %convolution_bitcast_fusion.1) | data formatting | bytes 24576 | tf_op jit(solution)/shard_map/reshape | solution.py:225
  42.9 4.4 %all-to-all-start.1 = ((f32[8,3,128]{2,1,0:T(4,128)}), f32[8,3,128]{2,1,0:T(4,128)S(1)}, u32[]{:S(2)}, u32[]{:S(2)}) async-start(f32[8,3,128]{2,1,0:T(4,128)} %reshape.68), calls=%async_computation.1 | async-start | bytes 32768 | tf_op jit(solution)/shard_map/all_to_all | solution.py:226
  47.3 7.8 %shard_map.95 = f32[4,16,16,128]{3,2,1,0:T(8,128)} custom-call(f32[16]{0:T(128)} %diff_ref.3, f32[1,256]{1,0:T(1,128)} %fusion.19.cor_ref, f32[64,16,128]{2,1,0:T(8,128)} %bitcast.29, f32[5,16,128]{2,1,0:T(8,128)} %pad_maximum_fusion.1.aux_ref, f32[69,3,128]{2,1,0:T(4,128)} %copy-done.2, f32[69,3,128]{2,1,0:T(4,128)} %copy-done.3, ...), custom_call_target="tpu_custom_call" | custom-call | tf_op jit(solution)/shard_map/pallas_call | solution.py:140
  55.1 0.9 %convolution_bitcast_fusion.2 = f32[10,128]{1,0:T(8,128)} fusion(f32[8,3,128]{2,1,0:T(4,128)S(1)} %all-to-all-done.1, s32[8,3]{0,1:T(4,128)S(1)} %copy-done.6), kind=kOutput, calls=%fused_computation.4 | convolution fusion | flops 368880 | bytes 17504 | tf_op jit(solution)/shard_map/isb,isa->ba/dot_general | solution.py:227
  (20 shorter events, 0.1 us)
Async XLA Ops:
  0.6 14.6 %copy-start = (bf16[16,3,128,128]{3,2,1,0:T(8,128)(2,1)S(1)}, bf16[16,3,128,128]{3,2,1,0:T(8,128)(2,1)}, u32[]{:S(2)}) copy-start(bf16[16,3,128,128]{3,2,1,0:T(8,128)(2,1)} %param.9) | copy-start | bytes 4718596
  2.1 12.2 %all-to-all-start = ((bf16[8,4,10,128]{3,1,2,0:T(4,128)(2,1)}), bf16[8,4,10,128]{3,1,2,0:T(4,128)(2,1)S(1)}, u32[]{:S(2)}, u32[]{:S(2)}) async-start(bf16[8,4,10,128]{3,1,2,0:T(4,128)(2,1)} %broadcast_in_dim.10), calls=%async_computation | async-start | bytes 163840 | tf_op jit(solution)/shard_map/all_to_all | solution.py:188
  10.2 1.0 %copy-start.5 = (s32[16,128]{1,0:T(8,128)S(1)}, s32[16,128]{1,0:T(8,128)}, u32[]{:S(2)}) copy-start(s32[16,128]{1,0:T(8,128)} %param.14) | copy-start | bytes 24580
  10.2 1.0 %copy-start.4 = (s32[16,3]{0,1:T(4,128)S(1)}, s32[16,3]{0,1:T(4,128)}, u32[]{:S(2)}) copy-start(s32[16,3]{0,1:T(4,128)} %param.10) | copy-start | bytes 580
  11.0 4.9 %copy-start.1 = (f32[4,16,16,128]{3,2,1,0:T(8,128)S(1)}, f32[4,16,16,128]{3,2,1,0:T(8,128)}, u32[]{:S(2)}) copy-start(f32[4,16,16,128]{3,2,1,0:T(8,128)} %param.13) | copy-start | bytes 1572868
  16.0 6.1 %collective-permute-start = (f32[69,3,128]{2,1,0:T(4,128)S(1)}, f32[69,3,128]{2,1,0:T(4,128)S(1)}, u32[]{:S(2)}, u32[]{:S(2)}) collective-permute-start(f32[69,3,128]{2,1,0:T(4,128)S(1)} %get-tuple-element.5), channel_id=1, source_target_pairs={{4,0},{8,4},{12,8},{16,12},{20,16},{24,20},{28,24},{5,1},{9,5},{13... | collective-permute-start | bytes 317960 | tf_op jit(solution)/shard_map/ppermute | solution.py:161
  17.5 7.4 %collective-permute-start.1 = (f32[69,3,128]{2,1,0:T(4,128)S(1)}, f32[69,3,128]{2,1,0:T(4,128)S(1)}, u32[]{:S(2)}, u32[]{:S(2)}) collective-permute-start(f32[69,3,128]{2,1,0:T(4,128)S(1)} %get-tuple-element.4), channel_id=1, source_target_pairs={{0,4},{4,8},{8,12},{12,16},{16,20},{20,24},{24,28},{1,5},{5,9},{9,... | collective-permute-start | bytes 317960 | tf_op jit(solution)/shard_map/ppermute | solution.py:160
  22.1 16.2 %copy-start.2 = (f32[69,3,128]{2,1,0:T(4,128)}, f32[69,3,128]{2,1,0:T(4,128)S(1)}, u32[]{:S(2)}) copy-start(f32[69,3,128]{2,1,0:T(4,128)S(1)} %collective-permute-done.high_ref) | copy-start | bytes 317956
  25.0 13.3 %copy-start.3 = (f32[69,3,128]{2,1,0:T(4,128)}, f32[69,3,128]{2,1,0:T(4,128)S(1)}, u32[]{:S(2)}) copy-start(f32[69,3,128]{2,1,0:T(4,128)S(1)} %collective-permute-done.1.low_ref) | copy-start | bytes 317956
  25.4 11.5 %collective-permute-start.3 = (f32[69,24,3]{0,1,2:T(8,128)S(1)}, f32[69,24,3]{0,1,2:T(8,128)S(1)}, u32[]{:S(2)}, u32[]{:S(2)}) collective-permute-start(f32[69,24,3]{0,1,2:T(8,128)S(1)} %get-tuple-element.10), channel_id=1, source_target_pairs={{0,1},{1,2},{2,3},{4,5},{5,6},{6,7},{8,9},{9,10},{10,11},{12,13},{... | collective-permute-start | bytes 59624 | tf_op jit(solution)/shard_map/ppermute | solution.py:213
  30.4 5.3 %collective-permute-start.2 = (f32[69,24,3]{0,1,2:T(8,128)S(1)}, f32[69,24,3]{0,1,2:T(8,128)S(1)}, u32[]{:S(2)}, u32[]{:S(2)}) collective-permute-start(f32[69,24,3]{0,1,2:T(8,128)S(1)} %get-tuple-element.11), channel_id=1, source_target_pairs={{1,0},{2,1},{3,2},{5,4},{6,5},{7,6},{9,8},{10,9},{11,10},{13,12},{... | collective-permute-start | bytes 59624 | tf_op jit(solution)/shard_map/ppermute | solution.py:214
  42.3 12.8 %copy-start.6 = (s32[8,3]{0,1:T(4,128)S(1)}, s32[8,3]{0,1:T(4,128)}, u32[]{:S(2)}) copy-start(s32[8,3]{0,1:T(4,128)} %param.12) | copy-start | bytes 292
  42.9 12.2 %all-to-all-start.1 = ((f32[8,3,128]{2,1,0:T(4,128)}), f32[8,3,128]{2,1,0:T(4,128)S(1)}, u32[]{:S(2)}, u32[]{:S(2)}) async-start(f32[8,3,128]{2,1,0:T(4,128)} %reshape.68), calls=%async_computation.1 | async-start | bytes 32768 | tf_op jit(solution)/shard_map/all_to_all | solution.py:226

commit v14 on v13

--- a/solution.py
+++ b/solution.py
@@ -29,30 +29,29 @@
     tall, wide = source.shape[1], source.shape[2]
     width = high_ref.shape[1]
 
+    north_rows = [north_ref[s] for s in range(width)]
+    south_rows = [south_ref[s] for s in range(width)]
+
     def assemble(ch, inner):
         source[ch, :rows, :lanes] = inner
         source[ch, rows:, :] = jnp.zeros((tall - rows, wide), jnp.float32)
         source[ch, :rows, lanes:] = jnp.zeros((rows, wide - lanes), jnp.float32)
         source[ch, rows : rows + width, :lanes] = high_ref[ch]
         source[ch, tall - width :, :lanes] = low_ref[ch]
-        source[ch, :, lanes : lanes + width] = north_ref[ch]
-        source[ch, :, wide - width :] = south_ref[ch]
-
-    def assemble_state(ch, carry):
-        assemble(ch, state_ref[ch])
-        return carry
-
-    def assemble_aux(index, carry):
-        assemble(channels + index, aux_ref[index])
-        return carry
+        for s in range(width):
+            source[ch, :, lanes + s : lanes + s + 1] = north_rows[s][:, ch : ch + 1]
+            far = wide - width + s
+            source[ch, :, far : far + 1] = south_rows[s][:, ch : ch + 1]
 
     if surface_only:
         for f in range(fields):
             for l in range(min(levels, STEPS + 1)):
                 assemble(f * levels + l, state_ref[f * levels + l])
     else:
-        lax.fori_loop(0, channels, assemble_state, 0, unroll=4)
-    lax.fori_loop(0, aux_ref.shape[0], assemble_aux, 0, unroll=True)
+        for ch in range(channels):
+            assemble(ch, state_ref[ch])
+    for index in range(aux_ref.shape[0]):
+        assemble(channels + index, aux_ref[index])
 
     def aux(index):
         return source[channels + index]
@@ -210,8 +209,8 @@
     count = lax.axis_size("oy")
     forward = [(i, i + 1) for i in range(count - 1)]
     backward = [(target, source) for source, target in forward]
-    south = lax.ppermute(south_edge, "oy", forward)
-    north = lax.ppermute(north_edge, "oy", backward)
+    south = jnp.transpose(lax.ppermute(south_edge, "oy", forward), (2, 1, 0))
+    north = jnp.transpose(lax.ppermute(north_edge, "oy", backward), (2, 1, 0))
     lane = jnp.arange(wide, dtype=jnp.int32)
     offset = jnp.where(lane < lat_cells + STEPS, lane, lane - wide)
     latitude = (lat_start + offset).astype(jnp.float32)

time: 56.5 us -> 61.2 us (1.083)
  waiting for transfers between devices: 7.47 us -> 10 us
  local copies, waits for them, and re-layouts: 9.46 us -> 11.3 us
  other arithmetic: 2.77 us -> 4.28 us
  Pallas kernels: 10.4 us -> 9.52 us
    ppermute x1, waiting for transfers between devices: 2.46 us -> 7.11 us  [shifted(): lax.ppermute(lax.slice_in_dim(block, size - width, None, axis=dim), axis,...]
    ppermute x2, waiting for transfers between devices: 2.73 us -> 0.01 us  [the longest x1 0.01 us: per_device(): north = jnp.transpose(lax.ppermute(north_edge, 'oy', backward), (2, 1, 0))]
    concatenate x1, other arithmetic: 0.05 us -> 2.24 us  [per_device(): packed = jnp.concatenate([inner, aux], axis=0)]
    ppermute x1, waiting for transfers between devices: 0.01 us -> 1.69 us  [shifted(): lax.ppermute(lax.slice_in_dim(block, 0, width, axis=dim), axis, backward)]
    reshape x0 -> x1, local copies, waits for them, and re-layouts: none -> 1.58 us  [per_device(): inner = ocean_state.reshape(fields * levels, rows, lat_cells)]
    broadcast_in_dim x0 -> x1, local copies, waits for them, and re-layouts: none -> 1.43 us  [per_device(): aux = jnp.concatenate([forcing, wetness[None]], axis=0)]
    dot_general x1, local copies, waits for them, and re-layouts: 0.01 us -> 1.43 us  [per_device(): jnp.einsum('tkfa,tkra->ftr', picks, remap_weights, preferred_element_type...]
    ppermute x2, starting transfers between devices: 6.86 us -> 5.56 us  [the longest x1 3.16 us: per_device(): south = jnp.transpose(lax.ppermute(south_edge, 'oy', forward), (2, 1, 0))]
  transfers between devices with their start and end apart: 6 -> 6, of which waited for: 3 -> 3; matrix products, arithmetic and copies ran while one was open for 12% -> 12% of each run, Pallas kernels for 14% -> 12%
where the time goes in v14:
time: 61.2 us; the launch traced here: 60.7 us
  starting transfers between devices  22.6 us (37%)
  local copies, waits for them, and re-layouts  11.3 us (18%)
  waiting for transfers between devices  10 us (16%)
  Pallas kernels  9.52 us (16%)
  other arithmetic  4.28 us (7%)
  matrix products  2.15 us (4%)
  between operations  0.82 us (1%)
    pallas_call x2, Pallas kernels, call(): pl.pallas_call(functools.partial(stencil_kernel, surface_only=surface_onl...  9.52 us
    ppermute x1, waiting for transfers between devices, shifted(): lax.ppermute(lax.slice_in_dim(block, size - width, None, axis=dim), axis,...  7.11 us
    all_to_all x1, starting transfers between devices, per_device(): incoming = lax.all_to_all(outgoing, 'ox', 0, 0, tiled=True)  6.35 us
    all_to_all x1, starting transfers between devices, per_device(): returned = lax.all_to_all(per_slot, 'ox', 0, 0, tiled=True)  5.28 us
    ppermute x1, starting transfers between devices, shifted(): lax.ppermute(lax.slice_in_dim(block, size - width, None, axis=dim), axis,...  3.99 us
    ppermute x1, starting transfers between devices, per_device(): south = jnp.transpose(lax.ppermute(south_edge, 'oy', forward), (2, 1, 0))  3.16 us
    ppermute x1, starting transfers between devices, per_device(): north = jnp.transpose(lax.ppermute(north_edge, 'oy', backward), (2, 1, 0))  2.4 us
    concatenate x1, other arithmetic, per_device(): packed = jnp.concatenate([inner, aux], axis=0)  2.24 us
  transfers between devices with their start and end apart: 6, of which 3 were waited for; matrix products, arithmetic and copies ran while one was open for 12% of the time, Pallas kernels for 12%

profile of v14, /device:TPU:1, one launch (start us, length us, event | category | flops | bytes accessed | tf_op | source)
XLA Modules:
  0.0 60.7 jit_solution(12330630864350869533)
XLA Ops:
  0.6 0.0 copy-start
  0.6 0.0 copy-start.5
  0.7 1.5 %broadcast_in_dim.10 = bf16[8,4,10,128]{3,1,2,0:T(4,128)(2,1)} broadcast(bf16[4,10,128]{2,0,1:T(4,128)(2,1)} %param.8), dimensions={1,2,3} | broadcast | bytes 92160 | tf_op jit(solution)/shard_map/broadcast_in_dim | solution.py:186
  2.1 6.4 %all-to-all-start = ((bf16[8,4,10,128]{3,1,2,0:T(4,128)(2,1)}), bf16[8,4,10,128]{3,1,2,0:T(4,128)(2,1)S(1)}, u32[]{:S(2)}, u32[]{:S(2)}) async-start(bf16[8,4,10,128]{3,1,2,0:T(4,128)(2,1)} %broadcast_in_dim.10), calls=%async_computation | async-start | bytes 163840 | tf_op jit(solution)/shard_map/all_to_all | solution.py:187
  8.5 1.6 %copy.54 = f32[64,16,128]{0,1,2:T(8,128)S(1)} copy(f32[64,16,128]{2,1,0:T(8,128)} %bitcast.33) | data formatting | bytes 1048576 | tf_op jit(solution)/shard_map/reshape | solution.py:196
  10.1 0.0 copy-done.5
  10.1 0.1 copy.47
  10.2 0.1 reshape.71
  10.3 0.1 copy.46
  10.4 0.1 reshape.67
  10.5 0.8 %gather_fusion = s32[48]{0:T(128)S(1)} fusion(s32[24]{0:T(128)S(1)} %reshape.67, s32[1024]{0:T(1024)S(1)} %pad_clamp_fusion), kind=kCustom, calls=%fused_computation | custom fusion | bytes 576 | tf_op jit(solution)/shard_map/gather | solution.py:189
  11.2 0.1 gather.9
  11.3 0.1 copy.48
  11.5 0.1 copy.51
  11.5 0.1 reshape.77
  11.6 1.4 %copy.55 = f32[1,16,128]{0,1,2:T(8,128)} copy(f32[1,16,128]{2,1,0:T(8,128)S(1)} %convert_bitcast_fusion) | data formatting | bytes 16384 | tf_op jit(solution)/shard_map/broadcast_in_dim | solution.py:197
  13.1 0.1 pad.6.clone
  13.2 1.2 %all-to-all-done = bf16[8,4,10,128]{3,1,2,0:T(4,128)(2,1)S(1)} async-done(((bf16[8,4,10,128]{3,1,2,0:T(4,128)(2,1)}), bf16[8,4,10,128]{3,1,2,0:T(4,128)(2,1)S(1)}, u32[]{:S(2)}, u32[]{:S(2)}) %all-to-all-start) | async-done | bytes 81952 | tf_op jit(solution)/shard_map/all_to_all | solution.py:187
  14.4 0.9 %gather_fusion.1 = bf16[48,4,128]{2,1,0:T(4,128)(2,1)S(1)} fusion(bf16[8,4,10,128]{3,1,2,0:T(4,128)(2,1)S(1)} %all-to-all-done, s32[48]{0:T(128)S(1)} %reshape.77), kind=kCustom, calls=%fused_computation.1 | custom fusion | bytes 98688 | tf_op jit(solution)/shard_map/gather | solution.py:190
  15.3 0.0 copy-done
  15.3 0.6 %convolution_bitcast_fusion = f32[16,4,128]{2,1,0:T(4,128)S(1)} fusion(bf16[16,3,4,128]{3,2,1,0:T(4,128)(2,1)S(1)} %bitcast.36, bf16[16,3,128,128]{3,2,1,0:T(8,128)(2,1)S(1)} %copy-done), kind=kOutput, calls=%fused_computation.2 | convolution fusion | flops 6291456 | bytes 1654784 | tf_op jit(solution)/shard_map/tkfa,tkra->ftr/dot_general | solution.py:191
  15.9 1.4 %copy.52 = f32[16,4,128]{1,0,2:T(8,128)} copy(f32[16,4,128]{2,1,0:T(4,128)S(1)} %convolution_bitcast_fusion) | data formatting | bytes 65536 | tf_op jit(solution)/shard_map/tkfa,tkra->ftr/dot_general | solution.py:191
  17.3 2.2 %pad_maximum_fusion = f32[69,16,128]{0,1,2:T(8,128)S(1)} fusion(f32[1,16,128]{0,1,2:T(8,128)} %copy.55, f32[4,16,128]{0,1,2:T(8,128)} %bitcast.31, f32[64,16,128]{0,1,2:T(8,128)S(1)} %copy.54), kind=kLoop, calls=%fused_computation.5 | loop fusion | flops 282624 | bytes 1130496 | tf_op jit(solution)/shard_map/concatenate | solution.py:198
  19.6 0.1 fusion.26
  19.7 1.4 %collective-permute-start = (f32[69,3,128]{0,1,2:T(4,128)S(1)}, f32[69,3,128]{0,1,2:T(4,128)S(1)}, u32[]{:S(2)}, u32[]{:S(2)}) collective-permute-start(f32[69,3,128]{0,1,2:T(4,128)S(1)} %get-tuple-element.5), channel_id=1, source_target_pairs={{4,0},{8,4},{12,8},{16,12},{20,16},{24,20},{28,24},{5,1},{9,5},{13... | collective-permute-start | bytes 317960 | tf_op jit(solution)/shard_map/ppermute | solution.py:160
  21.1 0.6 fusion.25.cor_ref
  21.7 4.0 %collective-permute-start.1 = (f32[69,3,128]{0,1,2:T(4,128)S(1)}, f32[69,3,128]{0,1,2:T(4,128)S(1)}, u32[]{:S(2)}, u32[]{:S(2)}) collective-permute-start(f32[69,3,128]{0,1,2:T(4,128)S(1)} %get-tuple-element.4), channel_id=1, source_target_pairs={{0,4},{4,8},{8,12},{12,16},{16,20},{20,24},{24,28},{1,5},{5,9},{9,... | collective-permute-start | bytes 317960 | tf_op jit(solution)/shard_map/ppermute | solution.py:159
  25.7 1.7 %collective-permute-done = f32[69,3,128]{0,1,2:T(4,128)S(1)} collective-permute-done((f32[69,3,128]{0,1,2:T(4,128)S(1)}, f32[69,3,128]{0,1,2:T(4,128)S(1)}, u32[]{:S(2)}, u32[]{:S(2)}) %collective-permute-start) | collective-permute-done | bytes 106016 | tf_op jit(solution)/shard_map/ppermute | solution.py:160
  27.4 7.1 %collective-permute-done.1 = f32[69,3,128]{0,1,2:T(4,128)S(1)} collective-permute-done((f32[69,3,128]{0,1,2:T(4,128)S(1)}, f32[69,3,128]{0,1,2:T(4,128)S(1)}, u32[]{:S(2)}, u32[]{:S(2)}) %collective-permute-start.1) | collective-permute-done | bytes 106016 | tf_op jit(solution)/shard_map/ppermute | solution.py:159
  34.5 0.1 fusion.2
  34.6 2.4 %collective-permute-start.2 = (f32[69,24,3]{0,1,2:T(8,128)S(1)}, f32[69,24,3]{0,1,2:T(8,128)S(1)}, u32[]{:S(2)}, u32[]{:S(2)}) collective-permute-start(f32[69,24,3]{0,1,2:T(8,128)S(1)} %get-tuple-element.3), channel_id=1, source_target_pairs={{1,0},{2,1},{3,2},{5,4},{6,5},{7,6},{9,8},{10,9},{11,10},{13,12},{... | collective-permute-start | bytes 59624 | tf_op jit(solution)/shard_map/ppermute | solution.py:213
  37.0 3.2 %collective-permute-start.3 = (f32[69,24,3]{0,1,2:T(8,128)S(1)}, f32[69,24,3]{0,1,2:T(8,128)S(1)}, u32[]{:S(2)}, u32[]{:S(2)}) collective-permute-start(f32[69,24,3]{0,1,2:T(8,128)S(1)} %get-tuple-element.2), channel_id=1, source_target_pairs={{0,1},{1,2},{2,3},{4,5},{5,6},{6,7},{8,9},{9,10},{10,11},{12,13},{... | collective-permute-start | bytes 59624 | tf_op jit(solution)/shard_map/ppermute | solution.py:212
  40.2 0.6 %pad_maximum_fusion.1.aux_ref = f32[5,16,128]{2,1,0:T(8,128)} fusion(f32[1,16,128]{2,1,0:T(8,128)S(1)} %convert_bitcast_fusion, f32[4,16,128]{2,1,0:T(8,128)S(1)} %bitcast.41), kind=kLoop, calls=%fused_computation.6 | loop fusion | flops 10240 | bytes 81920 | tf_op jit(solution)/shard_map/concatenate | solution.py:197
  40.8 0.8 %copy.56.high_ref = f32[69,3,128]{2,1,0:T(4,128)} copy(f32[69,3,128]{0,1,2:T(4,128)S(1)} %collective-permute-done) | data formatting | bytes 211968 | tf_op jit(solution)/shard_map/ppermute | solution.py:160
  41.6 0.8 %copy.57.low_ref = f32[69,3,128]{2,1,0:T(4,128)} copy(f32[69,3,128]{0,1,2:T(4,128)S(1)} %collective-permute-done.1) | data formatting | bytes 211968 | tf_op jit(solution)/shard_map/ppermute | solution.py:159
  42.4 0.0 collective-permute-done.2
  42.4 0.0 collective-permute-done.3
  42.4 0.6 copy-done.3
  43.0 0.0 copy-done.4
  43.0 2.4 %shard_map.96 = f32[16,128]{1,0:T(8,128)} custom-call(f32[16]{0:T(128)} %diff_ref.3, f32[1,256]{1,0:T(1,128)} %fusion.25.cor_ref, f32[64,16,128]{2,1,0:T(8,128)} %bitcast.34, f32[5,16,128]{2,1,0:T(8,128)} %pad_maximum_fusion.1.aux_ref, f32[69,3,128]{2,1,0:T(4,128)} %copy.56.high_ref, f32[69,3,128]{2,1,0:T(4,128)} %copy.57.low_ref, f32[3,24,69]{2,1,0:T(8,128)} %bitcast.37, ...), custom_call_target="tpu_custom_call" | custom-call | tf_op jit(solution)/shard_map/pallas_call | solution.py:139
  45.5 0.7 %convert_bitcast_fusion.1 = bf16[16,128,1,1]{1,0,2,3:T(8,128)(2,1)S(1)} fusion(f32[16,128]{1,0:T(8,128)} %shard_map.96), kind=kLoop, calls=%fused_computation.33 | loop fusion | flops 2048 | bytes 12288 | tf_op jit(solution)/shard_map/convert_element_type | solution.py:219
  46.2 0.4 fusion.10
  46.5 0.3 convolution_bitcast_fusion.1
  46.8 0.6 %reshape.68 = f32[8,3,128]{2,1,0:T(4,128)} reshape(f32[24,128]{1,0:T(8,128)S(1)} %convolution_bitcast_fusion.1) | data formatting | bytes 24576 | tf_op jit(solution)/shard_map/reshape | solution.py:224
  47.4 5.3 %all-to-all-start.1 = ((f32[8,3,128]{2,1,0:T(4,128)}), f32[8,3,128]{2,1,0:T(4,128)S(1)}, u32[]{:S(2)}, u32[]{:S(2)}) async-start(f32[8,3,128]{2,1,0:T(4,128)} %reshape.68), calls=%async_computation.1 | async-start | bytes 32768 | tf_op jit(solution)/shard_map/all_to_all | solution.py:225
  52.7 7.1 %shard_map.95 = f32[4,16,16,128]{3,2,1,0:T(8,128)} custom-call(f32[16]{0:T(128)} %diff_ref.3, f32[1,256]{1,0:T(1,128)} %fusion.25.cor_ref, f32[64,16,128]{2,1,0:T(8,128)} %bitcast.35, f32[5,16,128]{2,1,0:T(8,128)} %pad_maximum_fusion.1.aux_ref, f32[69,3,128]{2,1,0:T(4,128)} %copy.56.high_ref, f32[69,3,128]{2,1,0:T(4,128)} %copy.57.low_ref, ...), custom_call_target="tpu_custom_call" | custom-call | tf_op jit(solution)/shard_map/pallas_call | solution.py:139
  59.8 0.0 all-to-all-done.1
  59.8 0.9 %convolution_bitcast_fusion.2 = f32[10,128]{1,0:T(8,128)} fusion(f32[8,3,128]{2,1,0:T(4,128)S(1)} %all-to-all-done.1, s32[8,3]{0,1:T(4,128)S(1)} %copy-done.8), kind=kOutput, calls=%fused_computation.4 | convolution fusion | flops 368880 | bytes 17504 | tf_op jit(solution)/shard_map/isb,isa->ba/dot_general | solution.py:226
  (20 shorter events, 0.1 us)
Async XLA Ops:
  0.6 14.6 %copy-start = (bf16[16,3,128,128]{3,2,1,0:T(8,128)(2,1)S(1)}, bf16[16,3,128,128]{3,2,1,0:T(8,128)(2,1)}, u32[]{:S(2)}) copy-start(bf16[16,3,128,128]{3,2,1,0:T(8,128)(2,1)} %param.9) | copy-start | bytes 4718596
  0.6 9.4 %copy-start.5 = (s32[16,3]{0,1:T(4,128)S(1)}, s32[16,3]{0,1:T(4,128)}, u32[]{:S(2)}) copy-start(s32[16,3]{0,1:T(4,128)} %param.10) | copy-start | bytes 580
  0.7 9.6 %copy-start.7 = (s32[8,3]{0,1:T(4,128)S(1)}, s32[8,3]{0,1:T(4,128)}, u32[]{:S(2)}) copy-start(s32[8,3]{0,1:T(4,128)} %param.11) | copy-start | bytes 292
  2.1 12.2 %all-to-all-start = ((bf16[8,4,10,128]{3,1,2,0:T(4,128)(2,1)}), bf16[8,4,10,128]{3,1,2,0:T(4,128)(2,1)S(1)}, u32[]{:S(2)}, u32[]{:S(2)}) async-start(bf16[8,4,10,128]{3,1,2,0:T(4,128)(2,1)} %broadcast_in_dim.10), calls=%async_computation | async-start | bytes 163840 | tf_op jit(solution)/shard_map/all_to_all | solution.py:187
  10.5 1.2 %copy-start.6 = (s32[16,128]{1,0:T(8,128)S(1)}, s32[16,128]{1,0:T(8,128)}, u32[]{:S(2)}) copy-start(s32[16,128]{1,0:T(8,128)} %param.14) | copy-start | bytes 24580
  17.3 17.2 %copy-start.2 = (f32[16,4,128]{1,0,2:T(8,128)S(1)}, f32[16,4,128]{1,0,2:T(8,128)}, u32[]{:S(2)}) copy-start(f32[16,4,128]{1,0,2:T(8,128)} %copy.52) | copy-start | bytes 98308
  19.6 14.9 %copy-start.1 = (f32[1,16,128]{0,1,2:T(8,128)S(1)}, f32[1,16,128]{0,1,2:T(8,128)}, u32[]{:S(2)}) copy-start(f32[1,16,128]{0,1,2:T(8,128)} %copy.55) | copy-start | bytes 24580
  19.7 7.7 %collective-permute-start = (f32[69,3,128]{0,1,2:T(4,128)S(1)}, f32[69,3,128]{0,1,2:T(4,128)S(1)}, u32[]{:S(2)}, u32[]{:S(2)}) collective-permute-start(f32[69,3,128]{0,1,2:T(4,128)S(1)} %get-tuple-element.5), channel_id=1, source_target_pairs={{4,0},{8,4},{12,8},{16,12},{20,16},{24,20},{28,24},{5,1},{9,5},{13... | collective-permute-start | bytes 317960 | tf_op jit(solution)/shard_map/ppermute | solution.py:160
  21.7 12.8 %collective-permute-start.1 = (f32[69,3,128]{0,1,2:T(4,128)S(1)}, f32[69,3,128]{0,1,2:T(4,128)S(1)}, u32[]{:S(2)}, u32[]{:S(2)}) collective-permute-start(f32[69,3,128]{0,1,2:T(4,128)S(1)} %get-tuple-element.4), channel_id=1, source_target_pairs={{0,4},{4,8},{8,12},{12,16},{16,20},{20,24},{24,28},{1,5},{5,9},{9,... | collective-permute-start | bytes 317960 | tf_op jit(solution)/shard_map/ppermute | solution.py:159
  34.6 7.8 %collective-permute-start.2 = (f32[69,24,3]{0,1,2:T(8,128)S(1)}, f32[69,24,3]{0,1,2:T(8,128)S(1)}, u32[]{:S(2)}, u32[]{:S(2)}) collective-permute-start(f32[69,24,3]{0,1,2:T(8,128)S(1)} %get-tuple-element.3), channel_id=1, source_target_pairs={{1,0},{2,1},{3,2},{5,4},{6,5},{7,6},{9,8},{10,9},{11,10},{13,12},{... | collective-permute-start | bytes 59624 | tf_op jit(solution)/shard_map/ppermute | solution.py:213
  37.0 5.4 %collective-permute-start.3 = (f32[69,24,3]{0,1,2:T(8,128)S(1)}, f32[69,24,3]{0,1,2:T(8,128)S(1)}, u32[]{:S(2)}, u32[]{:S(2)}) collective-permute-start(f32[69,24,3]{0,1,2:T(8,128)S(1)} %get-tuple-element.2), channel_id=1, source_target_pairs={{0,1},{1,2},{2,3},{4,5},{5,6},{6,7},{8,9},{9,10},{10,11},{12,13},{... | collective-permute-start | bytes 59624 | tf_op jit(solution)/shard_map/ppermute | solution.py:212
  42.4 0.6 %copy-start.3 = (f32[69,24,3]{0,1,2:T(8,128)}, f32[69,24,3]{0,1,2:T(8,128)S(1)}, u32[]{:S(2)}) copy-start(f32[69,24,3]{0,1,2:T(8,128)S(1)} %collective-permute-done.2) | copy-start | bytes 59620
  42.4 0.6 %copy-start.4 = (f32[69,24,3]{0,1,2:T(8,128)}, f32[69,24,3]{0,1,2:T(8,128)S(1)}, u32[]{:S(2)}) copy-start(f32[69,24,3]{0,1,2:T(8,128)S(1)} %collective-permute-done.3) | copy-start | bytes 59620
  46.2 13.6 %copy-start.8 = (s32[8,3]{0,1:T(4,128)S(1)}, s32[8,3]{0,1:T(4,128)}, u32[]{:S(2)}) copy-start(s32[8,3]{0,1:T(4,128)} %param.12) | copy-start | bytes 292
  47.4 12.4 %all-to-all-start.1 = ((f32[8,3,128]{2,1,0:T(4,128)}), f32[8,3,128]{2,1,0:T(4,128)S(1)}, u32[]{:S(2)}, u32[]{:S(2)}) async-start(f32[8,3,128]{2,1,0:T(4,128)} %reshape.68), calls=%async_computation.1 | async-start | bytes 32768 | tf_op jit(solution)/shard_map/all_to_all | solution.py:225

commit v15 on v14

--- a/solution.py
+++ b/solution.py
@@ -4,6 +4,7 @@
 import jax.numpy as jnp
 from jax import lax
 from jax.experimental import pallas as pl
+from jax.experimental.layout import Layout, with_layout_constraint
 from jax.experimental.pallas import tpu as pltpu
 from jax.sharding import PartitionSpec as P
 
@@ -196,9 +197,12 @@
     inner = ocean_state.reshape(fields * levels, rows, lat_cells)
     aux = jnp.concatenate([forcing, wetness[None]], axis=0)
     packed = jnp.concatenate([inner, aux], axis=0)
+    packed = with_layout_constraint(packed, Layout((0, 1, 2)))
     tall = -(-(rows + 2 * STEPS) // 8) * 8
     wide = -(-(lat_cells + 2 * STEPS) // 128) * 128
     low, high = shifted(packed, "ox", 1, STEPS)
+    low = with_layout_constraint(low, Layout((0, 1, 2)))
+    high = with_layout_constraint(high, Layout((0, 1, 2)))
     gap = jnp.zeros((packed.shape[0], tall - rows - 2 * STEPS, STEPS), jnp.float32)
     south_edge = jnp.concatenate(
         [packed[:, :, -STEPS:], high[:, :, -STEPS:], gap, low[:, :, -STEPS:]], axis=1

time: 61.2 us -> 51.8 us (0.85)
  waiting for transfers between devices: 10 us -> 5.33 us
  local copies, waits for them, and re-layouts: 11.3 us -> 7.44 us
  other arithmetic: 4.28 us -> 2.74 us
    ppermute x1, waiting for transfers between devices: 7.11 us -> 2.58 us  [shifted(): lax.ppermute(lax.slice_in_dim(block, size - width, None, axis=dim), axis,...]
    concatenate x1, other arithmetic: 2.24 us -> 0.05 us  [per_device(): packed = jnp.concatenate([inner, aux], axis=0)]
    unnamed x19 -> x25, local copies, waits for them, and re-layouts: 0.73 us -> 2.47 us
    ppermute x1, waiting for transfers between devices: 1.69 us -> 0.01 us  [shifted(): lax.ppermute(lax.slice_in_dim(block, 0, width, axis=dim), axis, backward)]
    reshape x1 -> x0, local copies, waits for them, and re-layouts: 1.58 us -> none  [per_device(): inner = ocean_state.reshape(fields * levels, rows, lat_cells)]
    ppermute x2 -> x0, local copies, waits for them, and re-layouts: 1.57 us -> none  [the longest x1 0.79 us: shifted(): lax.ppermute(lax.slice_in_dim(block, size - width, None, axis=dim), axis,...]
    broadcast_in_dim x1 -> x0, local copies, waits for them, and re-layouts: 1.43 us -> none  [per_device(): aux = jnp.concatenate([forcing, wetness[None]], axis=0)]
    dot_general x1, local copies, waits for them, and re-layouts: 1.43 us -> 0.01 us  [per_device(): jnp.einsum('tkfa,tkra->ftr', picks, remap_weights, preferred_element_type...]
  transfers between devices with their start and end apart: 6 -> 6, of which waited for: 3 -> 3; matrix products, arithmetic and copies ran while one was open for 12% -> 10% of each run, Pallas kernels for 12% -> 14%
where the time goes in v15:
time: 51.8 us; the launch traced here: 50.8 us
  starting transfers between devices  22.9 us (44%)
  Pallas kernels  9.52 us (18%)
  local copies, waits for them, and re-layouts  7.44 us (14%)
  waiting for transfers between devices  5.33 us (10%)
  other arithmetic  2.74 us (5%)
  matrix products  2.15 us (4%)
  between operations  0.77 us (1%)
    pallas_call x2, Pallas kernels, call(): pl.pallas_call(functools.partial(stencil_kernel, surface_only=surface_onl...  9.52 us
    all_to_all x1, starting transfers between devices, per_device(): incoming = lax.all_to_all(outgoing, 'ox', 0, 0, tiled=True)  6.35 us
    all_to_all x1, starting transfers between devices, per_device(): returned = lax.all_to_all(per_slot, 'ox', 0, 0, tiled=True)  4.37 us
    ppermute x1, starting transfers between devices, shifted(): lax.ppermute(lax.slice_in_dim(block, size - width, None, axis=dim), axis,...  3.99 us
    ppermute x1, starting transfers between devices, per_device(): north = jnp.transpose(lax.ppermute(north_edge, 'oy', backward), (2, 1, 0))  3.81 us
    ppermute x1, starting transfers between devices, per_device(): south = jnp.transpose(lax.ppermute(south_edge, 'oy', forward), (2, 1, 0))  3.05 us
    ppermute x1, waiting for transfers between devices, shifted(): lax.ppermute(lax.slice_in_dim(block, size - width, None, axis=dim), axis,...  2.58 us
    unnamed x25, local copies, waits for them, and re-layouts  2.47 us
  transfers between devices with their start and end apart: 6, of which 3 were waited for; matrix products, arithmetic and copies ran while one was open for 10% of the time, Pallas kernels for 14%

profile of v15, /device:TPU:1, one launch (start us, length us, event | category | flops | bytes accessed | tf_op | source)
XLA Modules:
  0.0 50.8 jit_solution(7769802844823635984)
XLA Ops:
  0.6 0.0 copy-start
  0.6 1.5 %broadcast_in_dim.10 = bf16[8,4,10,128]{3,1,2,0:T(4,128)(2,1)} broadcast(bf16[4,10,128]{2,0,1:T(4,128)(2,1)} %param.8), dimensions={1,2,3} | broadcast | bytes 92160 | tf_op jit(solution)/shard_map/broadcast_in_dim | solution.py:187
  2.1 6.4 %all-to-all-start = ((bf16[8,4,10,128]{3,1,2,0:T(4,128)(2,1)}), bf16[8,4,10,128]{3,1,2,0:T(4,128)(2,1)S(1)}, u32[]{:S(2)}, u32[]{:S(2)}) async-start(bf16[8,4,10,128]{3,1,2,0:T(4,128)(2,1)} %broadcast_in_dim.10), calls=%async_computation | async-start | bytes 163840 | tf_op jit(solution)/shard_map/all_to_all | solution.py:188
  8.5 0.7 %compare_select_fusion.2 = s32[16,3]{0,1:T(4,128)S(1)} fusion(s32[16,3]{0,1:T(4,128)} %param.10), kind=kLoop, calls=%fused_computation.22 | loop fusion | flops 144 | bytes 384 | tf_op jit(solution)/shard_map/select_n | solution.py:190
  9.2 0.1 copy.40
  9.2 0.1 reshape.71
  9.4 0.8 %copy.39 = s32[8,3]{1,0:T(8,128)S(1)} copy(s32[8,3]{0,1:T(4,128)} %param.11) | data formatting | bytes 192 | tf_op args[3]
  10.1 0.1 reshape.67
  10.2 0.8 %gather_fusion = s32[48]{0:T(128)S(1)} fusion(s32[24]{0:T(128)S(1)} %reshape.67, s32[1024]{0:T(1024)S(1)} %pad_clamp_fusion), kind=kCustom, calls=%fused_computation | custom fusion | bytes 576 | tf_op jit(solution)/shard_map/gather | solution.py:190
  11.0 0.1 gather.9
  11.1 0.1 copy.41
  11.1 0.0 copy-done.6
  11.2 0.1 copy.44
  11.3 0.1 reshape.77
  11.4 0.1 pad.6.clone
  11.5 0.6 %fusion.19.cor_ref = f32[1,256]{1,0:T(1,128)} fusion(s32[]{:T(128)S(6)} %mul.16), kind=kLoop, calls=%fused_computation.41 | loop fusion | flops 2304 | bytes 1028 | tf_op jit(solution)/shard_map/mul | solution.py:221
  12.0 2.3 %all-to-all-done = bf16[8,4,10,128]{3,1,2,0:T(4,128)(2,1)S(1)} async-done(((bf16[8,4,10,128]{3,1,2,0:T(4,128)(2,1)}), bf16[8,4,10,128]{3,1,2,0:T(4,128)(2,1)S(1)}, u32[]{:S(2)}, u32[]{:S(2)}) %all-to-all-start) | async-done | bytes 81952 | tf_op jit(solution)/shard_map/all_to_all | solution.py:188
  14.3 0.9 %gather_fusion.1 = bf16[48,4,128]{2,1,0:T(4,128)(2,1)S(1)} fusion(bf16[8,4,10,128]{3,1,2,0:T(4,128)(2,1)S(1)} %all-to-all-done, s32[48]{0:T(128)S(1)} %reshape.77), kind=kCustom, calls=%fused_computation.1 | custom fusion | bytes 98688 | tf_op jit(solution)/shard_map/gather | solution.py:191
  15.2 0.6 %convolution_bitcast_fusion = f32[16,4,128]{2,1,0:T(4,128)S(1)} fusion(bf16[16,3,4,128]{3,2,1,0:T(4,128)(2,1)S(1)} %bitcast.35, bf16[16,3,128,128]{3,2,1,0:T(8,128)(2,1)S(1)} %copy-done), kind=kOutput, calls=%fused_computation.2 | convolution fusion | flops 6291456 | bytes 1654784 | tf_op jit(solution)/shard_map/tkfa,tkra->ftr/dot_general | solution.py:192
  15.9 0.1 pad_maximum_fusion
  15.9 0.1 fusion.21
  16.0 1.3 %collective-permute-start = (f32[69,3,128]{2,1,0:T(4,128)S(1)}, f32[69,3,128]{2,1,0:T(4,128)S(1)}, u32[]{:S(2)}, u32[]{:S(2)}) collective-permute-start(f32[69,3,128]{2,1,0:T(4,128)S(1)} %get-tuple-element.5), channel_id=1, source_target_pairs={{4,0},{8,4},{12,8},{16,12},{20,16},{24,20},{28,24},{5,1},{9,5},{13... | collective-permute-start | bytes 317960 | tf_op jit(solution)/shard_map/ppermute | solution.py:161
  17.3 0.2 fusion.20
  17.5 4.0 %collective-permute-start.1 = (f32[69,3,128]{2,1,0:T(4,128)S(1)}, f32[69,3,128]{2,1,0:T(4,128)S(1)}, u32[]{:S(2)}, u32[]{:S(2)}) collective-permute-start(f32[69,3,128]{2,1,0:T(4,128)S(1)} %get-tuple-element.4), channel_id=1, source_target_pairs={{0,4},{4,8},{8,12},{12,16},{16,20},{20,24},{24,28},{1,5},{5,9},{9,... | collective-permute-start | bytes 317960 | tf_op jit(solution)/shard_map/ppermute | solution.py:160
  21.5 0.3 copy.56
  21.8 0.3 copy.59
  22.1 0.1 fusion.22
  22.3 0.1 copy.57
  22.4 2.6 %collective-permute-done.1.low_ref = f32[69,3,128]{2,1,0:T(4,128)S(1)} collective-permute-done((f32[69,3,128]{2,1,0:T(4,128)S(1)}, f32[69,3,128]{2,1,0:T(4,128)S(1)}, u32[]{:S(2)}, u32[]{:S(2)}) %collective-permute-start.1) | collective-permute-done | bytes 106016 | tf_op jit(solution)/shard_map/ppermute | solution.py:160
  25.0 0.1 fusion.23
  25.1 0.1 copy.58
  25.2 0.1 copy.60
  25.3 0.1 copy.61
  25.5 0.1 pad_maximum_fusion.3
  25.5 3.8 %collective-permute-start.2 = (f32[69,24,3]{0,1,2:T(8,128)S(1)}, f32[69,24,3]{0,1,2:T(8,128)S(1)}, u32[]{:S(2)}, u32[]{:S(2)}) collective-permute-start(f32[69,24,3]{0,1,2:T(8,128)S(1)} %get-tuple-element.11), channel_id=1, source_target_pairs={{1,0},{2,1},{3,2},{5,4},{6,5},{7,6},{9,8},{10,9},{11,10},{13,12},{... | collective-permute-start | bytes 59624 | tf_op jit(solution)/shard_map/ppermute | solution.py:217
  29.4 3.0 %collective-permute-start.3 = (f32[69,24,3]{0,1,2:T(8,128)S(1)}, f32[69,24,3]{0,1,2:T(8,128)S(1)}, u32[]{:S(2)}, u32[]{:S(2)}) collective-permute-start(f32[69,24,3]{0,1,2:T(8,128)S(1)} %get-tuple-element.10), channel_id=1, source_target_pairs={{0,1},{1,2},{2,3},{4,5},{5,6},{6,7},{8,9},{9,10},{10,11},{12,13},{... | collective-permute-start | bytes 59624 | tf_op jit(solution)/shard_map/ppermute | solution.py:216
  32.4 0.6 %pad_maximum_fusion.1.aux_ref = f32[5,16,128]{2,1,0:T(8,128)} fusion(f32[1,16,128]{2,1,0:T(8,128)S(1)} %convert_bitcast_fusion, f32[4,16,128]{2,1,0:T(8,128)S(1)} %bitcast.34), kind=kLoop, calls=%fused_computation.6 | loop fusion | flops 10240 | bytes 81920 | tf_op jit(solution)/shard_map/concatenate | solution.py:198
  33.0 0.4 collective-permute-done.3
  33.5 0.2 copy-done.4
  33.7 0.4 copy-done.5
  34.1 2.4 %shard_map.96 = f32[16,128]{1,0:T(8,128)} custom-call(f32[16]{0:T(128)} %diff_ref.3, f32[1,256]{1,0:T(1,128)} %fusion.19.cor_ref, f32[64,16,128]{2,1,0:T(8,128)} %bitcast.30, f32[5,16,128]{2,1,0:T(8,128)} %pad_maximum_fusion.1.aux_ref, f32[69,3,128]{2,1,0:T(4,128)} %copy-done.2, f32[69,3,128]{2,1,0:T(4,128)} %copy-done.3, f32[3,24,69]{2,1,0:T(8,128)} %bitcast.36, ...), custom_call_target="tpu_custom_call" | custom-call | tf_op jit(solution)/shard_map/pallas_call | solution.py:140
  36.5 0.7 %convert_bitcast_fusion.1 = bf16[16,128,1,1]{1,0,2,3:T(8,128)(2,1)S(1)} fusion(f32[16,128]{1,0:T(8,128)} %shard_map.96), kind=kLoop, calls=%fused_computation.25 | loop fusion | flops 2048 | bytes 12288 | tf_op jit(solution)/shard_map/convert_element_type | solution.py:223
  37.2 0.4 fusion.4
  37.6 0.3 convolution_bitcast_fusion.1
  37.9 0.6 %reshape.68 = f32[8,3,128]{2,1,0:T(4,128)} reshape(f32[24,128]{1,0:T(8,128)S(1)} %convolution_bitcast_fusion.1) | data formatting | bytes 24576 | tf_op jit(solution)/shard_map/reshape | solution.py:228
  38.5 4.4 %all-to-all-start.1 = ((f32[8,3,128]{2,1,0:T(4,128)}), f32[8,3,128]{2,1,0:T(4,128)S(1)}, u32[]{:S(2)}, u32[]{:S(2)}) async-start(f32[8,3,128]{2,1,0:T(4,128)} %reshape.68), calls=%async_computation.1 | async-start | bytes 32768 | tf_op jit(solution)/shard_map/all_to_all | solution.py:229
  42.9 7.1 %shard_map.95 = f32[4,16,16,128]{3,2,1,0:T(8,128)} custom-call(f32[16]{0:T(128)} %diff_ref.3, f32[1,256]{1,0:T(1,128)} %fusion.19.cor_ref, f32[64,16,128]{2,1,0:T(8,128)} %bitcast.31, f32[5,16,128]{2,1,0:T(8,128)} %pad_maximum_fusion.1.aux_ref, f32[69,3,128]{2,1,0:T(4,128)} %copy-done.2, f32[69,3,128]{2,1,0:T(4,128)} %copy-done.3, f32[3,24,69]{2,1,0:T(8,128)} %bitcast.37, ...), custom_call_target="tpu_custom_call" | custom-call | tf_op jit(solution)/shard_map/pallas_call | solution.py:140
  49.9 0.9 %convolution_bitcast_fusion.2 = f32[10,128]{1,0:T(8,128)} fusion(f32[8,3,128]{2,1,0:T(4,128)S(1)} %all-to-all-done.1, s32[8,3]{0,1:T(4,128)S(1)} %copy-done.8), kind=kOutput, calls=%fused_computation.4 | convolution fusion | flops 368880 | bytes 17504 | tf_op jit(solution)/shard_map/isb,isa->ba/dot_general | solution.py:230
  (22 shorter events, 0.1 us)
Async XLA Ops:
  0.6 14.6 %copy-start = (bf16[16,3,128,128]{3,2,1,0:T(8,128)(2,1)S(1)}, bf16[16,3,128,128]{3,2,1,0:T(8,128)(2,1)}, u32[]{:S(2)}) copy-start(bf16[16,3,128,128]{3,2,1,0:T(8,128)(2,1)} %param.9) | copy-start | bytes 4718596
  2.1 12.2 %all-to-all-start = ((bf16[8,4,10,128]{3,1,2,0:T(4,128)(2,1)}), bf16[8,4,10,128]{3,1,2,0:T(4,128)(2,1)S(1)}, u32[]{:S(2)}, u32[]{:S(2)}) async-start(bf16[8,4,10,128]{3,1,2,0:T(4,128)(2,1)} %broadcast_in_dim.10), calls=%async_computation | async-start | bytes 163840 | tf_op jit(solution)/shard_map/all_to_all | solution.py:188
  10.2 1.0 %copy-start.7 = (s32[16,128]{1,0:T(8,128)S(1)}, s32[16,128]{1,0:T(8,128)}, u32[]{:S(2)}) copy-start(s32[16,128]{1,0:T(8,128)} %param.14) | copy-start | bytes 24580
  10.2 1.0 %copy-start.6 = (s32[16,3]{0,1:T(4,128)S(1)}, s32[16,3]{0,1:T(4,128)}, u32[]{:S(2)}) copy-start(s32[16,3]{0,1:T(4,128)} %param.10) | copy-start | bytes 580
  11.0 4.9 %copy-start.1 = (f32[4,16,16,128]{3,2,1,0:T(8,128)S(1)}, f32[4,16,16,128]{3,2,1,0:T(8,128)}, u32[]{:S(2)}) copy-start(f32[4,16,16,128]{3,2,1,0:T(8,128)} %param.13) | copy-start | bytes 1572868
  16.0 6.1 %collective-permute-start = (f32[69,3,128]{2,1,0:T(4,128)S(1)}, f32[69,3,128]{2,1,0:T(4,128)S(1)}, u32[]{:S(2)}, u32[]{:S(2)}) collective-permute-start(f32[69,3,128]{2,1,0:T(4,128)S(1)} %get-tuple-element.5), channel_id=1, source_target_pairs={{4,0},{8,4},{12,8},{16,12},{20,16},{24,20},{28,24},{5,1},{9,5},{13... | collective-permute-start | bytes 317960 | tf_op jit(solution)/shard_map/ppermute | solution.py:161
  17.5 7.4 %collective-permute-start.1 = (f32[69,3,128]{2,1,0:T(4,128)S(1)}, f32[69,3,128]{2,1,0:T(4,128)S(1)}, u32[]{:S(2)}, u32[]{:S(2)}) collective-permute-start(f32[69,3,128]{2,1,0:T(4,128)S(1)} %get-tuple-element.4), channel_id=1, source_target_pairs={{0,4},{4,8},{8,12},{12,16},{16,20},{20,24},{24,28},{1,5},{5,9},{9,... | collective-permute-start | bytes 317960 | tf_op jit(solution)/shard_map/ppermute | solution.py:160
  22.1 11.3 %copy-start.2 = (f32[69,3,128]{2,1,0:T(4,128)}, f32[69,3,128]{2,1,0:T(4,128)S(1)}, u32[]{:S(2)}) copy-start(f32[69,3,128]{2,1,0:T(4,128)S(1)} %collective-permute-done.high_ref) | copy-start | bytes 317956
  25.0 8.5 %copy-start.3 = (f32[69,3,128]{2,1,0:T(4,128)}, f32[69,3,128]{2,1,0:T(4,128)S(1)}, u32[]{:S(2)}) copy-start(f32[69,3,128]{2,1,0:T(4,128)S(1)} %collective-permute-done.1.low_ref) | copy-start | bytes 317956
  25.5 7.5 %collective-permute-start.2 = (f32[69,24,3]{0,1,2:T(8,128)S(1)}, f32[69,24,3]{0,1,2:T(8,128)S(1)}, u32[]{:S(2)}, u32[]{:S(2)}) collective-permute-start(f32[69,24,3]{0,1,2:T(8,128)S(1)} %get-tuple-element.11), channel_id=1, source_target_pairs={{1,0},{2,1},{3,2},{5,4},{6,5},{7,6},{9,8},{10,9},{11,10},{13,12},{... | collective-permute-start | bytes 59624 | tf_op jit(solution)/shard_map/ppermute | solution.py:217
  29.4 4.1 %collective-permute-start.3 = (f32[69,24,3]{0,1,2:T(8,128)S(1)}, f32[69,24,3]{0,1,2:T(8,128)S(1)}, u32[]{:S(2)}, u32[]{:S(2)}) collective-permute-start(f32[69,24,3]{0,1,2:T(8,128)S(1)} %get-tuple-element.10), channel_id=1, source_target_pairs={{0,1},{1,2},{2,3},{4,5},{5,6},{6,7},{8,9},{9,10},{10,11},{12,13},{... | collective-permute-start | bytes 59624 | tf_op jit(solution)/shard_map/ppermute | solution.py:216
  33.0 0.6 %copy-start.4 = (f32[69,24,3]{0,1,2:T(8,128)}, f32[69,24,3]{0,1,2:T(8,128)S(1)}, u32[]{:S(2)}) copy-start(f32[69,24,3]{0,1,2:T(8,128)S(1)} %collective-permute-done.2) | copy-start | bytes 59620
  33.5 0.6 %copy-start.5 = (f32[69,24,3]{0,1,2:T(8,128)}, f32[69,24,3]{0,1,2:T(8,128)S(1)}, u32[]{:S(2)}) copy-start(f32[69,24,3]{0,1,2:T(8,128)S(1)} %collective-permute-done.3) | copy-start | bytes 59620
  37.2 12.7 %copy-start.8 = (s32[8,3]{0,1:T(4,128)S(1)}, s32[8,3]{0,1:T(4,128)}, u32[]{:S(2)}) copy-start(s32[8,3]{0,1:T(4,128)} %param.12) | copy-start | bytes 292
  38.5 11.5 %all-to-all-start.1 = ((f32[8,3,128]{2,1,0:T(4,128)}), f32[8,3,128]{2,1,0:T(4,128)S(1)}, u32[]{:S(2)}, u32[]{:S(2)}) async-start(f32[8,3,128]{2,1,0:T(4,128)} %reshape.68), calls=%async_computation.1 | async-start | bytes 32768 | tf_op jit(solution)/shard_map/all_to_all | solution.py:229

commit v16 on v15

--- a/solution.py
+++ b/solution.py
@@ -117,7 +117,7 @@
         if not surface_only:
             out_ref[f, l] = value
         elif f == 2:
-            out_ref[...] = value
+            out_ref[...] = value.astype(out_ref.dtype)
 
     writers = [write_first, write_second]
     for repeat in range(STEPS):
@@ -136,10 +136,10 @@
     vmem = pl.BlockSpec(memory_space=pltpu.VMEM)
     operands = (diffusivity, coriolis, state, aux, high, low, north, south)
 
-    def call(surface_only, shape):
+    def call(surface_only, shape, dtype):
         return pl.pallas_call(
             functools.partial(stencil_kernel, surface_only=surface_only),
-            out_shape=jax.ShapeDtypeStruct(shape, jnp.float32),
+            out_shape=jax.ShapeDtypeStruct(shape, dtype),
             in_specs=[pl.BlockSpec(memory_space=pltpu.SMEM)] + [vmem] * 7,
             out_specs=vmem,
             scratch_shapes=[
@@ -149,7 +149,7 @@
             ],
         )(*operands)
 
-    return call(True, (rows, lanes)), call(False, out_shape)
+    return call(True, (rows, lanes), jnp.bfloat16), call(False, out_shape, jnp.float32)
 
 
 def shifted(block, axis, dim, width):
@@ -220,7 +220,7 @@
     latitude = (lat_start + offset).astype(jnp.float32)
     coriolis_wide = (coriolis_coef * (2.0 * (latitude + 0.5) / lat_total - 1.0))[None, :]
     top, state = run_steps(inner, aux, high, low, north, south, coriolis_wide, diffusivity, ocean_state.shape)
-    surface = top.astype(jnp.bfloat16)
+    surface = top
     pieces = jnp.einsum("tkra,tr->tka", remap_weights, surface, preferred_element_type=jnp.float32)
     slot_line = jnp.arange(slots, dtype=jnp.int32)
     to_slot = (tile_slots[:, :, None] == slot_line[None, None, :]).astype(jnp.float32)

time: 51.8 us -> 51.8 us (level)
  matrix products: 2.15 us -> 2.85 us
  other arithmetic: 2.74 us -> 2.04 us
    convert_element_type x1 -> x0, other arithmetic: 0.7 us -> none  [per_device(): surface = top.astype(jnp.bfloat16)]
    dot_general x1, matrix products: 0.38 us -> 1.07 us  [per_device(): jnp.einsum('tkra,tr->tka', remap_weights, surface, preferred_element_type...]
where the time goes in v16:
time: 51.8 us; the launch traced here: 50.8 us
  starting transfers between devices  22.9 us (44%)
  Pallas kernels  9.51 us (18%)
  local copies, waits for them, and re-layouts  7.44 us (14%)
  waiting for transfers between devices  5.33 us (10%)
  matrix products  2.85 us (6%)
  other arithmetic  2.04 us (4%)
  between operations  0.77 us (1%)
    pallas_call x2, Pallas kernels, call(): pl.pallas_call(functools.partial(stencil_kernel, surface_only=surface_onl...  9.51 us
    all_to_all x1, starting transfers between devices, per_device(): incoming = lax.all_to_all(outgoing, 'ox', 0, 0, tiled=True)  6.35 us
    all_to_all x1, starting transfers between devices, per_device(): returned = lax.all_to_all(per_slot, 'ox', 0, 0, tiled=True)  4.37 us
    ppermute x1, starting transfers between devices, shifted(): lax.ppermute(lax.slice_in_dim(block, size - width, None, axis=dim), axis,...  3.99 us
    ppermute x1, starting transfers between devices, per_device(): north = jnp.transpose(lax.ppermute(north_edge, 'oy', backward), (2, 1, 0))  3.81 us
    ppermute x1, starting transfers between devices, per_device(): south = jnp.transpose(lax.ppermute(south_edge, 'oy', forward), (2, 1, 0))  3.04 us
    ppermute x1, waiting for transfers between devices, shifted(): lax.ppermute(lax.slice_in_dim(block, size - width, None, axis=dim), axis,...  2.58 us
    unnamed x25, local copies, waits for them, and re-layouts  2.47 us
  transfers between devices with their start and end apart: 6, of which 3 were waited for; matrix products, arithmetic and copies ran while one was open for 10% of the time, Pallas kernels for 14%

profile of v16, /device:TPU:1, one launch (start us, length us, event | category | flops | bytes accessed | tf_op | source)
XLA Modules:
  0.0 50.8 jit_solution(16621322250364201234)
XLA Ops:
  0.6 0.0 copy-start
  0.6 1.5 %broadcast_in_dim.10 = bf16[8,4,10,128]{3,1,2,0:T(4,128)(2,1)} broadcast(bf16[4,10,128]{2,0,1:T(4,128)(2,1)} %param.8), dimensions={1,2,3} | broadcast | bytes 92160 | tf_op jit(solution)/shard_map/broadcast_in_dim | solution.py:187
  2.1 6.4 %all-to-all-start = ((bf16[8,4,10,128]{3,1,2,0:T(4,128)(2,1)}), bf16[8,4,10,128]{3,1,2,0:T(4,128)(2,1)S(1)}, u32[]{:S(2)}, u32[]{:S(2)}) async-start(bf16[8,4,10,128]{3,1,2,0:T(4,128)(2,1)} %broadcast_in_dim.10), calls=%async_computation | async-start | bytes 163840 | tf_op jit(solution)/shard_map/all_to_all | solution.py:188
  8.5 0.7 %compare_select_fusion.2 = s32[16,3]{0,1:T(4,128)S(1)} fusion(s32[16,3]{0,1:T(4,128)} %param.10), kind=kLoop, calls=%fused_computation.22 | loop fusion | flops 144 | bytes 384 | tf_op jit(solution)/shard_map/select_n | solution.py:190
  9.2 0.1 copy.40
  9.2 0.1 reshape.71
  9.4 0.8 %copy.39 = s32[8,3]{1,0:T(8,128)S(1)} copy(s32[8,3]{0,1:T(4,128)} %param.11) | data formatting | bytes 192 | tf_op args[3]
  10.1 0.1 reshape.67
  10.2 0.8 %gather_fusion = s32[48]{0:T(128)S(1)} fusion(s32[24]{0:T(128)S(1)} %reshape.67, s32[1024]{0:T(1024)S(1)} %pad_clamp_fusion), kind=kCustom, calls=%fused_computation | custom fusion | bytes 576 | tf_op jit(solution)/shard_map/gather | solution.py:190
  11.0 0.1 gather.9
  11.1 0.1 copy.41
  11.1 0.0 copy-done.6
  11.2 0.1 copy.44
  11.3 0.1 reshape.77
  11.4 0.1 pad.6.clone
  11.5 0.6 %fusion.19.cor_ref = f32[1,256]{1,0:T(1,128)} fusion(s32[]{:T(128)S(6)} %mul.16), kind=kLoop, calls=%fused_computation.40 | loop fusion | flops 2304 | bytes 1028 | tf_op jit(solution)/shard_map/mul | solution.py:221
  12.0 2.3 %all-to-all-done = bf16[8,4,10,128]{3,1,2,0:T(4,128)(2,1)S(1)} async-done(((bf16[8,4,10,128]{3,1,2,0:T(4,128)(2,1)}), bf16[8,4,10,128]{3,1,2,0:T(4,128)(2,1)S(1)}, u32[]{:S(2)}, u32[]{:S(2)}) %all-to-all-start) | async-done | bytes 81952 | tf_op jit(solution)/shard_map/all_to_all | solution.py:188
  14.3 0.9 %gather_fusion.1 = bf16[48,4,128]{2,1,0:T(4,128)(2,1)S(1)} fusion(bf16[8,4,10,128]{3,1,2,0:T(4,128)(2,1)S(1)} %all-to-all-done, s32[48]{0:T(128)S(1)} %reshape.77), kind=kCustom, calls=%fused_computation.1 | custom fusion | bytes 98688 | tf_op jit(solution)/shard_map/gather | solution.py:191
  15.2 0.6 %convolution_bitcast_fusion = f32[16,4,128]{2,1,0:T(4,128)S(1)} fusion(bf16[16,3,4,128]{3,2,1,0:T(4,128)(2,1)S(1)} %bitcast.34, bf16[16,3,128,128]{3,2,1,0:T(8,128)(2,1)S(1)} %copy-done), kind=kOutput, calls=%fused_computation.2 | convolution fusion | flops 6291456 | bytes 1654784 | tf_op jit(solution)/shard_map/tkfa,tkra->ftr/dot_general | solution.py:192
  15.9 0.1 pad_maximum_fusion
  15.9 0.1 fusion.21
  16.0 1.3 %collective-permute-start = (f32[69,3,128]{2,1,0:T(4,128)S(1)}, f32[69,3,128]{2,1,0:T(4,128)S(1)}, u32[]{:S(2)}, u32[]{:S(2)}) collective-permute-start(f32[69,3,128]{2,1,0:T(4,128)S(1)} %get-tuple-element.5), channel_id=1, source_target_pairs={{4,0},{8,4},{12,8},{16,12},{20,16},{24,20},{28,24},{5,1},{9,5},{13... | collective-permute-start | bytes 317960 | tf_op jit(solution)/shard_map/ppermute | solution.py:161
  17.3 0.2 fusion.20
  17.5 4.0 %collective-permute-start.1 = (f32[69,3,128]{2,1,0:T(4,128)S(1)}, f32[69,3,128]{2,1,0:T(4,128)S(1)}, u32[]{:S(2)}, u32[]{:S(2)}) collective-permute-start(f32[69,3,128]{2,1,0:T(4,128)S(1)} %get-tuple-element.4), channel_id=1, source_target_pairs={{0,4},{4,8},{8,12},{12,16},{16,20},{20,24},{24,28},{1,5},{5,9},{9,... | collective-permute-start | bytes 317960 | tf_op jit(solution)/shard_map/ppermute | solution.py:160
  21.5 0.3 copy.56
  21.8 0.3 copy.59
  22.1 0.1 fusion.22
  22.3 0.1 copy.57
  22.4 2.6 %collective-permute-done.1.low_ref = f32[69,3,128]{2,1,0:T(4,128)S(1)} collective-permute-done((f32[69,3,128]{2,1,0:T(4,128)S(1)}, f32[69,3,128]{2,1,0:T(4,128)S(1)}, u32[]{:S(2)}, u32[]{:S(2)}) %collective-permute-start.1) | collective-permute-done | bytes 106016 | tf_op jit(solution)/shard_map/ppermute | solution.py:160
  25.0 0.1 fusion.23
  25.1 0.1 copy.58
  25.2 0.1 copy.60
  25.3 0.1 copy.61
  25.5 0.1 pad_maximum_fusion.3
  25.5 3.8 %collective-permute-start.2 = (f32[69,24,3]{0,1,2:T(8,128)S(1)}, f32[69,24,3]{0,1,2:T(8,128)S(1)}, u32[]{:S(2)}, u32[]{:S(2)}) collective-permute-start(f32[69,24,3]{0,1,2:T(8,128)S(1)} %get-tuple-element.11), channel_id=1, source_target_pairs={{1,0},{2,1},{3,2},{5,4},{6,5},{7,6},{9,8},{10,9},{11,10},{13,12},{... | collective-permute-start | bytes 59624 | tf_op jit(solution)/shard_map/ppermute | solution.py:217
  29.4 3.0 %collective-permute-start.3 = (f32[69,24,3]{0,1,2:T(8,128)S(1)}, f32[69,24,3]{0,1,2:T(8,128)S(1)}, u32[]{:S(2)}, u32[]{:S(2)}) collective-permute-start(f32[69,24,3]{0,1,2:T(8,128)S(1)} %get-tuple-element.10), channel_id=1, source_target_pairs={{0,1},{1,2},{2,3},{4,5},{5,6},{6,7},{8,9},{9,10},{10,11},{12,13},{... | collective-permute-start | bytes 59624 | tf_op jit(solution)/shard_map/ppermute | solution.py:216
  32.4 0.6 %pad_maximum_fusion.1.aux_ref = f32[5,16,128]{2,1,0:T(8,128)} fusion(f32[1,16,128]{2,1,0:T(8,128)S(1)} %convert_bitcast_fusion, f32[4,16,128]{2,1,0:T(8,128)S(1)} %bitcast.33), kind=kLoop, calls=%fused_computation.6 | loop fusion | flops 10240 | bytes 81920 | tf_op jit(solution)/shard_map/concatenate | solution.py:198
  33.0 0.0 collective-permute-done.2
  33.0 0.4 collective-permute-done.3
  33.5 0.2 copy-done.4
  33.7 0.4 copy-done.5
  34.1 2.4 %shard_map.96 = bf16[16,128]{1,0:T(8,128)(2,1)} custom-call(f32[16]{0:T(128)} %diff_ref.3, f32[1,256]{1,0:T(1,128)} %fusion.19.cor_ref, f32[64,16,128]{2,1,0:T(8,128)} %bitcast.29, f32[5,16,128]{2,1,0:T(8,128)} %pad_maximum_fusion.1.aux_ref, f32[69,3,128]{2,1,0:T(4,128)} %copy-done.2, f32[69,3,128]{2,1,0:T(4,128)} %copy-done.3, f32[3,24,69]{2,1,0:T(8,128)} %bitcast.35, ...), custom_call_target="tpu_custom_call" | custom-call | tf_op jit(solution)/shard_map/pallas_call | solution.py:140
  36.5 1.1 %fusion.4 = f32[16,1,3,128]{3,1,2,0:T(1,128)S(1)} fusion(bf16[16,3,128,128]{3,2,1,0:T(8,128)(2,1)S(1)} %copy-done, bf16[16,128,1,1]{1,0,2,3:T(8,128)(2,1)} %bitcast.39), kind=kOutput, calls=%fused_computation.16 | convolution fusion | flops 1572864 | bytes 1601536 | tf_op jit(solution)/shard_map/tkra,tr->tka/dot_general | solution.py:224
  37.6 0.3 convolution_bitcast_fusion.1
  37.9 0.6 %reshape.68 = f32[8,3,128]{2,1,0:T(4,128)} reshape(f32[24,128]{1,0:T(8,128)S(1)} %convolution_bitcast_fusion.1) | data formatting | bytes 24576 | tf_op jit(solution)/shard_map/reshape | solution.py:228
  38.5 4.4 %all-to-all-start.1 = ((f32[8,3,128]{2,1,0:T(4,128)}), f32[8,3,128]{2,1,0:T(4,128)S(1)}, u32[]{:S(2)}, u32[]{:S(2)}) async-start(f32[8,3,128]{2,1,0:T(4,128)} %reshape.68), calls=%async_computation.1 | async-start | bytes 32768 | tf_op jit(solution)/shard_map/all_to_all | solution.py:229
  42.8 7.1 %shard_map.95 = f32[4,16,16,128]{3,2,1,0:T(8,128)} custom-call(f32[16]{0:T(128)} %diff_ref.3, f32[1,256]{1,0:T(1,128)} %fusion.19.cor_ref, f32[64,16,128]{2,1,0:T(8,128)} %bitcast.30, f32[5,16,128]{2,1,0:T(8,128)} %pad_maximum_fusion.1.aux_ref, f32[69,3,128]{2,1,0:T(4,128)} %copy-done.2, f32[69,3,128]{2,1,0:T(4,128)} %copy-done.3, f32[3,24,69]{2,1,0:T(8,128)} %bitcast.36, ...), custom_call_target="tpu_custom_call" | custom-call | tf_op jit(solution)/shard_map/pallas_call | solution.py:140
  49.9 0.9 %convolution_bitcast_fusion.2 = f32[10,128]{1,0:T(8,128)} fusion(f32[8,3,128]{2,1,0:T(4,128)S(1)} %all-to-all-done.1, s32[8,3]{0,1:T(4,128)S(1)} %copy-done.8), kind=kOutput, calls=%fused_computation.4 | convolution fusion | flops 368880 | bytes 17504 | tf_op jit(solution)/shard_map/isb,isa->ba/dot_general | solution.py:230
  (21 shorter events, 0.1 us)
Async XLA Ops:
  0.6 14.6 %copy-start = (bf16[16,3,128,128]{3,2,1,0:T(8,128)(2,1)S(1)}, bf16[16,3,128,128]{3,2,1,0:T(8,128)(2,1)}, u32[]{:S(2)}) copy-start(bf16[16,3,128,128]{3,2,1,0:T(8,128)(2,1)} %param.9) | copy-start | bytes 4718596
  2.1 12.2 %all-to-all-start = ((bf16[8,4,10,128]{3,1,2,0:T(4,128)(2,1)}), bf16[8,4,10,128]{3,1,2,0:T(4,128)(2,1)S(1)}, u32[]{:S(2)}, u32[]{:S(2)}) async-start(bf16[8,4,10,128]{3,1,2,0:T(4,128)(2,1)} %broadcast_in_dim.10), calls=%async_computation | async-start | bytes 163840 | tf_op jit(solution)/shard_map/all_to_all | solution.py:188
  10.2 1.0 %copy-start.7 = (s32[16,128]{1,0:T(8,128)S(1)}, s32[16,128]{1,0:T(8,128)}, u32[]{:S(2)}) copy-start(s32[16,128]{1,0:T(8,128)} %param.14) | copy-start | bytes 24580
  10.2 1.0 %copy-start.6 = (s32[16,3]{0,1:T(4,128)S(1)}, s32[16,3]{0,1:T(4,128)}, u32[]{:S(2)}) copy-start(s32[16,3]{0,1:T(4,128)} %param.10) | copy-start | bytes 580
  11.0 4.9 %copy-start.1 = (f32[4,16,16,128]{3,2,1,0:T(8,128)S(1)}, f32[4,16,16,128]{3,2,1,0:T(8,128)}, u32[]{:S(2)}) copy-start(f32[4,16,16,128]{3,2,1,0:T(8,128)} %param.13) | copy-start | bytes 1572868
  16.0 6.1 %collective-permute-start = (f32[69,3,128]{2,1,0:T(4,128)S(1)}, f32[69,3,128]{2,1,0:T(4,128)S(1)}, u32[]{:S(2)}, u32[]{:S(2)}) collective-permute-start(f32[69,3,128]{2,1,0:T(4,128)S(1)} %get-tuple-element.5), channel_id=1, source_target_pairs={{4,0},{8,4},{12,8},{16,12},{20,16},{24,20},{28,24},{5,1},{9,5},{13... | collective-permute-start | bytes 317960 | tf_op jit(solution)/shard_map/ppermute | solution.py:161
  17.5 7.4 %collective-permute-start.1 = (f32[69,3,128]{2,1,0:T(4,128)S(1)}, f32[69,3,128]{2,1,0:T(4,128)S(1)}, u32[]{:S(2)}, u32[]{:S(2)}) collective-permute-start(f32[69,3,128]{2,1,0:T(4,128)S(1)} %get-tuple-element.4), channel_id=1, source_target_pairs={{0,4},{4,8},{8,12},{12,16},{16,20},{20,24},{24,28},{1,5},{5,9},{9,... | collective-permute-start | bytes 317960 | tf_op jit(solution)/shard_map/ppermute | solution.py:160
  22.1 11.3 %copy-start.2 = (f32[69,3,128]{2,1,0:T(4,128)}, f32[69,3,128]{2,1,0:T(4,128)S(1)}, u32[]{:S(2)}) copy-start(f32[69,3,128]{2,1,0:T(4,128)S(1)} %collective-permute-done.high_ref) | copy-start | bytes 317956
  25.0 8.5 %copy-start.3 = (f32[69,3,128]{2,1,0:T(4,128)}, f32[69,3,128]{2,1,0:T(4,128)S(1)}, u32[]{:S(2)}) copy-start(f32[69,3,128]{2,1,0:T(4,128)S(1)} %collective-permute-done.1.low_ref) | copy-start | bytes 317956
  25.5 7.5 %collective-permute-start.2 = (f32[69,24,3]{0,1,2:T(8,128)S(1)}, f32[69,24,3]{0,1,2:T(8,128)S(1)}, u32[]{:S(2)}, u32[]{:S(2)}) collective-permute-start(f32[69,24,3]{0,1,2:T(8,128)S(1)} %get-tuple-element.11), channel_id=1, source_target_pairs={{1,0},{2,1},{3,2},{5,4},{6,5},{7,6},{9,8},{10,9},{11,10},{13,12},{... | collective-permute-start | bytes 59624 | tf_op jit(solution)/shard_map/ppermute | solution.py:217
  29.4 4.1 %collective-permute-start.3 = (f32[69,24,3]{0,1,2:T(8,128)S(1)}, f32[69,24,3]{0,1,2:T(8,128)S(1)}, u32[]{:S(2)}, u32[]{:S(2)}) collective-permute-start(f32[69,24,3]{0,1,2:T(8,128)S(1)} %get-tuple-element.10), channel_id=1, source_target_pairs={{0,1},{1,2},{2,3},{4,5},{5,6},{6,7},{8,9},{9,10},{10,11},{12,13},{... | collective-permute-start | bytes 59624 | tf_op jit(solution)/shard_map/ppermute | solution.py:216
  33.0 0.6 %copy-start.4 = (f32[69,24,3]{0,1,2:T(8,128)}, f32[69,24,3]{0,1,2:T(8,128)S(1)}, u32[]{:S(2)}) copy-start(f32[69,24,3]{0,1,2:T(8,128)S(1)} %collective-permute-done.2) | copy-start | bytes 59620
  33.5 0.6 %copy-start.5 = (f32[69,24,3]{0,1,2:T(8,128)}, f32[69,24,3]{0,1,2:T(8,128)S(1)}, u32[]{:S(2)}) copy-start(f32[69,24,3]{0,1,2:T(8,128)S(1)} %collective-permute-done.3) | copy-start | bytes 59620
  36.5 13.4 %copy-start.8 = (s32[8,3]{0,1:T(4,128)S(1)}, s32[8,3]{0,1:T(4,128)}, u32[]{:S(2)}) copy-start(s32[8,3]{0,1:T(4,128)} %param.12) | copy-start | bytes 292
  38.5 11.5 %all-to-all-start.1 = ((f32[8,3,128]{2,1,0:T(4,128)}), f32[8,3,128]{2,1,0:T(4,128)S(1)}, u32[]{:S(2)}, u32[]{:S(2)}) async-start(f32[8,3,128]{2,1,0:T(4,128)} %reshape.68), calls=%async_computation.1 | async-start | bytes 32768 | tf_op jit(solution)/shard_map/all_to_all | solution.py:229

commit v17 on v16

--- a/solution.py
+++ b/solution.py
@@ -21,12 +21,12 @@
 
 
 def stencil_kernel(
-    diff_ref, cor_ref, state_ref, aux_ref, high_ref, low_ref, north_ref, south_ref,
-    out_ref, source, first, second, surface_only,
+    diff_ref, cor_ref, state_ref, high_ref, low_ref, north_ref, south_ref,
+    out_ref, source, first, second, surface_only, levels,
 ):
     fields = 4
-    channels, rows, lanes = state_ref.shape
-    levels = channels // fields
+    channels = fields * levels
+    rows, lanes = state_ref.shape[1], state_ref.shape[2]
     tall, wide = source.shape[1], source.shape[2]
     width = high_ref.shape[1]
 
@@ -51,8 +51,8 @@
     else:
         for ch in range(channels):
             assemble(ch, state_ref[ch])
-    for index in range(aux_ref.shape[0]):
-        assemble(channels + index, aux_ref[index])
+    for index in range(channels, state_ref.shape[0]):
+        assemble(index, state_ref[index])
 
     def aux(index):
         return source[channels + index]
@@ -127,25 +127,26 @@
         one_step(read, write, repeat == STEPS - 1, count)
 
 
-def run_steps(state, aux, high, low, north, south, coriolis, diffusivity, out_shape):
-    channels = state.shape[0] + aux.shape[0]
+def run_steps(state, high, low, north, south, coriolis, diffusivity, out_shape):
+    channels = state.shape[0]
+    fields, levels = out_shape[0], out_shape[1]
     rows, lanes = state.shape[1], state.shape[2]
     width = high.shape[1]
     tall = -(-(rows + 2 * width) // 8) * 8
     wide = -(-(lanes + 2 * width) // 128) * 128
     vmem = pl.BlockSpec(memory_space=pltpu.VMEM)
-    operands = (diffusivity, coriolis, state, aux, high, low, north, south)
+    operands = (diffusivity, coriolis, state, high, low, north, south)
 
     def call(surface_only, shape, dtype):
         return pl.pallas_call(
-            functools.partial(stencil_kernel, surface_only=surface_only),
+            functools.partial(stencil_kernel, surface_only=surface_only, levels=levels),
             out_shape=jax.ShapeDtypeStruct(shape, dtype),
-            in_specs=[pl.BlockSpec(memory_space=pltpu.SMEM)] + [vmem] * 7,
+            in_specs=[pl.BlockSpec(memory_space=pltpu.SMEM)] + [vmem] * 6,
             out_specs=vmem,
             scratch_shapes=[
                 pltpu.VMEM((channels, tall, wide), jnp.float32),
-                pltpu.VMEM((state.shape[0], tall, wide), jnp.float32),
-                pltpu.VMEM((state.shape[0], tall, wide), jnp.float32),
+                pltpu.VMEM((fields * levels, tall, wide), jnp.float32),
+                pltpu.VMEM((fields * levels, tall, wide), jnp.float32),
             ],
         )(*operands)
 
@@ -219,7 +220,7 @@
     offset = jnp.where(lane < lat_cells + STEPS, lane, lane - wide)
     latitude = (lat_start + offset).astype(jnp.float32)
     coriolis_wide = (coriolis_coef * (2.0 * (latitude + 0.5) / lat_total - 1.0))[None, :]
-    top, state = run_steps(inner, aux, high, low, north, south, coriolis_wide, diffusivity, ocean_state.shape)
+    top, state = run_steps(packed, high, low, north, south, coriolis_wide, diffusivity, ocean_state.shape)
     surface = top
     pieces = jnp.einsum("tkra,tr->tka", remap_weights, surface, preferred_element_type=jnp.float32)
     slot_line = jnp.arange(slots, dtype=jnp.int32)

time: 51.8 us -> 53.4 us (1.031)
  local copies, waits for them, and re-layouts: 7.44 us -> 9.34 us
    slice x1, local copies, waits for them, and re-layouts: 0.05 us -> 0.84 us  [shifted(): lax.slice_in_dim(block, size - width, None, axis=dim)]
    concatenate x1, other arithmetic: 0.08 us -> 0.74 us  [per_device(): jnp.concatenate([packed[:, :, -STEPS:], high[:, :, -STEPS:], gap, low[:,...]
    concatenate x1 -> x0, other arithmetic: 0.61 us -> none  [per_device(): aux = jnp.concatenate([forcing, wetness[None]], axis=0)]
    unnamed x25 -> x31, local copies, waits for them, and re-layouts: 2.47 us -> 3.07 us
  transfers between devices with their start and end apart: 6 -> 6, of which waited for: 3 -> 3; matrix products, arithmetic and copies ran while one was open for 10% -> 11% of each run, Pallas kernels for 14% -> 13%
where the time goes in v17:
time: 53.4 us; the launch traced here: 52.4 us
  starting transfers between devices  22.7 us (43%)
  Pallas kernels  9.48 us (18%)
  local copies, waits for them, and re-layouts  9.34 us (17%)
  waiting for transfers between devices  5.13 us (10%)
  matrix products  2.85 us (5%)
  other arithmetic  2.11 us (4%)
  between operations  0.77 us (1%)
    pallas_call x2, Pallas kernels, call(): pl.pallas_call(functools.partial(stencil_kernel, surface_only=surface_onl...  9.48 us
    all_to_all x1, starting transfers between devices, per_device(): incoming = lax.all_to_all(outgoing, 'ox', 0, 0, tiled=True)  6.35 us
    all_to_all x1, starting transfers between devices, per_device(): returned = lax.all_to_all(per_slot, 'ox', 0, 0, tiled=True)  4.26 us
    ppermute x1, starting transfers between devices, shifted(): lax.ppermute(lax.slice_in_dim(block, size - width, None, axis=dim), axis,...  3.99 us
    ppermute x1, starting transfers between devices, per_device(): north = jnp.transpose(lax.ppermute(north_edge, 'oy', backward), (2, 1, 0))  3.8 us
    unnamed x31, local copies, waits for them, and re-layouts  3.07 us
    ppermute x1, starting transfers between devices, per_device(): south = jnp.transpose(lax.ppermute(south_edge, 'oy', forward), (2, 1, 0))  3.05 us
    all_to_all x1, waiting for transfers between devices, per_device(): incoming = lax.all_to_all(outgoing, 'ox', 0, 0, tiled=True)  2.39 us
  transfers between devices with their start and end apart: 6, of which 3 were waited for; matrix products, arithmetic and copies ran while one was open for 11% of the time, Pallas kernels for 13%

profile of v17, /device:TPU:1, one launch (start us, length us, event | category | flops | bytes accessed | tf_op | source)
XLA Modules:
  0.0 52.4 jit_solution(3114981668050945272)
XLA Ops:
  0.6 0.0 copy-start
  0.6 1.5 %broadcast_in_dim.10 = bf16[8,4,10,128]{3,1,2,0:T(4,128)(2,1)} broadcast(bf16[4,10,128]{2,0,1:T(4,128)(2,1)} %param.8), dimensions={1,2,3} | broadcast | bytes 92160 | tf_op jit(solution)/shard_map/broadcast_in_dim | solution.py:188
  2.1 6.4 %all-to-all-start = ((bf16[8,4,10,128]{3,1,2,0:T(4,128)(2,1)}), bf16[8,4,10,128]{3,1,2,0:T(4,128)(2,1)S(1)}, u32[]{:S(2)}, u32[]{:S(2)}) async-start(bf16[8,4,10,128]{3,1,2,0:T(4,128)(2,1)} %broadcast_in_dim.10), calls=%async_computation | async-start | bytes 163840 | tf_op jit(solution)/shard_map/all_to_all | solution.py:189
  8.5 0.7 %compare_select_fusion.2 = s32[16,3]{0,1:T(4,128)S(1)} fusion(s32[16,3]{0,1:T(4,128)} %param.10), kind=kLoop, calls=%fused_computation.21 | loop fusion | flops 144 | bytes 384 | tf_op jit(solution)/shard_map/select_n | solution.py:191
  9.2 0.1 copy.40
  9.2 0.1 reshape.71
  9.4 0.8 %copy.39 = s32[8,3]{1,0:T(8,128)S(1)} copy(s32[8,3]{0,1:T(4,128)} %param.11) | data formatting | bytes 192 | tf_op args[3]
  10.1 0.1 reshape.67
  10.2 0.8 %gather_fusion = s32[48]{0:T(128)S(1)} fusion(s32[24]{0:T(128)S(1)} %reshape.67, s32[1024]{0:T(1024)S(1)} %pad_clamp_fusion), kind=kCustom, calls=%fused_computation | custom fusion | bytes 576 | tf_op jit(solution)/shard_map/gather | solution.py:191
  11.0 0.1 gather.9
  11.1 0.1 copy.41
  11.2 0.1 copy.44
  11.3 0.1 reshape.77
  11.4 0.6 %pad.6.clone = f32[24]{0:T(128)} pad(f32[2]{0:T(128)S(1)} %broadcast_in_dim.28, f32[]{:T(128)} %constant.59), padding=19_3 | pad | bytes 108 | tf_op jit(solution)/shard_map/concatenate | solution.py:211
  12.0 2.4 %all-to-all-done = bf16[8,4,10,128]{3,1,2,0:T(4,128)(2,1)S(1)} async-done(((bf16[8,4,10,128]{3,1,2,0:T(4,128)(2,1)}), bf16[8,4,10,128]{3,1,2,0:T(4,128)(2,1)S(1)}, u32[]{:S(2)}, u32[]{:S(2)}) %all-to-all-start) | async-done | bytes 81952 | tf_op jit(solution)/shard_map/all_to_all | solution.py:189
  14.3 0.9 %gather_fusion.1 = bf16[48,4,128]{2,1,0:T(4,128)(2,1)S(1)} fusion(bf16[8,4,10,128]{3,1,2,0:T(4,128)(2,1)S(1)} %all-to-all-done, s32[48]{0:T(128)S(1)} %reshape.77), kind=kCustom, calls=%fused_computation.1 | custom fusion | bytes 98688 | tf_op jit(solution)/shard_map/gather | solution.py:192
  15.2 0.6 %convolution_bitcast_fusion = f32[16,4,128]{2,1,0:T(4,128)S(1)} fusion(bf16[16,3,4,128]{3,2,1,0:T(4,128)(2,1)S(1)} %bitcast.30, bf16[16,3,128,128]{3,2,1,0:T(8,128)(2,1)S(1)} %copy-done), kind=kOutput, calls=%fused_computation.2 | convolution fusion | flops 6291456 | bytes 1654784 | tf_op jit(solution)/shard_map/tkfa,tkra->ftr/dot_general | solution.py:193
  15.9 0.1 pad_maximum_fusion.state_ref
  16.0 0.8 %fusion.21 = (f32[69,3,128]{2,1,0:T(4,128)}, f32[69,3,128]{2,1,0:T(4,128)}) fusion(f32[69,16,128]{2,1,0:T(8,128)S(1)} %pad_maximum_fusion.state_ref), kind=kLoop, calls=%fused_computation.41 | loop fusion | bytes 423936 | tf_op jit(solution)/shard_map/slice | solution.py:161
  16.8 1.3 %collective-permute-start = (f32[69,3,128]{2,1,0:T(4,128)}, f32[69,3,128]{2,1,0:T(4,128)S(1)}, u32[]{:S(2)}, u32[]{:S(2)}) collective-permute-start(f32[69,3,128]{2,1,0:T(4,128)} %get-tuple-element.5), channel_id=1, source_target_pairs={{4,0},{8,4},{12,8},{16,12},{20,16},{24,20},{28,24},{5,1},{9,5},{13... | collective-permute-start | bytes 317960 | tf_op jit(solution)/shard_map/ppermute | solution.py:162
  18.1 0.2 fusion.20
  18.3 4.0 %collective-permute-start.1 = (f32[69,3,128]{2,1,0:T(4,128)}, f32[69,3,128]{2,1,0:T(4,128)S(1)}, u32[]{:S(2)}, u32[]{:S(2)}) collective-permute-start(f32[69,3,128]{2,1,0:T(4,128)} %get-tuple-element.4), channel_id=1, source_target_pairs={{0,4},{4,8},{8,12},{12,16},{16,20},{20,24},{24,28},{1,5},{5,9},{9,... | collective-permute-start | bytes 317960 | tf_op jit(solution)/shard_map/ppermute | solution.py:161
  22.3 0.9 %copy.56 = f32[69,16,3]{0,1,2:T(8,128)} copy(f32[69,16,3]{2,1,0:T(8,128)S(1)} %get-tuple-element.3) | data formatting | bytes 26496
  23.2 0.3 copy.59
  23.5 0.0 collective-permute-done.high_ref
  23.5 0.1 fusion.22
  23.7 0.1 copy.57
  23.8 2.3 %collective-permute-done.1.low_ref = f32[69,3,128]{2,1,0:T(4,128)S(1)} collective-permute-done((f32[69,3,128]{2,1,0:T(4,128)}, f32[69,3,128]{2,1,0:T(4,128)S(1)}, u32[]{:S(2)}, u32[]{:S(2)}) %collective-permute-start.1) | collective-permute-done | bytes 106016 | tf_op jit(solution)/shard_map/ppermute | solution.py:161
  26.1 0.1 fusion.23
  26.2 0.0 copy-start.9
  26.2 0.1 copy.58
  26.3 0.1 copy.60
  26.4 0.1 copy.61
  26.6 0.7 %pad_maximum_fusion.2 = (f32[69,24,3]{0,1,2:T(8,128)S(1)}, f32[69,24,3]{0,1,2:T(8,128)S(1)}) fusion(f32[69,3,3]{0,1,2:T(4,128)S(1)} %copy.61, f32[69,3,3]{0,1,2:T(4,128)S(1)} %copy.60, f32[69,16,3]{0,1,2:T(8,128)S(1)} %copy.59, f32[24]{0:T(128)} %pad.6.clone, f32[69,3,3]{0,1,2:T(4,128)S(1)} %copy.58, f32[69,3,3]{0,1,2:T(4,128)S(1)} %copy.57, ...), kind=kLoop, calls=%fused_computation.7 | loop fusion | flops 29808 | bytes 76272 | tf_op jit(solution)/shard_map/concatenate | solution.py:208
  27.3 3.8 %collective-permute-start.2 = (f32[69,24,3]{0,1,2:T(8,128)S(1)}, f32[69,24,3]{0,1,2:T(8,128)S(1)}, u32[]{:S(2)}, u32[]{:S(2)}) collective-permute-start(f32[69,24,3]{0,1,2:T(8,128)S(1)} %get-tuple-element.11), channel_id=1, source_target_pairs={{1,0},{2,1},{3,2},{5,4},{6,5},{7,6},{9,8},{10,9},{11,10},{13,12},{... | collective-permute-start | bytes 59624 | tf_op jit(solution)/shard_map/ppermute | solution.py:218
  31.1 3.0 %collective-permute-start.3 = (f32[69,24,3]{0,1,2:T(8,128)S(1)}, f32[69,24,3]{0,1,2:T(8,128)S(1)}, u32[]{:S(2)}, u32[]{:S(2)}) collective-permute-start(f32[69,24,3]{0,1,2:T(8,128)S(1)} %get-tuple-element.10), channel_id=1, source_target_pairs={{0,1},{1,2},{2,3},{4,5},{5,6},{6,7},{8,9},{9,10},{10,11},{12,13},{... | collective-permute-start | bytes 59624 | tf_op jit(solution)/shard_map/ppermute | solution.py:217
  34.2 0.6 %fusion.19.cor_ref = f32[1,256]{1,0:T(1,128)} fusion(s32[]{:T(128)S(6)} %mul.16), kind=kLoop, calls=%fused_computation.39 | loop fusion | flops 2304 | bytes 1028 | tf_op jit(solution)/shard_map/mul | solution.py:222
  34.8 0.4 collective-permute-done.3
  35.2 0.2 copy-done.5
  35.4 0.4 copy-done.6
  35.8 2.4 %shard_map.96 = bf16[16,128]{1,0:T(8,128)(2,1)} custom-call(f32[16]{0:T(128)} %diff_ref.3, f32[1,256]{1,0:T(1,128)} %fusion.19.cor_ref, f32[69,16,128]{2,1,0:T(8,128)} %copy-done.1, f32[69,3,128]{2,1,0:T(4,128)} %copy-done.2, f32[69,3,128]{2,1,0:T(4,128)} %copy-done.3, f32[3,24,69]{2,1,0:T(8,128)} %bitcast.31, f32[3,24,69]{2,1,0:T(8,128)} %bitcast.33), custom_call_target="tpu_custom_call" | custom-call | tf_op jit(solution)/shard_map/pallas_call | solution.py:141
  38.2 1.1 %fusion.4 = f32[16,1,3,128]{3,1,2,0:T(1,128)S(1)} fusion(bf16[16,3,128,128]{3,2,1,0:T(8,128)(2,1)S(1)} %copy-done, bf16[16,128,1,1]{1,0,2,3:T(8,128)(2,1)} %bitcast.36), kind=kOutput, calls=%fused_computation.15 | convolution fusion | flops 1572864 | bytes 1601536 | tf_op jit(solution)/shard_map/tkra,tr->tka/dot_general | solution.py:225
  39.3 0.3 convolution_bitcast_fusion.1
  39.6 0.6 %reshape.68 = f32[8,3,128]{2,1,0:T(4,128)} reshape(f32[24,128]{1,0:T(8,128)S(1)} %convolution_bitcast_fusion.1) | data formatting | bytes 24576 | tf_op jit(solution)/shard_map/reshape | solution.py:229
  40.2 4.3 %all-to-all-start.1 = ((f32[8,3,128]{2,1,0:T(4,128)}), f32[8,3,128]{2,1,0:T(4,128)S(1)}, u32[]{:S(2)}, u32[]{:S(2)}) async-start(f32[8,3,128]{2,1,0:T(4,128)} %reshape.68), calls=%async_computation.1 | async-start | bytes 32768 | tf_op jit(solution)/shard_map/all_to_all | solution.py:230
  44.5 7.1 %shard_map.95 = f32[4,16,16,128]{3,2,1,0:T(8,128)} custom-call(f32[16]{0:T(128)} %diff_ref.3, f32[1,256]{1,0:T(1,128)} %fusion.19.cor_ref, f32[69,16,128]{2,1,0:T(8,128)} %copy-done.1, f32[69,3,128]{2,1,0:T(4,128)} %copy-done.2, f32[69,3,128]{2,1,0:T(4,128)} %copy-done.3, f32[3,24,69]{2,1,0:T(8,128)} %bitcast.32, f32[3,24,69]{2,1,0:T(8,128)} %bitcast.34), custom_call_target="tpu_custom_call" | custom-call | tf_op jit(solution)/shard_map/pallas_call | solution.py:141
  51.5 0.0 all-to-all-done.1
  51.5 0.9 %convolution_bitcast_fusion.2 = f32[10,128]{1,0:T(8,128)} fusion(f32[8,3,128]{2,1,0:T(4,128)S(1)} %all-to-all-done.1, s32[8,3]{0,1:T(4,128)S(1)} %copy-done.11), kind=kOutput, calls=%fused_computation.4 | convolution fusion | flops 368880 | bytes 17504 | tf_op jit(solution)/shard_map/isb,isa->ba/dot_general | solution.py:231
  (26 shorter events, 0.1 us)
Async XLA Ops:
  0.6 14.6 %copy-start = (bf16[16,3,128,128]{3,2,1,0:T(8,128)(2,1)S(1)}, bf16[16,3,128,128]{3,2,1,0:T(8,128)(2,1)}, u32[]{:S(2)}) copy-start(bf16[16,3,128,128]{3,2,1,0:T(8,128)(2,1)} %param.9) | copy-start | bytes 4718596
  2.1 12.2 %all-to-all-start = ((bf16[8,4,10,128]{3,1,2,0:T(4,128)(2,1)}), bf16[8,4,10,128]{3,1,2,0:T(4,128)(2,1)S(1)}, u32[]{:S(2)}, u32[]{:S(2)}) async-start(bf16[8,4,10,128]{3,1,2,0:T(4,128)(2,1)} %broadcast_in_dim.10), calls=%async_computation | async-start | bytes 163840 | tf_op jit(solution)/shard_map/all_to_all | solution.py:189
  10.2 1.0 %copy-start.8 = (s32[16,3]{0,1:T(4,128)S(1)}, s32[16,3]{0,1:T(4,128)}, u32[]{:S(2)}) copy-start(s32[16,3]{0,1:T(4,128)} %param.10) | copy-start | bytes 580
  10.2 1.8 %copy-start.10 = (s32[16,128]{1,0:T(8,128)S(1)}, s32[16,128]{1,0:T(8,128)}, u32[]{:S(2)}) copy-start(s32[16,128]{1,0:T(8,128)} %param.14) | copy-start | bytes 24580
  11.0 4.9 %copy-start.4 = (f32[4,16,16,128]{3,2,1,0:T(8,128)S(1)}, f32[4,16,16,128]{3,2,1,0:T(8,128)}, u32[]{:S(2)}) copy-start(f32[4,16,16,128]{3,2,1,0:T(8,128)} %param.13) | copy-start | bytes 1572868
  15.9 7.3 %copy-start.1 = (f32[69,16,128]{2,1,0:T(8,128)}, f32[69,16,128]{2,1,0:T(8,128)S(1)}, u32[]{:S(2)}) copy-start(f32[69,16,128]{2,1,0:T(8,128)S(1)} %pad_maximum_fusion.state_ref) | copy-start | bytes 1695748
  16.8 6.7 %collective-permute-start = (f32[69,3,128]{2,1,0:T(4,128)}, f32[69,3,128]{2,1,0:T(4,128)S(1)}, u32[]{:S(2)}, u32[]{:S(2)}) collective-permute-start(f32[69,3,128]{2,1,0:T(4,128)} %get-tuple-element.5), channel_id=1, source_target_pairs={{4,0},{8,4},{12,8},{16,12},{20,16},{24,20},{28,24},{5,1},{9,5},{13... | collective-permute-start | bytes 317960 | tf_op jit(solution)/shard_map/ppermute | solution.py:162
  18.3 7.8 %collective-permute-start.1 = (f32[69,3,128]{2,1,0:T(4,128)}, f32[69,3,128]{2,1,0:T(4,128)S(1)}, u32[]{:S(2)}, u32[]{:S(2)}) collective-permute-start(f32[69,3,128]{2,1,0:T(4,128)} %get-tuple-element.4), channel_id=1, source_target_pairs={{0,4},{4,8},{8,12},{12,16},{16,20},{20,24},{24,28},{1,5},{5,9},{9,... | collective-permute-start | bytes 317960 | tf_op jit(solution)/shard_map/ppermute | solution.py:161
  23.2 3.4 %copy-start.7 = (f32[69,16,3]{0,1,2:T(8,128)S(1)}, f32[69,16,3]{0,1,2:T(8,128)}, u32[]{:S(2)}) copy-start(f32[69,16,3]{0,1,2:T(8,128)} %copy.56) | copy-start | bytes 39748
  23.5 11.7 %copy-start.2 = (f32[69,3,128]{2,1,0:T(4,128)}, f32[69,3,128]{2,1,0:T(4,128)S(1)}, u32[]{:S(2)}) copy-start(f32[69,3,128]{2,1,0:T(4,128)S(1)} %collective-permute-done.high_ref) | copy-start | bytes 317956
  26.1 9.2 %copy-start.3 = (f32[69,3,128]{2,1,0:T(4,128)}, f32[69,3,128]{2,1,0:T(4,128)S(1)}, u32[]{:S(2)}) copy-start(f32[69,3,128]{2,1,0:T(4,128)S(1)} %collective-permute-done.1.low_ref) | copy-start | bytes 317956
  26.2 13.1 %copy-start.9 = (s32[16,3]{0,1:T(4,128)S(1)}, s32[16,3]{0,1:T(4,128)}, u32[]{:S(2)}) copy-start(s32[16,3]{0,1:T(4,128)} %param.10) | copy-start | bytes 580
  27.3 7.5 %collective-permute-start.2 = (f32[69,24,3]{0,1,2:T(8,128)S(1)}, f32[69,24,3]{0,1,2:T(8,128)S(1)}, u32[]{:S(2)}, u32[]{:S(2)}) collective-permute-start(f32[69,24,3]{0,1,2:T(8,128)S(1)} %get-tuple-element.11), channel_id=1, source_target_pairs={{1,0},{2,1},{3,2},{5,4},{6,5},{7,6},{9,8},{10,9},{11,10},{13,12},{... | collective-permute-start | bytes 59624 | tf_op jit(solution)/shard_map/ppermute | solution.py:218
  31.1 4.1 %collective-permute-start.3 = (f32[69,24,3]{0,1,2:T(8,128)S(1)}, f32[69,24,3]{0,1,2:T(8,128)S(1)}, u32[]{:S(2)}, u32[]{:S(2)}) collective-permute-start(f32[69,24,3]{0,1,2:T(8,128)S(1)} %get-tuple-element.10), channel_id=1, source_target_pairs={{0,1},{1,2},{2,3},{4,5},{5,6},{6,7},{8,9},{9,10},{10,11},{12,13},{... | collective-permute-start | bytes 59624 | tf_op jit(solution)/shard_map/ppermute | solution.py:217
  34.8 0.6 %copy-start.5 = (f32[69,24,3]{0,1,2:T(8,128)}, f32[69,24,3]{0,1,2:T(8,128)S(1)}, u32[]{:S(2)}) copy-start(f32[69,24,3]{0,1,2:T(8,128)S(1)} %collective-permute-done.2) | copy-start | bytes 59620
  35.2 0.6 %copy-start.6 = (f32[69,24,3]{0,1,2:T(8,128)}, f32[69,24,3]{0,1,2:T(8,128)S(1)}, u32[]{:S(2)}) copy-start(f32[69,24,3]{0,1,2:T(8,128)S(1)} %collective-permute-done.3) | copy-start | bytes 59620
  38.2 13.3 %copy-start.11 = (s32[8,3]{0,1:T(4,128)S(1)}, s32[8,3]{0,1:T(4,128)}, u32[]{:S(2)}) copy-start(s32[8,3]{0,1:T(4,128)} %param.12) | copy-start | bytes 292
  40.2 11.3 %all-to-all-start.1 = ((f32[8,3,128]{2,1,0:T(4,128)}), f32[8,3,128]{2,1,0:T(4,128)S(1)}, u32[]{:S(2)}, u32[]{:S(2)}) async-start(f32[8,3,128]{2,1,0:T(4,128)} %reshape.68), calls=%async_computation.1 | async-start | bytes 32768 | tf_op jit(solution)/shard_map/all_to_all | solution.py:230

commit v18 on v16

--- a/solution.py
+++ b/solution.py
@@ -222,13 +222,17 @@
     top, state = run_steps(inner, aux, high, low, north, south, coriolis_wide, diffusivity, ocean_state.shape)
     surface = top
     pieces = jnp.einsum("tkra,tr->tka", remap_weights, surface, preferred_element_type=jnp.float32)
-    slot_line = jnp.arange(slots, dtype=jnp.int32)
-    to_slot = (tile_slots[:, :, None] == slot_line[None, None, :]).astype(jnp.float32)
+    room = -(-capacity // 8) * 8
+    slot_of = (tile_slots // capacity) * room + tile_slots % capacity
+    slot_line = jnp.arange(owners * room, dtype=jnp.int32)
+    to_slot = (slot_of[:, :, None] == slot_line[None, None, :]).astype(jnp.float32)
     per_slot = jnp.einsum("tks,tka->sa", to_slot, pieces, precision=lax.Precision.HIGHEST)
-    per_slot = per_slot.reshape(owners, capacity, block_width)
+    per_slot = per_slot.reshape(owners, room, block_width)
     returned = lax.all_to_all(per_slot, "ox", 0, 0, tiled=True)
+    wide_send = jnp.pad(send_blocks, ((0, 0), (0, room - capacity)), constant_values=-1)
+    to_room = wide_send[:, :, None] == block_line[None, None, :]
     atmos_surface = jnp.einsum(
-        "isb,isa->ba", to_block.astype(jnp.float32), returned, precision=lax.Precision.HIGHEST
+        "isb,isa->ba", to_room.astype(jnp.float32), returned, precision=lax.Precision.HIGHEST
     )
     return (state, atmos_surface)
 

time: 51.8 us -> 51.9 us (level)
  matrix products: 2.85 us -> 3.47 us
  local copies, waits for them, and re-layouts: 7.44 us -> 6.9 us
    add x0 -> x1, other arithmetic: none -> 0.7 us  [per_device(): slot_of = tile_slots // capacity * room + tile_slots % capacity]
    select_n x1 -> x0, other arithmetic: 0.68 us -> none  [per_device(): block_of = need_blocks.reshape(-1)[tile_slots]]
    dot_general x1, matrix products: 0.27 us -> 0.9 us  [per_device(): jnp.einsum('tks,tka->sa', to_slot, pieces, precision=lax.Precision.HIGHEST)]
    reshape x1 -> x0, local copies, waits for them, and re-layouts: 0.62 us -> none  [per_device(): per_slot = per_slot.reshape(owners, capacity, block_width)]
    unnamed x25 -> x26, local copies, waits for them, and re-layouts: 2.47 us -> 2.54 us
where the time goes in v18:
time: 51.9 us; the launch traced here: 50.9 us
  starting transfers between devices  22.9 us (44%)
  Pallas kernels  9.51 us (18%)
  local copies, waits for them, and re-layouts  6.9 us (13%)
  waiting for transfers between devices  5.33 us (10%)
  matrix products  3.47 us (7%)
  other arithmetic  2.04 us (4%)
  between operations  0.77 us (1%)
    pallas_call x2, Pallas kernels, call(): pl.pallas_call(functools.partial(stencil_kernel, surface_only=surface_onl...  9.51 us
    all_to_all x1, starting transfers between devices, per_device(): incoming = lax.all_to_all(outgoing, 'ox', 0, 0, tiled=True)  6.35 us
    all_to_all x1, starting transfers between devices, per_device(): returned = lax.all_to_all(per_slot, 'ox', 0, 0, tiled=True)  4.37 us
    ppermute x1, starting transfers between devices, shifted(): lax.ppermute(lax.slice_in_dim(block, size - width, None, axis=dim), axis,...  3.99 us
    ppermute x1, starting transfers between devices, per_device(): north = jnp.transpose(lax.ppermute(north_edge, 'oy', backward), (2, 1, 0))  3.81 us
    ppermute x1, starting transfers between devices, per_device(): south = jnp.transpose(lax.ppermute(south_edge, 'oy', forward), (2, 1, 0))  3.05 us
    ppermute x1, waiting for transfers between devices, shifted(): lax.ppermute(lax.slice_in_dim(block, size - width, None, axis=dim), axis,...  2.58 us
    unnamed x26, local copies, waits for them, and re-layouts  2.54 us
  transfers between devices with their start and end apart: 6, of which 3 were waited for; matrix products, arithmetic and copies ran while one was open for 10% of the time, Pallas kernels for 14%

profile of v18, /device:TPU:1, one launch (start us, length us, event | category | flops | bytes accessed | tf_op | source)
XLA Modules:
  0.0 50.9 jit_solution(14718728650008268872)
XLA Ops:
  0.6 0.0 copy-start
  0.6 1.5 %broadcast_in_dim.10 = bf16[8,4,10,128]{3,1,2,0:T(4,128)(2,1)} broadcast(bf16[4,10,128]{2,0,1:T(4,128)(2,1)} %param.8), dimensions={1,2,3} | broadcast | bytes 92160 | tf_op jit(solution)/shard_map/broadcast_in_dim | solution.py:187
  2.1 6.4 %all-to-all-start = ((bf16[8,4,10,128]{3,1,2,0:T(4,128)(2,1)}), bf16[8,4,10,128]{3,1,2,0:T(4,128)(2,1)S(1)}, u32[]{:S(2)}, u32[]{:S(2)}) async-start(bf16[8,4,10,128]{3,1,2,0:T(4,128)(2,1)} %broadcast_in_dim.10), calls=%async_computation | async-start | bytes 163840 | tf_op jit(solution)/shard_map/all_to_all | solution.py:188
  8.5 0.7 %fusion.6 = (s32[16,3]{0,1:T(4,128)S(1)}, s32[16,3]{0,1:T(4,128)S(1)}) fusion(s32[16,3]{0,1:T(4,128)} %param.10), kind=kLoop, calls=%fused_computation.26 | loop fusion | flops 816 | bytes 576 | tf_op jit(solution)/shard_map/add | solution.py:226
  9.2 0.1 copy.26
  9.3 0.1 reshape.71
  9.4 0.8 %copy.25 = s32[8,3]{1,0:T(8,128)S(1)} copy(s32[8,3]{0,1:T(4,128)} %param.11) | data formatting | bytes 192 | tf_op args[3]
  10.1 0.1 reshape.67
  10.2 0.8 %gather_fusion = s32[48]{0:T(128)S(1)} fusion(s32[24]{0:T(128)S(1)} %reshape.67, s32[1024]{0:T(1024)S(1)} %pad_clamp_fusion), kind=kCustom, calls=%fused_computation | custom fusion | bytes 576 | tf_op jit(solution)/shard_map/gather | solution.py:190
  11.0 0.1 gather.9
  11.1 0.1 copy.27
  11.2 0.0 copy-done.6
  11.2 0.1 copy.30
  11.3 0.1 reshape.77
  11.4 0.1 pad.11.clone
  11.5 0.6 %fusion.19.cor_ref = f32[1,256]{1,0:T(1,128)} fusion(s32[]{:T(128)S(6)} %mul.19), kind=kLoop, calls=%fused_computation.41 | loop fusion | flops 2304 | bytes 1028 | tf_op jit(solution)/shard_map/mul | solution.py:221
  12.0 2.3 %all-to-all-done = bf16[8,4,10,128]{3,1,2,0:T(4,128)(2,1)S(1)} async-done(((bf16[8,4,10,128]{3,1,2,0:T(4,128)(2,1)}), bf16[8,4,10,128]{3,1,2,0:T(4,128)(2,1)S(1)}, u32[]{:S(2)}, u32[]{:S(2)}) %all-to-all-start) | async-done | bytes 81952 | tf_op jit(solution)/shard_map/all_to_all | solution.py:188
  14.3 0.9 %gather_fusion.1 = bf16[48,4,128]{2,1,0:T(4,128)(2,1)S(1)} fusion(bf16[8,4,10,128]{3,1,2,0:T(4,128)(2,1)S(1)} %all-to-all-done, s32[48]{0:T(128)S(1)} %reshape.77), kind=kCustom, calls=%fused_computation.1 | custom fusion | bytes 98688 | tf_op jit(solution)/shard_map/gather | solution.py:191
  15.2 0.6 %convolution_bitcast_fusion = f32[16,4,128]{2,1,0:T(4,128)S(1)} fusion(bf16[16,3,4,128]{3,2,1,0:T(4,128)(2,1)S(1)} %bitcast.37, bf16[16,3,128,128]{3,2,1,0:T(8,128)(2,1)S(1)} %copy-done), kind=kOutput, calls=%fused_computation.2 | convolution fusion | flops 6291456 | bytes 1654784 | tf_op jit(solution)/shard_map/tkfa,tkra->ftr/dot_general | solution.py:192
  15.9 0.1 pad_maximum_fusion
  15.9 0.1 fusion.21
  16.0 1.3 %collective-permute-start = (f32[69,3,128]{2,1,0:T(4,128)S(1)}, f32[69,3,128]{2,1,0:T(4,128)S(1)}, u32[]{:S(2)}, u32[]{:S(2)}) collective-permute-start(f32[69,3,128]{2,1,0:T(4,128)S(1)} %get-tuple-element.5), channel_id=1, source_target_pairs={{4,0},{8,4},{12,8},{16,12},{20,16},{24,20},{28,24},{5,1},{9,5},{13... | collective-permute-start | bytes 317960 | tf_op jit(solution)/shard_map/ppermute | solution.py:161
  17.3 0.2 fusion.20
  17.5 4.0 %collective-permute-start.1 = (f32[69,3,128]{2,1,0:T(4,128)S(1)}, f32[69,3,128]{2,1,0:T(4,128)S(1)}, u32[]{:S(2)}, u32[]{:S(2)}) collective-permute-start(f32[69,3,128]{2,1,0:T(4,128)S(1)} %get-tuple-element.4), channel_id=1, source_target_pairs={{0,4},{4,8},{8,12},{12,16},{16,20},{20,24},{24,28},{1,5},{5,9},{9,... | collective-permute-start | bytes 317960 | tf_op jit(solution)/shard_map/ppermute | solution.py:160
  21.5 0.3 copy.42
  21.8 0.3 copy.45
  22.1 0.0 collective-permute-done.high_ref
  22.1 0.1 fusion.22
  22.3 0.1 copy.43
  22.4 2.6 %collective-permute-done.1.low_ref = f32[69,3,128]{2,1,0:T(4,128)S(1)} collective-permute-done((f32[69,3,128]{2,1,0:T(4,128)S(1)}, f32[69,3,128]{2,1,0:T(4,128)S(1)}, u32[]{:S(2)}, u32[]{:S(2)}) %collective-permute-start.1) | collective-permute-done | bytes 106016 | tf_op jit(solution)/shard_map/ppermute | solution.py:160
  25.0 0.1 fusion.23
  25.1 0.1 copy.44
  25.2 0.1 copy.46
  25.3 0.1 copy.47
  25.5 0.1 pad_maximum_fusion.3
  25.6 3.8 %collective-permute-start.2 = (f32[69,24,3]{0,1,2:T(8,128)S(1)}, f32[69,24,3]{0,1,2:T(8,128)S(1)}, u32[]{:S(2)}, u32[]{:S(2)}) collective-permute-start(f32[69,24,3]{0,1,2:T(8,128)S(1)} %get-tuple-element.13), channel_id=1, source_target_pairs={{1,0},{2,1},{3,2},{5,4},{6,5},{7,6},{9,8},{10,9},{11,10},{13,12},{... | collective-permute-start | bytes 59624 | tf_op jit(solution)/shard_map/ppermute | solution.py:217
  29.4 3.0 %collective-permute-start.3 = (f32[69,24,3]{0,1,2:T(8,128)S(1)}, f32[69,24,3]{0,1,2:T(8,128)S(1)}, u32[]{:S(2)}, u32[]{:S(2)}) collective-permute-start(f32[69,24,3]{0,1,2:T(8,128)S(1)} %get-tuple-element.12), channel_id=1, source_target_pairs={{0,1},{1,2},{2,3},{4,5},{5,6},{6,7},{8,9},{9,10},{10,11},{12,13},{... | collective-permute-start | bytes 59624 | tf_op jit(solution)/shard_map/ppermute | solution.py:216
  32.4 0.6 %pad_maximum_fusion.1.aux_ref = f32[5,16,128]{2,1,0:T(8,128)} fusion(f32[1,16,128]{2,1,0:T(8,128)S(1)} %convert_bitcast_fusion, f32[4,16,128]{2,1,0:T(8,128)S(1)} %bitcast.36), kind=kLoop, calls=%fused_computation.6 | loop fusion | flops 10240 | bytes 81920 | tf_op jit(solution)/shard_map/concatenate | solution.py:198
  33.0 0.4 collective-permute-done.3
  33.5 0.2 copy-done.4
  33.6 0.4 copy-done.5
  34.1 2.4 %shard_map.96 = bf16[16,128]{1,0:T(8,128)(2,1)} custom-call(f32[16]{0:T(128)} %diff_ref.3, f32[1,256]{1,0:T(1,128)} %fusion.19.cor_ref, f32[64,16,128]{2,1,0:T(8,128)} %bitcast.32, f32[5,16,128]{2,1,0:T(8,128)} %pad_maximum_fusion.1.aux_ref, f32[69,3,128]{2,1,0:T(4,128)} %copy-done.2, f32[69,3,128]{2,1,0:T(4,128)} %copy-done.3, f32[3,24,69]{2,1,0:T(8,128)} %bitcast.38, ...), custom_call_target="tpu_custom_call" | custom-call | tf_op jit(solution)/shard_map/pallas_call | solution.py:140
  36.5 1.1 %fusion.4 = f32[16,1,3,128]{3,1,2,0:T(1,128)S(1)} fusion(bf16[16,3,128,128]{3,2,1,0:T(8,128)(2,1)S(1)} %copy-done, bf16[16,128,1,1]{1,0,2,3:T(8,128)(2,1)} %bitcast.42), kind=kOutput, calls=%fused_computation.16 | convolution fusion | flops 1572864 | bytes 1601536 | tf_op jit(solution)/shard_map/tkra,tr->tka/dot_general | solution.py:224
  37.6 0.9 %convolution_bitcast_fusion.1 = f32[8,8,128]{2,1,0:T(8,128)} fusion(f32[16,1,3,128]{3,1,2,0:T(1,128)S(1)} %fusion.4, s32[16,3]{0,1:T(4,128)S(1)} %get-tuple-element.10), kind=kOutput, calls=%fused_computation.3 | convolution fusion | flops 4721664 | bytes 57536 | tf_op jit(solution)/shard_map/tks,tka->sa/dot_general | solution.py:229
  38.5 4.4 %all-to-all-start.1 = ((f32[8,8,128]{2,1,0:T(8,128)}), f32[8,8,128]{2,1,0:T(8,128)S(1)}, u32[]{:S(2)}, u32[]{:S(2)}) async-start(f32[8,8,128]{2,1,0:T(8,128)} %convolution_bitcast_fusion.1), calls=%async_computation.1 | async-start | bytes 65536 | tf_op jit(solution)/shard_map/all_to_all | solution.py:231
  42.8 0.1 copy.48
  42.9 7.1 %shard_map.95 = f32[4,16,16,128]{3,2,1,0:T(8,128)} custom-call(f32[16]{0:T(128)} %diff_ref.3, f32[1,256]{1,0:T(1,128)} %fusion.19.cor_ref, f32[64,16,128]{2,1,0:T(8,128)} %bitcast.33, f32[5,16,128]{2,1,0:T(8,128)} %pad_maximum_fusion.1.aux_ref, f32[69,3,128]{2,1,0:T(4,128)} %copy-done.2, f32[69,3,128]{2,1,0:T(4,128)} %copy-done.3, f32[3,24,69]{2,1,0:T(8,128)} %bitcast.39, ...), custom_call_target="tpu_custom_call" | custom-call | tf_op jit(solution)/shard_map/pallas_call | solution.py:140
  50.0 0.9 %convolution_bitcast_fusion.2 = f32[10,128]{1,0:T(8,128)} fusion(f32[8,8,128]{2,1,0:T(8,128)S(1)} %all-to-all-done.1, s32[8,8]{1,0:T(8,128)S(1)} %pad.4.clone), kind=kOutput, calls=%fused_computation.4 | convolution fusion | flops 983680 | bytes 38144 | tf_op jit(solution)/shard_map/isb,isa->ba/dot_general | solution.py:234
  (22 shorter events, 0.1 us)
Async XLA Ops:
  0.6 14.6 %copy-start = (bf16[16,3,128,128]{3,2,1,0:T(8,128)(2,1)S(1)}, bf16[16,3,128,128]{3,2,1,0:T(8,128)(2,1)}, u32[]{:S(2)}) copy-start(bf16[16,3,128,128]{3,2,1,0:T(8,128)(2,1)} %param.9) | copy-start | bytes 4718596
  2.1 12.2 %all-to-all-start = ((bf16[8,4,10,128]{3,1,2,0:T(4,128)(2,1)}), bf16[8,4,10,128]{3,1,2,0:T(4,128)(2,1)S(1)}, u32[]{:S(2)}, u32[]{:S(2)}) async-start(bf16[8,4,10,128]{3,1,2,0:T(4,128)(2,1)} %broadcast_in_dim.10), calls=%async_computation | async-start | bytes 163840 | tf_op jit(solution)/shard_map/all_to_all | solution.py:188
  10.2 1.0 %copy-start.7 = (s32[16,128]{1,0:T(8,128)S(1)}, s32[16,128]{1,0:T(8,128)}, u32[]{:S(2)}) copy-start(s32[16,128]{1,0:T(8,128)} %param.14) | copy-start | bytes 24580
  10.2 1.0 %copy-start.6 = (s32[16,3]{0,1:T(4,128)S(1)}, s32[16,3]{0,1:T(4,128)}, u32[]{:S(2)}) copy-start(s32[16,3]{0,1:T(4,128)} %param.10) | copy-start | bytes 580
  11.0 4.9 %copy-start.1 = (f32[4,16,16,128]{3,2,1,0:T(8,128)S(1)}, f32[4,16,16,128]{3,2,1,0:T(8,128)}, u32[]{:S(2)}) copy-start(f32[4,16,16,128]{3,2,1,0:T(8,128)} %param.13) | copy-start | bytes 1572868
  16.0 6.1 %collective-permute-start = (f32[69,3,128]{2,1,0:T(4,128)S(1)}, f32[69,3,128]{2,1,0:T(4,128)S(1)}, u32[]{:S(2)}, u32[]{:S(2)}) collective-permute-start(f32[69,3,128]{2,1,0:T(4,128)S(1)} %get-tuple-element.5), channel_id=1, source_target_pairs={{4,0},{8,4},{12,8},{16,12},{20,16},{24,20},{28,24},{5,1},{9,5},{13... | collective-permute-start | bytes 317960 | tf_op jit(solution)/shard_map/ppermute | solution.py:161
  17.5 7.4 %collective-permute-start.1 = (f32[69,3,128]{2,1,0:T(4,128)S(1)}, f32[69,3,128]{2,1,0:T(4,128)S(1)}, u32[]{:S(2)}, u32[]{:S(2)}) collective-permute-start(f32[69,3,128]{2,1,0:T(4,128)S(1)} %get-tuple-element.4), channel_id=1, source_target_pairs={{0,4},{4,8},{8,12},{12,16},{16,20},{20,24},{24,28},{1,5},{5,9},{9,... | collective-permute-start | bytes 317960 | tf_op jit(solution)/shard_map/ppermute | solution.py:160
  22.1 11.3 %copy-start.2 = (f32[69,3,128]{2,1,0:T(4,128)}, f32[69,3,128]{2,1,0:T(4,128)S(1)}, u32[]{:S(2)}) copy-start(f32[69,3,128]{2,1,0:T(4,128)S(1)} %collective-permute-done.high_ref) | copy-start | bytes 317956
  25.0 8.5 %copy-start.3 = (f32[69,3,128]{2,1,0:T(4,128)}, f32[69,3,128]{2,1,0:T(4,128)S(1)}, u32[]{:S(2)}) copy-start(f32[69,3,128]{2,1,0:T(4,128)S(1)} %collective-permute-done.1.low_ref) | copy-start | bytes 317956
  25.2 17.6 %copy-start.8 = (s32[8,3]{0,1:T(4,128)S(1)}, s32[8,3]{0,1:T(4,128)}, u32[]{:S(2)}) copy-start(s32[8,3]{0,1:T(4,128)} %param.12) | copy-start | bytes 292
  25.6 7.5 %collective-permute-start.2 = (f32[69,24,3]{0,1,2:T(8,128)S(1)}, f32[69,24,3]{0,1,2:T(8,128)S(1)}, u32[]{:S(2)}, u32[]{:S(2)}) collective-permute-start(f32[69,24,3]{0,1,2:T(8,128)S(1)} %get-tuple-element.13), channel_id=1, source_target_pairs={{1,0},{2,1},{3,2},{5,4},{6,5},{7,6},{9,8},{10,9},{11,10},{13,12},{... | collective-permute-start | bytes 59624 | tf_op jit(solution)/shard_map/ppermute | solution.py:217
  29.4 4.1 %collective-permute-start.3 = (f32[69,24,3]{0,1,2:T(8,128)S(1)}, f32[69,24,3]{0,1,2:T(8,128)S(1)}, u32[]{:S(2)}, u32[]{:S(2)}) collective-permute-start(f32[69,24,3]{0,1,2:T(8,128)S(1)} %get-tuple-element.12), channel_id=1, source_target_pairs={{0,1},{1,2},{2,3},{4,5},{5,6},{6,7},{8,9},{9,10},{10,11},{12,13},{... | collective-permute-start | bytes 59624 | tf_op jit(solution)/shard_map/ppermute | solution.py:216
  33.0 0.6 %copy-start.4 = (f32[69,24,3]{0,1,2:T(8,128)}, f32[69,24,3]{0,1,2:T(8,128)S(1)}, u32[]{:S(2)}) copy-start(f32[69,24,3]{0,1,2:T(8,128)S(1)} %collective-permute-done.2) | copy-start | bytes 59620
  33.5 0.6 %copy-start.5 = (f32[69,24,3]{0,1,2:T(8,128)}, f32[69,24,3]{0,1,2:T(8,128)S(1)}, u32[]{:S(2)}) copy-start(f32[69,24,3]{0,1,2:T(8,128)S(1)} %collective-permute-done.3) | copy-start | bytes 59620
  38.5 11.5 %all-to-all-start.1 = ((f32[8,8,128]{2,1,0:T(8,128)}), f32[8,8,128]{2,1,0:T(8,128)S(1)}, u32[]{:S(2)}, u32[]{:S(2)}) async-start(f32[8,8,128]{2,1,0:T(8,128)} %convolution_bitcast_fusion.1), calls=%async_computation.1 | async-start | bytes 65536 | tf_op jit(solution)/shard_map/all_to_all | solution.py:231

commit v19 on v16

--- a/solution.py
+++ b/solution.py
@@ -221,10 +221,10 @@
     coriolis_wide = (coriolis_coef * (2.0 * (latitude + 0.5) / lat_total - 1.0))[None, :]
     top, state = run_steps(inner, aux, high, low, north, south, coriolis_wide, diffusivity, ocean_state.shape)
     surface = top
-    pieces = jnp.einsum("tkra,tr->tka", remap_weights, surface, preferred_element_type=jnp.float32)
     slot_line = jnp.arange(slots, dtype=jnp.int32)
-    to_slot = (tile_slots[:, :, None] == slot_line[None, None, :]).astype(jnp.float32)
-    per_slot = jnp.einsum("tks,tka->sa", to_slot, pieces, precision=lax.Precision.HIGHEST)
+    to_slot = tile_slots[None, :, :] == slot_line[:, None, None]
+    spread = jnp.where(to_slot[:, :, :, None], surface[None, :, None, :], jnp.zeros((), surface.dtype))
+    per_slot = jnp.einsum("stkr,tkra->sa", spread, remap_weights, preferred_element_type=jnp.float32)
     per_slot = per_slot.reshape(owners, capacity, block_width)
     returned = lax.all_to_all(per_slot, "ox", 0, 0, tiled=True)
     atmos_surface = jnp.einsum(

time: 51.8 us -> 52 us (level)
  waiting for transfers between devices: 5.33 us -> 4.57 us
  other arithmetic: 2.04 us -> 2.79 us
    all_to_all x1, waiting for transfers between devices: 2.32 us -> 1.56 us  [per_device(): incoming = lax.all_to_all(outgoing, 'ox', 0, 0, tiled=True)]
    eq x0 -> x1, other arithmetic: none -> 0.75 us  [per_device(): to_slot = tile_slots[None, :, :] == slot_line[:, None, None]]
    dot_general x2 -> x1, matrix products: 1.35 us -> 1.09 us  [per_device(): jnp.einsum('stkr,tkra->sa', spread, remap_weights, preferred_element_type...]
  transfers between devices with their start and end apart: 6 -> 6, of which waited for: 3 -> 3; matrix products, arithmetic and copies ran while one was open for 10% -> 12% of each run, Pallas kernels for 14% -> 14%
where the time goes in v19:
time: 52 us; the launch traced here: 51 us
  starting transfers between devices  23.3 us (45%)
  Pallas kernels  9.51 us (18%)
  local copies, waits for them, and re-layouts  7.43 us (14%)
  waiting for transfers between devices  4.57 us (9%)
  other arithmetic  2.79 us (5%)
  matrix products  2.59 us (5%)
  between operations  0.77 us (1%)
    pallas_call x2, Pallas kernels, call(): pl.pallas_call(functools.partial(stencil_kernel, surface_only=surface_onl...  9.51 us
    all_to_all x1, starting transfers between devices, per_device(): incoming = lax.all_to_all(outgoing, 'ox', 0, 0, tiled=True)  6.35 us
    all_to_all x1, starting transfers between devices, per_device(): returned = lax.all_to_all(per_slot, 'ox', 0, 0, tiled=True)  4.81 us
    ppermute x1, starting transfers between devices, shifted(): lax.ppermute(lax.slice_in_dim(block, size - width, None, axis=dim), axis,...  3.99 us
    ppermute x1, starting transfers between devices, per_device(): north = jnp.transpose(lax.ppermute(north_edge, 'oy', backward), (2, 1, 0))  3.81 us
    ppermute x1, starting transfers between devices, per_device(): south = jnp.transpose(lax.ppermute(south_edge, 'oy', forward), (2, 1, 0))  3.05 us
    ppermute x1, waiting for transfers between devices, shifted(): lax.ppermute(lax.slice_in_dim(block, size - width, None, axis=dim), axis,...  2.58 us
    unnamed x25, local copies, waits for them, and re-layouts  2.47 us
  transfers between devices with their start and end apart: 6, of which 3 were waited for; matrix products, arithmetic and copies ran while one was open for 12% of the time, Pallas kernels for 14%

profile of v19, /device:TPU:1, one launch (start us, length us, event | category | flops | bytes accessed | tf_op | source)
XLA Modules:
  0.0 51.0 jit_solution(6990501112806854493)
XLA Ops:
  0.6 0.0 copy-start
  0.6 1.5 %broadcast_in_dim.46 = bf16[8,4,10,128]{3,1,2,0:T(4,128)(2,1)} broadcast(bf16[4,10,128]{2,0,1:T(4,128)(2,1)} %param.8), dimensions={1,2,3} | broadcast | bytes 92160 | tf_op jit(solution)/shard_map/broadcast_in_dim | solution.py:187
  2.1 6.4 %all-to-all-start = ((bf16[8,4,10,128]{3,1,2,0:T(4,128)(2,1)}), bf16[8,4,10,128]{3,1,2,0:T(4,128)(2,1)S(1)}, u32[]{:S(2)}, u32[]{:S(2)}) async-start(bf16[8,4,10,128]{3,1,2,0:T(4,128)(2,1)} %broadcast_in_dim.46), calls=%async_computation | async-start | bytes 163840 | tf_op jit(solution)/shard_map/all_to_all | solution.py:188
  8.5 0.7 %compare_select_fusion.2 = s32[16,3]{0,1:T(4,128)S(1)} fusion(s32[16,3]{0,1:T(4,128)} %param.10), kind=kLoop, calls=%fused_computation.23 | loop fusion | flops 144 | bytes 384 | tf_op jit(solution)/shard_map/select_n | solution.py:190
  9.2 0.8 %iota_compare_fusion = pred[24,16,3]{0,1,2:T(8,128)(4,1)S(1)} fusion(s32[16,3]{0,1:T(4,128)} %param.10), kind=kLoop, calls=%fused_computation.16 | loop fusion | flops 1152 | bytes 1344 | tf_op jit(solution)/shard_map/eq | solution.py:225
  9.9 0.1 copy.42
  10.0 0.1 reshape.75
  10.1 0.8 %copy.41 = s32[8,3]{1,0:T(8,128)S(1)} copy(s32[8,3]{0,1:T(4,128)} %param.11) | data formatting | bytes 192 | tf_op args[3]
  10.9 0.1 reshape.71
  11.0 0.8 %gather_fusion = s32[48]{0:T(128)S(1)} fusion(s32[24]{0:T(128)S(1)} %reshape.71, s32[1024]{0:T(1024)S(1)} %pad_clamp_fusion), kind=kCustom, calls=%fused_computation | custom fusion | bytes 576 | tf_op jit(solution)/shard_map/gather | solution.py:190
  11.7 0.1 gather.9
  11.8 0.1 copy.43
  11.9 0.0 copy-done.6
  11.9 0.1 copy.46
  12.0 0.1 reshape.81
  12.1 0.1 pad.6.clone
  12.2 0.6 %fusion.23.cor_ref = f32[1,256]{1,0:T(1,128)} fusion(s32[]{:T(128)S(6)} %mul.16), kind=kLoop, calls=%fused_computation.41 | loop fusion | flops 2304 | bytes 1028 | tf_op jit(solution)/shard_map/mul | solution.py:221
  12.8 1.6 %all-to-all-done = bf16[8,4,10,128]{3,1,2,0:T(4,128)(2,1)S(1)} async-done(((bf16[8,4,10,128]{3,1,2,0:T(4,128)(2,1)}), bf16[8,4,10,128]{3,1,2,0:T(4,128)(2,1)S(1)}, u32[]{:S(2)}, u32[]{:S(2)}) %all-to-all-start) | async-done | bytes 81952 | tf_op jit(solution)/shard_map/all_to_all | solution.py:188
  14.3 0.9 %gather_fusion.1 = bf16[48,4,128]{2,1,0:T(4,128)(2,1)S(1)} fusion(bf16[8,4,10,128]{3,1,2,0:T(4,128)(2,1)S(1)} %all-to-all-done, s32[48]{0:T(128)S(1)} %reshape.81), kind=kCustom, calls=%fused_computation.1 | custom fusion | bytes 98688 | tf_op jit(solution)/shard_map/gather | solution.py:191
  15.2 0.6 %convolution_bitcast_fusion = f32[16,4,128]{2,1,0:T(4,128)S(1)} fusion(bf16[16,3,4,128]{3,2,1,0:T(4,128)(2,1)S(1)} %bitcast.31, bf16[16,3,128,128]{3,2,1,0:T(8,128)(2,1)S(1)} %copy-done), kind=kOutput, calls=%fused_computation.4 | convolution fusion | flops 6291456 | bytes 1654784 | tf_op jit(solution)/shard_map/tkfa,tkra->ftr/dot_general | solution.py:192
  15.9 0.1 pad_maximum_fusion
  16.0 0.1 fusion.26
  16.0 1.3 %collective-permute-start = (f32[69,3,128]{2,1,0:T(4,128)S(1)}, f32[69,3,128]{2,1,0:T(4,128)S(1)}, u32[]{:S(2)}, u32[]{:S(2)}) collective-permute-start(f32[69,3,128]{2,1,0:T(4,128)S(1)} %get-tuple-element.5), channel_id=1, source_target_pairs={{4,0},{8,4},{12,8},{16,12},{20,16},{24,20},{28,24},{5,1},{9,5},{13... | collective-permute-start | bytes 317960 | tf_op jit(solution)/shard_map/ppermute | solution.py:161
  17.3 0.2 fusion.25
  17.5 4.0 %collective-permute-start.1 = (f32[69,3,128]{2,1,0:T(4,128)S(1)}, f32[69,3,128]{2,1,0:T(4,128)S(1)}, u32[]{:S(2)}, u32[]{:S(2)}) collective-permute-start(f32[69,3,128]{2,1,0:T(4,128)S(1)} %get-tuple-element.4), channel_id=1, source_target_pairs={{0,4},{4,8},{8,12},{12,16},{16,20},{20,24},{24,28},{1,5},{5,9},{9,... | collective-permute-start | bytes 317960 | tf_op jit(solution)/shard_map/ppermute | solution.py:160
  21.5 0.3 copy.58
  21.8 0.3 copy.61
  22.1 0.0 collective-permute-done.high_ref
  22.1 0.1 fusion.27
  22.3 0.1 copy.59
  22.4 2.6 %collective-permute-done.1.low_ref = f32[69,3,128]{2,1,0:T(4,128)S(1)} collective-permute-done((f32[69,3,128]{2,1,0:T(4,128)S(1)}, f32[69,3,128]{2,1,0:T(4,128)S(1)}, u32[]{:S(2)}, u32[]{:S(2)}) %collective-permute-start.1) | collective-permute-done | bytes 106016 | tf_op jit(solution)/shard_map/ppermute | solution.py:160
  25.0 0.1 fusion.28
  25.1 0.1 copy.60
  25.2 0.1 copy.62
  25.3 0.1 copy.63
  25.5 0.1 pad_maximum_fusion.3
  25.5 3.8 %collective-permute-start.2 = (f32[69,24,3]{0,1,2:T(8,128)S(1)}, f32[69,24,3]{0,1,2:T(8,128)S(1)}, u32[]{:S(2)}, u32[]{:S(2)}) collective-permute-start(f32[69,24,3]{0,1,2:T(8,128)S(1)} %get-tuple-element.11), channel_id=1, source_target_pairs={{1,0},{2,1},{3,2},{5,4},{6,5},{7,6},{9,8},{10,9},{11,10},{13,12},{... | collective-permute-start | bytes 59624 | tf_op jit(solution)/shard_map/ppermute | solution.py:217
  29.4 3.0 %collective-permute-start.3 = (f32[69,24,3]{0,1,2:T(8,128)S(1)}, f32[69,24,3]{0,1,2:T(8,128)S(1)}, u32[]{:S(2)}, u32[]{:S(2)}) collective-permute-start(f32[69,24,3]{0,1,2:T(8,128)S(1)} %get-tuple-element.10), channel_id=1, source_target_pairs={{0,1},{1,2},{2,3},{4,5},{5,6},{6,7},{8,9},{9,10},{10,11},{12,13},{... | collective-permute-start | bytes 59624 | tf_op jit(solution)/shard_map/ppermute | solution.py:216
  32.4 0.6 %pad_maximum_fusion.1.aux_ref = f32[5,16,128]{2,1,0:T(8,128)} fusion(f32[1,16,128]{2,1,0:T(8,128)S(1)} %convert_bitcast_fusion, f32[4,16,128]{2,1,0:T(8,128)S(1)} %bitcast.30), kind=kLoop, calls=%fused_computation.12 | loop fusion | flops 10240 | bytes 81920 | tf_op jit(solution)/shard_map/concatenate | solution.py:198
  33.0 0.4 collective-permute-done.3
  33.5 0.2 copy-done.4
  33.7 0.4 copy-done.5
  34.1 2.4 %shard_map.96 = bf16[16,128]{1,0:T(8,128)(2,1)} custom-call(f32[16]{0:T(128)} %diff_ref.3, f32[1,256]{1,0:T(1,128)} %fusion.23.cor_ref, f32[64,16,128]{2,1,0:T(8,128)} %bitcast.26, f32[5,16,128]{2,1,0:T(8,128)} %pad_maximum_fusion.1.aux_ref, f32[69,3,128]{2,1,0:T(4,128)} %copy-done.2, f32[69,3,128]{2,1,0:T(4,128)} %copy-done.3, f32[3,24,69]{2,1,0:T(8,128)} %bitcast.32, ...), custom_call_target="tpu_custom_call" | custom-call | tf_op jit(solution)/shard_map/pallas_call | solution.py:140
  36.5 1.1 %fusion.2 = f32[24,128]{1,0:T(8,128)S(1)} fusion(bf16[16,3,128,128]{3,2,1,0:T(8,128)(2,1)S(1)} %copy-done, pred[24,16,3]{0,1,2:T(8,128)(4,1)S(1)} %iota_compare_fusion, bf16[16,128]{1,0:T(8,128)(2,1)} %shard_map.96), kind=kOutput, calls=%fused_computation.5 | convolution fusion | flops 37896192 | bytes 1590400 | tf_op jit(solution)/shard_map/stkr,tkra->sa/dot_general | solution.py:227
  37.6 0.6 %reshape.72 = f32[8,3,128]{2,1,0:T(4,128)} reshape(f32[24,128]{1,0:T(8,128)S(1)} %fusion.2) | data formatting | bytes 24576 | tf_op jit(solution)/shard_map/reshape | solution.py:228
  38.2 4.8 %all-to-all-start.1 = ((f32[8,3,128]{2,1,0:T(4,128)}), f32[8,3,128]{2,1,0:T(4,128)S(1)}, u32[]{:S(2)}, u32[]{:S(2)}) async-start(f32[8,3,128]{2,1,0:T(4,128)} %reshape.72), calls=%async_computation.1 | async-start | bytes 32768 | tf_op jit(solution)/shard_map/all_to_all | solution.py:229
  43.0 7.1 %shard_map.95 = f32[4,16,16,128]{3,2,1,0:T(8,128)} custom-call(f32[16]{0:T(128)} %diff_ref.3, f32[1,256]{1,0:T(1,128)} %fusion.23.cor_ref, f32[64,16,128]{2,1,0:T(8,128)} %bitcast.27, f32[5,16,128]{2,1,0:T(8,128)} %pad_maximum_fusion.1.aux_ref, f32[69,3,128]{2,1,0:T(4,128)} %copy-done.2, f32[69,3,128]{2,1,0:T(4,128)} %copy-done.3, f32[3,24,69]{2,1,0:T(8,128)} %bitcast.33, ...), custom_call_target="tpu_custom_call" | custom-call | tf_op jit(solution)/shard_map/pallas_call | solution.py:140
  50.1 0.9 %convolution_bitcast_fusion.1 = f32[10,128]{1,0:T(8,128)} fusion(f32[8,3,128]{2,1,0:T(4,128)S(1)} %all-to-all-done.1, s32[8,3]{0,1:T(4,128)S(1)} %copy-done.8), kind=kOutput, calls=%fused_computation.6 | convolution fusion | flops 368880 | bytes 17504 | tf_op jit(solution)/shard_map/isb,isa->ba/dot_general | solution.py:230
  (21 shorter events, 0.1 us)
Async XLA Ops:
  0.6 14.6 %copy-start = (bf16[16,3,128,128]{3,2,1,0:T(8,128)(2,1)S(1)}, bf16[16,3,128,128]{3,2,1,0:T(8,128)(2,1)}, u32[]{:S(2)}) copy-start(bf16[16,3,128,128]{3,2,1,0:T(8,128)(2,1)} %param.9) | copy-start | bytes 4718596
  2.1 12.2 %all-to-all-start = ((bf16[8,4,10,128]{3,1,2,0:T(4,128)(2,1)}), bf16[8,4,10,128]{3,1,2,0:T(4,128)(2,1)S(1)}, u32[]{:S(2)}, u32[]{:S(2)}) async-start(bf16[8,4,10,128]{3,1,2,0:T(4,128)(2,1)} %broadcast_in_dim.46), calls=%async_computation | async-start | bytes 163840 | tf_op jit(solution)/shard_map/all_to_all | solution.py:188
  10.9 1.0 %copy-start.7 = (s32[16,128]{1,0:T(8,128)S(1)}, s32[16,128]{1,0:T(8,128)}, u32[]{:S(2)}) copy-start(s32[16,128]{1,0:T(8,128)} %param.14) | copy-start | bytes 24580
  10.9 1.0 %copy-start.6 = (s32[16,3]{0,1:T(4,128)S(1)}, s32[16,3]{0,1:T(4,128)}, u32[]{:S(2)}) copy-start(s32[16,3]{0,1:T(4,128)} %param.10) | copy-start | bytes 580
  11.7 4.2 %copy-start.1 = (f32[4,16,16,128]{3,2,1,0:T(8,128)S(1)}, f32[4,16,16,128]{3,2,1,0:T(8,128)}, u32[]{:S(2)}) copy-start(f32[4,16,16,128]{3,2,1,0:T(8,128)} %param.13) | copy-start | bytes 1572868
  16.0 6.1 %collective-permute-start = (f32[69,3,128]{2,1,0:T(4,128)S(1)}, f32[69,3,128]{2,1,0:T(4,128)S(1)}, u32[]{:S(2)}, u32[]{:S(2)}) collective-permute-start(f32[69,3,128]{2,1,0:T(4,128)S(1)} %get-tuple-element.5), channel_id=1, source_target_pairs={{4,0},{8,4},{12,8},{16,12},{20,16},{24,20},{28,24},{5,1},{9,5},{13... | collective-permute-start | bytes 317960 | tf_op jit(solution)/shard_map/ppermute | solution.py:161
  17.5 7.4 %collective-permute-start.1 = (f32[69,3,128]{2,1,0:T(4,128)S(1)}, f32[69,3,128]{2,1,0:T(4,128)S(1)}, u32[]{:S(2)}, u32[]{:S(2)}) collective-permute-start(f32[69,3,128]{2,1,0:T(4,128)S(1)} %get-tuple-element.4), channel_id=1, source_target_pairs={{0,4},{4,8},{8,12},{12,16},{16,20},{20,24},{24,28},{1,5},{5,9},{9,... | collective-permute-start | bytes 317960 | tf_op jit(solution)/shard_map/ppermute | solution.py:160
  22.1 11.3 %copy-start.2 = (f32[69,3,128]{2,1,0:T(4,128)}, f32[69,3,128]{2,1,0:T(4,128)S(1)}, u32[]{:S(2)}) copy-start(f32[69,3,128]{2,1,0:T(4,128)S(1)} %collective-permute-done.high_ref) | copy-start | bytes 317956
  25.0 8.5 %copy-start.3 = (f32[69,3,128]{2,1,0:T(4,128)}, f32[69,3,128]{2,1,0:T(4,128)S(1)}, u32[]{:S(2)}) copy-start(f32[69,3,128]{2,1,0:T(4,128)S(1)} %collective-permute-done.1.low_ref) | copy-start | bytes 317956
  25.5 7.5 %collective-permute-start.2 = (f32[69,24,3]{0,1,2:T(8,128)S(1)}, f32[69,24,3]{0,1,2:T(8,128)S(1)}, u32[]{:S(2)}, u32[]{:S(2)}) collective-permute-start(f32[69,24,3]{0,1,2:T(8,128)S(1)} %get-tuple-element.11), channel_id=1, source_target_pairs={{1,0},{2,1},{3,2},{5,4},{6,5},{7,6},{9,8},{10,9},{11,10},{13,12},{... | collective-permute-start | bytes 59624 | tf_op jit(solution)/shard_map/ppermute | solution.py:217
  29.4 4.1 %collective-permute-start.3 = (f32[69,24,3]{0,1,2:T(8,128)S(1)}, f32[69,24,3]{0,1,2:T(8,128)S(1)}, u32[]{:S(2)}, u32[]{:S(2)}) collective-permute-start(f32[69,24,3]{0,1,2:T(8,128)S(1)} %get-tuple-element.10), channel_id=1, source_target_pairs={{0,1},{1,2},{2,3},{4,5},{5,6},{6,7},{8,9},{9,10},{10,11},{12,13},{... | collective-permute-start | bytes 59624 | tf_op jit(solution)/shard_map/ppermute | solution.py:216
  33.0 0.6 %copy-start.4 = (f32[69,24,3]{0,1,2:T(8,128)}, f32[69,24,3]{0,1,2:T(8,128)S(1)}, u32[]{:S(2)}) copy-start(f32[69,24,3]{0,1,2:T(8,128)S(1)} %collective-permute-done.2) | copy-start | bytes 59620
  33.5 0.6 %copy-start.5 = (f32[69,24,3]{0,1,2:T(8,128)}, f32[69,24,3]{0,1,2:T(8,128)S(1)}, u32[]{:S(2)}) copy-start(f32[69,24,3]{0,1,2:T(8,128)S(1)} %collective-permute-done.3) | copy-start | bytes 59620
  36.5 13.6 %copy-start.8 = (s32[8,3]{0,1:T(4,128)S(1)}, s32[8,3]{0,1:T(4,128)}, u32[]{:S(2)}) copy-start(s32[8,3]{0,1:T(4,128)} %param.12) | copy-start | bytes 292
  38.2 11.9 %all-to-all-start.1 = ((f32[8,3,128]{2,1,0:T(4,128)}), f32[8,3,128]{2,1,0:T(4,128)S(1)}, u32[]{:S(2)}, u32[]{:S(2)}) async-start(f32[8,3,128]{2,1,0:T(4,128)} %reshape.72), calls=%async_computation.1 | async-start | bytes 32768 | tf_op jit(solution)/shard_map/all_to_all | solution.py:229

commit v20 on v18

--- a/solution.py
+++ b/solution.py
@@ -221,12 +221,12 @@
     coriolis_wide = (coriolis_coef * (2.0 * (latitude + 0.5) / lat_total - 1.0))[None, :]
     top, state = run_steps(inner, aux, high, low, north, south, coriolis_wide, diffusivity, ocean_state.shape)
     surface = top
-    pieces = jnp.einsum("tkra,tr->tka", remap_weights, surface, preferred_element_type=jnp.float32)
     room = -(-capacity // 8) * 8
     slot_of = (tile_slots // capacity) * room + tile_slots % capacity
     slot_line = jnp.arange(owners * room, dtype=jnp.int32)
-    to_slot = (slot_of[:, :, None] == slot_line[None, None, :]).astype(jnp.float32)
-    per_slot = jnp.einsum("tks,tka->sa", to_slot, pieces, precision=lax.Precision.HIGHEST)
+    to_slot = slot_of[None, :, :] == slot_line[:, None, None]
+    spread = jnp.where(to_slot[:, :, :, None], surface[None, :, None, :], jnp.zeros((), surface.dtype))
+    per_slot = jnp.einsum("stkr,tkra->sa", spread, remap_weights, preferred_element_type=jnp.float32)
     per_slot = per_slot.reshape(owners, room, block_width)
     returned = lax.all_to_all(per_slot, "ox", 0, 0, tiled=True)
     wide_send = jnp.pad(send_blocks, ((0, 0), (0, room - capacity)), constant_values=-1)

time: 51.9 us -> 51.9 us (level)
  the two profiles are of different devices: /device:TPU:1 before, /device:TPU:6 now
where the time goes in v20:
time: 51.9 us; the launch traced here: 51.3 us
  starting transfers between devices  21.6 us (42%)
  Pallas kernels  9.51 us (18%)
  waiting for transfers between devices  7.04 us (14%)
  local copies, waits for them, and re-layouts  6.89 us (13%)
  matrix products  3.41 us (7%)
  other arithmetic  2.12 us (4%)
  between operations  0.77 us (1%)
    pallas_call x2, Pallas kernels, call(): pl.pallas_call(functools.partial(stencil_kernel, surface_only=surface_onl...  9.51 us
    all_to_all x1, starting transfers between devices, per_device(): incoming = lax.all_to_all(outgoing, 'ox', 0, 0, tiled=True)  6.34 us
    all_to_all x1, starting transfers between devices, per_device(): returned = lax.all_to_all(per_slot, 'ox', 0, 0, tiled=True)  4.19 us
    ppermute x1, starting transfers between devices, shifted(): lax.ppermute(lax.slice_in_dim(block, 0, width, axis=dim), axis, backward)  3.59 us
    ppermute x1, starting transfers between devices, shifted(): lax.ppermute(lax.slice_in_dim(block, size - width, None, axis=dim), axis,...  3.15 us
    ppermute x1, waiting for transfers between devices, shifted(): lax.ppermute(lax.slice_in_dim(block, size - width, None, axis=dim), axis,...  2.67 us
    unnamed x26, local copies, waits for them, and re-layouts  2.53 us
    ppermute x1, starting transfers between devices, per_device(): south = jnp.transpose(lax.ppermute(south_edge, 'oy', forward), (2, 1, 0))  2.4 us
  transfers between devices with their start and end apart: 6, of which 4 were waited for; matrix products, arithmetic and copies ran while one was open for 10% of the time, Pallas kernels for 14%

profile of v20, /device:TPU:6, one launch (start us, length us, event | category | flops | bytes accessed | tf_op | source)
XLA Modules:
  0.0 51.3 jit_solution(2322598101295091164)
XLA Ops:
  0.6 0.0 copy-start
  0.6 1.5 %broadcast_in_dim.46 = bf16[8,4,10,128]{3,1,2,0:T(4,128)(2,1)} broadcast(bf16[4,10,128]{2,0,1:T(4,128)(2,1)} %param.8), dimensions={1,2,3} | broadcast | bytes 92160 | tf_op jit(solution)/shard_map/broadcast_in_dim | solution.py:187
  2.1 6.3 %all-to-all-start = ((bf16[8,4,10,128]{3,1,2,0:T(4,128)(2,1)}), bf16[8,4,10,128]{3,1,2,0:T(4,128)(2,1)S(1)}, u32[]{:S(2)}, u32[]{:S(2)}) async-start(bf16[8,4,10,128]{3,1,2,0:T(4,128)(2,1)} %broadcast_in_dim.46), calls=%async_computation | async-start | bytes 163840 | tf_op jit(solution)/shard_map/all_to_all | solution.py:188
  8.5 0.7 %fusion.10 = (s32[16,3]{0,1:T(4,128)S(1)}, s32[16,3]{0,1:T(4,128)S(1)}) fusion(s32[16,3]{0,1:T(4,128)} %param.10), kind=kLoop, calls=%fused_computation.27 | loop fusion | flops 816 | bytes 576 | tf_op jit(solution)/shard_map/add | solution.py:225
  9.2 0.1 copy.27
  9.2 0.1 reshape.75
  9.3 0.8 %copy.26 = s32[8,3]{1,0:T(8,128)S(1)} copy(s32[8,3]{0,1:T(4,128)} %param.11) | data formatting | bytes 192 | tf_op args[3]
  10.1 0.1 reshape.71
  10.2 0.8 %gather_fusion = s32[48]{0:T(128)S(1)} fusion(s32[24]{0:T(128)S(1)} %reshape.71, s32[1024]{0:T(1024)S(1)} %pad_clamp_fusion), kind=kCustom, calls=%fused_computation | custom fusion | bytes 576 | tf_op jit(solution)/shard_map/gather | solution.py:190
  11.0 0.1 gather.9
  11.0 0.1 copy.28
  11.1 0.1 iota_compare_fusion.2
  11.2 0.0 copy-done.6
  11.3 0.1 copy.31
  11.3 0.1 reshape.81
  11.4 0.1 pad.11.clone
  11.5 0.6 %fusion.23.cor_ref = f32[1,256]{1,0:T(1,128)} fusion(s32[]{:T(128)S(6)} %mul.19), kind=kLoop, calls=%fused_computation.42 | loop fusion | flops 2304 | bytes 1028 | tf_op jit(solution)/shard_map/mul | solution.py:221
  12.1 1.7 %all-to-all-done = bf16[8,4,10,128]{3,1,2,0:T(4,128)(2,1)S(1)} async-done(((bf16[8,4,10,128]{3,1,2,0:T(4,128)(2,1)}), bf16[8,4,10,128]{3,1,2,0:T(4,128)(2,1)S(1)}, u32[]{:S(2)}, u32[]{:S(2)}) %all-to-all-start) | async-done | bytes 81952 | tf_op jit(solution)/shard_map/all_to_all | solution.py:188
  13.8 0.9 %gather_fusion.1 = bf16[48,4,128]{2,1,0:T(4,128)(2,1)S(1)} fusion(bf16[8,4,10,128]{3,1,2,0:T(4,128)(2,1)S(1)} %all-to-all-done, s32[48]{0:T(128)S(1)} %reshape.81), kind=kCustom, calls=%fused_computation.1 | custom fusion | bytes 98688 | tf_op jit(solution)/shard_map/gather | solution.py:191
  14.7 0.6 %convolution_bitcast_fusion = f32[16,4,128]{2,1,0:T(4,128)S(1)} fusion(bf16[16,3,4,128]{3,2,1,0:T(4,128)(2,1)S(1)} %bitcast.34, bf16[16,3,128,128]{3,2,1,0:T(8,128)(2,1)S(1)} %copy-done), kind=kOutput, calls=%fused_computation.4 | convolution fusion | flops 6291456 | bytes 1654784 | tf_op jit(solution)/shard_map/tkfa,tkra->ftr/dot_general | solution.py:192
  15.3 0.1 pad_maximum_fusion
  15.4 0.1 fusion.26
  15.5 3.6 %collective-permute-start = (f32[69,3,128]{2,1,0:T(4,128)S(1)}, f32[69,3,128]{2,1,0:T(4,128)S(1)}, u32[]{:S(2)}, u32[]{:S(2)}) collective-permute-start(f32[69,3,128]{2,1,0:T(4,128)S(1)} %get-tuple-element.5), channel_id=1, source_target_pairs={{4,0},{8,4},{12,8},{16,12},{20,16},{24,20},{28,24},{5,1},{9,5},{13... | collective-permute-start | bytes 317960 | tf_op jit(solution)/shard_map/ppermute | solution.py:161
  19.1 0.2 fusion.25
  19.3 3.1 %collective-permute-start.1 = (f32[69,3,128]{2,1,0:T(4,128)S(1)}, f32[69,3,128]{2,1,0:T(4,128)S(1)}, u32[]{:S(2)}, u32[]{:S(2)}) collective-permute-start(f32[69,3,128]{2,1,0:T(4,128)S(1)} %get-tuple-element.4), channel_id=1, source_target_pairs={{0,4},{4,8},{8,12},{12,16},{16,20},{20,24},{24,28},{1,5},{5,9},{9,... | collective-permute-start | bytes 317960 | tf_op jit(solution)/shard_map/ppermute | solution.py:160
  22.4 0.3 copy.43
  22.7 0.3 copy.46
  23.0 0.4 collective-permute-done.high_ref
  23.4 0.1 fusion.27
  23.6 0.1 copy.44
  23.7 2.7 %collective-permute-done.1.low_ref = f32[69,3,128]{2,1,0:T(4,128)S(1)} collective-permute-done((f32[69,3,128]{2,1,0:T(4,128)S(1)}, f32[69,3,128]{2,1,0:T(4,128)S(1)}, u32[]{:S(2)}, u32[]{:S(2)}) %collective-permute-start.1) | collective-permute-done | bytes 106016 | tf_op jit(solution)/shard_map/ppermute | solution.py:160
  26.4 0.1 fusion.28
  26.5 0.1 copy.45
  26.6 0.1 copy.47
  26.7 0.1 copy.48
  26.9 0.1 pad_maximum_fusion.3
  26.9 1.9 %collective-permute-start.2 = (f32[69,24,3]{0,1,2:T(8,128)S(1)}, f32[69,24,3]{0,1,2:T(8,128)S(1)}, u32[]{:S(2)}, u32[]{:S(2)}) collective-permute-start(f32[69,24,3]{0,1,2:T(8,128)S(1)} %get-tuple-element.13), channel_id=1, source_target_pairs={{1,0},{2,1},{3,2},{5,4},{6,5},{7,6},{9,8},{10,9},{11,10},{13,12},{... | collective-permute-start | bytes 59624 | tf_op jit(solution)/shard_map/ppermute | solution.py:217
  28.9 2.4 %collective-permute-start.3 = (f32[69,24,3]{0,1,2:T(8,128)S(1)}, f32[69,24,3]{0,1,2:T(8,128)S(1)}, u32[]{:S(2)}, u32[]{:S(2)}) collective-permute-start(f32[69,24,3]{0,1,2:T(8,128)S(1)} %get-tuple-element.12), channel_id=1, source_target_pairs={{0,1},{1,2},{2,3},{4,5},{5,6},{6,7},{8,9},{9,10},{10,11},{12,13},{... | collective-permute-start | bytes 59624 | tf_op jit(solution)/shard_map/ppermute | solution.py:216
  31.3 0.6 %pad_maximum_fusion.1.aux_ref = f32[5,16,128]{2,1,0:T(8,128)} fusion(f32[1,16,128]{2,1,0:T(8,128)S(1)} %convert_bitcast_fusion, f32[4,16,128]{2,1,0:T(8,128)S(1)} %bitcast.33), kind=kLoop, calls=%fused_computation.12 | loop fusion | flops 10240 | bytes 81920 | tf_op jit(solution)/shard_map/concatenate | solution.py:198
  31.9 0.0 collective-permute-done.2
  31.9 2.2 %collective-permute-done.3 = f32[69,24,3]{0,1,2:T(8,128)S(1)} collective-permute-done((f32[69,24,3]{0,1,2:T(8,128)S(1)}, f32[69,24,3]{0,1,2:T(8,128)S(1)}, u32[]{:S(2)}, u32[]{:S(2)}) %collective-permute-start.3) | collective-permute-done | bytes 19904 | tf_op jit(solution)/shard_map/ppermute | solution.py:216
  34.2 0.6 %copy-done.5 = f32[69,24,3]{0,1,2:T(8,128)} copy-done((f32[69,24,3]{0,1,2:T(8,128)}, f32[69,24,3]{0,1,2:T(8,128)S(1)}, u32[]{:S(2)}) %copy-start.5) | copy-done | bytes 19896
  34.8 2.4 %shard_map.96 = bf16[16,128]{1,0:T(8,128)(2,1)} custom-call(f32[16]{0:T(128)} %diff_ref.3, f32[1,256]{1,0:T(1,128)} %fusion.23.cor_ref, f32[64,16,128]{2,1,0:T(8,128)} %bitcast.29, f32[5,16,128]{2,1,0:T(8,128)} %pad_maximum_fusion.1.aux_ref, f32[69,3,128]{2,1,0:T(4,128)} %copy-done.2, f32[69,3,128]{2,1,0:T(4,128)} %copy-done.3, f32[3,24,69]{2,1,0:T(8,128)} %bitcast.35, ...), custom_call_target="tpu_custom_call" | custom-call | tf_op jit(solution)/shard_map/pallas_call | solution.py:140
  37.2 1.9 %fusion.2 = f32[8,8,128]{2,1,0:T(8,128)} fusion(bf16[16,3,128,128]{3,2,1,0:T(8,128)(2,1)S(1)} %copy-done, pred[64,16,3]{0,1,2:T(8,128)(4,1)S(1)} %iota_compare_fusion.2, bf16[16,128]{1,0:T(8,128)(2,1)} %shard_map.96), kind=kOutput, calls=%fused_computation.5 | convolution fusion | flops 101056512 | bytes 1612800 | tf_op jit(solution)/shard_map/stkr,tkra->sa/dot_general | solution.py:229
  39.1 4.2 %all-to-all-start.1 = ((f32[8,8,128]{2,1,0:T(8,128)}), f32[8,8,128]{2,1,0:T(8,128)S(1)}, u32[]{:S(2)}, u32[]{:S(2)}) async-start(f32[8,8,128]{2,1,0:T(8,128)} %fusion.2), calls=%async_computation.1 | async-start | bytes 65536 | tf_op jit(solution)/shard_map/all_to_all | solution.py:231
  43.3 0.1 copy.49
  43.4 7.1 %shard_map.95 = f32[4,16,16,128]{3,2,1,0:T(8,128)} custom-call(f32[16]{0:T(128)} %diff_ref.3, f32[1,256]{1,0:T(1,128)} %fusion.23.cor_ref, f32[64,16,128]{2,1,0:T(8,128)} %bitcast.30, f32[5,16,128]{2,1,0:T(8,128)} %pad_maximum_fusion.1.aux_ref, f32[69,3,128]{2,1,0:T(4,128)} %copy-done.2, f32[69,3,128]{2,1,0:T(4,128)} %copy-done.3, f32[3,24,69]{2,1,0:T(8,128)} %bitcast.36, ...), custom_call_target="tpu_custom_call" | custom-call | tf_op jit(solution)/shard_map/pallas_call | solution.py:140
  50.4 0.9 %convolution_bitcast_fusion.1 = f32[10,128]{1,0:T(8,128)} fusion(f32[8,8,128]{2,1,0:T(8,128)S(1)} %all-to-all-done.1, s32[8,8]{1,0:T(8,128)S(1)} %pad.4.clone), kind=kOutput, calls=%fused_computation.6 | convolution fusion | flops 983680 | bytes 38144 | tf_op jit(solution)/shard_map/isb,isa->ba/dot_general | solution.py:234
  (22 shorter events, 0.1 us)
Async XLA Ops:
  0.6 14.1 %copy-start = (bf16[16,3,128,128]{3,2,1,0:T(8,128)(2,1)S(1)}, bf16[16,3,128,128]{3,2,1,0:T(8,128)(2,1)}, u32[]{:S(2)}) copy-start(bf16[16,3,128,128]{3,2,1,0:T(8,128)(2,1)} %param.9) | copy-start | bytes 4718596
  2.1 11.7 %all-to-all-start = ((bf16[8,4,10,128]{3,1,2,0:T(4,128)(2,1)}), bf16[8,4,10,128]{3,1,2,0:T(4,128)(2,1)S(1)}, u32[]{:S(2)}, u32[]{:S(2)}) async-start(bf16[8,4,10,128]{3,1,2,0:T(4,128)(2,1)} %broadcast_in_dim.46), calls=%async_computation | async-start | bytes 163840 | tf_op jit(solution)/shard_map/all_to_all | solution.py:188
  10.2 1.0 %copy-start.7 = (s32[16,128]{1,0:T(8,128)S(1)}, s32[16,128]{1,0:T(8,128)}, u32[]{:S(2)}) copy-start(s32[16,128]{1,0:T(8,128)} %param.14) | copy-start | bytes 24580
  10.2 1.0 %copy-start.6 = (s32[16,3]{0,1:T(4,128)S(1)}, s32[16,3]{0,1:T(4,128)}, u32[]{:S(2)}) copy-start(s32[16,3]{0,1:T(4,128)} %param.10) | copy-start | bytes 580
  11.0 4.4 %copy-start.1 = (f32[4,16,16,128]{3,2,1,0:T(8,128)S(1)}, f32[4,16,16,128]{3,2,1,0:T(8,128)}, u32[]{:S(2)}) copy-start(f32[4,16,16,128]{3,2,1,0:T(8,128)} %param.13) | copy-start | bytes 1572868
  15.5 8.0 %collective-permute-start = (f32[69,3,128]{2,1,0:T(4,128)S(1)}, f32[69,3,128]{2,1,0:T(4,128)S(1)}, u32[]{:S(2)}, u32[]{:S(2)}) collective-permute-start(f32[69,3,128]{2,1,0:T(4,128)S(1)} %get-tuple-element.5), channel_id=1, source_target_pairs={{4,0},{8,4},{12,8},{16,12},{20,16},{24,20},{28,24},{5,1},{9,5},{13... | collective-permute-start | bytes 317960 | tf_op jit(solution)/shard_map/ppermute | solution.py:161
  19.3 7.1 %collective-permute-start.1 = (f32[69,3,128]{2,1,0:T(4,128)S(1)}, f32[69,3,128]{2,1,0:T(4,128)S(1)}, u32[]{:S(2)}, u32[]{:S(2)}) collective-permute-start(f32[69,3,128]{2,1,0:T(4,128)S(1)} %get-tuple-element.4), channel_id=1, source_target_pairs={{0,4},{4,8},{8,12},{12,16},{16,20},{20,24},{24,28},{1,5},{5,9},{9,... | collective-permute-start | bytes 317960 | tf_op jit(solution)/shard_map/ppermute | solution.py:160
  23.4 10.7 %copy-start.2 = (f32[69,3,128]{2,1,0:T(4,128)}, f32[69,3,128]{2,1,0:T(4,128)S(1)}, u32[]{:S(2)}) copy-start(f32[69,3,128]{2,1,0:T(4,128)S(1)} %collective-permute-done.high_ref) | copy-start | bytes 317956
  26.4 7.8 %copy-start.3 = (f32[69,3,128]{2,1,0:T(4,128)}, f32[69,3,128]{2,1,0:T(4,128)S(1)}, u32[]{:S(2)}) copy-start(f32[69,3,128]{2,1,0:T(4,128)S(1)} %collective-permute-done.1.low_ref) | copy-start | bytes 317956
  26.9 5.0 %collective-permute-start.2 = (f32[69,24,3]{0,1,2:T(8,128)S(1)}, f32[69,24,3]{0,1,2:T(8,128)S(1)}, u32[]{:S(2)}, u32[]{:S(2)}) collective-permute-start(f32[69,24,3]{0,1,2:T(8,128)S(1)} %get-tuple-element.13), channel_id=1, source_target_pairs={{1,0},{2,1},{3,2},{5,4},{6,5},{7,6},{9,8},{10,9},{11,10},{13,12},{... | collective-permute-start | bytes 59624 | tf_op jit(solution)/shard_map/ppermute | solution.py:217
  28.9 5.3 %collective-permute-start.3 = (f32[69,24,3]{0,1,2:T(8,128)S(1)}, f32[69,24,3]{0,1,2:T(8,128)S(1)}, u32[]{:S(2)}, u32[]{:S(2)}) collective-permute-start(f32[69,24,3]{0,1,2:T(8,128)S(1)} %get-tuple-element.12), channel_id=1, source_target_pairs={{0,1},{1,2},{2,3},{4,5},{5,6},{6,7},{8,9},{9,10},{10,11},{12,13},{... | collective-permute-start | bytes 59624 | tf_op jit(solution)/shard_map/ppermute | solution.py:216
  31.9 2.3 %copy-start.4 = (f32[69,24,3]{0,1,2:T(8,128)}, f32[69,24,3]{0,1,2:T(8,128)S(1)}, u32[]{:S(2)}) copy-start(f32[69,24,3]{0,1,2:T(8,128)S(1)} %collective-permute-done.2) | copy-start | bytes 59620
  34.1 0.6 %copy-start.5 = (f32[69,24,3]{0,1,2:T(8,128)}, f32[69,24,3]{0,1,2:T(8,128)S(1)}, u32[]{:S(2)}) copy-start(f32[69,24,3]{0,1,2:T(8,128)S(1)} %collective-permute-done.3) | copy-start | bytes 59620
  37.2 6.1 %copy-start.8 = (s32[8,3]{0,1:T(4,128)S(1)}, s32[8,3]{0,1:T(4,128)}, u32[]{:S(2)}) copy-start(s32[8,3]{0,1:T(4,128)} %param.12) | copy-start | bytes 292
  39.1 11.4 %all-to-all-start.1 = ((f32[8,8,128]{2,1,0:T(8,128)}), f32[8,8,128]{2,1,0:T(8,128)S(1)}, u32[]{:S(2)}, u32[]{:S(2)}) async-start(f32[8,8,128]{2,1,0:T(8,128)} %fusion.2), calls=%async_computation.1 | async-start | bytes 65536 | tf_op jit(solution)/shard_map/all_to_all | solution.py:231

commit v21 on v16

--- a/solution.py
+++ b/solution.py
@@ -203,6 +203,7 @@
     low, high = shifted(packed, "ox", 1, STEPS)
     low = with_layout_constraint(low, Layout((0, 1, 2)))
     high = with_layout_constraint(high, Layout((0, 1, 2)))
+    aux, high, low = lax.optimization_barrier((aux, high, low))
     gap = jnp.zeros((packed.shape[0], tall - rows - 2 * STEPS, STEPS), jnp.float32)
     south_edge = jnp.concatenate(
         [packed[:, :, -STEPS:], high[:, :, -STEPS:], gap, low[:, :, -STEPS:]], axis=1

time: 51.8 us -> 51.7 us (level)
    all_to_all x1, waiting for transfers between devices: 2.32 us -> 2.9 us  [per_device(): incoming = lax.all_to_all(outgoing, 'ox', 0, 0, tiled=True)]
    unnamed x25 -> x21, local copies, waits for them, and re-layouts: 2.47 us -> 2 us
  transfers between devices with their start and end apart: 6 -> 6, of which waited for: 3 -> 3; matrix products, arithmetic and copies ran while one was open for 10% -> 9% of each run, Pallas kernels for 14% -> 14%
where the time goes in v21:
time: 51.7 us; the launch traced here: 50.6 us
  starting transfers between devices  22.8 us (44%)
  Pallas kernels  9.51 us (18%)
  local copies, waits for them, and re-layouts  7.02 us (14%)
  waiting for transfers between devices  5.64 us (11%)
  matrix products  2.85 us (6%)
  other arithmetic  2.06 us (4%)
  between operations  0.77 us (1%)
    pallas_call x2, Pallas kernels, call(): pl.pallas_call(functools.partial(stencil_kernel, surface_only=surface_onl...  9.51 us
    all_to_all x1, starting transfers between devices, per_device(): incoming = lax.all_to_all(outgoing, 'ox', 0, 0, tiled=True)  6.35 us
    all_to_all x1, starting transfers between devices, per_device(): returned = lax.all_to_all(per_slot, 'ox', 0, 0, tiled=True)  4.3 us
    ppermute x1, starting transfers between devices, shifted(): lax.ppermute(lax.slice_in_dim(block, size - width, None, axis=dim), axis,...  3.99 us
    ppermute x1, starting transfers between devices, per_device(): north = jnp.transpose(lax.ppermute(north_edge, 'oy', backward), (2, 1, 0))  3.8 us
    ppermute x1, starting transfers between devices, per_device(): south = jnp.transpose(lax.ppermute(south_edge, 'oy', forward), (2, 1, 0))  3.05 us
    all_to_all x1, waiting for transfers between devices, per_device(): incoming = lax.all_to_all(outgoing, 'ox', 0, 0, tiled=True)  2.9 us
    ppermute x1, waiting for transfers between devices, shifted(): lax.ppermute(lax.slice_in_dim(block, size - width, None, axis=dim), axis,...  2.29 us
  transfers between devices with their start and end apart: 6, of which 3 were waited for; matrix products, arithmetic and copies ran while one was open for 9% of the time, Pallas kernels for 14%

profile of v21, /device:TPU:1, one launch (start us, length us, event | category | flops | bytes accessed | tf_op | source)
XLA Modules:
  0.0 50.6 jit_solution(15332899365848250036)
XLA Ops:
  0.6 0.0 copy-start
  0.6 1.5 %broadcast_in_dim.10 = bf16[8,4,10,128]{3,1,2,0:T(4,128)(2,1)} broadcast(bf16[4,10,128]{2,0,1:T(4,128)(2,1)} %param.8), dimensions={1,2,3} | broadcast | bytes 92160 | tf_op jit(solution)/shard_map/broadcast_in_dim | solution.py:187
  2.1 6.4 %all-to-all-start = ((bf16[8,4,10,128]{3,1,2,0:T(4,128)(2,1)}), bf16[8,4,10,128]{3,1,2,0:T(4,128)(2,1)S(1)}, u32[]{:S(2)}, u32[]{:S(2)}) async-start(bf16[8,4,10,128]{3,1,2,0:T(4,128)(2,1)} %broadcast_in_dim.10), calls=%async_computation | async-start | bytes 163840 | tf_op jit(solution)/shard_map/all_to_all | solution.py:188
  8.5 0.7 %compare_select_fusion.2 = s32[16,3]{0,1:T(4,128)S(1)} fusion(s32[16,3]{0,1:T(4,128)} %param.10), kind=kLoop, calls=%fused_computation.22 | loop fusion | flops 144 | bytes 384 | tf_op jit(solution)/shard_map/select_n | solution.py:190
  9.2 0.1 copy.40
  9.2 0.1 reshape.71
  9.4 0.8 %copy.39 = s32[8,3]{1,0:T(8,128)S(1)} copy(s32[8,3]{0,1:T(4,128)} %param.11) | data formatting | bytes 192 | tf_op args[3]
  10.1 0.1 reshape.67
  10.2 0.8 %gather_fusion = s32[48]{0:T(128)S(1)} fusion(s32[24]{0:T(128)S(1)} %reshape.67, s32[1024]{0:T(1024)S(1)} %pad_clamp_fusion), kind=kCustom, calls=%fused_computation | custom fusion | bytes 576 | tf_op jit(solution)/shard_map/gather | solution.py:190
  11.0 0.1 gather.9
  11.1 0.1 copy.41
  11.1 0.0 copy-done.6
  11.2 0.1 copy.44
  11.3 0.1 reshape.77
  11.4 0.1 pad.6.clone
  11.4 0.0 copy-done.7
  11.4 2.9 %all-to-all-done = bf16[8,4,10,128]{3,1,2,0:T(4,128)(2,1)S(1)} async-done(((bf16[8,4,10,128]{3,1,2,0:T(4,128)(2,1)}), bf16[8,4,10,128]{3,1,2,0:T(4,128)(2,1)S(1)}, u32[]{:S(2)}, u32[]{:S(2)}) %all-to-all-start) | async-done | bytes 81952 | tf_op jit(solution)/shard_map/all_to_all | solution.py:188
  14.3 0.9 %gather_fusion.1 = bf16[48,4,128]{2,1,0:T(4,128)(2,1)S(1)} fusion(bf16[8,4,10,128]{3,1,2,0:T(4,128)(2,1)S(1)} %all-to-all-done, s32[48]{0:T(128)S(1)} %reshape.77), kind=kCustom, calls=%fused_computation.1 | custom fusion | bytes 98688 | tf_op jit(solution)/shard_map/gather | solution.py:191
  15.2 0.6 %convolution_bitcast_fusion = f32[16,4,128]{2,1,0:T(4,128)S(1)} fusion(bf16[16,3,4,128]{3,2,1,0:T(4,128)(2,1)S(1)} %bitcast.34, bf16[16,3,128,128]{3,2,1,0:T(8,128)(2,1)S(1)} %copy-done), kind=kOutput, calls=%fused_computation.2 | convolution fusion | flops 6291456 | bytes 1654784 | tf_op jit(solution)/shard_map/tkfa,tkra->ftr/dot_general | solution.py:192
  15.9 0.1 pad_maximum_fusion
  15.9 0.1 fusion.21
  16.0 0.2 fusion.20
  16.2 1.3 %collective-permute-start = (f32[69,3,128]{2,1,0:T(4,128)S(1)}, f32[69,3,128]{2,1,0:T(4,128)S(1)}, u32[]{:S(2)}, u32[]{:S(2)}) collective-permute-start(f32[69,3,128]{2,1,0:T(4,128)S(1)} %get-tuple-element.11), channel_id=1, source_target_pairs={{4,0},{8,4},{12,8},{16,12},{20,16},{24,20},{28,24},{5,1},{9,5},{13... | collective-permute-start | bytes 317960 | tf_op jit(solution)/shard_map/ppermute | solution.py:161
  17.5 4.0 %collective-permute-start.1 = (f32[69,3,128]{2,1,0:T(4,128)S(1)}, f32[69,3,128]{2,1,0:T(4,128)S(1)}, u32[]{:S(2)}, u32[]{:S(2)}) collective-permute-start(f32[69,3,128]{2,1,0:T(4,128)S(1)} %get-tuple-element.10), channel_id=1, source_target_pairs={{0,4},{4,8},{8,12},{12,16},{16,20},{20,24},{24,28},{1,5},{5,9},{9,... | collective-permute-start | bytes 317960 | tf_op jit(solution)/shard_map/ppermute | solution.py:160
  21.5 0.3 copy.56
  21.8 0.3 copy.57
  22.1 0.6 %pad_maximum_fusion.1.aux_ref = f32[5,16,128]{2,1,0:T(8,128)} fusion(f32[1,16,128]{2,1,0:T(8,128)S(1)} %convert_bitcast_fusion, f32[4,16,128]{2,1,0:T(8,128)S(1)} %bitcast.33), kind=kLoop, calls=%fused_computation.6 | loop fusion | flops 10240 | bytes 81920 | tf_op jit(solution)/shard_map/concatenate | solution.py:198
  22.7 0.0 collective-permute-done.high_ref
  22.7 2.3 %collective-permute-done.1.low_ref = f32[69,3,128]{2,1,0:T(4,128)S(1)} collective-permute-done((f32[69,3,128]{2,1,0:T(4,128)S(1)}, f32[69,3,128]{2,1,0:T(4,128)S(1)}, u32[]{:S(2)}, u32[]{:S(2)}) %collective-permute-start.1) | collective-permute-done | bytes 106016 | tf_op jit(solution)/shard_map/ppermute | solution.py:160
  25.0 0.2 copy.47
  25.2 0.2 copy.48
  25.4 0.1 pad_maximum_fusion.3
  25.5 3.8 %collective-permute-start.2 = (f32[69,24,3]{0,1,2:T(8,128)S(1)}, f32[69,24,3]{0,1,2:T(8,128)S(1)}, u32[]{:S(2)}, u32[]{:S(2)}) collective-permute-start(f32[69,24,3]{0,1,2:T(8,128)S(1)} %get-tuple-element.17), channel_id=1, source_target_pairs={{1,0},{2,1},{3,2},{5,4},{6,5},{7,6},{9,8},{10,9},{11,10},{13,12},{... | collective-permute-start | bytes 59624 | tf_op jit(solution)/shard_map/ppermute | solution.py:218
  29.3 3.0 %collective-permute-start.3 = (f32[69,24,3]{0,1,2:T(8,128)S(1)}, f32[69,24,3]{0,1,2:T(8,128)S(1)}, u32[]{:S(2)}, u32[]{:S(2)}) collective-permute-start(f32[69,24,3]{0,1,2:T(8,128)S(1)} %get-tuple-element.16), channel_id=1, source_target_pairs={{0,1},{1,2},{2,3},{4,5},{5,6},{6,7},{8,9},{9,10},{10,11},{12,13},{... | collective-permute-start | bytes 59624 | tf_op jit(solution)/shard_map/ppermute | solution.py:217
  32.3 0.6 %fusion.19.cor_ref = f32[1,256]{1,0:T(1,128)} fusion(s32[]{:T(128)S(6)} %mul.16), kind=kLoop, calls=%fused_computation.40 | loop fusion | flops 2304 | bytes 1028 | tf_op jit(solution)/shard_map/mul | solution.py:222
  32.9 0.0 collective-permute-done.2
  32.9 0.4 collective-permute-done.3
  33.4 0.0 copy-done.3
  33.4 0.2 copy-done.4
  33.5 0.4 copy-done.5
  34.0 2.4 %shard_map.96 = bf16[16,128]{1,0:T(8,128)(2,1)} custom-call(f32[16]{0:T(128)} %diff_ref.3, f32[1,256]{1,0:T(1,128)} %fusion.19.cor_ref, f32[64,16,128]{2,1,0:T(8,128)} %bitcast.29, f32[5,16,128]{2,1,0:T(8,128)} %pad_maximum_fusion.1.aux_ref, f32[69,3,128]{2,1,0:T(4,128)} %copy-done.2, f32[69,3,128]{2,1,0:T(4,128)} %copy-done.3, f32[3,24,69]{2,1,0:T(8,128)} %bitcast.35, ...), custom_call_target="tpu_custom_call" | custom-call | tf_op jit(solution)/shard_map/pallas_call | solution.py:140
  36.4 1.1 %fusion.4 = f32[16,1,3,128]{3,1,2,0:T(1,128)S(1)} fusion(bf16[16,3,128,128]{3,2,1,0:T(8,128)(2,1)S(1)} %copy-done, bf16[16,128,1,1]{1,0,2,3:T(8,128)(2,1)} %bitcast.39), kind=kOutput, calls=%fused_computation.16 | convolution fusion | flops 1572864 | bytes 1601536 | tf_op jit(solution)/shard_map/tkra,tr->tka/dot_general | solution.py:225
  37.5 0.3 convolution_bitcast_fusion.1
  37.8 0.6 %reshape.68 = f32[8,3,128]{2,1,0:T(4,128)} reshape(f32[24,128]{1,0:T(8,128)S(1)} %convolution_bitcast_fusion.1) | data formatting | bytes 24576 | tf_op jit(solution)/shard_map/reshape | solution.py:229
  38.4 4.3 %all-to-all-start.1 = ((f32[8,3,128]{2,1,0:T(4,128)}), f32[8,3,128]{2,1,0:T(4,128)S(1)}, u32[]{:S(2)}, u32[]{:S(2)}) async-start(f32[8,3,128]{2,1,0:T(4,128)} %reshape.68), calls=%async_computation.1 | async-start | bytes 32768 | tf_op jit(solution)/shard_map/all_to_all | solution.py:230
  42.7 7.1 %shard_map.95 = f32[4,16,16,128]{3,2,1,0:T(8,128)} custom-call(f32[16]{0:T(128)} %diff_ref.3, f32[1,256]{1,0:T(1,128)} %fusion.19.cor_ref, f32[64,16,128]{2,1,0:T(8,128)} %bitcast.30, f32[5,16,128]{2,1,0:T(8,128)} %pad_maximum_fusion.1.aux_ref, f32[69,3,128]{2,1,0:T(4,128)} %copy-done.2, f32[69,3,128]{2,1,0:T(4,128)} %copy-done.3, f32[3,24,69]{2,1,0:T(8,128)} %bitcast.36, ...), custom_call_target="tpu_custom_call" | custom-call | tf_op jit(solution)/shard_map/pallas_call | solution.py:140
  49.8 0.0 all-to-all-done.1
  49.8 0.9 %convolution_bitcast_fusion.2 = f32[10,128]{1,0:T(8,128)} fusion(f32[8,3,128]{2,1,0:T(4,128)S(1)} %all-to-all-done.1, s32[8,3]{0,1:T(4,128)S(1)} %copy-done.8), kind=kOutput, calls=%fused_computation.4 | convolution fusion | flops 368880 | bytes 17504 | tf_op jit(solution)/shard_map/isb,isa->ba/dot_general | solution.py:231
  (18 shorter events, 0.1 us)
Async XLA Ops:
  0.6 14.6 %copy-start = (bf16[16,3,128,128]{3,2,1,0:T(8,128)(2,1)S(1)}, bf16[16,3,128,128]{3,2,1,0:T(8,128)(2,1)}, u32[]{:S(2)}) copy-start(bf16[16,3,128,128]{3,2,1,0:T(8,128)(2,1)} %param.9) | copy-start | bytes 4718596
  2.1 12.2 %all-to-all-start = ((bf16[8,4,10,128]{3,1,2,0:T(4,128)(2,1)}), bf16[8,4,10,128]{3,1,2,0:T(4,128)(2,1)S(1)}, u32[]{:S(2)}, u32[]{:S(2)}) async-start(bf16[8,4,10,128]{3,1,2,0:T(4,128)(2,1)} %broadcast_in_dim.10), calls=%async_computation | async-start | bytes 163840 | tf_op jit(solution)/shard_map/all_to_all | solution.py:188
  10.2 1.0 %copy-start.6 = (s32[16,3]{0,1:T(4,128)S(1)}, s32[16,3]{0,1:T(4,128)}, u32[]{:S(2)}) copy-start(s32[16,3]{0,1:T(4,128)} %param.10) | copy-start | bytes 580
  10.2 1.2 %copy-start.7 = (s32[16,128]{1,0:T(8,128)S(1)}, s32[16,128]{1,0:T(8,128)}, u32[]{:S(2)}) copy-start(s32[16,128]{1,0:T(8,128)} %param.14) | copy-start | bytes 24580
  11.0 4.9 %copy-start.1 = (f32[4,16,16,128]{3,2,1,0:T(8,128)S(1)}, f32[4,16,16,128]{3,2,1,0:T(8,128)}, u32[]{:S(2)}) copy-start(f32[4,16,16,128]{3,2,1,0:T(8,128)} %param.13) | copy-start | bytes 1572868
  16.2 6.5 %collective-permute-start = (f32[69,3,128]{2,1,0:T(4,128)S(1)}, f32[69,3,128]{2,1,0:T(4,128)S(1)}, u32[]{:S(2)}, u32[]{:S(2)}) collective-permute-start(f32[69,3,128]{2,1,0:T(4,128)S(1)} %get-tuple-element.11), channel_id=1, source_target_pairs={{4,0},{8,4},{12,8},{16,12},{20,16},{24,20},{28,24},{5,1},{9,5},{13... | collective-permute-start | bytes 317960 | tf_op jit(solution)/shard_map/ppermute | solution.py:161
  17.5 7.5 %collective-permute-start.1 = (f32[69,3,128]{2,1,0:T(4,128)S(1)}, f32[69,3,128]{2,1,0:T(4,128)S(1)}, u32[]{:S(2)}, u32[]{:S(2)}) collective-permute-start(f32[69,3,128]{2,1,0:T(4,128)S(1)} %get-tuple-element.10), channel_id=1, source_target_pairs={{0,4},{4,8},{8,12},{12,16},{16,20},{20,24},{24,28},{1,5},{5,9},{9,... | collective-permute-start | bytes 317960 | tf_op jit(solution)/shard_map/ppermute | solution.py:160
  22.7 10.6 %copy-start.2 = (f32[69,3,128]{2,1,0:T(4,128)}, f32[69,3,128]{2,1,0:T(4,128)S(1)}, u32[]{:S(2)}) copy-start(f32[69,3,128]{2,1,0:T(4,128)S(1)} %collective-permute-done.high_ref) | copy-start | bytes 317956
  25.0 8.3 %copy-start.3 = (f32[69,3,128]{2,1,0:T(4,128)}, f32[69,3,128]{2,1,0:T(4,128)S(1)}, u32[]{:S(2)}) copy-start(f32[69,3,128]{2,1,0:T(4,128)S(1)} %collective-permute-done.1.low_ref) | copy-start | bytes 317956
  25.5 7.5 %collective-permute-start.2 = (f32[69,24,3]{0,1,2:T(8,128)S(1)}, f32[69,24,3]{0,1,2:T(8,128)S(1)}, u32[]{:S(2)}, u32[]{:S(2)}) collective-permute-start(f32[69,24,3]{0,1,2:T(8,128)S(1)} %get-tuple-element.17), channel_id=1, source_target_pairs={{1,0},{2,1},{3,2},{5,4},{6,5},{7,6},{9,8},{10,9},{11,10},{13,12},{... | collective-permute-start | bytes 59624 | tf_op jit(solution)/shard_map/ppermute | solution.py:218
  29.3 4.1 %collective-permute-start.3 = (f32[69,24,3]{0,1,2:T(8,128)S(1)}, f32[69,24,3]{0,1,2:T(8,128)S(1)}, u32[]{:S(2)}, u32[]{:S(2)}) collective-permute-start(f32[69,24,3]{0,1,2:T(8,128)S(1)} %get-tuple-element.16), channel_id=1, source_target_pairs={{0,1},{1,2},{2,3},{4,5},{5,6},{6,7},{8,9},{9,10},{10,11},{12,13},{... | collective-permute-start | bytes 59624 | tf_op jit(solution)/shard_map/ppermute | solution.py:217
  32.9 0.6 %copy-start.4 = (f32[69,24,3]{0,1,2:T(8,128)}, f32[69,24,3]{0,1,2:T(8,128)S(1)}, u32[]{:S(2)}) copy-start(f32[69,24,3]{0,1,2:T(8,128)S(1)} %collective-permute-done.2) | copy-start | bytes 59620
  33.4 0.6 %copy-start.5 = (f32[69,24,3]{0,1,2:T(8,128)}, f32[69,24,3]{0,1,2:T(8,128)S(1)}, u32[]{:S(2)}) copy-start(f32[69,24,3]{0,1,2:T(8,128)S(1)} %collective-permute-done.3) | copy-start | bytes 59620
  36.4 13.4 %copy-start.8 = (s32[8,3]{0,1:T(4,128)S(1)}, s32[8,3]{0,1:T(4,128)}, u32[]{:S(2)}) copy-start(s32[8,3]{0,1:T(4,128)} %param.12) | copy-start | bytes 292
  38.4 11.4 %all-to-all-start.1 = ((f32[8,3,128]{2,1,0:T(4,128)}), f32[8,3,128]{2,1,0:T(4,128)S(1)}, u32[]{:S(2)}, u32[]{:S(2)}) async-start(f32[8,3,128]{2,1,0:T(4,128)} %reshape.68), calls=%async_computation.1 | async-start | bytes 32768 | tf_op jit(solution)/shard_map/all_to_all | solution.py:230

commit v22 on v21

--- a/solution.py
+++ b/solution.py
@@ -188,7 +188,13 @@
     incoming = lax.all_to_all(outgoing, "ox", 0, 0, tiled=True)
     owner_of = tile_slots // capacity
     block_of = need_blocks.reshape(-1)[tile_slots]
-    picks = incoming[owner_of, :, block_of, :]
+    owner_line = jnp.arange(owners, dtype=jnp.int32)
+    choose = (owner_of[:, :, None, None] == owner_line[None, None, :, None]) & (
+        block_of[:, :, None, None] == block_line[None, None, None, :]
+    )
+    picks = jnp.einsum(
+        "tkqb,qfba->tkfa", choose.astype(incoming.dtype), incoming, preferred_element_type=jnp.float32
+    ).astype(incoming.dtype)
     forcing = jnp.einsum("tkfa,tkra->ftr", picks, remap_weights, preferred_element_type=jnp.float32)
     fields, levels, rows, lat_cells = ocean_state.shape
     lat_total = lat_cells * lax.axis_size("oy")

time: 51.7 us -> 51.1 us (0.988)
  local copies, waits for them, and re-layouts: 7.02 us -> 5.96 us
    gather x1 -> x0, local copies, waits for them, and re-layouts: 0.89 us -> none  [per_device(): picks = incoming[owner_of, :, block_of, :]]
where the time goes in v22:
time: 51.1 us; the launch traced here: 50.1 us
  starting transfers between devices  22.8 us (45%)
  Pallas kernels  9.51 us (19%)
  local copies, waits for them, and re-layouts  5.96 us (12%)
  waiting for transfers between devices  5.75 us (11%)
  matrix products  3.16 us (6%)
  other arithmetic  2.11 us (4%)
  between operations  0.79 us (2%)
    pallas_call x2, Pallas kernels, call(): pl.pallas_call(functools.partial(stencil_kernel, surface_only=surface_onl...  9.51 us
    all_to_all x1, starting transfers between devices, per_device(): incoming = lax.all_to_all(outgoing, 'ox', 0, 0, tiled=True)  6.35 us
    all_to_all x1, starting transfers between devices, per_device(): returned = lax.all_to_all(per_slot, 'ox', 0, 0, tiled=True)  4.3 us
    ppermute x1, starting transfers between devices, shifted(): lax.ppermute(lax.slice_in_dim(block, size - width, None, axis=dim), axis,...  3.99 us
    ppermute x1, starting transfers between devices, per_device(): north = jnp.transpose(lax.ppermute(north_edge, 'oy', backward), (2, 1, 0))  3.8 us
    ppermute x1, starting transfers between devices, per_device(): south = jnp.transpose(lax.ppermute(south_edge, 'oy', forward), (2, 1, 0))  3.05 us
    all_to_all x1, waiting for transfers between devices, per_device(): incoming = lax.all_to_all(outgoing, 'ox', 0, 0, tiled=True)  2.99 us
    ppermute x1, waiting for transfers between devices, shifted(): lax.ppermute(lax.slice_in_dim(block, size - width, None, axis=dim), axis,...  2.29 us
  transfers between devices with their start and end apart: 6, of which 3 were waited for; matrix products, arithmetic and copies ran while one was open for 9% of the time, Pallas kernels for 14%

profile of v22, /device:TPU:1, one launch (start us, length us, event | category | flops | bytes accessed | tf_op | source)
XLA Modules:
  0.0 50.1 jit_solution(8737938745123140099)
XLA Ops:
  0.6 0.0 copy-start
  0.6 1.5 %broadcast_in_dim.9 = bf16[8,4,10,128]{3,1,2,0:T(4,128)(2,1)} broadcast(bf16[4,10,128]{2,0,1:T(4,128)(2,1)} %param.8), dimensions={1,2,3} | broadcast | bytes 92160 | tf_op jit(solution)/shard_map/broadcast_in_dim | solution.py:187
  2.1 6.4 %all-to-all-start = ((bf16[8,4,10,128]{3,1,2,0:T(4,128)(2,1)}), bf16[8,4,10,128]{3,1,2,0:T(4,128)(2,1)S(1)}, u32[]{:S(2)}, u32[]{:S(2)}) async-start(bf16[8,4,10,128]{3,1,2,0:T(4,128)(2,1)} %broadcast_in_dim.9), calls=%async_computation | async-start | bytes 163840 | tf_op jit(solution)/shard_map/all_to_all | solution.py:188
  8.5 0.7 %add_select_fusion = (s32[16,3]{0,1:T(4,128)S(1)}, s32[16,3]{0,1:T(4,128)S(1)}) fusion(s32[16,3]{0,1:T(4,128)} %param.10), kind=kLoop, calls=%fused_computation.33 | loop fusion | flops 528 | bytes 576 | tf_op jit(solution)/shard_map/jit(floor_divide)/jit(_where)/select_n | solution.py:189
  9.2 0.1 copy.35
  9.3 0.1 reshape.74
  9.4 0.8 %copy.34 = s32[8,3]{1,0:T(8,128)S(1)} copy(s32[8,3]{0,1:T(4,128)} %param.11) | data formatting | bytes 192 | tf_op args[3]
  10.1 0.1 reshape.70
  10.2 0.8 %gather_fusion = s32[48]{0:T(128)S(1)} fusion(s32[24]{0:T(128)S(1)} %reshape.70, s32[1024]{0:T(1024)S(1)} %pad_clamp_fusion), kind=kCustom, calls=%fused_computation | custom fusion | bytes 576 | tf_op jit(solution)/shard_map/gather | solution.py:190
  11.0 0.1 reshape.73
  11.1 0.1 copy.36
  11.1 0.1 iota_compare_fusion.1
  11.2 0.0 copy-done.6
  11.3 0.1 pad.6.clone
  11.3 3.0 %all-to-all-done = bf16[8,4,10,128]{3,1,2,0:T(4,128)(2,1)S(1)} async-done(((bf16[8,4,10,128]{3,1,2,0:T(4,128)(2,1)}), bf16[8,4,10,128]{3,1,2,0:T(4,128)(2,1)S(1)}, u32[]{:S(2)}, u32[]{:S(2)}) %all-to-all-start) | async-done | bytes 81952 | tf_op jit(solution)/shard_map/all_to_all | solution.py:188
  14.3 0.3 fusion
  14.7 0.0 copy-done
  14.7 0.6 %convolution_bitcast_fusion.1 = f32[16,4,128]{2,1,0:T(4,128)S(1)} fusion(bf16[16,3,128,128]{3,2,1,0:T(8,128)(2,1)S(1)} %copy-done, bf16[16,3,4,128]{3,0,2,1:T(8,128)(2,1)S(1)} %fusion), kind=kOutput, calls=%fused_computation.3 | convolution fusion | flops 6291456 | bytes 1654784 | tf_op jit(solution)/shard_map/tkfa,tkra->ftr/dot_general | solution.py:198
  15.3 0.1 pad_maximum_fusion
  15.4 0.1 fusion.23
  15.4 0.2 fusion.22
  15.7 1.3 %collective-permute-start = (f32[69,3,128]{2,1,0:T(4,128)S(1)}, f32[69,3,128]{2,1,0:T(4,128)S(1)}, u32[]{:S(2)}, u32[]{:S(2)}) collective-permute-start(f32[69,3,128]{2,1,0:T(4,128)S(1)} %get-tuple-element.11), channel_id=1, source_target_pairs={{4,0},{8,4},{12,8},{16,12},{20,16},{24,20},{28,24},{5,1},{9,5},{13... | collective-permute-start | bytes 317960 | tf_op jit(solution)/shard_map/ppermute | solution.py:161
  17.0 4.0 %collective-permute-start.1 = (f32[69,3,128]{2,1,0:T(4,128)S(1)}, f32[69,3,128]{2,1,0:T(4,128)S(1)}, u32[]{:S(2)}, u32[]{:S(2)}) collective-permute-start(f32[69,3,128]{2,1,0:T(4,128)S(1)} %get-tuple-element.10), channel_id=1, source_target_pairs={{0,4},{4,8},{8,12},{12,16},{16,20},{20,24},{24,28},{1,5},{5,9},{9,... | collective-permute-start | bytes 317960 | tf_op jit(solution)/shard_map/ppermute | solution.py:160
  21.0 0.3 copy.52
  21.3 0.3 copy.53
  21.6 0.6 %pad_maximum_fusion.1.aux_ref = f32[5,16,128]{2,1,0:T(8,128)} fusion(f32[1,16,128]{2,1,0:T(8,128)S(1)} %convert_bitcast_fusion, f32[4,16,128]{2,1,0:T(8,128)S(1)} %bitcast.38), kind=kLoop, calls=%fused_computation.14 | loop fusion | flops 10240 | bytes 81920 | tf_op jit(solution)/shard_map/concatenate | solution.py:204
  22.2 0.0 collective-permute-done.high_ref
  22.2 2.3 %collective-permute-done.1.low_ref = f32[69,3,128]{2,1,0:T(4,128)S(1)} collective-permute-done((f32[69,3,128]{2,1,0:T(4,128)S(1)}, f32[69,3,128]{2,1,0:T(4,128)S(1)}, u32[]{:S(2)}, u32[]{:S(2)}) %collective-permute-start.1) | collective-permute-done | bytes 106016 | tf_op jit(solution)/shard_map/ppermute | solution.py:160
  24.5 0.2 copy.41
  24.6 0.0 copy-start.7
  24.6 0.2 copy.42
  24.8 0.1 pad_maximum_fusion.3
  24.9 3.8 %collective-permute-start.2 = (f32[69,24,3]{0,1,2:T(8,128)S(1)}, f32[69,24,3]{0,1,2:T(8,128)S(1)}, u32[]{:S(2)}, u32[]{:S(2)}) collective-permute-start(f32[69,24,3]{0,1,2:T(8,128)S(1)} %get-tuple-element.19), channel_id=1, source_target_pairs={{1,0},{2,1},{3,2},{5,4},{6,5},{7,6},{9,8},{10,9},{11,10},{13,12},{... | collective-permute-start | bytes 59624 | tf_op jit(solution)/shard_map/ppermute | solution.py:224
  28.7 3.0 %collective-permute-start.3 = (f32[69,24,3]{0,1,2:T(8,128)S(1)}, f32[69,24,3]{0,1,2:T(8,128)S(1)}, u32[]{:S(2)}, u32[]{:S(2)}) collective-permute-start(f32[69,24,3]{0,1,2:T(8,128)S(1)} %get-tuple-element.18), channel_id=1, source_target_pairs={{0,1},{1,2},{2,3},{4,5},{5,6},{6,7},{8,9},{9,10},{10,11},{12,13},{... | collective-permute-start | bytes 59624 | tf_op jit(solution)/shard_map/ppermute | solution.py:223
  31.8 0.6 %fusion.21.cor_ref = f32[1,256]{1,0:T(1,128)} fusion(s32[]{:T(128)S(6)} %mul.16), kind=kLoop, calls=%fused_computation.42 | loop fusion | flops 2304 | bytes 1028 | tf_op jit(solution)/shard_map/mul | solution.py:228
  32.3 0.0 collective-permute-done.2
  32.3 0.5 collective-permute-done.3
  32.8 0.0 copy-done.2
  32.8 0.2 copy-done.4
  33.0 0.4 copy-done.5
  33.4 2.4 %shard_map.96 = bf16[16,128]{1,0:T(8,128)(2,1)} custom-call(f32[16]{0:T(128)} %diff_ref.3, f32[1,256]{1,0:T(1,128)} %fusion.21.cor_ref, f32[64,16,128]{2,1,0:T(8,128)} %bitcast.34, f32[5,16,128]{2,1,0:T(8,128)} %pad_maximum_fusion.1.aux_ref, f32[69,3,128]{2,1,0:T(4,128)} %copy-done.2, f32[69,3,128]{2,1,0:T(4,128)} %copy-done.3, f32[3,24,69]{2,1,0:T(8,128)} %bitcast.39, ...), custom_call_target="tpu_custom_call" | custom-call | tf_op jit(solution)/shard_map/pallas_call | solution.py:140
  35.9 1.1 %fusion.12 = f32[16,1,3,128]{3,1,2,0:T(1,128)S(1)} fusion(bf16[16,3,128,128]{3,2,1,0:T(8,128)(2,1)S(1)} %copy-done, bf16[16,128,1,1]{1,0,2,3:T(8,128)(2,1)} %bitcast.43), kind=kOutput, calls=%fused_computation.26 | convolution fusion | flops 1572864 | bytes 1601536 | tf_op jit(solution)/shard_map/tkra,tr->tka/dot_general | solution.py:231
  36.9 0.3 convolution_bitcast_fusion.2
  37.2 0.6 %reshape.71 = f32[8,3,128]{2,1,0:T(4,128)} reshape(f32[24,128]{1,0:T(8,128)S(1)} %convolution_bitcast_fusion.2) | data formatting | bytes 24576 | tf_op jit(solution)/shard_map/reshape | solution.py:235
  37.8 4.3 %all-to-all-start.1 = ((f32[8,3,128]{2,1,0:T(4,128)}), f32[8,3,128]{2,1,0:T(4,128)S(1)}, u32[]{:S(2)}, u32[]{:S(2)}) async-start(f32[8,3,128]{2,1,0:T(4,128)} %reshape.71), calls=%async_computation.1 | async-start | bytes 32768 | tf_op jit(solution)/shard_map/all_to_all | solution.py:236
  42.1 7.1 %shard_map.95 = f32[4,16,16,128]{3,2,1,0:T(8,128)} custom-call(f32[16]{0:T(128)} %diff_ref.3, f32[1,256]{1,0:T(1,128)} %fusion.21.cor_ref, f32[64,16,128]{2,1,0:T(8,128)} %bitcast.35, f32[5,16,128]{2,1,0:T(8,128)} %pad_maximum_fusion.1.aux_ref, f32[69,3,128]{2,1,0:T(4,128)} %copy-done.2, f32[69,3,128]{2,1,0:T(4,128)} %copy-done.3, f32[3,24,69]{2,1,0:T(8,128)} %bitcast.40, ...), custom_call_target="tpu_custom_call" | custom-call | tf_op jit(solution)/shard_map/pallas_call | solution.py:140
  49.2 0.0 all-to-all-done.1
  49.2 0.9 %convolution_bitcast_fusion.3 = f32[10,128]{1,0:T(8,128)} fusion(f32[8,3,128]{2,1,0:T(4,128)S(1)} %all-to-all-done.1, s32[8,3]{0,1:T(4,128)S(1)} %copy-done.8), kind=kOutput, calls=%fused_computation.5 | convolution fusion | flops 368880 | bytes 17504 | tf_op jit(solution)/shard_map/isb,isa->ba/dot_general | solution.py:237
  (17 shorter events, 0.1 us)
Async XLA Ops:
  0.6 14.0 %copy-start = (bf16[16,3,128,128]{3,2,1,0:T(8,128)(2,1)S(1)}, bf16[16,3,128,128]{3,2,1,0:T(8,128)(2,1)}, u32[]{:S(2)}) copy-start(bf16[16,3,128,128]{3,2,1,0:T(8,128)(2,1)} %param.9) | copy-start | bytes 4718596
  2.1 12.2 %all-to-all-start = ((bf16[8,4,10,128]{3,1,2,0:T(4,128)(2,1)}), bf16[8,4,10,128]{3,1,2,0:T(4,128)(2,1)S(1)}, u32[]{:S(2)}, u32[]{:S(2)}) async-start(bf16[8,4,10,128]{3,1,2,0:T(4,128)(2,1)} %broadcast_in_dim.9), calls=%async_computation | async-start | bytes 163840 | tf_op jit(solution)/shard_map/all_to_all | solution.py:188
  10.2 1.0 %copy-start.6 = (s32[16,128]{1,0:T(8,128)S(1)}, s32[16,128]{1,0:T(8,128)}, u32[]{:S(2)}) copy-start(s32[16,128]{1,0:T(8,128)} %param.14) | copy-start | bytes 24580
  11.0 4.3 %copy-start.1 = (f32[4,16,16,128]{3,2,1,0:T(8,128)S(1)}, f32[4,16,16,128]{3,2,1,0:T(8,128)}, u32[]{:S(2)}) copy-start(f32[4,16,16,128]{3,2,1,0:T(8,128)} %param.13) | copy-start | bytes 1572868
  15.7 6.5 %collective-permute-start = (f32[69,3,128]{2,1,0:T(4,128)S(1)}, f32[69,3,128]{2,1,0:T(4,128)S(1)}, u32[]{:S(2)}, u32[]{:S(2)}) collective-permute-start(f32[69,3,128]{2,1,0:T(4,128)S(1)} %get-tuple-element.11), channel_id=1, source_target_pairs={{4,0},{8,4},{12,8},{16,12},{20,16},{24,20},{28,24},{5,1},{9,5},{13... | collective-permute-start | bytes 317960 | tf_op jit(solution)/shard_map/ppermute | solution.py:161
  17.0 7.5 %collective-permute-start.1 = (f32[69,3,128]{2,1,0:T(4,128)S(1)}, f32[69,3,128]{2,1,0:T(4,128)S(1)}, u32[]{:S(2)}, u32[]{:S(2)}) collective-permute-start(f32[69,3,128]{2,1,0:T(4,128)S(1)} %get-tuple-element.10), channel_id=1, source_target_pairs={{0,4},{4,8},{8,12},{12,16},{16,20},{20,24},{24,28},{1,5},{5,9},{9,... | collective-permute-start | bytes 317960 | tf_op jit(solution)/shard_map/ppermute | solution.py:160
  22.2 10.6 %copy-start.2 = (f32[69,3,128]{2,1,0:T(4,128)}, f32[69,3,128]{2,1,0:T(4,128)S(1)}, u32[]{:S(2)}) copy-start(f32[69,3,128]{2,1,0:T(4,128)S(1)} %collective-permute-done.high_ref) | copy-start | bytes 317956
  24.5 8.3 %copy-start.3 = (f32[69,3,128]{2,1,0:T(4,128)}, f32[69,3,128]{2,1,0:T(4,128)S(1)}, u32[]{:S(2)}) copy-start(f32[69,3,128]{2,1,0:T(4,128)S(1)} %collective-permute-done.1.low_ref) | copy-start | bytes 317956
  24.6 12.3 %copy-start.7 = (s32[16,3]{0,1:T(4,128)S(1)}, s32[16,3]{0,1:T(4,128)}, u32[]{:S(2)}) copy-start(s32[16,3]{0,1:T(4,128)} %param.10) | copy-start | bytes 580
  24.9 7.4 %collective-permute-start.2 = (f32[69,24,3]{0,1,2:T(8,128)S(1)}, f32[69,24,3]{0,1,2:T(8,128)S(1)}, u32[]{:S(2)}, u32[]{:S(2)}) collective-permute-start(f32[69,24,3]{0,1,2:T(8,128)S(1)} %get-tuple-element.19), channel_id=1, source_target_pairs={{1,0},{2,1},{3,2},{5,4},{6,5},{7,6},{9,8},{10,9},{11,10},{13,12},{... | collective-permute-start | bytes 59624 | tf_op jit(solution)/shard_map/ppermute | solution.py:224
  28.7 4.1 %collective-permute-start.3 = (f32[69,24,3]{0,1,2:T(8,128)S(1)}, f32[69,24,3]{0,1,2:T(8,128)S(1)}, u32[]{:S(2)}, u32[]{:S(2)}) collective-permute-start(f32[69,24,3]{0,1,2:T(8,128)S(1)} %get-tuple-element.18), channel_id=1, source_target_pairs={{0,1},{1,2},{2,3},{4,5},{5,6},{6,7},{8,9},{9,10},{10,11},{12,13},{... | collective-permute-start | bytes 59624 | tf_op jit(solution)/shard_map/ppermute | solution.py:223
  32.3 0.6 %copy-start.4 = (f32[69,24,3]{0,1,2:T(8,128)}, f32[69,24,3]{0,1,2:T(8,128)S(1)}, u32[]{:S(2)}) copy-start(f32[69,24,3]{0,1,2:T(8,128)S(1)} %collective-permute-done.2) | copy-start | bytes 59620
  32.8 0.6 %copy-start.5 = (f32[69,24,3]{0,1,2:T(8,128)}, f32[69,24,3]{0,1,2:T(8,128)S(1)}, u32[]{:S(2)}) copy-start(f32[69,24,3]{0,1,2:T(8,128)S(1)} %collective-permute-done.3) | copy-start | bytes 59620
  35.8 13.4 %copy-start.8 = (s32[8,3]{0,1:T(4,128)S(1)}, s32[8,3]{0,1:T(4,128)}, u32[]{:S(2)}) copy-start(s32[8,3]{0,1:T(4,128)} %param.12) | copy-start | bytes 292
  37.8 11.4 %all-to-all-start.1 = ((f32[8,3,128]{2,1,0:T(4,128)}), f32[8,3,128]{2,1,0:T(4,128)S(1)}, u32[]{:S(2)}, u32[]{:S(2)}) async-start(f32[8,3,128]{2,1,0:T(4,128)} %reshape.71), calls=%async_computation.1 | async-start | bytes 32768 | tf_op jit(solution)/shard_map/all_to_all | solution.py:236
